TPU v7x, 128 devices: a whole 4x4x4 slice. The times are simulated.
128 devices in a mesh: ctx: 16 (over z_lo, y, core), ch: 8 (over z_hi, x).
Axes of the slice: x: 4, y: 4, z: 4 (z_hi: 2, z_lo: 2; z = z_hi * 2 + z_lo), core: 2. Of those that a mesh axis runs over, the one named last changes fastest.
Arguments:
- inputs: bfloat16 [512, 512, 1024], P('ctx', None, 'ch'), may hold values from -600 to 600
- norm_gain: float32 [1024], P('ch'), may hold values from 0.1 to 1.9
- conv_taps: float32 [2, 3, 1024], P(None, None, 'ch'), may hold values from -3 to 3
- factor_one: bfloat16 [512, 512], replicated, may hold values from -0.25 to 0.25
- factor_two: bfloat16 [512, 512], replicated, may hold values from -0.25 to 0.25
- kernel: bfloat16 [512, 512, 1024], P(None, 'ctx', 'ch'), may hold values from -5 to 5
- grad_out: bfloat16 [512, 512, 1024], P('ctx', None, 'ch'), may hold values from -5 to 5
Outputs:
- input_grad: bfloat16 [512, 512, 1024], P('ctx', None, 'ch')
- kernel_grad: bfloat16 [512, 512, 1024], P(None, 'ctx', 'ch')
- factor_one_grad: float32 [512, 512], replicated
- factor_two_grad: float32 [512, 512], replicated
- gain_grad: float32 [1024], P('ch')
- taps_grad: float32 [2, 3, 1024], P(None, None, 'ch')
All inputs are finite; a program needn't handle non-finite values.
Results may differ from a plain program's by a relative error of at most 0.0081.
Values may be sent and summed in bfloat16 or wider, within the bound.
No kernel may reach another device: no remote copies, remote signals or barrier semaphores. Data moves between devices by JAX's collectives and lax.ppermute only.
A program may use at most 192 MiB of HBM per device.

v0:
```python
import math

import jax
import jax.numpy as jnp
from jax import lax
from jax.sharding import PartitionSpec as P

OUTER = 512
INNER = 512
WIDTH = 1024


def shifted(value, axis, steps):
    count = lax.axis_size(axis)
    initial, last = (max(0, -steps), min(count, count - steps))
    return lax.ppermute(value, axis, [(source, source + steps) for source in range(initial, last)])


def on_device(inputs, norm_gain, conv_taps, factor_one, factor_two, kernel, grad_out):
    local_outer, inner, chans = inputs.shape
    rows = local_outer * inner
    taps_count = conv_taps.shape[1]
    flat_in = inputs.reshape(rows, chans).astype(jnp.float32)
    squares = lax.psum(jnp.sum(flat_in * flat_in, axis=1), "ch")
    inverse = lax.rsqrt(squares / WIDTH + 1e-05)
    hat = flat_in * inverse[:, None]
    normed = (hat * norm_gain).astype(jnp.bfloat16)
    earlier = shifted(normed[rows - (taps_count - 1) :], "ctx", 1)
    extended = jnp.concatenate([earlier, normed], 0)
    value_pre = jnp.zeros((rows, chans), jnp.float32)
    gate_pre = jnp.zeros((rows, chans), jnp.float32)
    for offset in range(taps_count):
        window = extended[taps_count - 1 - offset : taps_count - 1 - offset + rows]
        value_pre = value_pre + conv_taps[0, offset] * window
        gate_pre = gate_pre + conv_taps[1, offset] * window
    mixed_in = value_pre.astype(jnp.bfloat16).reshape(local_outer, inner, chans)
    gate = jax.nn.sigmoid(gate_pre)
    cotangent = grad_out.reshape(rows, chans).astype(jnp.float32)
    section_one = jnp.einsum(
        "ijc,jk->ikc", mixed_in, factor_one, preferred_element_type=jnp.float32
    ).astype(jnp.bfloat16)
    out_grad = (cotangent * gate).astype(jnp.bfloat16).reshape(local_outer, inner, chans)
    columns = lax.all_to_all(section_one, "ctx", split_axis=1, concat_axis=0, tiled=True)
    kern = kernel.astype(jnp.float32)
    spectrum = (columns.astype(jnp.float32) * kern).astype(jnp.bfloat16)
    section_two = jnp.einsum(
        "ijc,ik->kjc", spectrum, factor_two, preferred_element_type=jnp.float32
    ).astype(jnp.bfloat16)
    back_rows = lax.all_to_all(section_two, "ctx", split_axis=0, concat_axis=1, tiled=True)
    grad_columns = lax.all_to_all(out_grad, "ctx", split_axis=1, concat_axis=0, tiled=True)
    grad_spec = jnp.einsum(
        "kjc,ik->ijc", grad_columns, factor_two, preferred_element_type=jnp.float32
    )
    kernel_grad = (grad_spec * columns.astype(jnp.float32)).astype(jnp.bfloat16)
    grad_section = (grad_spec * kern).astype(jnp.bfloat16)
    two_part = jnp.einsum("ijc,kjc->ik", spectrum, grad_columns, preferred_element_type=jnp.float32)
    grad_rows = lax.all_to_all(grad_section, "ctx", split_axis=0, concat_axis=1, tiled=True)
    back_flat = back_rows.reshape(rows, chans).astype(jnp.float32)
    grad_gate_pre = cotangent * back_flat * gate * (1.0 - gate)
    grad_mixed = jnp.einsum(
        "ikc,jk->ijc", grad_rows, factor_one, preferred_element_type=jnp.float32
    ).reshape(rows, chans)
    one_part = jnp.einsum("ijc,ikc->jk", mixed_in, grad_rows, preferred_element_type=jnp.float32)
    one_total, two_total = lax.psum((one_part, two_part), ("ctx", "ch"))
    later_value, later_gate = shifted(
        (grad_mixed[: taps_count - 1], grad_gate_pre[: taps_count - 1]), "ctx", -1
    )
    ext_value = jnp.concatenate([grad_mixed, later_value], 0)
    ext_gate = jnp.concatenate([grad_gate_pre, later_gate], 0)
    grad_normed = jnp.zeros((rows, chans), jnp.float32)
    value_taps = []
    gate_taps = []
    for offset in range(taps_count):
        grad_normed = grad_normed + conv_taps[0, offset] * ext_value[offset : offset + rows]
        grad_normed = grad_normed + conv_taps[1, offset] * ext_gate[offset : offset + rows]
        window = extended[taps_count - 1 - offset : taps_count - 1 - offset + rows]
        value_taps.append(jnp.sum(grad_mixed * window, axis=0))
        gate_taps.append(jnp.sum(grad_gate_pre * window, axis=0))
    tap_part = jnp.stack([jnp.stack(value_taps), jnp.stack(gate_taps)])
    gain_part = jnp.sum(grad_normed * hat, axis=0)
    gain_total, taps_total = lax.psum((gain_part, tap_part), "ctx")
    scaled = grad_normed * norm_gain
    row_mean = (
        lax.psum(jnp.sum(scaled * hat, axis=1).astype(jnp.bfloat16), "ch").astype(jnp.float32)
        / WIDTH
    )
    input_grad = (
        (inverse[:, None] * (scaled - hat * row_mean[:, None]))
        .astype(jnp.bfloat16)
        .reshape(local_outer, inner, chans)
    )
    seq_scale = 1.0 / math.sqrt(OUTER * INNER)
    factor_one_grad = one_total / math.sqrt(OUTER * WIDTH)
    factor_two_grad = two_total / math.sqrt(INNER * WIDTH)
    return (
        input_grad,
        kernel_grad,
        factor_one_grad,
        factor_two_grad,
        gain_total * seq_scale,
        taps_total * seq_scale,
    )


def solution(mesh):
    in_specs = (
        P("ctx", None, "ch"),
        P("ch"),
        P(None, None, "ch"),
        P(),
        P(),
        P(None, "ctx", "ch"),
        P("ctx", None, "ch"),
    )
    out_specs = (P("ctx", None, "ch"), P(None, "ctx", "ch"), P(), P(), P("ch"), P(None, None, "ch"))
    return jax.shard_map(
        on_device, mesh=mesh, in_specs=in_specs, out_specs=out_specs, check_vma=False
    )
```

profile of v0, /device:TPU:1, one launch (start us, length us, event | category | flops | bytes accessed | tf_op | source)
XLA Modules:
  0.0 595.7 jit_solution(9241242994487293887)
XLA Ops:
  7.2 6.5 %copy.43 = bf16[32,512,128]{1,2,0:T(8,128)(2,1)} copy(bf16[32,512,128]{2,1,0:T(8,128)(2,1)} %param.7) | data formatting | bytes 8388608 | tf_op args[0]
  13.7 3.1 multiply_reduce_fusion.3
  17.5 7.1 %copy.44 = f32[32,512,128]{2,1,0:T(8,128)} copy(bf16[32,512,128]{1,2,0:T(8,128)(2,1)} %copy.43) | data formatting | bytes 12582912 | tf_op jit(solution)/shard_map/convert_element_type | solution.py:23
  24.6 75.1 %all-reduce.5.cloned.1.call-done = f32[16384]{0:T(1024)} async-done(((f32[16384]{0:T(1024)}), f32[16384]{0:T(1024)}) %all-reduce.5.cloned.1.call-update) | async-done | bytes 65552 | tf_op jit(solution)/shard_map/psum | solution.py:24
  100.7 5.5 multiply_convert_fusion.2
  106.2 9.4 %collective-permute-start = (bf16[2,128]{1,0:T(2,128)(2,1)S(1)}, bf16[2,128]{1,0:T(2,128)(2,1)S(1)}, u32[]{:S(2)}, u32[]{:S(2)}) collective-permute-start(bf16[2,128]{1,0:T(2,128)(2,1)S(1)} %slice.68), channel_id=1, source_target_pairs={{0,8},{8,16},{16,24},{24,32},{32,40},{40,48},{48,56},{56,64},{64,7... | collective-permute-start | bytes 1544 | tf_op jit(solution)/shard_map/ppermute | solution.py:16
  116.3 6.5 %fusion.10 = (bf16[16384,128]{1,0:T(8,128)(2,1)}, bf16[16384,128]{1,0:T(8,128)(2,1)S(1)}) fusion(bf16[32,512,128]{2,1,0:T(8,128)(2,1)S(1)} %copy-done.9, bf16[16384,128]{1,0:T(8,128)(2,1)S(1)} %multiply_convert_fusion.2, bf16[2,128]{1,0:T(2,128)(2,1)S(1)} %collective-permute-done, f32[128]{0:T(128)S(1)} %get-tuple-element.44, f32[128]{0:T(128)S(1)} %get-tuple-element.45, ...), kind=kLoop, calls=%fused_computation.29 | loop fusion | flops 44040192 | bytes 16779264 | tf_op jit(solution)/shard_map/convert_element_type | solution.py:42
  122.8 3.0 fusion.21
  125.9 1.9 copy-done.7
  127.8 4.4 convert_bitcast_fusion.3
  132.2 7.9 %copy.55 = bf16[32,512,128]{2,0,1:T(8,128)(2,1)} copy(bf16[32,512,128]{1,2,0:T(8,128)(2,1)} %convert_bitcast_fusion.3) | data formatting | bytes 8388608 | tf_op jit(solution)/shard_map/convert_element_type | solution.py:41
  140.1 5.6 all-to-all-start.2
  145.6 6.9 %copy.45 = bf16[32,512,128]{2,0,1:T(8,128)(2,1)} copy(bf16[32,512,128]{2,1,0:T(8,128)(2,1)} %bitcast.103) | data formatting | bytes 8388608 | tf_op jit(solution)/shard_map/reshape | solution.py:42
  152.6 48.9 %all-to-all-done.2 = bf16[32,512,128]{2,0,1:T(8,128)(2,1)} async-done(((bf16[32,512,128]{2,0,1:T(8,128)(2,1)}), bf16[32,512,128]{2,0,1:T(8,128)(2,1)}, u32[]{:S(2)}, u32[]{:S(2)}) %all-to-all-start.2) | async-done | bytes 4194336 | tf_op jit(solution)/shard_map/all_to_all | solution.py:43
  201.5 5.5 all-to-all-start
  207.0 7.6 %copy.49 = bf16[512,32,128]{0,2,1:T(8,128)(2,1)} copy(bf16[512,32,128]{2,1,0:T(8,128)(2,1)} %param.12) | data formatting | bytes 8388608 | tf_op args[5]
  214.5 3.8 copy.56
  219.5 4.2 copy.57
  223.8 9.9 %copy.58 = f32[512,32,128]{0,2,1:T(8,128)} copy(f32[512,32,128]{2,1,0:T(8,128)} %bitcast.102) | data formatting | bytes 16777216 | tf_op jit(solution)/shard_map/convert_element_type | solution.py:45
  233.7 8.9 %convert_bitcast_fusion.2 = bf16[512,32,128]{0,2,1:T(8,128)(2,1)} fusion(bf16[512,512]{1,0:T(8,128)(2,1)S(1)} %copy-done, f32[512,32,128]{0,2,1:T(8,128)} %copy.58, bf16[512,32,128]{0,2,1:T(8,128)(2,1)} %copy.49), kind=kOutput, calls=%fused_computation.66 | convolution fusion | flops 2155872256 | bytes 17301504 | tf_op jit(solution)/shard_map/ijc,ik->kjc/dot_general | solution.py:46
  242.6 7.9 %copy.59 = bf16[512,32,128]{2,1,0:T(8,128)(2,1)} copy(bf16[512,32,128]{0,2,1:T(8,128)(2,1)} %convert_bitcast_fusion.2) | data formatting | bytes 8388608 | tf_op jit(solution)/shard_map/convert_element_type | solution.py:48
  250.6 11.9 %all-to-all-done = bf16[32,512,128]{2,0,1:T(8,128)(2,1)} async-done(((bf16[32,512,128]{2,0,1:T(8,128)(2,1)}), bf16[32,512,128]{2,0,1:T(8,128)(2,1)}, u32[]{:S(2)}, u32[]{:S(2)}) %all-to-all-start) | async-done | bytes 4194336 | tf_op jit(solution)/shard_map/all_to_all | solution.py:50
  262.5 5.1 all-to-all-start.3
  267.6 4.1 copy.47
  271.7 12.6 %fusion.29 = (bf16[512,32,128]{0,2,1:T(8,128)(2,1)}, bf16[512,32,128]{0,2,1:T(8,128)(2,1)}) fusion(f32[512,32,128]{0,2,1:T(8,128)} %copy.58, bf16[512,32,128]{0,2,1:T(8,128)(2,1)S(1)} %copy-done.2, bf16[512,512]{1,0:T(8,128)(2,1)S(1)} %copy-done, bf16[512,32,128]{2,1,0:T(8,128)(2,1)S(1)} %bitcast.100), kind=kOutput, calls=%fused_computation.53 | convolution fusion | flops 2157969408 | bytes 25690112 | tf_op jit(solution)/shard_map/kjc,ik->ijc/dot_general | solution.py:51
  284.4 7.9 %copy.50 = bf16[512,32,128]{2,1,0:T(8,128)(2,1)} copy(bf16[512,32,128]{0,2,1:T(8,128)(2,1)} %get-tuple-element.42) | data formatting | bytes 8388608 | tf_op jit(solution)/shard_map/convert_element_type | solution.py:55
  292.3 31.2 %all-to-all-done.3 = bf16[512,32,128]{2,1,0:T(8,128)(2,1)} async-done(((bf16[512,32,128]{2,1,0:T(8,128)(2,1)}), bf16[512,32,128]{2,1,0:T(8,128)(2,1)}, u32[]{:S(2)}, u32[]{:S(2)}) %all-to-all-start.3) | async-done | bytes 4194336 | tf_op jit(solution)/shard_map/all_to_all | solution.py:49
  323.4 5.0 all-to-all-start.1
  328.5 7.8 %copy.64 = bf16[512,32,128]{2,1,0:T(8,128)(2,1)} copy(bf16[512,32,128]{0,2,1:T(8,128)(2,1)} %get-tuple-element.41) | data formatting | bytes 8388608
  336.4 11.0 %fusion.35 = f32[512,512]{1,0:T(8,128)} fusion(bf16[512,32,128]{2,1,0:T(8,128)(2,1)} %bitcast.101, f32[512,32,128]{0,2,1:T(8,128)} %copy.58, bf16[512,32,128]{0,2,1:T(8,128)(2,1)} %copy.49), kind=kOutput, calls=%fused_computation.73 | convolution fusion | flops 2153775104 | bytes 17825792 | tf_op jit(solution)/shard_map/ijc,kjc->ik/dot_general | solution.py:56
  347.4 3.4 convert_bitcast_fusion
  350.8 4.3 copy.60
  355.1 29.1 %all-to-all-done.1 = bf16[512,32,128]{2,1,0:T(8,128)(2,1)} async-done(((bf16[512,32,128]{2,1,0:T(8,128)(2,1)}), bf16[512,32,128]{2,1,0:T(8,128)(2,1)}, u32[]{:S(2)}, u32[]{:S(2)}) %all-to-all-start.1) | async-done | bytes 4194336 | tf_op jit(solution)/shard_map/all_to_all | solution.py:57
  384.2 3.6 copy.51
  387.8 1.9 copy-done.10
  389.7 3.3 convolution_bitcast_fusion.1
  393.1 10.3 %multiply_reduce_fusion = (f32[128]{0:T(128)S(1)}, f32[32,512,128]{1,2,0:T(8,128)}) fusion(f32[128]{0:T(128)S(1)} %copy-done.12, f32[32,512]{1,0:T(8,128)S(1)} %mul.250, bf16[32,512,128]{1,2,0:T(8,128)(2,1)} %copy.43, bf16[32,512,128]{2,1,0:T(8,128)(2,1)} %bitcast.108, bf16[512,512]{1,0:T(8,128)(2,1)S(1)} %copy-done.11), kind=kOutput, calls=%fused_computation.55 | convolution fusion | flops 2162163712 | bytes 17368064 | tf_op jit(solution)/shard_map/ikc,jk->ijc/dot_general | solution.py:60
  403.4 8.9 %copy.53 = f32[32,512,128]{2,1,0:T(8,128)} copy(f32[32,512,128]{1,2,0:T(8,128)} %get-tuple-element.50) | data formatting | bytes 16777216 | tf_op jit(solution)/shard_map/ikc,jk->ijc/transpose | solution.py:60
  413.0 14.0 %fusion.22 = (f32[128]{0:T(128)S(1)}, f32[128]{0:T(128)S(1)}, f32[128]{0:T(128)S(1)}, f32[128]{0:T(128)S(1)}, f32[128]{0:T(128)S(1)}, /*index=5*/f32[16384,128]{1,0:T(8,128)S(1)}) fusion(bf16[16384,128]{1,0:T(8,128)(2,1)} %copy-done.3, bf16[2,128]{1,0:T(2,128)(2,1)S(1)} %collective-permute-done, bf16[16384,128]{1,0:T(8,128)(2,1)} %copy-done.5, ...), kind=kLoop, calls=%fused_computation.41 | loop fusion | flops 60816768 | bytes 37753344 | tf_op jit(solution)/shard_map/reduce_sum | solution.py:78
  427.0 3.3 copy-done.6
  430.3 2.6 collective-permute-start.2
  436.2 1.9 collective-permute-done.1
  438.1 31.9 %multiply_reduce_fusion.1 = (f32[128]{0:T(128)S(1)}, bf16[16384]{0:T(1024)(128)(2,1)S(1)}, f32[16384,128]{1,0:T(8,128)}) fusion(f32[32,512,128]{2,1,0:T(8,128)} %copy.44, f32[16384]{0:T(1024)S(1)} %add_rsqrt_fusion, f32[128]{0:T(128)S(1)} %copy-done.12, f32[2,128]{1,0:T(2,128)S(1)} %collective-permute-done.2, f32[16384,128]{1,0:T(8,128)} %copy-done.6, ...), kind=kLoop, calls=%fused_computation.57 | loop fusion | flops 44023680 | bytes 33658880 | tf_op jit(solution)/shard_map/reduce_sum | solution.py:80
  470.1 31.7 %psum.43 = bf16[16384]{0:T(1024)(128)(2,1)S(1)} all-reduce(bf16[16384]{0:T(1024)(128)(2,1)S(1)} %get-tuple-element.25), channel_id=1, replica_groups=mesh['ctx'=16,'ch'=8] {'ch'}, use_global_device_ids=true, to_apply=%region_3.0 | all-reduce | flops 16384 | bytes 65536 | tf_op jit(solution)/shard_map/psum | solution.py:84
  501.8 11.5 %multiply_convert_fusion.1 = bf16[16384,128]{1,0:T(8,128)(2,1)} fusion(f32[16384,128]{1,0:T(8,128)} %get-tuple-element.38, f32[32,512,128]{2,1,0:T(8,128)} %copy.44, f32[16384]{0:T(1024)S(1)} %convert_multiply_fusion.15, f32[128]{0:T(128)S(1)} %copy-done.12, f32[16384]{0:T(1024)S(1)} %add_rsqrt_fusion), kind=kLoop, calls=%fused_computation.58 | loop fusion | flops 12582912 | bytes 21103104 | tf_op jit(solution)/shard_map/convert_element_type | solution.py:89
  513.3 31.7 %all-reduce.1 = (f32[128]{0:T(128)S(1)}, f32[2,3,128]{2,1,0:T(4,128)S(1)}) all-reduce(f32[128]{0:T(128)S(1)} %get-tuple-element.24, f32[2,3,128]{2,1,0:T(4,128)S(1)} %pad_maximum_fusion.3), channel_id=1, replica_groups=mesh['ctx'=16,'ch'=8] {'ctx'}, use_global_device_ids=true, to_apply=%region_7.0 | all-reduce | flops 896 | bytes 7168 | tf_op jit(solution)/shard_map/psum | solution.py:81
  546.2 39.4 %all-reduce.7.cloned.1.call-done = (f32[512,512]{1,0:T(8,128)}, f32[512,512]{1,0:T(8,128)}) async-done(((f32[512,512]{1,0:T(8,128)}, f32[512,512]{1,0:T(8,128)}), (f32[512,512]{1,0:T(8,128)}, f32[512,512]{1,0:T(8,128)})) %all-reduce.7.cloned.1.call-update) | async-done | bytes 2097168 | tf_op jit(solution)/shard_map/psum | solution.py:64
  585.5 3.1 broadcast_multiply_fusion
  (46 shorter events, 8.8 us)
Async XLA Ops:
  7.2 226.5 %copy-start = (bf16[512,512]{1,0:T(8,128)(2,1)S(1)}, bf16[512,512]{1,0:T(8,128)(2,1)}, u32[]{:S(2)}) copy-start(bf16[512,512]{1,0:T(8,128)(2,1)} %param.11) | copy-start | bytes 1572868
  7.2 92.5 %all-reduce.5.cloned.1.call-start = ((), (), s32[]{:S(2)}) async-start(), calls=%async_computation.4 | async-start | bytes 131072 | tf_op jit(solution)/shard_map/psum | solution.py:24
  13.7 87.0 %copy-start.12 = (f32[128]{0:T(128)S(1)}, f32[128]{0:T(128)}, u32[]{:S(2)}) copy-start(f32[128]{0:T(128)} %param.8) | copy-start | bytes 1540
  24.6 91.1 %copy-start.13 = (f32[2,3,128]{2,0,1:T(2,128)S(1)}, f32[2,3,128]{2,0,1:T(2,128)}, u32[]{:S(2)}) copy-start(f32[2,3,128]{2,0,1:T(2,128)} %param.9) | copy-start | bytes 9220
  99.7 16.6 %copy-start.9 = (bf16[32,512,128]{2,1,0:T(8,128)(2,1)S(1)}, bf16[32,512,128]{2,1,0:T(8,128)(2,1)}, u32[]{:S(2)}) copy-start(bf16[32,512,128]{2,1,0:T(8,128)(2,1)} %param.13) | copy-start | bytes 12582916
  106.2 16.6 %copy-start.3 = (bf16[16384,128]{1,0:T(8,128)(2,1)}, bf16[16384,128]{1,0:T(8,128)(2,1)S(1)}, u32[]{:S(2)}) copy-start(bf16[16384,128]{1,0:T(8,128)(2,1)S(1)} %multiply_convert_fusion.2) | copy-start | bytes 12582916
  106.2 10.1 %collective-permute-start = (bf16[2,128]{1,0:T(2,128)(2,1)S(1)}, bf16[2,128]{1,0:T(2,128)(2,1)S(1)}, u32[]{:S(2)}, u32[]{:S(2)}) collective-permute-start(bf16[2,128]{1,0:T(2,128)(2,1)S(1)} %slice.68), channel_id=1, source_target_pairs={{0,8},{8,16},{16,24},{24,32},{32,40},{40,48},{48,56},{56,64},{64,7... | collective-permute-start | bytes 1544 | tf_op jit(solution)/shard_map/ppermute | solution.py:16
  122.8 3.0 copy-start.5
  122.8 5.0 copy-start.11
  125.9 1.9 copy-start.7
  140.1 61.4 %all-to-all-start.2 = ((bf16[32,512,128]{2,0,1:T(8,128)(2,1)}), bf16[32,512,128]{2,0,1:T(8,128)(2,1)}, u32[]{:S(2)}, u32[]{:S(2)}) async-start(bf16[32,512,128]{2,0,1:T(8,128)(2,1)} %copy.55), calls=%async_computation.2 | async-start | bytes 8388608 | tf_op jit(solution)/shard_map/all_to_all | solution.py:43
  201.5 61.0 %all-to-all-start = ((bf16[32,512,128]{2,0,1:T(8,128)(2,1)}), bf16[32,512,128]{2,0,1:T(8,128)(2,1)}, u32[]{:S(2)}, u32[]{:S(2)}) async-start(bf16[32,512,128]{2,0,1:T(8,128)(2,1)} %copy.45), calls=%async_computation | async-start | bytes 8388608 | tf_op jit(solution)/shard_map/all_to_all | solution.py:50
  262.5 61.0 %all-to-all-start.3 = ((bf16[512,32,128]{2,1,0:T(8,128)(2,1)}), bf16[512,32,128]{2,1,0:T(8,128)(2,1)}, u32[]{:S(2)}, u32[]{:S(2)}) async-start(bf16[512,32,128]{2,1,0:T(8,128)(2,1)} %copy.59), calls=%async_computation.3 | async-start | bytes 8388608 | tf_op jit(solution)/shard_map/all_to_all | solution.py:49
  267.6 4.1 copy-start.2
  271.7 12.6 %copy-start.4 = (bf16[16,32,32,128]{3,2,1,0:T(8,128)(2,1)}, bf16[16,32,32,128]{3,2,1,0:T(8,128)(2,1)S(1)}, u32[]{:S(2)}) copy-start(bf16[16,32,32,128]{3,2,1,0:T(8,128)(2,1)S(1)} %copy.47) | copy-start | bytes 12582916
  323.4 60.7 %all-to-all-start.1 = ((bf16[512,32,128]{2,1,0:T(8,128)(2,1)}), bf16[512,32,128]{2,1,0:T(8,128)(2,1)}, u32[]{:S(2)}, u32[]{:S(2)}) async-start(bf16[512,32,128]{2,1,0:T(8,128)(2,1)} %copy.50), calls=%async_computation.1 | async-start | bytes 8388608 | tf_op jit(solution)/shard_map/all_to_all | solution.py:57
  328.5 257.0 %all-reduce.7.cloned.1.call-start = ((), (), s32[]{:S(2)}) async-start(), calls=%async_computation.5 | async-start | bytes 4194304 | tf_op jit(solution)/shard_map/psum | solution.py:64
  384.2 5.5 copy-start.8
  387.8 1.9 copy-start.10
  427.0 3.3 copy-start.6
  430.3 5.9 collective-permute-start.2
  432.9 5.3 collective-permute-start.1
  501.8 86.8 %copy-start.1 = (bf16[512,512]{1,0:T(8,128)(2,1)S(1)}, bf16[512,512]{1,0:T(8,128)(2,1)}, u32[]{:S(2)}) copy-start(bf16[512,512]{1,0:T(8,128)(2,1)} %param.11) | copy-start | bytes 1572868
Sparse Core Ops, SparseCore 0:
  17.6 82.0 all-reduce.4
  435.0 150.5 all-reduce.6
where the time goes:
time: 606 us; the launch traced here: 596 us
  waiting for transfers between devices  240 us (40%)
  local copies, waits for them, and re-layouts  108 us (18%)
  other arithmetic  84.7 us (14%)
  blocking collectives  63.4 us (10%)
  matrix products  50.6 us (8%)
  starting transfers between devices  35.2 us (6%)
  between operations  14.5 us (2%)
    psum x1, waiting for transfers between devices, on_device(): squares = lax.psum(jnp.sum(flat_in * flat_in, axis=1), 'ch')  75.1 us
    all_to_all x1, waiting for transfers between devices, on_device(): lax.all_to_all(section_one, 'ctx', split_axis=1, concat_axis=0, tiled=True)  48.9 us
    psum x1, waiting for transfers between devices, on_device(): one_total, two_total = lax.psum((one_part, two_part), ('ctx', 'ch'))  39.4 us
    reduce_sum x1, other arithmetic, on_device(): gain_part = jnp.sum(grad_normed * hat, axis=0)  31.9 us
    psum x1, blocking collectives, on_device(): lax.psum(jnp.sum(scaled * hat, axis=1).astype(jnp.bfloat16), 'ch')  31.7 us
    psum x1, blocking collectives, on_device(): gain_total, taps_total = lax.psum((gain_part, tap_part), 'ctx')  31.7 us
    all_to_all x1, waiting for transfers between devices, on_device(): lax.all_to_all(section_two, 'ctx', split_axis=0, concat_axis=1, tiled=True)  31.2 us
    unnamed x33, local copies, waits for them, and re-layouts  30.4 us
  transfers between devices with their start and end apart: 9, of which 9 were waited for; matrix products, arithmetic and copies ran while one was open for 26% of the time, Pallas kernels for 0%

commit v1 on v0

--- a/solution.py
+++ b/solution.py
@@ -16,12 +16,22 @@
     return lax.ppermute(value, axis, [(source, source + steps) for source in range(initial, last)])
 
 
+def tree_psum(value, axis):
+    count = lax.axis_size(axis)
+    step = 1
+    while step < count:
+        pairs = [(source, source ^ step) for source in range(count)]
+        value = jax.tree.map(lambda v, r: v + r, value, lax.ppermute(value, axis, pairs))
+        step *= 2
+    return value
+
+
 def on_device(inputs, norm_gain, conv_taps, factor_one, factor_two, kernel, grad_out):
     local_outer, inner, chans = inputs.shape
     rows = local_outer * inner
     taps_count = conv_taps.shape[1]
     flat_in = inputs.reshape(rows, chans).astype(jnp.float32)
-    squares = lax.psum(jnp.sum(flat_in * flat_in, axis=1), "ch")
+    squares = tree_psum(jnp.sum(flat_in * flat_in, axis=1), "ch")
     inverse = lax.rsqrt(squares / WIDTH + 1e-05)
     hat = flat_in * inverse[:, None]
     normed = (hat * norm_gain).astype(jnp.bfloat16)
@@ -54,6 +64,7 @@
     kernel_grad = (grad_spec * columns.astype(jnp.float32)).astype(jnp.bfloat16)
     grad_section = (grad_spec * kern).astype(jnp.bfloat16)
     two_part = jnp.einsum("ijc,kjc->ik", spectrum, grad_columns, preferred_element_type=jnp.float32)
+    two_total = lax.psum(two_part, ("ctx", "ch"))
     grad_rows = lax.all_to_all(grad_section, "ctx", split_axis=0, concat_axis=1, tiled=True)
     back_flat = back_rows.reshape(rows, chans).astype(jnp.float32)
     grad_gate_pre = cotangent * back_flat * gate * (1.0 - gate)
@@ -61,7 +72,8 @@
         "ikc,jk->ijc", grad_rows, factor_one, preferred_element_type=jnp.float32
     ).reshape(rows, chans)
     one_part = jnp.einsum("ijc,ikc->jk", mixed_in, grad_rows, preferred_element_type=jnp.float32)
-    one_total, two_total = lax.psum((one_part, two_part), ("ctx", "ch"))
+    two_total, one_part = lax.optimization_barrier((two_total, one_part))
+    one_total = lax.psum(one_part, ("ctx", "ch"))
     later_value, later_gate = shifted(
         (grad_mixed[: taps_count - 1], grad_gate_pre[: taps_count - 1]), "ctx", -1
     )
@@ -78,10 +90,10 @@
         gate_taps.append(jnp.sum(grad_gate_pre * window, axis=0))
     tap_part = jnp.stack([jnp.stack(value_taps), jnp.stack(gate_taps)])
     gain_part = jnp.sum(grad_normed * hat, axis=0)
-    gain_total, taps_total = lax.psum((gain_part, tap_part), "ctx")
+    gain_total, taps_total = tree_psum((gain_part, tap_part), "ctx")
     scaled = grad_normed * norm_gain
     row_mean = (
-        lax.psum(jnp.sum(scaled * hat, axis=1).astype(jnp.bfloat16), "ch").astype(jnp.float32)
+        tree_psum(jnp.sum(scaled * hat, axis=1), "ch")
         / WIDTH
     )
     input_grad = (

time: 606 us -> 712 us (1.17)
  waiting for transfers between devices: 240 us -> 407 us
  blocking collectives: 63.4 us -> 0 us
  starting transfers between devices: 35.2 us -> 54.1 us
    psum x2, waiting for transfers between devices: 115 us -> 255 us  [the longest x1 130 us: on_device(): two_total = lax.psum(two_part, ('ctx', 'ch'))]
    psum x2 -> x0, blocking collectives: 63.4 us -> none  [the longest x1 31.7 us: on_device(): lax.psum(jnp.sum(scaled * hat, axis=1).astype(jnp.bfloat16), 'ch')]
    ppermute x0 -> x14, starting transfers between devices: none -> 21.5 us  [tree_psum(): lax.ppermute(value, axis, pairs)]
    all_to_all x1, waiting for transfers between devices: 29.1 us -> 47.8 us  [on_device(): lax.all_to_all(grad_section, 'ctx', split_axis=0, concat_axis=1, tiled=True)]
    ppermute x0 -> x14, waiting for transfers between devices: none -> 8.12 us  [tree_psum(): lax.ppermute(value, axis, pairs)]
    reduce_sum x1, other arithmetic: 31.9 us -> 24.3 us  [on_device(): gain_part = jnp.sum(grad_normed * hat, axis=0)]
    unnamed x33 -> x39, local copies, waits for them, and re-layouts: 30.4 us -> 24.5 us
  transfers between devices with their start and end apart: 9 -> 23, of which waited for: 9 -> 15; matrix products, arithmetic and copies ran while one was open for 26% -> 18% of each run, Pallas kernels for 0% -> 0%
where the time goes in v1:
time: 712 us; the launch traced here: 704 us
  waiting for transfers between devices  407 us (57%)
  local copies, waits for them, and re-layouts  102 us (14%)
  other arithmetic  77.7 us (11%)
  starting transfers between devices  54.1 us (8%)
  matrix products  48.5 us (7%)
  between operations  14.6 us (2%)
    psum x1, waiting for transfers between devices, on_device(): two_total = lax.psum(two_part, ('ctx', 'ch'))  130 us
    psum x1, waiting for transfers between devices, on_device(): one_total = lax.psum(one_part, ('ctx', 'ch'))  125 us
    all_to_all x1, waiting for transfers between devices, on_device(): lax.all_to_all(section_one, 'ctx', split_axis=1, concat_axis=0, tiled=True)  48.8 us
    all_to_all x1, waiting for transfers between devices, on_device(): lax.all_to_all(grad_section, 'ctx', split_axis=0, concat_axis=1, tiled=True)  47.8 us
    all_to_all x1, waiting for transfers between devices, on_device(): lax.all_to_all(section_two, 'ctx', split_axis=0, concat_axis=1, tiled=True)  31.3 us
    unnamed x39, local copies, waits for them, and re-layouts  24.5 us
    reduce_sum x1, other arithmetic, on_device(): gain_part = jnp.sum(grad_normed * hat, axis=0)  24.3 us
    ppermute x14, starting transfers between devices, tree_psum(): lax.ppermute(value, axis, pairs)  21.5 us
  transfers between devices with their start and end apart: 23, of which 15 were waited for; matrix products, arithmetic and copies ran while one was open for 18% of the time, Pallas kernels for 0%

profile of v1, /device:TPU:1, one launch (start us, length us, event | category | flops | bytes accessed | tf_op | source)
XLA Modules:
  0.0 703.9 jit_solution(7908504238556587428)
XLA Ops:
  7.2 6.5 copy.43
  13.7 3.1 multiply_reduce_fusion.3
  16.8 2.1 collective-permute-start
  20.6 3.1 collective-permute-start.1
  25.3 3.9 collective-permute-start.2
  29.2 7.1 %copy.44 = f32[32,512,128]{2,1,0:T(8,128)} copy(bf16[32,512,128]{1,2,0:T(8,128)(2,1)} %copy.43) | data formatting | bytes 12582912 | tf_op jit(solution)/shard_map/convert_element_type | solution.py:33
  36.3 5.5 multiply_convert_fusion.2
  41.8 6.3 collective-permute-start.3
  48.9 6.5 fusion.10
  55.4 3.0 fusion.21
  60.4 4.5 convert_bitcast_fusion.3
  64.9 8.0 %copy.55 = bf16[32,512,128]{2,0,1:T(8,128)(2,1)} copy(bf16[32,512,128]{1,2,0:T(8,128)(2,1)} %convert_bitcast_fusion.3) | data formatting | bytes 8388608 | tf_op jit(solution)/shard_map/convert_element_type | solution.py:51
  72.9 6.6 all-to-all-start.2
  79.5 6.9 copy.45
  86.4 48.8 %all-to-all-done.2 = bf16[32,512,128]{2,0,1:T(8,128)(2,1)} async-done(((bf16[32,512,128]{2,0,1:T(8,128)(2,1)}), bf16[32,512,128]{2,0,1:T(8,128)(2,1)}, u32[]{:S(2)}, u32[]{:S(2)}) %all-to-all-start.2) | async-done | bytes 4194336 | tf_op jit(solution)/shard_map/all_to_all | solution.py:53
  135.2 4.9 all-to-all-start
  140.1 7.5 %copy.49 = bf16[512,32,128]{0,2,1:T(8,128)(2,1)} copy(bf16[512,32,128]{2,1,0:T(8,128)(2,1)} %param.12) | data formatting | bytes 8388608 | tf_op args[5]
  147.6 3.8 copy.56
  152.6 4.3 copy.57
  156.9 9.9 %copy.58 = f32[512,32,128]{0,2,1:T(8,128)} copy(f32[512,32,128]{2,1,0:T(8,128)} %bitcast.104) | data formatting | bytes 16777216 | tf_op jit(solution)/shard_map/convert_element_type | solution.py:55
  166.9 8.9 %convert_bitcast_fusion.2 = bf16[512,32,128]{0,2,1:T(8,128)(2,1)} fusion(bf16[512,512]{1,0:T(8,128)(2,1)S(1)} %copy-done, f32[512,32,128]{0,2,1:T(8,128)} %copy.58, bf16[512,32,128]{0,2,1:T(8,128)(2,1)} %copy.49), kind=kOutput, calls=%fused_computation.66 | convolution fusion | flops 2155872256 | bytes 17301504 | tf_op jit(solution)/shard_map/ijc,ik->kjc/dot_general | solution.py:56
  175.8 7.9 %copy.59 = bf16[512,32,128]{2,1,0:T(8,128)(2,1)} copy(bf16[512,32,128]{0,2,1:T(8,128)(2,1)} %convert_bitcast_fusion.2) | data formatting | bytes 8388608 | tf_op jit(solution)/shard_map/convert_element_type | solution.py:58
  183.7 12.1 %all-to-all-done = bf16[32,512,128]{2,0,1:T(8,128)(2,1)} async-done(((bf16[32,512,128]{2,0,1:T(8,128)(2,1)}), bf16[32,512,128]{2,0,1:T(8,128)(2,1)}, u32[]{:S(2)}, u32[]{:S(2)}) %all-to-all-start) | async-done | bytes 4194336 | tf_op jit(solution)/shard_map/all_to_all | solution.py:60
  195.8 5.1 all-to-all-start.3
  200.9 4.1 copy.47
  205.0 12.6 %fusion.29 = (bf16[512,32,128]{0,2,1:T(8,128)(2,1)}, bf16[512,32,128]{0,2,1:T(8,128)(2,1)}) fusion(f32[512,32,128]{0,2,1:T(8,128)} %copy.58, bf16[512,32,128]{0,2,1:T(8,128)(2,1)S(1)} %copy-done.3, bf16[512,512]{1,0:T(8,128)(2,1)S(1)} %copy-done, bf16[512,32,128]{2,1,0:T(8,128)(2,1)S(1)} %bitcast.102), kind=kOutput, calls=%fused_computation.53 | convolution fusion | flops 2157969408 | bytes 25690112 | tf_op jit(solution)/shard_map/kjc,ik->ijc/dot_general | solution.py:61
  217.6 7.9 %copy.50 = bf16[512,32,128]{2,1,0:T(8,128)(2,1)} copy(bf16[512,32,128]{0,2,1:T(8,128)(2,1)} %get-tuple-element.42) | data formatting | bytes 8388608 | tf_op jit(solution)/shard_map/convert_element_type | solution.py:65
  225.5 31.3 %all-to-all-done.3 = bf16[512,32,128]{2,1,0:T(8,128)(2,1)} async-done(((bf16[512,32,128]{2,1,0:T(8,128)(2,1)}), bf16[512,32,128]{2,1,0:T(8,128)(2,1)}, u32[]{:S(2)}, u32[]{:S(2)}) %all-to-all-start.3) | async-done | bytes 4194336 | tf_op jit(solution)/shard_map/all_to_all | solution.py:59
  256.8 4.9 all-to-all-start.1
  261.9 3.4 convert_bitcast_fusion
  265.3 4.3 copy.60
  269.5 47.8 %all-to-all-done.1 = bf16[512,32,128]{2,1,0:T(8,128)(2,1)} async-done(((bf16[512,32,128]{2,1,0:T(8,128)(2,1)}), bf16[512,32,128]{2,1,0:T(8,128)(2,1)}, u32[]{:S(2)}, u32[]{:S(2)}) %all-to-all-start.1) | async-done | bytes 4194336 | tf_op jit(solution)/shard_map/all_to_all | solution.py:68
  317.3 3.6 copy.51
  321.0 7.0 multiply_reduce_fusion
  328.0 9.0 %copy.53 = f32[32,512,128]{2,1,0:T(8,128)} copy(f32[32,512,128]{1,2,0:T(8,128)} %get-tuple-element.50) | data formatting | bytes 16777216 | tf_op jit(solution)/shard_map/ikc,jk->ijc/transpose | solution.py:71
  337.6 14.0 %fusion.22 = (f32[128]{0:T(128)S(1)}, f32[128]{0:T(128)S(1)}, f32[128]{0:T(128)S(1)}, f32[128]{0:T(128)S(1)}, f32[128]{0:T(128)S(1)}, /*index=5*/f32[16384,128]{1,0:T(8,128)S(1)}) fusion(bf16[16384,128]{1,0:T(8,128)(2,1)} %copy-done.4, bf16[2,128]{1,0:T(2,128)(2,1)S(1)} %collective-permute-done.3, bf16[16384,128]{1,0:T(8,128)(2,1)} %copy-done.7, ...), kind=kLoop, calls=%fused_computation.41 | loop fusion | flops 60816768 | bytes 37753344 | tf_op jit(solution)/shard_map/reduce_sum | solution.py:90
  351.6 2.6 collective-permute-start.5
  359.5 24.3 %multiply_reduce_fusion.1 = (f32[128]{0:T(128)S(1)}, f32[16384]{0:T(1024)S(1)}, f32[16384,128]{1,0:T(8,128)}) fusion(f32[32,512,128]{2,1,0:T(8,128)} %copy.44, f32[16384]{0:T(1024)S(1)} %add_rsqrt_fusion, f32[128]{0:T(128)S(1)} %copy-done.13, f32[2,128]{1,0:T(2,128)S(1)} %collective-permute-done.5, f32[16384,128]{1,0:T(8,128)} %copy-done.8, ...), kind=kLoop, calls=%fused_computation.57 | loop fusion | flops 44023680 | bytes 33691648 | tf_op jit(solution)/shard_map/reduce_sum | solution.py:92
  387.0 8.7 %fusion.35 = f32[512,512]{1,0:T(8,128)} fusion(bf16[512,32,128]{2,1,0:T(8,128)(2,1)} %bitcast.103, f32[512,32,128]{0,2,1:T(8,128)S(1)} %bitcast.99, bf16[512,32,128]{0,2,1:T(8,128)(2,1)} %copy.49), kind=kOutput, calls=%fused_computation.73 | convolution fusion | flops 2153775104 | bytes 17825792 | tf_op jit(solution)/shard_map/ijc,kjc->ik/dot_general | solution.py:66
  395.8 7.9 %copy.64 = bf16[512,32,128]{2,1,0:T(8,128)(2,1)} copy(bf16[512,32,128]{0,2,1:T(8,128)(2,1)} %get-tuple-element.41) | data formatting | bytes 8388608
  405.1 6.8 convolution_bitcast_fusion.1
  411.9 130.2 %all-reduce.3.cloned.1.call-done = f32[512,512]{1,0:T(8,128)} async-done(((f32[512,512]{1,0:T(8,128)}), f32[512,512]{1,0:T(8,128)}) %all-reduce.3.cloned.1.call-update) | async-done | bytes 1048592 | tf_op jit(solution)/shard_map/psum | solution.py:67
  545.1 2.3 broadcast_multiply_fusion
  551.1 2.1 collective-permute-done.7
  553.3 2.4 collective-permute-start.8
  558.3 11.5 %multiply_convert_fusion.1 = bf16[16384,128]{1,0:T(8,128)(2,1)} fusion(f32[16384,128]{1,0:T(8,128)} %get-tuple-element.38, f32[32,512,128]{2,1,0:T(8,128)} %copy.44, f32[16384]{0:T(1024)S(1)} %add_multiply_fusion, f32[128]{0:T(128)S(1)} %copy-done.13, f32[16384]{0:T(1024)S(1)} %add_rsqrt_fusion), kind=kLoop, calls=%fused_computation.58 | loop fusion | flops 12582912 | bytes 21103104 | tf_op jit(solution)/shard_map/convert_element_type | solution.py:101
  569.8 124.7 %all-reduce.5.cloned.1.call-done = f32[512,512]{1,0:T(8,128)} async-done(((f32[512,512]{1,0:T(8,128)}), f32[512,512]{1,0:T(8,128)}) %all-reduce.5.cloned.1.call-update) | async-done | bytes 1048592 | tf_op jit(solution)/shard_map/psum | solution.py:76
  694.5 2.3 broadcast_multiply_fusion.1
  (90 shorter events, 27.3 us)
Async XLA Ops:
  7.2 159.7 %copy-start = (bf16[512,512]{1,0:T(8,128)(2,1)S(1)}, bf16[512,512]{1,0:T(8,128)(2,1)}, u32[]{:S(2)}) copy-start(bf16[512,512]{1,0:T(8,128)(2,1)} %param.11) | copy-start | bytes 1572868
  13.7 22.7 %copy-start.13 = (f32[128]{0:T(128)S(1)}, f32[128]{0:T(128)}, u32[]{:S(2)}) copy-start(f32[128]{0:T(128)} %param.8) | copy-start | bytes 1540
  16.8 3.8 collective-permute-start
  20.6 4.7 collective-permute-start.1
  25.3 11.0 %collective-permute-start.2 = (f32[16384]{0:T(1024)S(1)}, f32[16384]{0:T(1024)S(1)}, u32[]{:S(2)}, u32[]{:S(2)}) collective-permute-start(f32[16384]{0:T(1024)S(1)} %add.83), channel_id=1, source_target_pairs={{0,4},{1,5},{2,6},{3,7},{4,0},{5,1},{6,2},{7,3},{8,12},{9,13},{10,... | collective-permute-start | bytes 196616 | tf_op jit(solution)/shard_map/ppermute | solution.py:24
  36.3 11.9 %copy-start.14 = (f32[2,3,128]{2,0,1:T(2,128)S(1)}, f32[2,3,128]{2,0,1:T(2,128)}, u32[]{:S(2)}) copy-start(f32[2,3,128]{2,0,1:T(2,128)} %param.9) | copy-start | bytes 9220
  36.3 12.6 %copy-start.10 = (bf16[32,512,128]{2,1,0:T(8,128)(2,1)S(1)}, bf16[32,512,128]{2,1,0:T(8,128)(2,1)}, u32[]{:S(2)}) copy-start(bf16[32,512,128]{2,1,0:T(8,128)(2,1)} %param.13) | copy-start | bytes 12582916
  41.8 13.6 %copy-start.4 = (bf16[16384,128]{1,0:T(8,128)(2,1)}, bf16[16384,128]{1,0:T(8,128)(2,1)S(1)}, u32[]{:S(2)}) copy-start(bf16[16384,128]{1,0:T(8,128)(2,1)S(1)} %multiply_convert_fusion.2) | copy-start | bytes 12582916
  41.8 7.1 %collective-permute-start.3 = (bf16[2,128]{1,0:T(2,128)(2,1)S(1)}, bf16[2,128]{1,0:T(2,128)(2,1)S(1)}, u32[]{:S(2)}, u32[]{:S(2)}) collective-permute-start(bf16[2,128]{1,0:T(2,128)(2,1)S(1)} %slice.68), channel_id=1, source_target_pairs={{0,8},{8,16},{16,24},{24,32},{32,40},{40,48},{48,56},{56,64},{64,7... | collective-permute-start | bytes 1544 | tf_op jit(solution)/shard_map/ppermute | solution.py:16
  55.4 3.0 copy-start.7
  55.4 5.0 copy-start.12
  58.4 1.9 copy-start.9
  72.9 62.3 %all-to-all-start.2 = ((bf16[32,512,128]{2,0,1:T(8,128)(2,1)}), bf16[32,512,128]{2,0,1:T(8,128)(2,1)}, u32[]{:S(2)}, u32[]{:S(2)}) async-start(bf16[32,512,128]{2,0,1:T(8,128)(2,1)} %copy.55), calls=%async_computation.2 | async-start | bytes 8388608 | tf_op jit(solution)/shard_map/all_to_all | solution.py:53
  135.2 60.6 %all-to-all-start = ((bf16[32,512,128]{2,0,1:T(8,128)(2,1)}), bf16[32,512,128]{2,0,1:T(8,128)(2,1)}, u32[]{:S(2)}, u32[]{:S(2)}) async-start(bf16[32,512,128]{2,0,1:T(8,128)(2,1)} %copy.45), calls=%async_computation | async-start | bytes 8388608 | tf_op jit(solution)/shard_map/all_to_all | solution.py:60
  195.8 61.0 %all-to-all-start.3 = ((bf16[512,32,128]{2,1,0:T(8,128)(2,1)}), bf16[512,32,128]{2,1,0:T(8,128)(2,1)}, u32[]{:S(2)}, u32[]{:S(2)}) async-start(bf16[512,32,128]{2,1,0:T(8,128)(2,1)} %copy.59), calls=%async_computation.3 | async-start | bytes 8388608 | tf_op jit(solution)/shard_map/all_to_all | solution.py:59
  200.9 4.1 copy-start.3
  205.0 12.6 %copy-start.5 = (bf16[16,32,32,128]{3,2,1,0:T(8,128)(2,1)}, bf16[16,32,32,128]{3,2,1,0:T(8,128)(2,1)S(1)}, u32[]{:S(2)}) copy-start(bf16[16,32,32,128]{3,2,1,0:T(8,128)(2,1)S(1)} %copy.47) | copy-start | bytes 12582916
  256.8 60.6 %all-to-all-start.1 = ((bf16[512,32,128]{2,1,0:T(8,128)(2,1)}), bf16[512,32,128]{2,1,0:T(8,128)(2,1)}, u32[]{:S(2)}, u32[]{:S(2)}) async-start(bf16[512,32,128]{2,1,0:T(8,128)(2,1)} %copy.50), calls=%async_computation.1 | async-start | bytes 8388608 | tf_op jit(solution)/shard_map/all_to_all | solution.py:68
  261.6 280.4 %all-reduce.3.cloned.1.call-start = ((), (), s32[]{:S(2)}) async-start(), calls=%async_computation.4 | async-start | bytes 2097152 | tf_op jit(solution)/shard_map/psum | solution.py:67
  317.3 3.6 copy-start.6
  320.9 7.1 %copy-start.11 = (bf16[32,16,32,128]{3,2,1,0:T(8,128)(2,1)}, bf16[32,16,32,128]{3,2,1,0:T(8,128)(2,1)S(1)}, u32[]{:S(2)}) copy-start(bf16[32,16,32,128]{3,2,1,0:T(8,128)(2,1)S(1)} %copy.51) | copy-start | bytes 12582916
  337.6 21.9 %copy-start.2 = (f32[32,512,128]{2,1,0:T(8,128)S(1)}, f32[32,512,128]{2,1,0:T(8,128)}, u32[]{:S(2)}) copy-start(f32[32,512,128]{2,1,0:T(8,128)} %copy.53) | copy-start | bytes 25165828
  351.6 4.6 copy-start.8
  351.6 5.9 collective-permute-start.5
  354.2 5.3 collective-permute-start.4
  356.2 30.9 %slice-start = ((s8[8388608]{0:T(1024)(128)(4,1)}), s8[4194304]{0:T(1024)(128)(4,1)S(1)}, s32[]{:S(2)}) async-start(s8[8388608]{0:T(1024)(128)(4,1)} %bitcast.98), calls=%async_computation.6 | async-start | bytes 8388608
  356.2 30.8 %slice-start.1 = ((s8[8388608]{0:T(1024)(128)(4,1)}), s8[4194304]{0:T(1024)(128)(4,1)S(1)}, s32[]{:S(2)}) async-start(s8[8388608]{0:T(1024)(128)(4,1)} %bitcast.98), calls=%async_computation.7 | async-start | bytes 8388608
  383.8 1.2 collective-permute-start.9
  383.8 21.1 %collective-permute-start.13 = (f32[2,3,128]{2,1,0:T(4,128)S(1)}, f32[2,3,128]{2,1,0:T(4,128)S(1)}, u32[]{:S(2)}, u32[]{:S(2)}) collective-permute-start(f32[2,3,128]{2,1,0:T(4,128)S(1)} %pad_maximum_fusion.3), channel_id=1, source_target_pairs={{0,8},{8,0},{16,24},{24,16},{32,40},{40,32},{48,56},{56,48},{64,72... | collective-permute-start | bytes 9224 | tf_op jit(solution)/shard_map/ppermute | solution.py:24
  385.0 18.7 %collective-permute-start.10 = (f32[128]{0:T(128)S(1)}, f32[128]{0:T(128)S(1)}, u32[]{:S(2)}, u32[]{:S(2)}) collective-permute-start(f32[128]{0:T(128)S(1)} %add.100), channel_id=1, source_target_pairs={{0,16},{8,24},{16,0},{24,8},{32,48},{40,56},{48,32},{56,40},{64,80... | collective-permute-start | bytes 1544 | tf_op jit(solution)/shard_map/ppermute | solution.py:24
  395.7 298.7 %all-reduce.5.cloned.1.call-start = ((), (), s32[]{:S(2)}) async-start(), calls=%async_computation.5 | async-start | bytes 2097152 | tf_op jit(solution)/shard_map/psum | solution.py:76
  403.7 138.9 %collective-permute-start.11 = (f32[128]{0:T(128)S(1)}, f32[128]{0:T(128)S(1)}, u32[]{:S(2)}, u32[]{:S(2)}) collective-permute-start(f32[128]{0:T(128)S(1)} %add.101), channel_id=1, source_target_pairs={{0,32},{8,40},{16,48},{24,56},{32,0},{40,8},{48,16},{56,24},{64,96... | collective-permute-start | bytes 1544 | tf_op jit(solution)/shard_map/ppermute | solution.py:24
  405.0 138.4 %collective-permute-start.14 = (f32[2,3,128]{2,1,0:T(4,128)S(1)}, f32[2,3,128]{2,1,0:T(4,128)S(1)}, u32[]{:S(2)}, u32[]{:S(2)}) collective-permute-start(f32[2,3,128]{2,1,0:T(4,128)S(1)} %fusion.42), channel_id=1, source_target_pairs={{0,16},{8,24},{16,0},{24,8},{32,48},{40,56},{48,32},{56,40},{64,80... | collective-permute-start | bytes 9224 | tf_op jit(solution)/shard_map/ppermute | solution.py:24
  542.1 6.5 collective-permute-start.6
  542.5 8.1 %collective-permute-start.12 = (f32[128]{0:T(128)S(1)}, f32[128]{0:T(128)S(1)}, u32[]{:S(2)}, u32[]{:S(2)}) collective-permute-start(f32[128]{0:T(128)S(1)} %add.102), channel_id=1, source_target_pairs={{0,64},{8,72},{16,80},{24,88},{32,96},{40,104},{48,112},{56,120},{... | collective-permute-start | bytes 1544 | tf_op jit(solution)/shard_map/ppermute | solution.py:24
  543.4 4.0 collective-permute-start.15
  547.4 8.2 %collective-permute-start.16 = (f32[2,3,128]{2,1,0:T(4,128)S(1)}, f32[2,3,128]{2,1,0:T(4,128)S(1)}, u32[]{:S(2)}, u32[]{:S(2)}) collective-permute-start(f32[2,3,128]{2,1,0:T(4,128)S(1)} %add.106), channel_id=1, source_target_pairs={{0,64},{8,72},{16,80},{24,88},{32,96},{40,104},{48,112},{56,120},{... | collective-permute-start | bytes 9224 | tf_op jit(solution)/shard_map/ppermute | solution.py:24
  548.6 4.7 collective-permute-start.7
  553.3 5.0 collective-permute-start.8
  558.2 138.5 %copy-start.1 = (bf16[512,512]{1,0:T(8,128)(2,1)S(1)}, bf16[512,512]{1,0:T(8,128)(2,1)}, u32[]{:S(2)}) copy-start(bf16[512,512]{1,0:T(8,128)(2,1)} %param.11) | copy-start | bytes 1572868
Sparse Core Ops, SparseCore 0:
  395.9 146.1 all-reduce.2
  547.4 147.0 all-reduce.4

commit v2 on v1

--- a/solution.py
+++ b/solution.py
@@ -24,6 +24,31 @@
         value = jax.tree.map(lambda v, r: v + r, value, lax.ppermute(value, axis, pairs))
         step *= 2
     return value
+
+
+def exchange(value, axis, step):
+    count = lax.axis_size(axis)
+    return lax.ppermute(value, axis, [(source, source ^ step) for source in range(count)])
+
+
+def tree_allreduce(value, rounds):
+    kept = []
+    for axis, step in rounds:
+        upper = (lax.axis_index(axis) // step) % 2 == 1
+        half = value.shape[0] // 2
+        low, high = value[:half], value[half:]
+        keep = jnp.where(upper, high, low)
+        value = keep + exchange(jnp.where(upper, low, high), axis, step)
+        kept.append((axis, step, upper))
+    for axis, step, upper in reversed(kept):
+        other = exchange(value, axis, step)
+        value = jnp.where(
+            upper, jnp.concatenate([other, value]), jnp.concatenate([value, other])
+        )
+    return value
+
+
+FACTOR_ROUNDS = (("ctx", 1), ("ctx", 2), ("ch", 1), ("ctx", 8), ("ctx", 4), ("ch", 2), ("ch", 4))
 
 
 def on_device(inputs, norm_gain, conv_taps, factor_one, factor_two, kernel, grad_out):
@@ -64,7 +89,7 @@
     kernel_grad = (grad_spec * columns.astype(jnp.float32)).astype(jnp.bfloat16)
     grad_section = (grad_spec * kern).astype(jnp.bfloat16)
     two_part = jnp.einsum("ijc,kjc->ik", spectrum, grad_columns, preferred_element_type=jnp.float32)
-    two_total = lax.psum(two_part, ("ctx", "ch"))
+    two_total = tree_allreduce(two_part, FACTOR_ROUNDS)
     grad_rows = lax.all_to_all(grad_section, "ctx", split_axis=0, concat_axis=1, tiled=True)
     back_flat = back_rows.reshape(rows, chans).astype(jnp.float32)
     grad_gate_pre = cotangent * back_flat * gate * (1.0 - gate)
@@ -72,8 +97,7 @@
         "ikc,jk->ijc", grad_rows, factor_one, preferred_element_type=jnp.float32
     ).reshape(rows, chans)
     one_part = jnp.einsum("ijc,ikc->jk", mixed_in, grad_rows, preferred_element_type=jnp.float32)
-    two_total, one_part = lax.optimization_barrier((two_total, one_part))
-    one_total = lax.psum(one_part, ("ctx", "ch"))
+    one_total = tree_allreduce(one_part, FACTOR_ROUNDS)
     later_value, later_gate = shifted(
         (grad_mixed[: taps_count - 1], grad_gate_pre[: taps_count - 1]), "ctx", -1
     )

time: 712 us -> 563 us (0.79)
  waiting for transfers between devices: 407 us -> 214 us
  starting transfers between devices: 54.1 us -> 106 us
  between operations: 14.6 us -> 1.76 us
    psum x2 -> x0, waiting for transfers between devices: 255 us -> none  [the longest x1 130 us: on_device(): two_total = lax.psum(two_part, ('ctx', 'ch'))]
    ppermute x0 -> x28, waiting for transfers between devices: none -> 127 us  [exchange(): lax.ppermute(value, axis, [(source, source ^ step) for source in range(co...]
    ppermute x0 -> x28, starting transfers between devices: none -> 48.3 us  [exchange(): lax.ppermute(value, axis, [(source, source ^ step) for source in range(co...]
    all_to_all x1, waiting for transfers between devices: 47.8 us -> 0.01 us  [on_device(): lax.all_to_all(grad_section, 'ctx', split_axis=0, concat_axis=1, tiled=True)]
    all_to_all x1, waiting for transfers between devices: 31.3 us -> 0.01 us  [on_device(): lax.all_to_all(section_two, 'ctx', split_axis=0, concat_axis=1, tiled=True)]
    all_to_all x1, waiting for transfers between devices: 12.1 us -> 35 us  [on_device(): lax.all_to_all(out_grad, 'ctx', split_axis=1, concat_axis=0, tiled=True)]
    unnamed x39 -> x47, local copies, waits for them, and re-layouts: 24.5 us -> 28.7 us
  transfers between devices with their start and end apart: 23 -> 49, of which waited for: 15 -> 21; matrix products, arithmetic and copies ran while one was open for 18% -> 30% of each run, Pallas kernels for 0% -> 0%
where the time goes in v2:
time: 563 us; the launch traced here: 555 us
  waiting for transfers between devices  214 us (38%)
  starting transfers between devices  106 us (19%)
  local copies, waits for them, and re-layouts  105 us (19%)
  other arithmetic  83.1 us (15%)
  matrix products  45.4 us (8%)
    ppermute x28, waiting for transfers between devices, exchange(): lax.ppermute(value, axis, [(source, source ^ step) for source in range(co...  127 us
    ppermute x28, starting transfers between devices, exchange(): lax.ppermute(value, axis, [(source, source ^ step) for source in range(co...  48.3 us
    all_to_all x1, waiting for transfers between devices, on_device(): lax.all_to_all(section_one, 'ctx', split_axis=1, concat_axis=0, tiled=True)  42.3 us
    all_to_all x1, waiting for transfers between devices, on_device(): lax.all_to_all(out_grad, 'ctx', split_axis=1, concat_axis=0, tiled=True)  35 us
    unnamed x47, local copies, waits for them, and re-layouts  28.7 us
    reduce_sum x1, other arithmetic, on_device(): gain_part = jnp.sum(grad_normed * hat, axis=0)  21.9 us
    ppermute x14, starting transfers between devices, tree_psum(): lax.ppermute(value, axis, pairs)  21.4 us
    reduce_sum x1, other arithmetic, on_device(): gate_taps.append(jnp.sum(grad_gate_pre * window, axis=0))  15.2 us
  transfers between devices with their start and end apart: 49, of which 21 were waited for; matrix products, arithmetic and copies ran while one was open for 30% of the time, Pallas kernels for 0%

profile of v2, /device:TPU:1, one launch (start us, length us, event | category | flops | bytes accessed | tf_op | source)
XLA Modules:
  0.0 555.4 jit_solution(13084382494776622928)
XLA Ops:
  0.6 6.5 %copy.43 = bf16[32,512,128]{1,2,0:T(8,128)(2,1)} copy(bf16[32,512,128]{2,1,0:T(8,128)(2,1)} %param.7) | data formatting | bytes 8388608 | tf_op args[0]
  7.1 3.1 multiply_reduce_fusion.3
  14.1 3.1 collective-permute-start.1
  18.8 3.9 collective-permute-start.2
  22.7 7.1 %copy.44 = f32[32,512,128]{2,1,0:T(8,128)} copy(bf16[32,512,128]{1,2,0:T(8,128)(2,1)} %copy.43) | data formatting | bytes 12582912 | tf_op jit(solution)/shard_map/convert_element_type | solution.py:58
  29.8 5.5 multiply_convert_fusion.2
  35.3 6.3 %collective-permute-start.3 = (bf16[2,128]{1,0:T(2,128)(2,1)S(1)}, bf16[2,128]{1,0:T(2,128)(2,1)S(1)}, u32[]{:S(2)}, u32[]{:S(2)}) collective-permute-start(bf16[2,128]{1,0:T(2,128)(2,1)S(1)} %slice.180), channel_id=1, source_target_pairs={{0,8},{8,16},{16,24},{24,32},{32,40},{40,48},{48,56},{56,64},{64,7... | collective-permute-start | bytes 1544 | tf_op jit(solution)/shard_map/ppermute | solution.py:16
  42.4 6.5 %fusion.10 = (bf16[16384,128]{1,0:T(8,128)(2,1)S(1)}, bf16[16384,128]{1,0:T(8,128)(2,1)}) fusion(bf16[32,512,128]{2,1,0:T(8,128)(2,1)S(1)} %copy-done.9, bf16[16384,128]{1,0:T(8,128)(2,1)S(1)} %multiply_convert_fusion.2, bf16[2,128]{1,0:T(2,128)(2,1)S(1)} %collective-permute-done.3, f32[128]{0:T(128)S(1)} %get-tuple-element.40, ...), kind=kLoop, calls=%fused_computation.29 | loop fusion | flops 44040192 | bytes 16779264 | tf_op jit(solution)/shard_map/convert_element_type | solution.py:77
  48.9 4.7 copy.45
  53.5 6.6 %all-to-all-start = ((bf16[32,512,128]{2,0,1:T(8,128)(2,1)}), bf16[32,512,128]{2,0,1:T(8,128)(2,1)}, u32[]{:S(2)}, u32[]{:S(2)}) async-start(bf16[32,512,128]{2,0,1:T(8,128)(2,1)} %copy.45), calls=%async_computation | async-start | bytes 8388608 | tf_op jit(solution)/shard_map/all_to_all | solution.py:85
  60.2 6.3 %fusion.21 = bf16[16384,128]{1,0:T(8,128)(2,1)S(1)} fusion(bf16[16384,128]{1,0:T(8,128)(2,1)} %copy-done.4, bf16[16384,128]{1,0:T(8,128)(2,1)} %get-tuple-element.36, f32[128]{0:T(128)S(1)} %get-tuple-element.43, f32[128]{0:T(128)S(1)} %get-tuple-element.44, f32[128]{0:T(128)S(1)} %get-tuple-element.39, bf16[2,128]{1,0:T(2,128)(2,1)S(1)} %collective-permute-done.3), kind=kLoop, calls=%fused_computation.40 | loop fusion | flops 25165824 | bytes 12584960 | tf_op jit(solution)/shard_map/convert_element_type | solution.py:71
  68.5 4.4 convert_bitcast_fusion.3
  73.0 7.9 %copy.55 = bf16[32,512,128]{2,0,1:T(8,128)(2,1)} copy(bf16[32,512,128]{1,2,0:T(8,128)(2,1)} %convert_bitcast_fusion.3) | data formatting | bytes 8388608 | tf_op jit(solution)/shard_map/convert_element_type | solution.py:76
  80.8 35.0 %all-to-all-done = bf16[32,512,128]{2,0,1:T(8,128)(2,1)} async-done(((bf16[32,512,128]{2,0,1:T(8,128)(2,1)}), bf16[32,512,128]{2,0,1:T(8,128)(2,1)}, u32[]{:S(2)}, u32[]{:S(2)}) %all-to-all-start) | async-done | bytes 4194336 | tf_op jit(solution)/shard_map/all_to_all | solution.py:85
  115.9 4.9 all-to-all-start.2
  120.7 7.5 %copy.49 = bf16[512,32,128]{0,2,1:T(8,128)(2,1)} copy(bf16[512,32,128]{2,1,0:T(8,128)(2,1)} %param.12) | data formatting | bytes 8388608 | tf_op args[5]
  128.2 5.9 %copy.47 = bf16[16,32,32,128]{3,2,1,0:T(8,128)(2,1)} copy(bf16[16,32,32,128]{3,1,2,0:T(8,128)(2,1)} %bitcast.9) | data formatting | bytes 8388608 | tf_op jit(solution)/shard_map/all_to_all | solution.py:85
  134.2 42.3 %all-to-all-done.2 = bf16[32,512,128]{2,0,1:T(8,128)(2,1)} async-done(((bf16[32,512,128]{2,0,1:T(8,128)(2,1)}), bf16[32,512,128]{2,0,1:T(8,128)(2,1)}, u32[]{:S(2)}, u32[]{:S(2)}) %all-to-all-start.2) | async-done | bytes 4194336 | tf_op jit(solution)/shard_map/all_to_all | solution.py:78
  176.4 3.8 copy.56
  181.4 4.3 copy.57
  185.7 10.0 %copy.58 = f32[512,32,128]{0,2,1:T(8,128)} copy(f32[512,32,128]{2,1,0:T(8,128)} %bitcast.106) | data formatting | bytes 16777216 | tf_op jit(solution)/shard_map/convert_element_type | solution.py:80
  195.7 10.3 %fusion.35 = f32[512,512]{1,0:T(8,128)S(1)} fusion(bf16[512,32,128]{2,1,0:T(8,128)(2,1)} %bitcast.104, f32[512,32,128]{0,2,1:T(8,128)} %copy.58, bf16[512,32,128]{0,2,1:T(8,128)(2,1)} %copy.49), kind=kOutput, calls=%fused_computation.73 | convolution fusion | flops 2153775104 | bytes 17825792 | tf_op jit(solution)/shard_map/ijc,kjc->ik/dot_general | solution.py:91
  208.7 9.1 %fusion.29 = (bf16[512,32,128]{0,2,1:T(8,128)(2,1)}, bf16[512,32,128]{0,2,1:T(8,128)(2,1)}) fusion(f32[512,32,128]{0,2,1:T(8,128)S(1)} %copy-done.2, bf16[512,32,128]{0,2,1:T(8,128)(2,1)S(1)} %copy-done.3, bf16[512,512]{1,0:T(8,128)(2,1)S(1)} %copy-done, bf16[512,32,128]{2,1,0:T(8,128)(2,1)S(1)} %bitcast.105), kind=kOutput, calls=%fused_computation.53 | convolution fusion | flops 2157969408 | bytes 25690112 | tf_op jit(solution)/shard_map/kjc,ik->ijc/dot_general | solution.py:86
  217.8 8.0 %copy.50 = bf16[512,32,128]{2,1,0:T(8,128)(2,1)} copy(bf16[512,32,128]{0,2,1:T(8,128)(2,1)} %get-tuple-element.38) | data formatting | bytes 8388608 | tf_op jit(solution)/shard_map/convert_element_type | solution.py:90
  225.8 4.5 all-to-all-start.1
  233.8 57.9 %collective-permute-done.24 = f32[128,512]{1,0:T(8,128)S(1)} collective-permute-done((f32[128,512]{1,0:T(8,128)S(1)}, f32[128,512]{1,0:T(8,128)S(1)}, u32[]{:S(2)}, u32[]{:S(2)}) %collective-permute-start.24) | collective-permute-done | bytes 262176 | tf_op jit(solution)/shard_map/ppermute | solution.py:31
  293.1 3.3 collective-permute-done.25
  296.5 3.1 collective-permute-done.26
  300.7 3.3 collective-permute-done.27
  304.0 2.8 collective-permute-start.28
  309.1 8.9 %convert_bitcast_fusion.2 = bf16[512,32,128]{0,2,1:T(8,128)(2,1)} fusion(bf16[512,512]{1,0:T(8,128)(2,1)S(1)} %copy-done, f32[512,32,128]{0,2,1:T(8,128)} %copy.58, bf16[512,32,128]{0,2,1:T(8,128)(2,1)} %copy.49), kind=kOutput, calls=%fused_computation.66 | convolution fusion | flops 2155872256 | bytes 17301504 | tf_op jit(solution)/shard_map/ijc,ik->kjc/dot_general | solution.py:81
  318.1 7.9 %copy.59 = bf16[512,32,128]{2,1,0:T(8,128)(2,1)} copy(bf16[512,32,128]{0,2,1:T(8,128)(2,1)} %convert_bitcast_fusion.2) | data formatting | bytes 8388608 | tf_op jit(solution)/shard_map/convert_element_type | solution.py:83
  326.0 9.4 %all-to-all-start.3 = ((bf16[512,32,128]{2,1,0:T(8,128)(2,1)}), bf16[512,32,128]{2,1,0:T(8,128)(2,1)}, u32[]{:S(2)}, u32[]{:S(2)}) async-start(bf16[512,32,128]{2,1,0:T(8,128)(2,1)} %copy.59), calls=%async_computation.3 | async-start | bytes 8388608 | tf_op jit(solution)/shard_map/all_to_all | solution.py:84
  337.9 41.3 %collective-permute-done.30 = f32[4,512]{1,0:T(4,128)S(1)} collective-permute-done((f32[4,512]{1,0:T(4,128)S(1)}, f32[4,512]{1,0:T(4,128)S(1)}, u32[]{:S(2)}, u32[]{:S(2)}) %collective-permute-start.30) | collective-permute-done | bytes 8224 | tf_op jit(solution)/shard_map/ppermute | solution.py:31
  383.8 8.0 %collective-permute-done.32 = f32[16,512]{1,0:T(8,128)S(1)} collective-permute-done((f32[16,512]{1,0:T(8,128)S(1)}, f32[16,512]{1,0:T(8,128)S(1)}, u32[]{:S(2)}, u32[]{:S(2)}) %collective-permute-start.32) | collective-permute-done | bytes 32800 | tf_op jit(solution)/shard_map/ppermute | solution.py:31
  396.4 3.4 copy.51
  405.2 4.6 collective-permute-start.35
  409.8 7.8 %copy.64 = bf16[512,32,128]{2,1,0:T(8,128)(2,1)} copy(bf16[512,32,128]{0,2,1:T(8,128)(2,1)} %get-tuple-element.37) | data formatting | bytes 8388608
  420.0 10.3 %multiply_reduce_fusion = (f32[128]{0:T(128)S(1)}, f32[32,512,128]{1,2,0:T(8,128)}) fusion(f32[128]{0:T(128)S(1)} %copy-done.15, f32[32,512]{1,0:T(8,128)S(1)} %mul.250, bf16[32,512,128]{1,2,0:T(8,128)(2,1)} %copy.43, bf16[32,512,128]{2,1,0:T(8,128)(2,1)} %bitcast.112, bf16[512,512]{1,0:T(8,128)(2,1)S(1)} %copy-done.14), kind=kOutput, calls=%fused_computation.55 | convolution fusion | flops 2162163712 | bytes 17368064 | tf_op jit(solution)/shard_map/ikc,jk->ijc/dot_general | solution.py:96
  430.8 3.4 convert_bitcast_fusion
  434.2 4.3 copy.60
  438.5 9.0 %copy.53 = f32[32,512,128]{2,1,0:T(8,128)} copy(f32[32,512,128]{1,2,0:T(8,128)} %get-tuple-element.46) | data formatting | bytes 16777216 | tf_op jit(solution)/shard_map/ikc,jk->ijc/transpose | solution.py:96
  448.3 15.2 %fusion.22 = (f32[128]{0:T(128)S(1)}, f32[128]{0:T(128)S(1)}, f32[128]{0:T(128)S(1)}, f32[128]{0:T(128)S(1)}, f32[128]{0:T(128)S(1)}, /*index=5*/f32[16384,128]{1,0:T(8,128)S(1)}) fusion(bf16[16384,128]{1,0:T(8,128)(2,1)} %copy-done.4, bf16[2,128]{1,0:T(2,128)(2,1)S(1)} %collective-permute-done.3, bf16[16384,128]{1,0:T(8,128)(2,1)} %get-tuple-element.36, ...), kind=kLoop, calls=%fused_computation.41 | loop fusion | flops 60816768 | bytes 37753344 | tf_op jit(solution)/shard_map/reduce_sum | solution.py:114
  463.6 3.2 copy-done.6
  474.5 21.9 %multiply_reduce_fusion.1 = (f32[128]{0:T(128)S(1)}, f32[16384]{0:T(1024)S(1)}, f32[16384,128]{1,0:T(8,128)}) fusion(f32[32,512,128]{2,1,0:T(8,128)S(1)} %bitcast.99, f32[16384]{0:T(1024)S(1)} %add_rsqrt_fusion, f32[128]{0:T(128)S(1)} %copy-done.15, f32[2,128]{1,0:T(2,128)S(1)} %collective-permute-done.5, f32[16384,128]{1,0:T(8,128)} %copy-done.6, ...), kind=kLoop, calls=%fused_computation.57 | loop fusion | flops 44023680 | bytes 33691648 | tf_op jit(solution)/shard_map/reduce_sum | solution.py:116
  530.5 2.9 collective-permute-done.8
  535.1 7.5 %collective-permute-start.22 = (f32[256,512]{1,0:T(8,128)S(1)}, f32[256,512]{1,0:T(8,128)S(1)}, u32[]{:S(2)}, u32[]{:S(2)}) collective-permute-start(f32[256,512]{1,0:T(8,128)S(1)} %maximum_select_fusion.2), channel_id=1, source_target_pairs={{0,8},{8,0},{16,24},{24,16},{32,40},{40,32},{48,56},{56,48},{64,72... | collective-permute-start | bytes 1572872 | tf_op jit(solution)/shard_map/ppermute | solution.py:31
  542.6 11.2 %multiply_convert_fusion.1 = bf16[16384,128]{1,0:T(8,128)(2,1)} fusion(f32[16384,128]{1,0:T(8,128)} %get-tuple-element.34, f32[32,512,128]{2,1,0:T(8,128)S(1)} %bitcast.99, f32[16384]{0:T(1024)S(1)} %add_multiply_fusion, f32[128]{0:T(128)S(1)} %copy-done.15, f32[16384]{0:T(1024)S(1)} %add_rsqrt_fusion), kind=kLoop, calls=%fused_computation.58 | loop fusion | flops 12582912 | bytes 21103104 | tf_op jit(solution)/shard_map/convert_element_type | solution.py:125
  (189 shorter events, 85.4 us)
Async XLA Ops:
  10.3 3.8 collective-permute-start
  14.1 4.7 collective-permute-start.1
  18.8 11.0 %collective-permute-start.2 = (f32[16384]{0:T(1024)S(1)}, f32[16384]{0:T(1024)S(1)}, u32[]{:S(2)}, u32[]{:S(2)}) collective-permute-start(f32[16384]{0:T(1024)S(1)} %add.157), channel_id=1, source_target_pairs={{0,4},{1,5},{2,6},{3,7},{4,0},{5,1},{6,2},{7,3},{8,12},{9,13},{10,... | collective-permute-start | bytes 196616 | tf_op jit(solution)/shard_map/ppermute | solution.py:24
  35.3 7.1 %collective-permute-start.3 = (bf16[2,128]{1,0:T(2,128)(2,1)S(1)}, bf16[2,128]{1,0:T(2,128)(2,1)S(1)}, u32[]{:S(2)}, u32[]{:S(2)}) collective-permute-start(bf16[2,128]{1,0:T(2,128)(2,1)S(1)} %slice.180), channel_id=1, source_target_pairs={{0,8},{8,16},{16,24},{24,32},{32,40},{40,48},{48,56},{56,64},{64,7... | collective-permute-start | bytes 1544 | tf_op jit(solution)/shard_map/ppermute | solution.py:16
  53.5 62.3 %all-to-all-start = ((bf16[32,512,128]{2,0,1:T(8,128)(2,1)}), bf16[32,512,128]{2,0,1:T(8,128)(2,1)}, u32[]{:S(2)}, u32[]{:S(2)}) async-start(bf16[32,512,128]{2,0,1:T(8,128)(2,1)} %copy.45), calls=%async_computation | async-start | bytes 8388608 | tf_op jit(solution)/shard_map/all_to_all | solution.py:85
  115.9 60.6 %all-to-all-start.2 = ((bf16[32,512,128]{2,0,1:T(8,128)(2,1)}), bf16[32,512,128]{2,0,1:T(8,128)(2,1)}, u32[]{:S(2)}, u32[]{:S(2)}) async-start(bf16[32,512,128]{2,0,1:T(8,128)(2,1)} %copy.55), calls=%async_computation.2 | async-start | bytes 8388608 | tf_op jit(solution)/shard_map/all_to_all | solution.py:78
  207.9 22.5 %collective-permute-start.23 = (f32[256,512]{1,0:T(8,128)}, f32[256,512]{1,0:T(8,128)}, u32[]{:S(2)}, u32[]{:S(2)}) collective-permute-start(f32[256,512]{1,0:T(8,128)} %slice_select_fusion), channel_id=1, source_target_pairs={{0,8},{8,0},{16,24},{24,16},{32,40},{40,32},{48,56},{56,48},{64,72... | collective-permute-start | bytes 1572872 | tf_op jit(solution)/shard_map/ppermute | solution.py:31
  225.8 100.2 %all-to-all-start.1 = ((bf16[512,32,128]{2,1,0:T(8,128)(2,1)}), bf16[512,32,128]{2,1,0:T(8,128)(2,1)}, u32[]{:S(2)}, u32[]{:S(2)}) async-start(bf16[512,32,128]{2,1,0:T(8,128)(2,1)} %copy.50), calls=%async_computation.1 | async-start | bytes 8388608 | tf_op jit(solution)/shard_map/all_to_all | solution.py:93
  231.6 60.1 %collective-permute-start.24 = (f32[128,512]{1,0:T(8,128)S(1)}, f32[128,512]{1,0:T(8,128)S(1)}, u32[]{:S(2)}, u32[]{:S(2)}) collective-permute-start(f32[128,512]{1,0:T(8,128)S(1)} %slice_select_fusion.2), channel_id=1, source_target_pairs={{0,16},{8,24},{16,0},{24,8},{32,48},{40,56},{48,32},{56,40},{64,80... | collective-permute-start | bytes 786440 | tf_op jit(solution)/shard_map/ppermute | solution.py:31
  291.8 4.5 collective-permute-start.25
  296.4 3.2 collective-permute-start.26
  299.6 4.3 collective-permute-start.27
  304.0 4.2 collective-permute-start.28
  308.2 27.3 %collective-permute-start.29 = (f32[4,512]{1,0:T(4,128)S(1)}, f32[4,512]{1,0:T(4,128)S(1)}, u32[]{:S(2)}, u32[]{:S(2)}) collective-permute-start(f32[4,512]{1,0:T(4,128)S(1)} %slice_select_fusion.12), channel_id=1, source_target_pairs={{0,4},{1,5},{2,6},{3,7},{4,0},{5,1},{6,2},{7,3},{8,12},{9,13},{10,... | collective-permute-start | bytes 24584 | tf_op jit(solution)/shard_map/ppermute | solution.py:31
  326.0 104.8 %all-to-all-start.3 = ((bf16[512,32,128]{2,1,0:T(8,128)(2,1)}), bf16[512,32,128]{2,1,0:T(8,128)(2,1)}, u32[]{:S(2)}, u32[]{:S(2)}) async-start(bf16[512,32,128]{2,1,0:T(8,128)(2,1)} %copy.59), calls=%async_computation.3 | async-start | bytes 8388608 | tf_op jit(solution)/shard_map/all_to_all | solution.py:84
  335.5 43.7 %collective-permute-start.30 = (f32[4,512]{1,0:T(4,128)S(1)}, f32[4,512]{1,0:T(4,128)S(1)}, u32[]{:S(2)}, u32[]{:S(2)}) collective-permute-start(f32[4,512]{1,0:T(4,128)S(1)} %select_add_fusion.12), channel_id=1, source_target_pairs={{0,4},{1,5},{2,6},{3,7},{4,0},{5,1},{6,2},{7,3},{8,12},{9,13},{10,... | collective-permute-start | bytes 24584 | tf_op jit(solution)/shard_map/ppermute | solution.py:31
  379.2 4.6 collective-permute-start.31
  383.8 8.0 %collective-permute-start.32 = (f32[16,512]{1,0:T(8,128)S(1)}, f32[16,512]{1,0:T(8,128)S(1)}, u32[]{:S(2)}, u32[]{:S(2)}) collective-permute-start(f32[16,512]{1,0:T(8,128)S(1)} %maximum_select_fusion.11), channel_id=1, source_target_pairs={{0,32},{8,40},{16,48},{24,56},{32,0},{40,8},{48,16},{56,24},{64,96... | collective-permute-start | bytes 98312 | tf_op jit(solution)/shard_map/ppermute | solution.py:31
  391.7 3.1 collective-permute-start.33
  394.9 10.3 %collective-permute-start.34 = (f32[64,512]{1,0:T(8,128)S(1)}, f32[64,512]{1,0:T(8,128)S(1)}, u32[]{:S(2)}, u32[]{:S(2)}) collective-permute-start(f32[64,512]{1,0:T(8,128)S(1)} %maximum_select_fusion.7), channel_id=1, source_target_pairs={{0,1},{1,0},{2,3},{3,2},{4,5},{5,4},{6,7},{7,6},{8,9},{9,8},{10,11... | collective-permute-start | bytes 393224 | tf_op jit(solution)/shard_map/ppermute | solution.py:31
  403.1 15.0 %collective-permute-start.9 = (f32[256,512]{1,0:T(8,128)}, f32[256,512]{1,0:T(8,128)}, u32[]{:S(2)}, u32[]{:S(2)}) collective-permute-start(f32[256,512]{1,0:T(8,128)} %slice_select_fusion.1), channel_id=1, source_target_pairs={{0,8},{8,0},{16,24},{24,16},{32,40},{40,32},{48,56},{56,48},{64,72... | collective-permute-start | bytes 1572872 | tf_op jit(solution)/shard_map/ppermute | solution.py:31
  405.2 12.4 %collective-permute-start.35 = (f32[128,512]{1,0:T(8,128)S(1)}, f32[128,512]{1,0:T(8,128)S(1)}, u32[]{:S(2)}, u32[]{:S(2)}) collective-permute-start(f32[128,512]{1,0:T(8,128)S(1)} %maximum_select_fusion.5), channel_id=1, source_target_pairs={{0,16},{8,24},{16,0},{24,8},{32,48},{40,56},{48,32},{56,40},{64,80... | collective-permute-start | bytes 786440 | tf_op jit(solution)/shard_map/ppermute | solution.py:31
  417.7 82.2 %collective-permute-start.36 = (f32[256,512]{1,0:T(8,128)S(1)}, f32[256,512]{1,0:T(8,128)}, u32[]{:S(2)}, u32[]{:S(2)}) collective-permute-start(f32[256,512]{1,0:T(8,128)S(1)} %maximum_select_fusion.3), channel_id=1, source_target_pairs={{0,8},{8,0},{16,24},{24,16},{32,40},{40,32},{48,56},{56,48},{64,72... | collective-permute-start | bytes 1572872 | tf_op jit(solution)/shard_map/ppermute | solution.py:31
  419.3 11.0 %collective-permute-start.10 = (f32[128,512]{1,0:T(8,128)S(1)}, f32[128,512]{1,0:T(8,128)S(1)}, u32[]{:S(2)}, u32[]{:S(2)}) collective-permute-start(f32[128,512]{1,0:T(8,128)S(1)} %slice_select_fusion.3), channel_id=1, source_target_pairs={{0,16},{8,24},{16,0},{24,8},{32,48},{40,56},{48,32},{56,40},{64,80... | collective-permute-start | bytes 786440 | tf_op jit(solution)/shard_map/ppermute | solution.py:31
  430.4 17.0 %collective-permute-start.11 = (f32[64,512]{1,0:T(8,128)S(1)}, f32[64,512]{1,0:T(8,128)S(1)}, u32[]{:S(2)}, u32[]{:S(2)}) collective-permute-start(f32[64,512]{1,0:T(8,128)S(1)} %slice_select_fusion.5), channel_id=1, source_target_pairs={{0,1},{1,0},{2,3},{3,2},{4,5},{5,4},{6,7},{7,6},{8,9},{9,8},{10,11... | collective-permute-start | bytes 393224 | tf_op jit(solution)/shard_map/ppermute | solution.py:31
  447.6 24.0 %collective-permute-start.12 = (f32[32,512]{1,0:T(8,128)S(1)}, f32[32,512]{1,0:T(8,128)S(1)}, u32[]{:S(2)}, u32[]{:S(2)}) collective-permute-start(f32[32,512]{1,0:T(8,128)S(1)} %slice_select_fusion.7), channel_id=1, source_target_pairs={{0,64},{8,72},{16,80},{24,88},{32,96},{40,104},{48,112},{56,120},{... | collective-permute-start | bytes 196616 | tf_op jit(solution)/shard_map/ppermute | solution.py:31
  466.8 7.0 %collective-permute-start.5 = (f32[2,128]{1,0:T(2,128)S(1)}, f32[2,128]{1,0:T(2,128)S(1)}, u32[]{:S(2)}, u32[]{:S(2)}) collective-permute-start(f32[2,128]{1,0:T(2,128)S(1)} %slice.186), channel_id=1, source_target_pairs={{8,0},{16,8},{24,16},{32,24},{40,32},{48,40},{56,48},{64,56},{72,6... | collective-permute-start | bytes 3080 | tf_op jit(solution)/shard_map/ppermute | solution.py:16
  469.6 4.9 collective-permute-start.4
  471.6 25.5 %collective-permute-start.13 = (f32[16,512]{1,0:T(8,128)S(1)}, f32[16,512]{1,0:T(8,128)S(1)}, u32[]{:S(2)}, u32[]{:S(2)}) collective-permute-start(f32[16,512]{1,0:T(8,128)S(1)} %slice_select_fusion.9), channel_id=1, source_target_pairs={{0,32},{8,40},{16,48},{24,56},{32,0},{40,8},{48,16},{56,24},{64,96... | collective-permute-start | bytes 98312 | tf_op jit(solution)/shard_map/ppermute | solution.py:31
  496.4 5.9 %collective-permute-start.37 = (f32[128]{0:T(128)S(1)}, f32[128]{0:T(128)S(1)}, u32[]{:S(2)}, u32[]{:S(2)}) collective-permute-start(f32[128]{0:T(128)S(1)} %get-tuple-element.24), channel_id=1, source_target_pairs={{0,8},{8,0},{16,24},{24,16},{32,40},{40,32},{48,56},{56,48},{64,72... | collective-permute-start | bytes 1544 | tf_op jit(solution)/shard_map/ppermute | solution.py:24
  497.1 5.6 %collective-permute-start.14 = (f32[8,512]{1,0:T(8,128)S(1)}, f32[8,512]{1,0:T(8,128)S(1)}, u32[]{:S(2)}, u32[]{:S(2)}) collective-permute-start(f32[8,512]{1,0:T(8,128)S(1)} %slice_select_fusion.11), channel_id=1, source_target_pairs={{0,2},{1,3},{2,0},{3,1},{4,6},{5,7},{6,4},{7,5},{8,10},{9,11},{10,... | collective-permute-start | bytes 49160 | tf_op jit(solution)/shard_map/ppermute | solution.py:31
  502.7 4.8 collective-permute-start.15
  505.0 6.8 %collective-permute-start.39 = (f32[128]{0:T(128)S(1)}, f32[128]{0:T(128)S(1)}, u32[]{:S(2)}, u32[]{:S(2)}) collective-permute-start(f32[128]{0:T(128)S(1)} %add.196), channel_id=1, source_target_pairs={{0,32},{8,40},{16,48},{24,56},{32,0},{40,8},{48,16},{56,24},{64,96... | collective-permute-start | bytes 1544 | tf_op jit(solution)/shard_map/ppermute | solution.py:24
  507.5 4.2 collective-permute-start.16
  509.0 5.0 collective-permute-start.41
  511.4 12.5 %collective-permute-start.6 = (f32[16384]{0:T(1024)S(1)}, f32[16384]{0:T(1024)S(1)}, u32[]{:S(2)}, u32[]{:S(2)}) collective-permute-start(f32[16384]{0:T(1024)S(1)} %get-tuple-element.25), channel_id=1, source_target_pairs={{0,1},{1,0},{2,3},{3,2},{4,5},{5,4},{6,7},{7,6},{8,9},{9,8},{10,11... | collective-permute-start | bytes 196616 | tf_op jit(solution)/shard_map/ppermute | solution.py:24
  511.8 10.0 %collective-permute-start.40 = (f32[128]{0:T(128)S(1)}, f32[128]{0:T(128)S(1)}, u32[]{:S(2)}, u32[]{:S(2)}) collective-permute-start(f32[128]{0:T(128)S(1)} %add.197), channel_id=1, source_target_pairs={{0,64},{8,72},{16,80},{24,88},{32,96},{40,104},{48,112},{56,120},{... | collective-permute-start | bytes 1544 | tf_op jit(solution)/shard_map/ppermute | solution.py:24
  511.8 4.3 collective-permute-start.17
  513.9 4.5 collective-permute-start.42
  516.1 4.3 collective-permute-start.18
  518.5 4.0 collective-permute-start.43
  520.4 5.3 collective-permute-start.19
  522.5 3.4 collective-permute-start.44
  524.0 4.7 collective-permute-start.7
  525.8 4.0 collective-permute-start.20
  528.7 4.7 collective-permute-start.8
  529.8 5.3 collective-permute-start.21
  535.1 18.7 %collective-permute-start.22 = (f32[256,512]{1,0:T(8,128)S(1)}, f32[256,512]{1,0:T(8,128)S(1)}, u32[]{:S(2)}, u32[]{:S(2)}) collective-permute-start(f32[256,512]{1,0:T(8,128)S(1)} %maximum_select_fusion.2), channel_id=1, source_target_pairs={{0,8},{8,0},{16,24},{24,16},{32,40},{40,32},{48,56},{56,48},{64,72... | collective-permute-start | bytes 1572872 | tf_op jit(solution)/shard_map/ppermute | solution.py:31
  (22 other events, 521.4 us)

commit v3 on v2

--- a/solution.py
+++ b/solution.py
@@ -90,6 +90,7 @@
     grad_section = (grad_spec * kern).astype(jnp.bfloat16)
     two_part = jnp.einsum("ijc,kjc->ik", spectrum, grad_columns, preferred_element_type=jnp.float32)
     two_total = tree_allreduce(two_part, FACTOR_ROUNDS)
+    back_rows, grad_section = lax.optimization_barrier((back_rows, grad_section))
     grad_rows = lax.all_to_all(grad_section, "ctx", split_axis=0, concat_axis=1, tiled=True)
     back_flat = back_rows.reshape(rows, chans).astype(jnp.float32)
     grad_gate_pre = cotangent * back_flat * gate * (1.0 - gate)

time: 563 us -> 535 us (0.950)
  waiting for transfers between devices: 214 us -> 190 us
  other arithmetic: 83.1 us -> 72.8 us
  starting transfers between devices: 106 us -> 112 us
    ppermute x28, waiting for transfers between devices: 127 us -> 86.1 us  [exchange(): lax.ppermute(value, axis, [(source, source ^ step) for source in range(co...]
    all_to_all x1, waiting for transfers between devices: 0.01 us -> 32.6 us  [on_device(): lax.all_to_all(section_two, 'ctx', split_axis=0, concat_axis=1, tiled=True)]
    all_to_all x1, waiting for transfers between devices: 35 us -> 12.1 us  [on_device(): lax.all_to_all(out_grad, 'ctx', split_axis=1, concat_axis=0, tiled=True)]
    convert_element_type x2 -> x0, local copies, waits for them, and re-layouts: 12.3 us -> none  [the longest x1 7.98 us: on_device(): grad_section = (grad_spec * kern).astype(jnp.bfloat16)]
    optimization_barrier x0 -> x1, local copies, waits for them, and re-layouts: none -> 7.97 us  [on_device(): lax.optimization_barrier((back_rows, grad_section))]
    all_to_all x1, waiting for transfers between devices: 42.3 us -> 48.8 us  [on_device(): lax.all_to_all(section_one, 'ctx', split_axis=1, concat_axis=0, tiled=True)]
    unnamed x47 -> x49, local copies, waits for them, and re-layouts: 28.7 us -> 28.8 us
  transfers between devices with their start and end apart: 49 -> 49, of which waited for: 21 -> 24; matrix products, arithmetic and copies ran while one was open for 30% -> 34% of each run, Pallas kernels for 0% -> 0%
where the time goes in v3:
time: 535 us; the launch traced here: 526 us
  waiting for transfers between devices  190 us (36%)
  starting transfers between devices  112 us (21%)
  local copies, waits for them, and re-layouts  107 us (20%)
  other arithmetic  72.8 us (14%)
  matrix products  43.1 us (8%)
    ppermute x28, waiting for transfers between devices, exchange(): lax.ppermute(value, axis, [(source, source ^ step) for source in range(co...  86.1 us
    ppermute x28, starting transfers between devices, exchange(): lax.ppermute(value, axis, [(source, source ^ step) for source in range(co...  53.9 us
    all_to_all x1, waiting for transfers between devices, on_device(): lax.all_to_all(section_one, 'ctx', split_axis=1, concat_axis=0, tiled=True)  48.8 us
    all_to_all x1, waiting for transfers between devices, on_device(): lax.all_to_all(section_two, 'ctx', split_axis=0, concat_axis=1, tiled=True)  32.6 us
    unnamed x49, local copies, waits for them, and re-layouts  28.8 us
    ppermute x14, starting transfers between devices, tree_psum(): lax.ppermute(value, axis, pairs)  23.1 us
    reduce_sum x1, other arithmetic, on_device(): gain_part = jnp.sum(grad_normed * hat, axis=0)  21.6 us
    reduce_sum x1, other arithmetic, on_device(): gate_taps.append(jnp.sum(grad_gate_pre * window, axis=0))  15 us
  transfers between devices with their start and end apart: 49, of which 24 were waited for; matrix products, arithmetic and copies ran while one was open for 34% of the time, Pallas kernels for 0%

profile of v3, /device:TPU:1, one launch (start us, length us, event | category | flops | bytes accessed | tf_op | source)
XLA Modules:
  0.0 526.2 jit_solution(15145877432180269577)
XLA Ops:
  0.6 6.5 %copy.43 = bf16[32,512,128]{1,2,0:T(8,128)(2,1)} copy(bf16[32,512,128]{2,1,0:T(8,128)(2,1)} %param.7) | data formatting | bytes 8388608 | tf_op args[0]
  7.1 3.1 multiply_reduce_fusion.3
  14.1 3.1 collective-permute-start.1
  18.8 3.9 collective-permute-start.2
  22.7 7.2 %copy.44 = f32[32,512,128]{2,1,0:T(8,128)} copy(bf16[32,512,128]{1,2,0:T(8,128)(2,1)} %copy.43) | data formatting | bytes 12582912 | tf_op jit(solution)/shard_map/convert_element_type | solution.py:58
  29.9 5.5 %multiply_convert_fusion.2 = bf16[16384,128]{1,0:T(8,128)(2,1)S(1)} fusion(f32[32,512,128]{2,1,0:T(8,128)} %copy.44, f32[128]{0:T(128)S(1)} %copy-done.14, f32[16384]{0:T(1024)S(1)} %add_rsqrt_fusion), kind=kLoop, calls=%fused_computation.59 | loop fusion | flops 6291456 | bytes 12648960 | tf_op jit(solution)/shard_map/convert_element_type | solution.py:62
  35.4 6.3 %collective-permute-start.3 = (bf16[2,128]{1,0:T(2,128)(2,1)S(1)}, bf16[2,128]{1,0:T(2,128)(2,1)S(1)}, u32[]{:S(2)}, u32[]{:S(2)}) collective-permute-start(bf16[2,128]{1,0:T(2,128)(2,1)S(1)} %slice.180), channel_id=1, source_target_pairs={{0,8},{8,16},{16,24},{24,32},{32,40},{40,48},{48,56},{56,64},{64,7... | collective-permute-start | bytes 1544 | tf_op jit(solution)/shard_map/ppermute | solution.py:16
  42.4 6.5 %fusion.10 = (bf16[16384,128]{1,0:T(8,128)(2,1)}, bf16[16384,128]{1,0:T(8,128)(2,1)S(1)}) fusion(bf16[32,512,128]{2,1,0:T(8,128)(2,1)S(1)} %copy-done.6, bf16[16384,128]{1,0:T(8,128)(2,1)S(1)} %multiply_convert_fusion.2, bf16[2,128]{1,0:T(2,128)(2,1)S(1)} %collective-permute-done.3, f32[128]{0:T(128)S(1)} %get-tuple-element.47, ...), kind=kLoop, calls=%fused_computation.29 | loop fusion | flops 44040192 | bytes 16779264 | tf_op jit(solution)/shard_map/convert_element_type | solution.py:77
  49.0 3.0 fusion.15
  54.1 4.5 convert_bitcast_fusion.2
  58.5 7.9 %copy.46 = bf16[32,512,128]{2,0,1:T(8,128)(2,1)} copy(bf16[32,512,128]{1,2,0:T(8,128)(2,1)} %convert_bitcast_fusion.2) | data formatting | bytes 8388608 | tf_op jit(solution)/shard_map/convert_element_type | solution.py:76
  66.4 6.6 %all-to-all-start = ((bf16[32,512,128]{2,0,1:T(8,128)(2,1)}), bf16[32,512,128]{2,0,1:T(8,128)(2,1)}, u32[]{:S(2)}, u32[]{:S(2)}) async-start(bf16[32,512,128]{2,0,1:T(8,128)(2,1)} %copy.46), calls=%async_computation | async-start | bytes 8388608 | tf_op jit(solution)/shard_map/all_to_all | solution.py:78
  73.1 6.9 %copy.53 = bf16[32,512,128]{2,0,1:T(8,128)(2,1)} copy(bf16[32,512,128]{2,1,0:T(8,128)(2,1)} %bitcast.111) | data formatting | bytes 8388608 | tf_op jit(solution)/shard_map/reshape | solution.py:77
  80.0 48.8 %all-to-all-done = bf16[32,512,128]{2,0,1:T(8,128)(2,1)} async-done(((bf16[32,512,128]{2,0,1:T(8,128)(2,1)}), bf16[32,512,128]{2,0,1:T(8,128)(2,1)}, u32[]{:S(2)}, u32[]{:S(2)}) %all-to-all-start) | async-done | bytes 4194336 | tf_op jit(solution)/shard_map/all_to_all | solution.py:78
  128.8 4.9 all-to-all-start.2
  133.6 7.5 %copy.49 = bf16[512,32,128]{0,2,1:T(8,128)(2,1)} copy(bf16[512,32,128]{2,1,0:T(8,128)(2,1)} %param.12) | data formatting | bytes 8388608 | tf_op args[5]
  141.1 3.8 copy.47
  146.1 4.3 copy.48
  150.4 10.0 %copy.50 = f32[512,32,128]{0,2,1:T(8,128)} copy(f32[512,32,128]{2,1,0:T(8,128)} %bitcast.109) | data formatting | bytes 16777216 | tf_op jit(solution)/shard_map/convert_element_type | solution.py:80
  160.4 8.9 %convert_bitcast_fusion.1 = bf16[512,32,128]{0,2,1:T(8,128)(2,1)} fusion(bf16[512,512]{1,0:T(8,128)(2,1)S(1)} %copy-done, f32[512,32,128]{0,2,1:T(8,128)} %copy.50, bf16[512,32,128]{0,2,1:T(8,128)(2,1)} %copy.49), kind=kOutput, calls=%fused_computation.65 | convolution fusion | flops 2155872256 | bytes 17301504 | tf_op jit(solution)/shard_map/ijc,ik->kjc/dot_general | solution.py:81
  169.3 7.9 %copy.51 = bf16[512,32,128]{2,1,0:T(8,128)(2,1)} copy(bf16[512,32,128]{0,2,1:T(8,128)(2,1)} %convert_bitcast_fusion.1) | data formatting | bytes 8388608 | tf_op jit(solution)/shard_map/convert_element_type | solution.py:83
  177.2 12.1 %all-to-all-done.2 = bf16[32,512,128]{2,0,1:T(8,128)(2,1)} async-done(((bf16[32,512,128]{2,0,1:T(8,128)(2,1)}), bf16[32,512,128]{2,0,1:T(8,128)(2,1)}, u32[]{:S(2)}, u32[]{:S(2)}) %all-to-all-start.2) | async-done | bytes 4194336 | tf_op jit(solution)/shard_map/all_to_all | solution.py:85
  189.3 5.4 %all-to-all-start.1 = ((bf16[512,32,128]{2,1,0:T(8,128)(2,1)}), bf16[512,32,128]{2,1,0:T(8,128)(2,1)}, u32[]{:S(2)}, u32[]{:S(2)}) async-start(bf16[512,32,128]{2,1,0:T(8,128)(2,1)} %copy.51), calls=%async_computation.1 | async-start | bytes 8388608 | tf_op jit(solution)/shard_map/all_to_all | solution.py:84
  194.8 4.1 copy.55
  198.9 8.1 %fusion.35 = f32[512,512]{1,0:T(8,128)S(1)} fusion(bf16[512,32,128]{2,1,0:T(8,128)(2,1)S(1)} %bitcast.107, f32[512,32,128]{0,2,1:T(8,128)} %copy.50, bf16[512,32,128]{0,2,1:T(8,128)(2,1)S(1)} %copy-done.3), kind=kOutput, calls=%fused_computation.72 | convolution fusion | flops 2153775104 | bytes 17825792 | tf_op jit(solution)/shard_map/ijc,kjc->ik/dot_general | solution.py:91
  208.9 9.0 %fusion.29 = (bf16[512,32,128]{0,2,1:T(8,128)(2,1)}, bf16[512,32,128]{0,2,1:T(8,128)(2,1)}) fusion(f32[512,32,128]{0,2,1:T(8,128)S(1)} %bitcast.102, bf16[512,32,128]{0,2,1:T(8,128)(2,1)S(1)} %copy-done.3, bf16[512,512]{1,0:T(8,128)(2,1)S(1)} %copy-done, bf16[512,32,128]{2,1,0:T(8,128)(2,1)S(1)} %bitcast.108), kind=kOutput, calls=%fused_computation.52 | convolution fusion | flops 2157969408 | bytes 25690112 | tf_op jit(solution)/shard_map/kjc,ik->ijc/dot_general | solution.py:86
  217.8 32.6 %all-to-all-done.1 = bf16[512,32,128]{2,1,0:T(8,128)(2,1)} async-done(((bf16[512,32,128]{2,1,0:T(8,128)(2,1)}), bf16[512,32,128]{2,1,0:T(8,128)(2,1)}, u32[]{:S(2)}, u32[]{:S(2)}) %all-to-all-start.1) | async-done | bytes 4194336 | tf_op jit(solution)/shard_map/all_to_all | solution.py:84
  250.5 5.4 %copy.52 = bf16[32,16,32,128]{3,2,1,0:T(8,128)(2,1)} copy(bf16[32,16,32,128]{3,2,0,1:T(8,128)(2,1)} %bitcast.13) | data formatting | bytes 8388608 | tf_op jit(solution)/shard_map/all_to_all | solution.py:84
  255.9 8.0 %copy.57 = bf16[512,32,128]{2,1,0:T(8,128)(2,1)} copy(bf16[512,32,128]{0,2,1:T(8,128)(2,1)} %get-tuple-element.8) | data formatting | bytes 8388608 | tf_op jit(solution)/shard_map/optimization_barrier | solution.py:93
  263.9 4.9 all-to-all-start.3
  271.9 58.1 %collective-permute-done.24 = f32[128,512]{1,0:T(8,128)S(1)} collective-permute-done((f32[128,512]{1,0:T(8,128)S(1)}, f32[128,512]{1,0:T(8,128)S(1)}, u32[]{:S(2)}, u32[]{:S(2)}) %collective-permute-start.24) | collective-permute-done | bytes 262176 | tf_op jit(solution)/shard_map/ppermute | solution.py:31
  331.3 3.2 collective-permute-done.25
  334.7 3.1 collective-permute-done.26
  339.0 3.1 collective-permute-done.27
  342.2 3.0 collective-permute-start.28
  347.5 3.1 collective-permute-done.29
  360.0 3.6 copy.58
  366.1 9.4 %collective-permute-start.9 = (f32[256,512]{1,0:T(8,128)S(1)}, f32[256,512]{1,0:T(8,128)S(1)}, u32[]{:S(2)}, u32[]{:S(2)}) collective-permute-start(f32[256,512]{1,0:T(8,128)S(1)} %slice_select_fusion.1), channel_id=1, source_target_pairs={{0,8},{8,0},{16,24},{24,16},{32,40},{40,32},{48,56},{56,48},{64,72... | collective-permute-start | bytes 1572872 | tf_op jit(solution)/shard_map/ppermute | solution.py:31
  385.3 7.8 %copy.64 = bf16[512,32,128]{2,1,0:T(8,128)(2,1)} copy(bf16[512,32,128]{0,2,1:T(8,128)(2,1)} %get-tuple-element.41) | data formatting | bytes 8388608
  397.0 10.4 %multiply_reduce_fusion = (f32[128]{0:T(128)S(1)}, f32[32,512,128]{1,2,0:T(8,128)}) fusion(f32[128]{0:T(128)S(1)} %copy-done.14, f32[32,512]{1,0:T(8,128)S(1)} %mul.250, bf16[32,512,128]{1,2,0:T(8,128)(2,1)} %copy.43, bf16[32,512,128]{2,1,0:T(8,128)(2,1)} %bitcast.116, bf16[512,512]{1,0:T(8,128)(2,1)S(1)} %copy-done.13), kind=kOutput, calls=%fused_computation.54 | convolution fusion | flops 2162163712 | bytes 17368064 | tf_op jit(solution)/shard_map/ikc,jk->ijc/dot_general | solution.py:97
  407.4 9.0 %copy.60 = f32[32,512,128]{2,1,0:T(8,128)} copy(f32[32,512,128]{1,2,0:T(8,128)} %get-tuple-element.50) | data formatting | bytes 16777216 | tf_op jit(solution)/shard_map/ikc,jk->ijc/transpose | solution.py:97
  417.8 15.0 %fusion.22 = (f32[128]{0:T(128)S(1)}, f32[128]{0:T(128)S(1)}, f32[128]{0:T(128)S(1)}, f32[128]{0:T(128)S(1)}, f32[128]{0:T(128)S(1)}, /*index=5*/f32[16384,128]{1,0:T(8,128)S(1)}) fusion(bf16[16384,128]{1,0:T(8,128)(2,1)} %copy-done.2, bf16[2,128]{1,0:T(2,128)(2,1)S(1)} %collective-permute-done.3, bf16[16384,128]{1,0:T(8,128)(2,1)} %copy-done.4, ...), kind=kLoop, calls=%fused_computation.41 | loop fusion | flops 62913920 | bytes 33559040 | tf_op jit(solution)/shard_map/reduce_sum | solution.py:115
  432.8 3.3 copy-done.5
  436.1 4.7 collective-permute-start.5
  445.9 21.6 %multiply_reduce_fusion.1 = (f32[128]{0:T(128)S(1)}, f32[16384]{0:T(1024)S(1)}, f32[16384,128]{1,0:T(8,128)}) fusion(f32[32,512,128]{2,1,0:T(8,128)S(1)} %bitcast.100, f32[16384]{0:T(1024)S(1)} %add_rsqrt_fusion, f32[128]{0:T(128)S(1)} %copy-done.14, f32[2,128]{1,0:T(2,128)S(1)} %collective-permute-done.5, f32[16384,128]{1,0:T(8,128)} %copy-done.5, ...), kind=kLoop, calls=%fused_computation.56 | loop fusion | flops 44023680 | bytes 33691648 | tf_op jit(solution)/shard_map/reduce_sum | solution.py:117
  473.7 4.5 collective-permute-start.39
  507.1 6.3 %collective-permute-start.22 = (f32[256,512]{1,0:T(8,128)S(1)}, f32[256,512]{1,0:T(8,128)S(1)}, u32[]{:S(2)}, u32[]{:S(2)}) collective-permute-start(f32[256,512]{1,0:T(8,128)S(1)} %maximum_select_fusion.2), channel_id=1, source_target_pairs={{0,8},{8,0},{16,24},{24,16},{32,40},{40,32},{48,56},{56,48},{64,72... | collective-permute-start | bytes 1572872 | tf_op jit(solution)/shard_map/ppermute | solution.py:31
  513.4 11.2 %multiply_convert_fusion.1 = bf16[16384,128]{1,0:T(8,128)(2,1)} fusion(f32[16384,128]{1,0:T(8,128)} %get-tuple-element.38, f32[32,512,128]{2,1,0:T(8,128)S(1)} %bitcast.100, f32[16384]{0:T(1024)S(1)} %add_multiply_fusion, f32[128]{0:T(128)S(1)} %copy-done.14, f32[16384]{0:T(1024)S(1)} %add_rsqrt_fusion), kind=kLoop, calls=%fused_computation.57 | loop fusion | flops 12582912 | bytes 21103104 | tf_op jit(solution)/shard_map/convert_element_type | solution.py:126
  (191 shorter events, 87.7 us)
Async XLA Ops:
  10.3 3.8 collective-permute-start
  14.1 4.7 collective-permute-start.1
  18.8 11.1 %collective-permute-start.2 = (f32[16384]{0:T(1024)S(1)}, f32[16384]{0:T(1024)S(1)}, u32[]{:S(2)}, u32[]{:S(2)}) collective-permute-start(f32[16384]{0:T(1024)S(1)} %add.157), channel_id=1, source_target_pairs={{0,4},{1,5},{2,6},{3,7},{4,0},{5,1},{6,2},{7,3},{8,12},{9,13},{10,... | collective-permute-start | bytes 196616 | tf_op jit(solution)/shard_map/ppermute | solution.py:24
  35.4 7.1 %collective-permute-start.3 = (bf16[2,128]{1,0:T(2,128)(2,1)S(1)}, bf16[2,128]{1,0:T(2,128)(2,1)S(1)}, u32[]{:S(2)}, u32[]{:S(2)}) collective-permute-start(bf16[2,128]{1,0:T(2,128)(2,1)S(1)} %slice.180), channel_id=1, source_target_pairs={{0,8},{8,16},{16,24},{24,32},{32,40},{40,48},{48,56},{56,64},{64,7... | collective-permute-start | bytes 1544 | tf_op jit(solution)/shard_map/ppermute | solution.py:16
  66.4 62.3 %all-to-all-start = ((bf16[32,512,128]{2,0,1:T(8,128)(2,1)}), bf16[32,512,128]{2,0,1:T(8,128)(2,1)}, u32[]{:S(2)}, u32[]{:S(2)}) async-start(bf16[32,512,128]{2,0,1:T(8,128)(2,1)} %copy.46), calls=%async_computation | async-start | bytes 8388608 | tf_op jit(solution)/shard_map/all_to_all | solution.py:78
  128.8 60.6 %all-to-all-start.2 = ((bf16[32,512,128]{2,0,1:T(8,128)(2,1)}), bf16[32,512,128]{2,0,1:T(8,128)(2,1)}, u32[]{:S(2)}, u32[]{:S(2)}) async-start(bf16[32,512,128]{2,0,1:T(8,128)(2,1)} %copy.53), calls=%async_computation.2 | async-start | bytes 8388608 | tf_op jit(solution)/shard_map/all_to_all | solution.py:85
  189.3 61.1 %all-to-all-start.1 = ((bf16[512,32,128]{2,1,0:T(8,128)(2,1)}), bf16[512,32,128]{2,1,0:T(8,128)(2,1)}, u32[]{:S(2)}, u32[]{:S(2)}) async-start(bf16[512,32,128]{2,1,0:T(8,128)(2,1)} %copy.51), calls=%async_computation.1 | async-start | bytes 8388608 | tf_op jit(solution)/shard_map/all_to_all | solution.py:84
  208.8 59.9 %collective-permute-start.23 = (f32[256,512]{1,0:T(8,128)}, f32[256,512]{1,0:T(8,128)}, u32[]{:S(2)}, u32[]{:S(2)}) collective-permute-start(f32[256,512]{1,0:T(8,128)} %slice_select_fusion), channel_id=1, source_target_pairs={{0,8},{8,0},{16,24},{24,16},{32,40},{40,32},{48,56},{56,48},{64,72... | collective-permute-start | bytes 1572872 | tf_op jit(solution)/shard_map/ppermute | solution.py:31
  263.9 96.2 %all-to-all-start.3 = ((bf16[512,32,128]{2,1,0:T(8,128)(2,1)}), bf16[512,32,128]{2,1,0:T(8,128)(2,1)}, u32[]{:S(2)}, u32[]{:S(2)}) async-start(bf16[512,32,128]{2,1,0:T(8,128)(2,1)} %copy.57), calls=%async_computation.3 | async-start | bytes 8388608 | tf_op jit(solution)/shard_map/all_to_all | solution.py:94
  270.0 60.0 %collective-permute-start.24 = (f32[128,512]{1,0:T(8,128)S(1)}, f32[128,512]{1,0:T(8,128)S(1)}, u32[]{:S(2)}, u32[]{:S(2)}) collective-permute-start(f32[128,512]{1,0:T(8,128)S(1)} %slice_select_fusion.2), channel_id=1, source_target_pairs={{0,16},{8,24},{16,0},{24,8},{32,48},{40,56},{48,32},{56,40},{64,80... | collective-permute-start | bytes 786440 | tf_op jit(solution)/shard_map/ppermute | solution.py:31
  330.0 4.5 collective-permute-start.25
  334.6 3.2 collective-permute-start.26
  337.8 4.3 collective-permute-start.27
  342.2 4.4 collective-permute-start.28
  346.6 4.1 collective-permute-start.29
  350.7 4.0 collective-permute-start.30
  354.7 4.2 collective-permute-start.31
  358.9 16.6 %collective-permute-start.32 = (f32[16,512]{1,0:T(8,128)S(1)}, f32[16,512]{1,0:T(8,128)S(1)}, u32[]{:S(2)}, u32[]{:S(2)}) collective-permute-start(f32[16,512]{1,0:T(8,128)S(1)} %maximum_select_fusion.11), channel_id=1, source_target_pairs={{0,32},{8,40},{16,48},{24,56},{32,0},{40,8},{48,16},{56,24},{64,96... | collective-permute-start | bytes 98312 | tf_op jit(solution)/shard_map/ppermute | solution.py:31
  366.1 17.6 %collective-permute-start.9 = (f32[256,512]{1,0:T(8,128)S(1)}, f32[256,512]{1,0:T(8,128)S(1)}, u32[]{:S(2)}, u32[]{:S(2)}) collective-permute-start(f32[256,512]{1,0:T(8,128)S(1)} %slice_select_fusion.1), channel_id=1, source_target_pairs={{0,8},{8,0},{16,24},{24,16},{32,40},{40,32},{48,56},{56,48},{64,72... | collective-permute-start | bytes 1572872 | tf_op jit(solution)/shard_map/ppermute | solution.py:31
  375.5 3.7 collective-permute-start.33
  379.2 4.3 collective-permute-start.34
  383.5 9.7 %collective-permute-start.35 = (f32[128,512]{1,0:T(8,128)S(1)}, f32[128,512]{1,0:T(8,128)S(1)}, u32[]{:S(2)}, u32[]{:S(2)}) collective-permute-start(f32[128,512]{1,0:T(8,128)S(1)} %maximum_select_fusion.5), channel_id=1, source_target_pairs={{0,16},{8,24},{16,0},{24,8},{32,48},{40,56},{48,32},{56,40},{64,80... | collective-permute-start | bytes 786440 | tf_op jit(solution)/shard_map/ppermute | solution.py:31
  384.0 11.7 %collective-permute-start.10 = (f32[128,512]{1,0:T(8,128)S(1)}, f32[128,512]{1,0:T(8,128)S(1)}, u32[]{:S(2)}, u32[]{:S(2)}) collective-permute-start(f32[128,512]{1,0:T(8,128)S(1)} %slice_select_fusion.3), channel_id=1, source_target_pairs={{0,16},{8,24},{16,0},{24,8},{32,48},{40,56},{48,32},{56,40},{64,80... | collective-permute-start | bytes 786440 | tf_op jit(solution)/shard_map/ppermute | solution.py:31
  393.2 76.9 %collective-permute-start.36 = (f32[256,512]{1,0:T(8,128)S(1)}, f32[256,512]{1,0:T(8,128)S(1)}, u32[]{:S(2)}, u32[]{:S(2)}) collective-permute-start(f32[256,512]{1,0:T(8,128)S(1)} %maximum_select_fusion.3), channel_id=1, source_target_pairs={{0,8},{8,0},{16,24},{24,16},{32,40},{40,32},{48,56},{56,48},{64,72... | collective-permute-start | bytes 1572872 | tf_op jit(solution)/shard_map/ppermute | solution.py:31
  395.7 20.6 %collective-permute-start.11 = (f32[64,512]{1,0:T(8,128)S(1)}, f32[64,512]{1,0:T(8,128)S(1)}, u32[]{:S(2)}, u32[]{:S(2)}) collective-permute-start(f32[64,512]{1,0:T(8,128)S(1)} %slice_select_fusion.5), channel_id=1, source_target_pairs={{0,1},{1,0},{2,3},{3,2},{4,5},{5,4},{6,7},{7,6},{8,9},{9,8},{10,11... | collective-permute-start | bytes 393224 | tf_op jit(solution)/shard_map/ppermute | solution.py:31
  416.4 26.3 %collective-permute-start.12 = (f32[32,512]{1,0:T(8,128)S(1)}, f32[32,512]{1,0:T(8,128)S(1)}, u32[]{:S(2)}, u32[]{:S(2)}) collective-permute-start(f32[32,512]{1,0:T(8,128)S(1)} %slice_select_fusion.7), channel_id=1, source_target_pairs={{0,64},{8,72},{16,80},{24,88},{32,96},{40,104},{48,112},{56,120},{... | collective-permute-start | bytes 196616 | tf_op jit(solution)/shard_map/ppermute | solution.py:31
  436.1 9.0 %collective-permute-start.5 = (f32[2,128]{1,0:T(2,128)S(1)}, f32[2,128]{1,0:T(2,128)S(1)}, u32[]{:S(2)}, u32[]{:S(2)}) collective-permute-start(f32[2,128]{1,0:T(2,128)S(1)} %slice.186), channel_id=1, source_target_pairs={{8,0},{16,8},{24,16},{32,24},{40,32},{48,40},{56,48},{64,56},{72,6... | collective-permute-start | bytes 3080 | tf_op jit(solution)/shard_map/ppermute | solution.py:16
  440.8 5.2 collective-permute-start.4
  442.7 24.8 %collective-permute-start.13 = (f32[16,512]{1,0:T(8,128)S(1)}, f32[16,512]{1,0:T(8,128)S(1)}, u32[]{:S(2)}, u32[]{:S(2)}) collective-permute-start(f32[16,512]{1,0:T(8,128)S(1)} %slice_select_fusion.9), channel_id=1, source_target_pairs={{0,32},{8,40},{16,48},{24,56},{32,0},{40,8},{48,16},{56,24},{64,96... | collective-permute-start | bytes 98312 | tf_op jit(solution)/shard_map/ppermute | solution.py:31
  467.5 3.7 collective-permute-start.37
  467.6 4.3 collective-permute-start.14
  471.9 6.2 %collective-permute-start.15 = (f32[4,512]{1,0:T(4,128)S(1)}, f32[4,512]{1,0:T(4,128)S(1)}, u32[]{:S(2)}, u32[]{:S(2)}) collective-permute-start(f32[4,512]{1,0:T(4,128)S(1)} %slice_select_fusion.13), channel_id=1, source_target_pairs={{0,4},{1,5},{2,6},{3,7},{4,0},{5,1},{6,2},{7,3},{8,12},{9,13},{10,... | collective-permute-start | bytes 24584 | tf_op jit(solution)/shard_map/ppermute | solution.py:31
  473.7 8.6 %collective-permute-start.39 = (f32[128]{0:T(128)S(1)}, f32[128]{0:T(128)S(1)}, u32[]{:S(2)}, u32[]{:S(2)}) collective-permute-start(f32[128]{0:T(128)S(1)} %add.196), channel_id=1, source_target_pairs={{0,32},{8,40},{16,48},{24,56},{32,0},{40,8},{48,16},{56,24},{64,96... | collective-permute-start | bytes 1544 | tf_op jit(solution)/shard_map/ppermute | solution.py:24
  478.2 4.2 collective-permute-start.16
  480.4 4.0 collective-permute-start.41
  482.3 12.2 %collective-permute-start.6 = (f32[16384]{0:T(1024)S(1)}, f32[16384]{0:T(1024)S(1)}, u32[]{:S(2)}, u32[]{:S(2)}) collective-permute-start(f32[16384]{0:T(1024)S(1)} %get-tuple-element.29), channel_id=1, source_target_pairs={{0,1},{1,0},{2,3},{3,2},{4,5},{5,4},{6,7},{7,6},{8,9},{9,8},{10,11... | collective-permute-start | bytes 196616 | tf_op jit(solution)/shard_map/ppermute | solution.py:24
  482.3 10.1 %collective-permute-start.40 = (f32[128]{0:T(128)S(1)}, f32[128]{0:T(128)S(1)}, u32[]{:S(2)}, u32[]{:S(2)}) collective-permute-start(f32[128]{0:T(128)S(1)} %add.197), channel_id=1, source_target_pairs={{0,64},{8,72},{16,80},{24,88},{32,96},{40,104},{48,112},{56,120},{... | collective-permute-start | bytes 1544 | tf_op jit(solution)/shard_map/ppermute | solution.py:24
  482.4 4.2 collective-permute-start.17
  484.4 5.0 collective-permute-start.42
  486.6 4.3 collective-permute-start.18
  489.4 4.0 collective-permute-start.43
  490.9 4.9 collective-permute-start.19
  493.5 2.9 collective-permute-start.44
  494.5 4.7 collective-permute-start.7
  495.8 5.9 %collective-permute-start.20 = (f32[64,512]{1,0:T(8,128)S(1)}, f32[64,512]{1,0:T(8,128)S(1)}, u32[]{:S(2)}, u32[]{:S(2)}) collective-permute-start(f32[64,512]{1,0:T(8,128)S(1)} %maximum_select_fusion.6), channel_id=1, source_target_pairs={{0,1},{1,0},{2,3},{3,2},{4,5},{5,4},{6,7},{7,6},{8,9},{9,8},{10,11... | collective-permute-start | bytes 393224 | tf_op jit(solution)/shard_map/ppermute | solution.py:31
  499.2 5.0 collective-permute-start.8
  501.7 5.3 %collective-permute-start.21 = (f32[128,512]{1,0:T(8,128)S(1)}, f32[128,512]{1,0:T(8,128)S(1)}, u32[]{:S(2)}, u32[]{:S(2)}) collective-permute-start(f32[128,512]{1,0:T(8,128)S(1)} %maximum_select_fusion.4), channel_id=1, source_target_pairs={{0,16},{8,24},{16,0},{24,8},{32,48},{40,56},{48,32},{56,40},{64,80... | collective-permute-start | bytes 786440 | tf_op jit(solution)/shard_map/ppermute | solution.py:31
  507.1 17.5 %collective-permute-start.22 = (f32[256,512]{1,0:T(8,128)S(1)}, f32[256,512]{1,0:T(8,128)S(1)}, u32[]{:S(2)}, u32[]{:S(2)}) collective-permute-start(f32[256,512]{1,0:T(8,128)S(1)} %maximum_select_fusion.2), channel_id=1, source_target_pairs={{0,8},{8,0},{16,24},{24,16},{32,40},{40,32},{48,56},{56,48},{64,72... | collective-permute-start | bytes 1572872 | tf_op jit(solution)/shard_map/ppermute | solution.py:31
  (23 other events, 419.9 us)

commit v4 on v3

--- a/solution.py
+++ b/solution.py
@@ -94,25 +94,29 @@
     grad_rows = lax.all_to_all(grad_section, "ctx", split_axis=0, concat_axis=1, tiled=True)
     back_flat = back_rows.reshape(rows, chans).astype(jnp.float32)
     grad_gate_pre = cotangent * back_flat * gate * (1.0 - gate)
+    later_gate = shifted(grad_gate_pre[: taps_count - 1], "ctx", -1)
+    ext_gate = jnp.concatenate([grad_gate_pre, later_gate], 0)
+    gate_normed = jnp.zeros((rows, chans), jnp.float32)
+    gate_taps = []
+    for offset in range(taps_count):
+        gate_normed = gate_normed + conv_taps[1, offset] * ext_gate[offset : offset + rows]
+        window = extended[taps_count - 1 - offset : taps_count - 1 - offset + rows]
+        gate_taps.append(jnp.sum(grad_gate_pre * window, axis=0))
+    gate_normed, gate_taps, grad_rows = lax.optimization_barrier((gate_normed, gate_taps, grad_rows))
     grad_mixed = jnp.einsum(
         "ikc,jk->ijc", grad_rows, factor_one, preferred_element_type=jnp.float32
     ).reshape(rows, chans)
     one_part = jnp.einsum("ijc,ikc->jk", mixed_in, grad_rows, preferred_element_type=jnp.float32)
     one_total = tree_allreduce(one_part, FACTOR_ROUNDS)
-    later_value, later_gate = shifted(
-        (grad_mixed[: taps_count - 1], grad_gate_pre[: taps_count - 1]), "ctx", -1
-    )
+    grad_mixed = lax.optimization_barrier(grad_mixed)
+    later_value = shifted(grad_mixed[: taps_count - 1], "ctx", -1)
     ext_value = jnp.concatenate([grad_mixed, later_value], 0)
-    ext_gate = jnp.concatenate([grad_gate_pre, later_gate], 0)
-    grad_normed = jnp.zeros((rows, chans), jnp.float32)
+    grad_normed = gate_normed
     value_taps = []
-    gate_taps = []
     for offset in range(taps_count):
         grad_normed = grad_normed + conv_taps[0, offset] * ext_value[offset : offset + rows]
-        grad_normed = grad_normed + conv_taps[1, offset] * ext_gate[offset : offset + rows]
         window = extended[taps_count - 1 - offset : taps_count - 1 - offset + rows]
         value_taps.append(jnp.sum(grad_mixed * window, axis=0))
-        gate_taps.append(jnp.sum(grad_gate_pre * window, axis=0))
     tap_part = jnp.stack([jnp.stack(value_taps), jnp.stack(gate_taps)])
     gain_part = jnp.sum(grad_normed * hat, axis=0)
     gain_total, taps_total = tree_psum((gain_part, tap_part), "ctx")

time: 535 us -> 547 us (1.022)
  waiting for transfers between devices: 190 us -> 219 us
  local copies, waits for them, and re-layouts: 107 us -> 91.6 us
  starting transfers between devices: 112 us -> 104 us
  other arithmetic: 72.8 us -> 80 us
    all_to_all x1, waiting for transfers between devices: 0.01 us -> 39.6 us  [on_device(): lax.all_to_all(grad_section, 'ctx', split_axis=0, concat_axis=1, tiled=True)]
    all_to_all x1, waiting for transfers between devices: 32.6 us -> 0.01 us  [on_device(): lax.all_to_all(section_two, 'ctx', split_axis=0, concat_axis=1, tiled=True)]
    all_to_all x1, waiting for transfers between devices: 12.1 us -> 35 us  [on_device(): lax.all_to_all(out_grad, 'ctx', split_axis=1, concat_axis=0, tiled=True)]
    add x0 -> x1, other arithmetic: none -> 16.3 us  [on_device(): gate_normed + conv_taps[1, offset] * ext_gate[offset:offset + rows]]
    ppermute x28, starting transfers between devices: 53.9 us -> 44.5 us  [exchange(): lax.ppermute(value, axis, [(source, source ^ step) for source in range(co...]
    convert_element_type x1 -> x0, local copies, waits for them, and re-layouts: 7.15 us -> none  [on_device(): flat_in = inputs.reshape(rows, chans).astype(jnp.float32)]
    reduce_sum x1, other arithmetic: 15 us -> 8.42 us  [on_device(): gate_taps.append(jnp.sum(grad_gate_pre * window, axis=0))]
    unnamed x49 -> x36, local copies, waits for them, and re-layouts: 28.8 us -> 22.3 us
  transfers between devices with their start and end apart: 49 -> 49, of which waited for: 24 -> 25; matrix products, arithmetic and copies ran while one was open for 34% -> 27% of each run, Pallas kernels for 0% -> 0%
where the time goes in v4:
time: 547 us; the launch traced here: 539 us
  waiting for transfers between devices  219 us (40%)
  starting transfers between devices  104 us (19%)
  local copies, waits for them, and re-layouts  91.6 us (17%)
  other arithmetic  80 us (15%)
  matrix products  43 us (8%)
    ppermute x28, waiting for transfers between devices, exchange(): lax.ppermute(value, axis, [(source, source ^ step) for source in range(co...  92.3 us
    ppermute x28, starting transfers between devices, exchange(): lax.ppermute(value, axis, [(source, source ^ step) for source in range(co...  44.5 us
    all_to_all x1, waiting for transfers between devices, on_device(): lax.all_to_all(section_one, 'ctx', split_axis=1, concat_axis=0, tiled=True)  42.3 us
    all_to_all x1, waiting for transfers between devices, on_device(): lax.all_to_all(grad_section, 'ctx', split_axis=0, concat_axis=1, tiled=True)  39.6 us
    all_to_all x1, waiting for transfers between devices, on_device(): lax.all_to_all(out_grad, 'ctx', split_axis=1, concat_axis=0, tiled=True)  35 us
    ppermute x14, starting transfers between devices, tree_psum(): lax.ppermute(value, axis, pairs)  23.5 us
    reduce_sum x1, other arithmetic, on_device(): value_taps.append(jnp.sum(grad_mixed * window, axis=0))  22.6 us
    unnamed x36, local copies, waits for them, and re-layouts  22.3 us
  transfers between devices with their start and end apart: 49, of which 25 were waited for; matrix products, arithmetic and copies ran while one was open for 27% of the time, Pallas kernels for 0%

profile of v4, /device:TPU:1, one launch (start us, length us, event | category | flops | bytes accessed | tf_op | source)
XLA Modules:
  0.0 539.3 jit_solution(1582776028269155248)
XLA Ops:
  0.7 4.6 multiply_reduce_fusion.2
  13.8 3.9 collective-permute-start.2
  19.4 4.4 multiply_convert_fusion.1
  23.8 6.9 %collective-permute-start.3 = (bf16[2,128]{1,0:T(2,128)(2,1)S(1)}, bf16[2,128]{1,0:T(2,128)(2,1)S(1)}, u32[]{:S(2)}, u32[]{:S(2)}) collective-permute-start(bf16[2,128]{1,0:T(2,128)(2,1)S(1)} %slice.182), channel_id=1, source_target_pairs={{0,8},{8,16},{16,24},{24,32},{32,40},{40,48},{48,56},{56,64},{64,7... | collective-permute-start | bytes 1544 | tf_op jit(solution)/shard_map/ppermute | solution.py:16
  31.5 6.5 %fusion.10 = (bf16[16384,128]{1,0:T(8,128)(2,1)S(1)}, bf16[16384,128]{1,0:T(8,128)(2,1)}) fusion(bf16[32,512,128]{2,1,0:T(8,128)(2,1)S(1)} %copy-done.10, bf16[16384,128]{1,0:T(8,128)(2,1)S(1)} %multiply_convert_fusion.1, bf16[2,128]{1,0:T(2,128)(2,1)S(1)} %collective-permute-done.3, f32[128]{0:T(128)S(1)} %get-tuple-element.65, ...), kind=kLoop, calls=%fused_computation.30 | loop fusion | flops 44040192 | bytes 16779264 | tf_op jit(solution)/shard_map/convert_element_type | solution.py:77
  38.0 4.7 copy.65
  42.7 6.9 %all-to-all-start.2 = ((bf16[32,512,128]{2,0,1:T(8,128)(2,1)}), bf16[32,512,128]{2,0,1:T(8,128)(2,1)}, u32[]{:S(2)}, u32[]{:S(2)}) async-start(bf16[32,512,128]{2,0,1:T(8,128)(2,1)} %copy.65), calls=%async_computation.2 | async-start | bytes 8388608 | tf_op jit(solution)/shard_map/all_to_all | solution.py:85
  49.6 6.3 %fusion.15 = bf16[16384,128]{1,0:T(8,128)(2,1)S(1)} fusion(bf16[16384,128]{1,0:T(8,128)(2,1)} %copy-done.3, bf16[16384,128]{1,0:T(8,128)(2,1)} %get-tuple-element.55, f32[128]{0:T(128)S(1)} %get-tuple-element.62, f32[128]{0:T(128)S(1)} %get-tuple-element.63, f32[128]{0:T(128)S(1)} %get-tuple-element.61, bf16[2,128]{1,0:T(2,128)(2,1)S(1)} %collective-permute-done.3), kind=kLoop, calls=%fused_computation.35 | loop fusion | flops 25165824 | bytes 12584960 | tf_op jit(solution)/shard_map/convert_element_type | solution.py:71
  57.9 4.4 convert_bitcast_fusion.2
  62.4 7.9 %copy.58 = bf16[32,512,128]{2,0,1:T(8,128)(2,1)} copy(bf16[32,512,128]{1,2,0:T(8,128)(2,1)} %convert_bitcast_fusion.2) | data formatting | bytes 8388608 | tf_op jit(solution)/shard_map/convert_element_type | solution.py:76
  70.3 35.0 %all-to-all-done.2 = bf16[32,512,128]{2,0,1:T(8,128)(2,1)} async-done(((bf16[32,512,128]{2,0,1:T(8,128)(2,1)}), bf16[32,512,128]{2,0,1:T(8,128)(2,1)}, u32[]{:S(2)}, u32[]{:S(2)}) %all-to-all-start.2) | async-done | bytes 4194336 | tf_op jit(solution)/shard_map/all_to_all | solution.py:85
  105.3 4.9 all-to-all-start
  110.2 7.5 %copy.61 = bf16[512,32,128]{0,2,1:T(8,128)(2,1)} copy(bf16[512,32,128]{2,1,0:T(8,128)(2,1)} %param.12) | data formatting | bytes 8388608 | tf_op args[5]
  117.7 5.9 %copy.67 = bf16[16,32,32,128]{3,2,1,0:T(8,128)(2,1)} copy(bf16[16,32,32,128]{3,1,2,0:T(8,128)(2,1)} %bitcast.23) | data formatting | bytes 8388608 | tf_op jit(solution)/shard_map/all_to_all | solution.py:85
  123.6 42.3 %all-to-all-done = bf16[32,512,128]{2,0,1:T(8,128)(2,1)} async-done(((bf16[32,512,128]{2,0,1:T(8,128)(2,1)}), bf16[32,512,128]{2,0,1:T(8,128)(2,1)}, u32[]{:S(2)}, u32[]{:S(2)}) %all-to-all-start) | async-done | bytes 4194336 | tf_op jit(solution)/shard_map/all_to_all | solution.py:78
  165.9 3.8 copy.59
  170.9 4.3 copy.60
  175.2 10.0 %copy.62 = f32[512,32,128]{0,2,1:T(8,128)} copy(f32[512,32,128]{2,1,0:T(8,128)} %bitcast.99) | data formatting | bytes 16777216 | tf_op jit(solution)/shard_map/convert_element_type | solution.py:80
  185.2 10.3 %fusion.36 = f32[512,512]{1,0:T(8,128)S(1)} fusion(bf16[512,32,128]{2,1,0:T(8,128)(2,1)} %bitcast.95, f32[512,32,128]{0,2,1:T(8,128)} %copy.62, bf16[512,32,128]{0,2,1:T(8,128)(2,1)} %copy.61), kind=kOutput, calls=%fused_computation.72 | convolution fusion | flops 2153775104 | bytes 17825792 | tf_op jit(solution)/shard_map/ijc,kjc->ik/dot_general | solution.py:91
  196.7 4.3 convert_bitcast_fusion.1
  201.0 7.9 %copy.63 = bf16[512,32,128]{2,1,0:T(8,128)(2,1)} copy(bf16[512,32,128]{0,2,1:T(8,128)(2,1)} %convert_bitcast_fusion.1) | data formatting | bytes 8388608 | tf_op jit(solution)/shard_map/convert_element_type | solution.py:83
  208.9 4.5 all-to-all-start.1
  215.9 59.0 %collective-permute-done.24 = f32[128,512]{1,0:T(8,128)S(1)} collective-permute-done((f32[128,512]{1,0:T(8,128)S(1)}, f32[128,512]{1,0:T(8,128)S(1)}, u32[]{:S(2)}, u32[]{:S(2)}) %collective-permute-start.24) | collective-permute-done | bytes 262176 | tf_op jit(solution)/shard_map/ppermute | solution.py:31
  276.2 3.3 collective-permute-done.25
  283.8 3.3 collective-permute-done.27
  290.0 13.8 %fusion.30 = (bf16[512,32,128]{0,2,1:T(8,128)(2,1)}, bf16[512,32,128]{0,2,1:T(8,128)(2,1)}) fusion(f32[512,32,128]{0,2,1:T(8,128)} %copy.62, bf16[512,32,128]{0,2,1:T(8,128)(2,1)} %copy.61, bf16[512,512]{1,0:T(8,128)(2,1)S(1)} %copy-done, bf16[512,32,128]{2,1,0:T(8,128)(2,1)} %bitcast.96), kind=kOutput, calls=%fused_computation.54 | convolution fusion | flops 2157969408 | bytes 25690112 | tf_op jit(solution)/shard_map/kjc,ik->ijc/dot_general | solution.py:86
  303.8 3.6 copy.64
  308.6 8.4 %fusion.26 = (f32[128]{0:T(128)S(1)}, f32[128]{0:T(128)S(1)}, f32[128]{0:T(128)S(1)}, f32[16384,128]{1,0:T(8,128)S(1)}) fusion(bf16[16384,128]{1,0:T(8,128)(2,1)S(1)} %copy-done.4, bf16[2,128]{1,0:T(2,128)(2,1)S(1)} %collective-permute-done.3, bf16[16384,128]{1,0:T(8,128)(2,1)S(1)} %copy-done.6, f32[128]{0:T(128)S(1)} %get-tuple-element.65, ...), kind=kLoop, calls=%fused_computation.46 | loop fusion | flops 54525568 | bytes 25169408 | tf_op jit(solution)/shard_map/reduce_sum | solution.py:104
  320.2 5.9 %collective-permute-start.4 = (f32[2,128]{1,0:T(2,128)S(1)}, f32[2,128]{1,0:T(2,128)S(1)}, u32[]{:S(2)}, u32[]{:S(2)}) collective-permute-start(f32[2,128]{1,0:T(2,128)S(1)} %slice.185), channel_id=1, source_target_pairs={{8,0},{16,8},{24,16},{32,24},{40,32},{48,40},{56,48},{64,56},{72,6... | collective-permute-start | bytes 3080 | tf_op jit(solution)/shard_map/ppermute | solution.py:16
  326.2 3.5 collective-permute-start.29
  329.7 7.9 %copy.69 = bf16[512,32,128]{2,1,0:T(8,128)(2,1)} copy(bf16[512,32,128]{0,2,1:T(8,128)(2,1)} %get-tuple-element.14) | data formatting | bytes 8388608 | tf_op jit(solution)/shard_map/optimization_barrier | solution.py:93
  337.6 4.4 all-to-all-start.3
  342.1 16.3 %fusion.7 = f32[16384,128]{1,0:T(8,128)} fusion(f32[16384,128]{1,0:T(8,128)} %copy-done.8, f32[2,128]{1,0:T(2,128)S(1)} %collective-permute-done.4, f32[128]{0:T(128)S(1)} %get-tuple-element.65, f32[128]{0:T(128)S(1)} %get-tuple-element.66, f32[128]{0:T(128)S(1)} %get-tuple-element.64), kind=kLoop, calls=%fused_computation.27 | loop fusion | flops 14680064 | bytes 16779776 | tf_op jit(solution)/shard_map/add | solution.py:102
  358.4 39.6 %all-to-all-done.3 = bf16[512,32,128]{2,1,0:T(8,128)(2,1)} async-done(((bf16[512,32,128]{2,1,0:T(8,128)(2,1)}), bf16[512,32,128]{2,1,0:T(8,128)(2,1)}, u32[]{:S(2)}, u32[]{:S(2)}) %all-to-all-start.3) | async-done | bytes 4194336 | tf_op jit(solution)/shard_map/all_to_all | solution.py:94
  398.0 3.6 copy.70
  404.8 3.8 collective-permute-done.30
  409.0 3.8 collective-permute-done.31
  413.7 3.3 collective-permute-done.32
  420.7 3.8 collective-permute-done.34
  427.6 7.8 %copy.76 = bf16[512,32,128]{2,1,0:T(8,128)(2,1)} copy(bf16[512,32,128]{0,2,1:T(8,128)(2,1)} %get-tuple-element.59) | data formatting | bytes 8388608
  435.5 6.8 %collective-permute-start.36 = (f32[256,512]{1,0:T(8,128)S(1)}, f32[256,512]{1,0:T(8,128)S(1)}, u32[]{:S(2)}, u32[]{:S(2)}) collective-permute-start(f32[256,512]{1,0:T(8,128)S(1)} %maximum_select_fusion.3), channel_id=1, source_target_pairs={{0,8},{8,0},{16,24},{24,16},{32,40},{40,32},{48,56},{56,48},{64,72... | collective-permute-start | bytes 1572872 | tf_op jit(solution)/shard_map/ppermute | solution.py:31
  443.1 7.9 %convolution_bitcast_fusion = f32[32,512,128]{1,2,0:T(8,128)} fusion(bf16[32,512,128]{2,1,0:T(8,128)(2,1)} %bitcast.101, bf16[512,512]{1,0:T(8,128)(2,1)S(1)} %copy-done.13), kind=kOutput, calls=%fused_computation.71 | convolution fusion | flops 2147483648 | bytes 13107200 | tf_op jit(solution)/shard_map/ikc,jk->ijc/dot_general | solution.py:106
  451.0 9.0 %copy.72 = f32[32,512,128]{2,1,0:T(8,128)} copy(f32[32,512,128]{1,2,0:T(8,128)} %convolution_bitcast_fusion) | data formatting | bytes 16777216 | tf_op jit(solution)/shard_map/ikc,jk->ijc/transpose | solution.py:106
  465.5 22.6 %fusion.23 = (f32[128]{0:T(128)S(1)}, f32[128]{0:T(128)S(1)}, f32[128]{0:T(128)S(1)}, f32[16384]{0:T(1024)S(1)}, f32[128]{0:T(128)S(1)}, /*index=5*/f32[16384,128]{1,0:T(8,128)S(1)}) fusion(f32[16384,128]{1,0:T(8,128)} %bitcast.98, bf16[16384,128]{1,0:T(8,128)(2,1)} %copy-done.3, bf16[2,128]{1,0:T(2,128)(2,1)S(1)} %collective-permute-done.3, ...), kind=kLoop, calls=%fused_computation.43 | loop fusion | flops 56606208 | bytes 37885440 | tf_op jit(solution)/shard_map/reduce_sum | solution.py:119
  516.8 3.8 collective-permute-start.8
  522.4 3.7 collective-permute-done.21
  526.1 6.1 %collective-permute-start.22 = (f32[256,512]{1,0:T(8,128)S(1)}, f32[256,512]{1,0:T(8,128)S(1)}, u32[]{:S(2)}, u32[]{:S(2)}) collective-permute-start(f32[256,512]{1,0:T(8,128)S(1)} %maximum_select_fusion.2), channel_id=1, source_target_pairs={{0,8},{8,0},{16,24},{24,16},{32,40},{40,32},{48,56},{56,48},{64,72... | collective-permute-start | bytes 1572872 | tf_op jit(solution)/shard_map/ppermute | solution.py:31
  532.2 5.8 %multiply_convert_fusion = bf16[16384,128]{1,0:T(8,128)(2,1)} fusion(f32[16384,128]{1,0:T(8,128)S(1)} %get-tuple-element.58, bf16[32,512,128]{2,1,0:T(8,128)(2,1)S(1)} %copy-done.5, f32[16384]{0:T(1024)S(1)} %add_multiply_fusion, f32[128]{0:T(128)S(1)} %copy-done.14, f32[16384]{0:T(1024)S(1)} %add_rsqrt_fusion), kind=kLoop, calls=%fused_computation.57 | loop fusion | flops 14680064 | bytes 16908800 | tf_op jit(solution)/shard_map/convert_element_type | solution.py:130
  (174 shorter events, 79.5 us)
Async XLA Ops:
  5.3 3.8 collective-permute-start
  9.1 4.7 collective-permute-start.1
  13.8 5.6 %collective-permute-start.2 = (f32[16384]{0:T(1024)S(1)}, f32[16384]{0:T(1024)S(1)}, u32[]{:S(2)}, u32[]{:S(2)}) collective-permute-start(f32[16384]{0:T(1024)S(1)} %add.157), channel_id=1, source_target_pairs={{0,4},{1,5},{2,6},{3,7},{4,0},{5,1},{6,2},{7,3},{8,12},{9,13},{10,... | collective-permute-start | bytes 196616 | tf_op jit(solution)/shard_map/ppermute | solution.py:24
  23.8 7.6 %collective-permute-start.3 = (bf16[2,128]{1,0:T(2,128)(2,1)S(1)}, bf16[2,128]{1,0:T(2,128)(2,1)S(1)}, u32[]{:S(2)}, u32[]{:S(2)}) collective-permute-start(bf16[2,128]{1,0:T(2,128)(2,1)S(1)} %slice.182), channel_id=1, source_target_pairs={{0,8},{8,16},{16,24},{24,32},{32,40},{40,48},{48,56},{56,64},{64,7... | collective-permute-start | bytes 1544 | tf_op jit(solution)/shard_map/ppermute | solution.py:16
  42.7 62.6 %all-to-all-start.2 = ((bf16[32,512,128]{2,0,1:T(8,128)(2,1)}), bf16[32,512,128]{2,0,1:T(8,128)(2,1)}, u32[]{:S(2)}, u32[]{:S(2)}) async-start(bf16[32,512,128]{2,0,1:T(8,128)(2,1)} %copy.65), calls=%async_computation.2 | async-start | bytes 8388608 | tf_op jit(solution)/shard_map/all_to_all | solution.py:85
  105.3 60.6 %all-to-all-start = ((bf16[32,512,128]{2,0,1:T(8,128)(2,1)}), bf16[32,512,128]{2,0,1:T(8,128)(2,1)}, u32[]{:S(2)}, u32[]{:S(2)}) async-start(bf16[32,512,128]{2,0,1:T(8,128)(2,1)} %copy.58), calls=%async_computation | async-start | bytes 8388608 | tf_op jit(solution)/shard_map/all_to_all | solution.py:78
  195.6 17.9 %collective-permute-start.23 = (f32[256,512]{1,0:T(8,128)S(1)}, f32[256,512]{1,0:T(8,128)S(1)}, u32[]{:S(2)}, u32[]{:S(2)}) collective-permute-start(f32[256,512]{1,0:T(8,128)S(1)} %slice_select_fusion), channel_id=1, source_target_pairs={{0,8},{8,0},{16,24},{24,16},{32,40},{40,32},{48,56},{56,48},{64,72... | collective-permute-start | bytes 1572872 | tf_op jit(solution)/shard_map/ppermute | solution.py:31
  208.9 94.9 %all-to-all-start.1 = ((bf16[512,32,128]{2,1,0:T(8,128)(2,1)}), bf16[512,32,128]{2,1,0:T(8,128)(2,1)}, u32[]{:S(2)}, u32[]{:S(2)}) async-start(bf16[512,32,128]{2,1,0:T(8,128)(2,1)} %copy.63), calls=%async_computation.1 | async-start | bytes 8388608 | tf_op jit(solution)/shard_map/all_to_all | solution.py:84
  213.7 61.2 %collective-permute-start.24 = (f32[128,512]{1,0:T(8,128)S(1)}, f32[128,512]{1,0:T(8,128)S(1)}, u32[]{:S(2)}, u32[]{:S(2)}) collective-permute-start(f32[128,512]{1,0:T(8,128)S(1)} %slice_select_fusion.2), channel_id=1, source_target_pairs={{0,16},{8,24},{16,0},{24,8},{32,48},{40,56},{48,32},{56,40},{64,80... | collective-permute-start | bytes 786440 | tf_op jit(solution)/shard_map/ppermute | solution.py:31
  274.9 4.5 collective-permute-start.25
  279.5 3.2 collective-permute-start.26
  282.8 4.3 collective-permute-start.27
  287.2 16.6 %collective-permute-start.28 = (f32[8,512]{1,0:T(8,128)S(1)}, f32[8,512]{1,0:T(8,128)S(1)}, u32[]{:S(2)}, u32[]{:S(2)}) collective-permute-start(f32[8,512]{1,0:T(8,128)S(1)} %slice_select_fusion.10), channel_id=1, source_target_pairs={{0,2},{1,3},{2,0},{3,1},{4,6},{5,7},{6,4},{7,5},{8,10},{9,11},{10,... | collective-permute-start | bytes 49160 | tf_op jit(solution)/shard_map/ppermute | solution.py:31
  320.2 21.9 %collective-permute-start.4 = (f32[2,128]{1,0:T(2,128)S(1)}, f32[2,128]{1,0:T(2,128)S(1)}, u32[]{:S(2)}, u32[]{:S(2)}) collective-permute-start(f32[2,128]{1,0:T(2,128)S(1)} %slice.185), channel_id=1, source_target_pairs={{8,0},{16,8},{24,16},{32,24},{40,32},{48,40},{56,48},{64,56},{72,6... | collective-permute-start | bytes 3080 | tf_op jit(solution)/shard_map/ppermute | solution.py:16
  326.2 78.3 %collective-permute-start.29 = (f32[4,512]{1,0:T(4,128)S(1)}, f32[4,512]{1,0:T(4,128)S(1)}, u32[]{:S(2)}, u32[]{:S(2)}) collective-permute-start(f32[4,512]{1,0:T(4,128)S(1)} %slice_select_fusion.12), channel_id=1, source_target_pairs={{0,4},{1,5},{2,6},{3,7},{4,0},{5,1},{6,2},{7,3},{8,12},{9,13},{10,... | collective-permute-start | bytes 24584 | tf_op jit(solution)/shard_map/ppermute | solution.py:31
  337.6 60.4 %all-to-all-start.3 = ((bf16[512,32,128]{2,1,0:T(8,128)(2,1)}), bf16[512,32,128]{2,1,0:T(8,128)(2,1)}, u32[]{:S(2)}, u32[]{:S(2)}) async-start(bf16[512,32,128]{2,1,0:T(8,128)(2,1)} %copy.69), calls=%async_computation.3 | async-start | bytes 8388608 | tf_op jit(solution)/shard_map/all_to_all | solution.py:94
  404.1 13.6 %collective-permute-start.9 = (f32[256,512]{1,0:T(8,128)S(1)}, f32[256,512]{1,0:T(8,128)S(1)}, u32[]{:S(2)}, u32[]{:S(2)}) collective-permute-start(f32[256,512]{1,0:T(8,128)S(1)} %slice_select_fusion.1), channel_id=1, source_target_pairs={{0,8},{8,0},{16,24},{24,16},{32,40},{40,32},{48,56},{56,48},{64,72... | collective-permute-start | bytes 1572872 | tf_op jit(solution)/shard_map/ppermute | solution.py:31
  404.5 4.1 collective-permute-start.30
  408.6 4.2 collective-permute-start.31
  412.8 4.3 collective-permute-start.32
  417.1 3.2 collective-permute-start.33
  417.9 9.2 %collective-permute-start.10 = (f32[128,512]{1,0:T(8,128)S(1)}, f32[128,512]{1,0:T(8,128)S(1)}, u32[]{:S(2)}, u32[]{:S(2)}) collective-permute-start(f32[128,512]{1,0:T(8,128)S(1)} %slice_select_fusion.3), channel_id=1, source_target_pairs={{0,16},{8,24},{16,0},{24,8},{32,48},{40,56},{48,32},{56,40},{64,80... | collective-permute-start | bytes 786440 | tf_op jit(solution)/shard_map/ppermute | solution.py:31
  420.3 4.2 collective-permute-start.34
  424.5 10.9 %collective-permute-start.35 = (f32[128,512]{1,0:T(8,128)S(1)}, f32[128,512]{1,0:T(8,128)S(1)}, u32[]{:S(2)}, u32[]{:S(2)}) collective-permute-start(f32[128,512]{1,0:T(8,128)S(1)} %maximum_select_fusion.5), channel_id=1, source_target_pairs={{0,16},{8,24},{16,0},{24,8},{32,48},{40,56},{48,32},{56,40},{64,80... | collective-permute-start | bytes 786440 | tf_op jit(solution)/shard_map/ppermute | solution.py:31
  427.2 15.1 %collective-permute-start.11 = (f32[64,512]{1,0:T(8,128)S(1)}, f32[64,512]{1,0:T(8,128)S(1)}, u32[]{:S(2)}, u32[]{:S(2)}) collective-permute-start(f32[64,512]{1,0:T(8,128)S(1)} %slice_select_fusion.5), channel_id=1, source_target_pairs={{0,1},{1,0},{2,3},{3,2},{4,5},{5,4},{6,7},{7,6},{8,9},{9,8},{10,11... | collective-permute-start | bytes 393224 | tf_op jit(solution)/shard_map/ppermute | solution.py:31
  435.5 54.6 %collective-permute-start.36 = (f32[256,512]{1,0:T(8,128)S(1)}, f32[256,512]{1,0:T(8,128)S(1)}, u32[]{:S(2)}, u32[]{:S(2)}) collective-permute-start(f32[256,512]{1,0:T(8,128)S(1)} %maximum_select_fusion.3), channel_id=1, source_target_pairs={{0,8},{8,0},{16,24},{24,16},{32,40},{40,32},{48,56},{56,48},{64,72... | collective-permute-start | bytes 1572872 | tf_op jit(solution)/shard_map/ppermute | solution.py:31
  442.4 20.5 %collective-permute-start.12 = (f32[32,512]{1,0:T(8,128)S(1)}, f32[32,512]{1,0:T(8,128)S(1)}, u32[]{:S(2)}, u32[]{:S(2)}) collective-permute-start(f32[32,512]{1,0:T(8,128)S(1)} %slice_select_fusion.7), channel_id=1, source_target_pairs={{0,64},{8,72},{16,80},{24,88},{32,96},{40,104},{48,112},{56,120},{... | collective-permute-start | bytes 196616 | tf_op jit(solution)/shard_map/ppermute | solution.py:31
  460.6 4.9 collective-permute-start.5
  462.9 25.3 %collective-permute-start.13 = (f32[16,512]{1,0:T(8,128)S(1)}, f32[16,512]{1,0:T(8,128)S(1)}, u32[]{:S(2)}, u32[]{:S(2)}) collective-permute-start(f32[16,512]{1,0:T(8,128)S(1)} %slice_select_fusion.9), channel_id=1, source_target_pairs={{0,32},{8,40},{16,48},{24,56},{32,0},{40,8},{48,16},{56,24},{64,96... | collective-permute-start | bytes 98312 | tf_op jit(solution)/shard_map/ppermute | solution.py:31
  488.1 3.1 collective-permute-start.37
  488.2 4.2 collective-permute-start.14
  492.4 4.1 collective-permute-start.15
  493.7 7.6 %collective-permute-start.39 = (f32[128]{0:T(128)S(1)}, f32[128]{0:T(128)S(1)}, u32[]{:S(2)}, u32[]{:S(2)}) collective-permute-start(f32[128]{0:T(128)S(1)} %add.196), channel_id=1, source_target_pairs={{0,32},{8,40},{16,48},{24,56},{32,0},{40,8},{48,16},{56,24},{64,96... | collective-permute-start | bytes 1544 | tf_op jit(solution)/shard_map/ppermute | solution.py:24
  496.5 5.0 collective-permute-start.16
  498.1 5.0 collective-permute-start.41
  500.1 12.0 %collective-permute-start.6 = (f32[16384]{0:T(1024)S(1)}, f32[16384]{0:T(1024)S(1)}, u32[]{:S(2)}, u32[]{:S(2)}) collective-permute-start(f32[16384]{0:T(1024)S(1)} %get-tuple-element.56), channel_id=1, source_target_pairs={{0,1},{1,0},{2,3},{3,2},{4,5},{5,4},{6,7},{7,6},{8,9},{9,8},{10,11... | collective-permute-start | bytes 196616 | tf_op jit(solution)/shard_map/ppermute | solution.py:24
  501.2 10.0 %collective-permute-start.40 = (f32[128]{0:T(128)S(1)}, f32[128]{0:T(128)S(1)}, u32[]{:S(2)}, u32[]{:S(2)}) collective-permute-start(f32[128]{0:T(128)S(1)} %add.197), channel_id=1, source_target_pairs={{0,64},{8,72},{16,80},{24,88},{32,96},{40,104},{48,112},{56,120},{... | collective-permute-start | bytes 1544 | tf_op jit(solution)/shard_map/ppermute | solution.py:24
  501.6 4.2 collective-permute-start.17
  503.2 4.3 collective-permute-start.42
  505.8 4.3 collective-permute-start.18
  507.5 4.3 collective-permute-start.43
  510.0 4.8 collective-permute-start.19
  511.8 3.1 collective-permute-start.44
  512.1 4.7 collective-permute-start.7
  514.8 5.9 %collective-permute-start.20 = (f32[64,512]{1,0:T(8,128)S(1)}, f32[64,512]{1,0:T(8,128)S(1)}, u32[]{:S(2)}, u32[]{:S(2)}) collective-permute-start(f32[64,512]{1,0:T(8,128)S(1)} %maximum_select_fusion.6), channel_id=1, source_target_pairs={{0,1},{1,0},{2,3},{3,2},{4,5},{5,4},{6,7},{7,6},{8,9},{9,8},{10,11... | collective-permute-start | bytes 393224 | tf_op jit(solution)/shard_map/ppermute | solution.py:31
  516.8 5.5 %collective-permute-start.8 = (f32[16384]{0:T(1024)S(1)}, f32[16384]{0:T(1024)S(1)}, u32[]{:S(2)}, u32[]{:S(2)}) collective-permute-start(f32[16384]{0:T(1024)S(1)} %add.172), channel_id=1, source_target_pairs={{0,4},{1,5},{2,6},{3,7},{4,0},{5,1},{6,2},{7,3},{8,12},{9,13},{10,... | collective-permute-start | bytes 196616 | tf_op jit(solution)/shard_map/ppermute | solution.py:24
  520.7 5.3 collective-permute-start.21
  526.1 11.9 %collective-permute-start.22 = (f32[256,512]{1,0:T(8,128)S(1)}, f32[256,512]{1,0:T(8,128)S(1)}, u32[]{:S(2)}, u32[]{:S(2)}) collective-permute-start(f32[256,512]{1,0:T(8,128)S(1)} %maximum_select_fusion.2), channel_id=1, source_target_pairs={{0,8},{8,0},{16,24},{24,16},{32,40},{40,32},{48,56},{56,48},{64,72... | collective-permute-start | bytes 1572872 | tf_op jit(solution)/shard_map/ppermute | solution.py:31
  (17 other events, 415.4 us)

commit v5 on v3

--- a/solution.py
+++ b/solution.py
@@ -46,6 +46,17 @@
             upper, jnp.concatenate([other, value]), jnp.concatenate([value, other])
         )
     return value
+
+
+def a2a_allreduce(value, axes):
+    count = 1
+    for axis in axes:
+        count *= lax.axis_size(axis)
+    pieces = value.reshape(count, -1)
+    gathered = lax.all_to_all(pieces, axes, 0, 0, tiled=True)
+    owned = jnp.sum(gathered, axis=0, keepdims=True)
+    spread = jnp.broadcast_to(owned, pieces.shape)
+    return lax.all_to_all(spread, axes, 0, 0, tiled=True).reshape(value.shape)
 
 
 FACTOR_ROUNDS = (("ctx", 1), ("ctx", 2), ("ch", 1), ("ctx", 8), ("ctx", 4), ("ch", 2), ("ch", 4))
@@ -98,7 +109,7 @@
         "ikc,jk->ijc", grad_rows, factor_one, preferred_element_type=jnp.float32
     ).reshape(rows, chans)
     one_part = jnp.einsum("ijc,ikc->jk", mixed_in, grad_rows, preferred_element_type=jnp.float32)
-    one_total = tree_allreduce(one_part, FACTOR_ROUNDS)
+    one_total = a2a_allreduce(one_part, ("ctx", "ch"))
     later_value, later_gate = shifted(
         (grad_mixed[: taps_count - 1], grad_gate_pre[: taps_count - 1]), "ctx", -1
     )

time: 535 us -> 536 us (level)
  waiting for transfers between devices: 190 us -> 199 us
  starting transfers between devices: 112 us -> 106 us
    ppermute x28 -> x14, starting transfers between devices: 53.9 us -> 18.2 us  [exchange(): lax.ppermute(value, axis, [(source, source ^ step) for source in range(co...]
    all_to_all x0 -> x2, starting transfers between devices: none -> 18.1 us  [the longest x1 11.3 us: a2a_allreduce(): return lax.all_to_all(spread, axes, 0, 0, tiled=True).reshape(value.shape)]
    ppermute x3, starting transfers between devices: 12.9 us -> 21.6 us  [shifted(): lax.ppermute(value, axis, [(source, source + steps) for source in range(i...]
    all_to_all x0 -> x2, waiting for transfers between devices: none -> 6.23 us  [the longest x1 6.22 us: a2a_allreduce(): return lax.all_to_all(spread, axes, 0, 0, tiled=True).reshape(value.shape)]
    unnamed x49 -> x39, local copies, waits for them, and re-layouts: 28.8 us -> 25.5 us
    ppermute x28 -> x14, waiting for transfers between devices: 86.1 us -> 83.5 us  [exchange(): lax.ppermute(value, axis, [(source, source ^ step) for source in range(co...]
  transfers between devices with their start and end apart: 49 -> 37, of which waited for: 24 -> 24; matrix products, arithmetic and copies ran while one was open for 34% -> 30% of each run, Pallas kernels for 0% -> 0%
where the time goes in v5:
time: 536 us; the launch traced here: 527 us
  waiting for transfers between devices  199 us (37%)
  local copies, waits for them, and re-layouts  109 us (20%)
  starting transfers between devices  106 us (20%)
  other arithmetic  68.6 us (13%)
  matrix products  43.3 us (8%)
    ppermute x14, waiting for transfers between devices, exchange(): lax.ppermute(value, axis, [(source, source ^ step) for source in range(co...  83.5 us
    all_to_all x1, waiting for transfers between devices, on_device(): lax.all_to_all(section_one, 'ctx', split_axis=1, concat_axis=0, tiled=True)  48.8 us
    all_to_all x1, waiting for transfers between devices, on_device(): lax.all_to_all(section_two, 'ctx', split_axis=0, concat_axis=1, tiled=True)  31.1 us
    ppermute x14, starting transfers between devices, tree_psum(): lax.ppermute(value, axis, pairs)  26.2 us
    unnamed x39, local copies, waits for them, and re-layouts  25.5 us
    ppermute x3, starting transfers between devices, shifted(): lax.ppermute(value, axis, [(source, source + steps) for source in range(i...  21.6 us
    ppermute x14, starting transfers between devices, exchange(): lax.ppermute(value, axis, [(source, source ^ step) for source in range(co...  18.2 us
    reduce_sum x1, other arithmetic, on_device(): gain_part = jnp.sum(grad_normed * hat, axis=0)  16.3 us
  transfers between devices with their start and end apart: 37, of which 24 were waited for; matrix products, arithmetic and copies ran while one was open for 30% of the time, Pallas kernels for 0%

profile of v5, /device:TPU:1, one launch (start us, length us, event | category | flops | bytes accessed | tf_op | source)
XLA Modules:
  0.0 527.3 jit_solution(13888315860517506204)
XLA Ops:
  0.6 6.5 %copy.43 = bf16[32,512,128]{1,2,0:T(8,128)(2,1)} copy(bf16[32,512,128]{2,1,0:T(8,128)(2,1)} %param.7) | data formatting | bytes 8388608 | tf_op args[0]
  7.1 3.1 multiply_reduce_fusion.3
  14.1 3.1 collective-permute-start.1
  18.8 3.9 collective-permute-start.2
  22.7 7.1 %copy.44 = f32[32,512,128]{2,1,0:T(8,128)} copy(bf16[32,512,128]{1,2,0:T(8,128)(2,1)} %copy.43) | data formatting | bytes 12582912 | tf_op jit(solution)/shard_map/convert_element_type | solution.py:69
  29.8 5.5 %multiply_convert_fusion.2 = bf16[16384,128]{1,0:T(8,128)(2,1)S(1)} fusion(f32[32,512,128]{2,1,0:T(8,128)} %copy.44, f32[128]{0:T(128)S(1)} %copy-done.13, f32[16384]{0:T(1024)S(1)} %add_rsqrt_fusion), kind=kLoop, calls=%fused_computation.59 | loop fusion | flops 6291456 | bytes 12648960 | tf_op jit(solution)/shard_map/convert_element_type | solution.py:73
  35.3 6.3 %collective-permute-start.3 = (bf16[2,128]{1,0:T(2,128)(2,1)S(1)}, bf16[2,128]{1,0:T(2,128)(2,1)S(1)}, u32[]{:S(2)}, u32[]{:S(2)}) collective-permute-start(bf16[2,128]{1,0:T(2,128)(2,1)S(1)} %slice.124), channel_id=1, source_target_pairs={{0,8},{8,16},{16,24},{24,32},{32,40},{40,48},{48,56},{56,64},{64,7... | collective-permute-start | bytes 1544 | tf_op jit(solution)/shard_map/ppermute | solution.py:16
  42.3 6.5 %fusion.10 = (bf16[16384,128]{1,0:T(8,128)(2,1)}, bf16[16384,128]{1,0:T(8,128)(2,1)S(1)}) fusion(bf16[32,512,128]{2,1,0:T(8,128)(2,1)S(1)} %copy-done.7, bf16[16384,128]{1,0:T(8,128)(2,1)S(1)} %multiply_convert_fusion.2, bf16[2,128]{1,0:T(2,128)(2,1)S(1)} %collective-permute-done.3, f32[128]{0:T(128)S(1)} %get-tuple-element.47, ...), kind=kLoop, calls=%fused_computation.29 | loop fusion | flops 44040192 | bytes 16779264 | tf_op jit(solution)/shard_map/convert_element_type | solution.py:88
  53.9 4.4 convert_bitcast_fusion.2
  58.3 8.0 %copy.46 = bf16[32,512,128]{2,0,1:T(8,128)(2,1)} copy(bf16[32,512,128]{1,2,0:T(8,128)(2,1)} %convert_bitcast_fusion.2) | data formatting | bytes 8388608 | tf_op jit(solution)/shard_map/convert_element_type | solution.py:87
  66.3 6.7 %all-to-all-start = ((bf16[32,512,128]{2,0,1:T(8,128)(2,1)}), bf16[32,512,128]{2,0,1:T(8,128)(2,1)}, u32[]{:S(2)}, u32[]{:S(2)}) async-start(bf16[32,512,128]{2,0,1:T(8,128)(2,1)} %copy.46), calls=%async_computation | async-start | bytes 8388608 | tf_op jit(solution)/shard_map/all_to_all | solution.py:89
  73.0 6.8 %copy.53 = bf16[32,512,128]{2,0,1:T(8,128)(2,1)} copy(bf16[32,512,128]{2,1,0:T(8,128)(2,1)} %bitcast.107) | data formatting | bytes 8388608 | tf_op jit(solution)/shard_map/reshape | solution.py:88
  79.8 48.8 %all-to-all-done = bf16[32,512,128]{2,0,1:T(8,128)(2,1)} async-done(((bf16[32,512,128]{2,0,1:T(8,128)(2,1)}), bf16[32,512,128]{2,0,1:T(8,128)(2,1)}, u32[]{:S(2)}, u32[]{:S(2)}) %all-to-all-start) | async-done | bytes 4194336 | tf_op jit(solution)/shard_map/all_to_all | solution.py:89
  128.7 4.9 all-to-all-start.2
  133.5 7.5 %copy.49 = bf16[512,32,128]{0,2,1:T(8,128)(2,1)} copy(bf16[512,32,128]{2,1,0:T(8,128)(2,1)} %param.12) | data formatting | bytes 8388608 | tf_op args[5]
  141.0 3.8 copy.47
  146.0 4.3 copy.48
  150.3 10.0 %copy.50 = f32[512,32,128]{0,2,1:T(8,128)} copy(f32[512,32,128]{2,1,0:T(8,128)} %bitcast.105) | data formatting | bytes 16777216 | tf_op jit(solution)/shard_map/convert_element_type | solution.py:91
  160.3 8.9 %convert_bitcast_fusion.1 = bf16[512,32,128]{0,2,1:T(8,128)(2,1)} fusion(bf16[512,512]{1,0:T(8,128)(2,1)S(1)} %copy-done, f32[512,32,128]{0,2,1:T(8,128)} %copy.50, bf16[512,32,128]{0,2,1:T(8,128)(2,1)} %copy.49), kind=kOutput, calls=%fused_computation.65 | convolution fusion | flops 2155872256 | bytes 17301504 | tf_op jit(solution)/shard_map/ijc,ik->kjc/dot_general | solution.py:92
  169.2 7.9 %copy.51 = bf16[512,32,128]{2,1,0:T(8,128)(2,1)} copy(bf16[512,32,128]{0,2,1:T(8,128)(2,1)} %convert_bitcast_fusion.1) | data formatting | bytes 8388608 | tf_op jit(solution)/shard_map/convert_element_type | solution.py:94
  177.1 12.1 %all-to-all-done.2 = bf16[32,512,128]{2,0,1:T(8,128)(2,1)} async-done(((bf16[32,512,128]{2,0,1:T(8,128)(2,1)}), bf16[32,512,128]{2,0,1:T(8,128)(2,1)}, u32[]{:S(2)}, u32[]{:S(2)}) %all-to-all-start.2) | async-done | bytes 4194336 | tf_op jit(solution)/shard_map/all_to_all | solution.py:96
  189.2 5.4 %all-to-all-start.1 = ((bf16[512,32,128]{2,1,0:T(8,128)(2,1)}), bf16[512,32,128]{2,1,0:T(8,128)(2,1)}, u32[]{:S(2)}, u32[]{:S(2)}) async-start(bf16[512,32,128]{2,1,0:T(8,128)(2,1)} %copy.51), calls=%async_computation.1 | async-start | bytes 8388608 | tf_op jit(solution)/shard_map/all_to_all | solution.py:95
  194.7 4.1 copy.55
  198.9 8.0 %fusion.35 = f32[512,512]{1,0:T(8,128)S(1)} fusion(bf16[512,32,128]{2,1,0:T(8,128)(2,1)S(1)} %bitcast.103, f32[512,32,128]{0,2,1:T(8,128)} %copy.50, bf16[512,32,128]{0,2,1:T(8,128)(2,1)S(1)} %copy-done.4), kind=kOutput, calls=%fused_computation.72 | convolution fusion | flops 2153775104 | bytes 17825792 | tf_op jit(solution)/shard_map/ijc,kjc->ik/dot_general | solution.py:102
  208.8 9.0 %fusion.29 = (bf16[512,32,128]{0,2,1:T(8,128)(2,1)}, bf16[512,32,128]{0,2,1:T(8,128)(2,1)}) fusion(f32[512,32,128]{0,2,1:T(8,128)S(1)} %bitcast.100, bf16[512,32,128]{0,2,1:T(8,128)(2,1)S(1)} %copy-done.4, bf16[512,512]{1,0:T(8,128)(2,1)S(1)} %copy-done, bf16[512,32,128]{2,1,0:T(8,128)(2,1)S(1)} %bitcast.104), kind=kOutput, calls=%fused_computation.52 | convolution fusion | flops 2157969408 | bytes 25690112 | tf_op jit(solution)/shard_map/kjc,ik->ijc/dot_general | solution.py:97
  219.3 31.1 %all-to-all-done.1 = bf16[512,32,128]{2,1,0:T(8,128)(2,1)} async-done(((bf16[512,32,128]{2,1,0:T(8,128)(2,1)}), bf16[512,32,128]{2,1,0:T(8,128)(2,1)}, u32[]{:S(2)}, u32[]{:S(2)}) %all-to-all-start.1) | async-done | bytes 4194336 | tf_op jit(solution)/shard_map/all_to_all | solution.py:95
  250.4 5.5 %copy.52 = bf16[32,16,32,128]{3,2,1,0:T(8,128)(2,1)} copy(bf16[32,16,32,128]{3,2,0,1:T(8,128)(2,1)} %bitcast.13) | data formatting | bytes 8388608 | tf_op jit(solution)/shard_map/all_to_all | solution.py:95
  255.8 7.9 %copy.57 = bf16[512,32,128]{2,1,0:T(8,128)(2,1)} copy(bf16[512,32,128]{0,2,1:T(8,128)(2,1)} %get-tuple-element.8) | data formatting | bytes 8388608 | tf_op jit(solution)/shard_map/optimization_barrier | solution.py:104
  263.7 4.9 all-to-all-start.3
  270.5 59.3 %collective-permute-done.10 = f32[128,512]{1,0:T(8,128)S(1)} collective-permute-done((f32[128,512]{1,0:T(8,128)S(1)}, f32[128,512]{1,0:T(8,128)S(1)}, u32[]{:S(2)}, u32[]{:S(2)}) %collective-permute-start.10) | collective-permute-done | bytes 262176 | tf_op jit(solution)/shard_map/ppermute | solution.py:31
  331.2 3.2 collective-permute-done.11
  342.0 3.0 collective-permute-start.14
  347.3 3.1 collective-permute-done.15
  363.1 3.3 collective-permute-done.19
  367.8 7.9 %copy.65 = bf16[512,32,128]{2,1,0:T(8,128)(2,1)} copy(bf16[512,32,128]{0,2,1:T(8,128)(2,1)} %get-tuple-element.41) | data formatting | bytes 8388608
  378.0 3.6 copy.58
  381.6 7.1 %multiply_reduce_fusion = (f32[128]{0:T(128)S(1)}, f32[32,512,128]{1,2,0:T(8,128)}) fusion(f32[128]{0:T(128)S(1)} %copy-done.13, f32[32,512]{1,0:T(8,128)S(1)} %mul.250, bf16[32,512,128]{1,2,0:T(8,128)(2,1)S(1)} %copy-done.6, bf16[32,512,128]{2,1,0:T(8,128)(2,1)S(1)} %bitcast.111, bf16[512,512]{1,0:T(8,128)(2,1)S(1)} %copy-done.12), kind=kOutput, calls=%fused_computation.54 | convolution fusion | flops 2162163712 | bytes 17368064 | tf_op jit(solution)/shard_map/ikc,jk->ijc/dot_general | solution.py:108
  388.7 9.0 %copy.60 = f32[32,512,128]{2,1,0:T(8,128)} copy(f32[32,512,128]{1,2,0:T(8,128)} %get-tuple-element.50) | data formatting | bytes 16777216 | tf_op jit(solution)/shard_map/ikc,jk->ijc/transpose | solution.py:108
  398.3 13.4 %fusion.22 = (f32[128]{0:T(128)S(1)}, f32[128]{0:T(128)S(1)}, f32[128]{0:T(128)S(1)}, f32[128]{0:T(128)S(1)}, f32[128]{0:T(128)S(1)}, /*index=5*/f32[16384,128]{1,0:T(8,128)S(1)}) fusion(bf16[16384,128]{1,0:T(8,128)(2,1)} %copy-done.3, bf16[2,128]{1,0:T(2,128)(2,1)S(1)} %collective-permute-done.3, bf16[16384,128]{1,0:T(8,128)(2,1)} %copy-done.5, ...), kind=kLoop, calls=%fused_computation.41 | loop fusion | flops 62913920 | bytes 33559040 | tf_op jit(solution)/shard_map/reduce_sum | solution.py:126
  411.8 12.9 %collective-permute-start.5 = (f32[2,128]{1,0:T(2,128)S(1)}, f32[2,128]{1,0:T(2,128)S(1)}, u32[]{:S(2)}, u32[]{:S(2)}) collective-permute-start(f32[2,128]{1,0:T(2,128)S(1)} %slice.130), channel_id=1, source_target_pairs={{8,0},{16,8},{24,16},{32,24},{40,32},{48,40},{56,48},{64,56},{72,6... | collective-permute-start | bytes 3080 | tf_op jit(solution)/shard_map/ppermute | solution.py:16
  429.6 16.3 %multiply_reduce_fusion.1 = (f32[128]{0:T(128)S(1)}, f32[16384]{0:T(1024)S(1)}, f32[16384,128]{1,0:T(8,128)}) fusion(f32[32,512,128]{2,1,0:T(8,128)} %copy.44, f32[16384]{0:T(1024)S(1)} %add_rsqrt_fusion, f32[128]{0:T(128)S(1)} %copy-done.13, f32[2,128]{1,0:T(2,128)S(1)} %collective-permute-done.5, f32[16384,128]{1,0:T(8,128)S(1)} %get-tuple-element.37, ...), kind=kLoop, calls=%fused_computation.56 | loop fusion | flops 44023680 | bytes 33691648 | tf_op jit(solution)/shard_map/reduce_sum | solution.py:128
  452.2 5.8 %convolution_bitcast_fusion.1 = f32[512,512]{1,0:T(8,128)S(1)} fusion(bf16[32,512,128]{2,1,0:T(8,128)(2,1)} %bitcast.110, bf16[32,512,128]{2,1,0:T(8,128)(2,1)} %bitcast.112), kind=kOutput, calls=%fused_computation.73 | convolution fusion | flops 2147483648 | bytes 9437184 | tf_op jit(solution)/shard_map/ijc,ikc->jk/dot_general | solution.py:111
  460.3 6.7 %all-to-all-start.4 = ((f32[128,1,2048]{2,1,0:T(1,128)}), f32[128,1,2048]{2,1,0:T(1,128)S(1)}, u32[]{:S(2)}, u32[]{:S(2)}) async-start(f32[128,1,2048]{2,1,0:T(1,128)} %all_to_all.72), calls=%async_computation.4 | async-start | bytes 2097152 | tf_op jit(solution)/shard_map/all_to_all | solution.py:56
  477.7 3.3 collective-permute-done.6
  481.0 4.2 collective-permute-start.7
  493.7 11.3 %all-to-all-start.5 = ((f32[128,1,2048]{2,1,0:T(1,128)}), f32[128,1,2048]{2,1,0:T(1,128)S(1)}, u32[]{:S(2)}, u32[]{:S(2)}) async-start(f32[128,1,2048]{2,1,0:T(1,128)} %broadcast_in_dim.2), calls=%async_computation.5 | async-start | bytes 2097152 | tf_op jit(solution)/shard_map/all_to_all | solution.py:59
  505.1 11.5 %multiply_convert_fusion.1 = bf16[16384,128]{1,0:T(8,128)(2,1)} fusion(f32[16384,128]{1,0:T(8,128)} %get-tuple-element.38, f32[32,512,128]{2,1,0:T(8,128)} %copy.44, f32[16384]{0:T(1024)S(1)} %add_multiply_fusion, f32[128]{0:T(128)S(1)} %copy-done.13, f32[16384]{0:T(1024)S(1)} %add_rsqrt_fusion), kind=kLoop, calls=%fused_computation.57 | loop fusion | flops 12582912 | bytes 21103104 | tf_op jit(solution)/shard_map/convert_element_type | solution.py:137
  516.6 6.2 %all-to-all-done.5 = f32[128,1,2048]{2,1,0:T(1,128)S(1)} async-done(((f32[128,1,2048]{2,1,0:T(1,128)}), f32[128,1,2048]{2,1,0:T(1,128)S(1)}, u32[]{:S(2)}, u32[]{:S(2)}) %all-to-all-start.5) | async-done | bytes 1048608 | tf_op jit(solution)/shard_map/all_to_all | solution.py:59
  (139 shorter events, 82.7 us)
Async XLA Ops:
  0.6 159.7 %copy-start = (bf16[512,512]{1,0:T(8,128)(2,1)S(1)}, bf16[512,512]{1,0:T(8,128)(2,1)}, u32[]{:S(2)}) copy-start(bf16[512,512]{1,0:T(8,128)(2,1)} %param.11) | copy-start | bytes 1572868
  7.1 22.7 %copy-start.13 = (f32[128]{0:T(128)S(1)}, f32[128]{0:T(128)}, u32[]{:S(2)}) copy-start(f32[128]{0:T(128)} %param.8) | copy-start | bytes 1540
  10.3 3.8 collective-permute-start
  14.1 4.7 collective-permute-start.1
  18.8 11.0 %collective-permute-start.2 = (f32[16384]{0:T(1024)S(1)}, f32[16384]{0:T(1024)S(1)}, u32[]{:S(2)}, u32[]{:S(2)}) collective-permute-start(f32[16384]{0:T(1024)S(1)} %add.129), channel_id=1, source_target_pairs={{0,4},{1,5},{2,6},{3,7},{4,0},{5,1},{6,2},{7,3},{8,12},{9,13},{10,... | collective-permute-start | bytes 196616 | tf_op jit(solution)/shard_map/ppermute | solution.py:24
  29.7 11.9 %copy-start.14 = (f32[2,3,128]{2,0,1:T(2,128)S(1)}, f32[2,3,128]{2,0,1:T(2,128)}, u32[]{:S(2)}) copy-start(f32[2,3,128]{2,0,1:T(2,128)} %param.9) | copy-start | bytes 9220
  29.8 12.6 %copy-start.7 = (bf16[32,512,128]{2,1,0:T(8,128)(2,1)S(1)}, bf16[32,512,128]{2,1,0:T(8,128)(2,1)}, u32[]{:S(2)}) copy-start(bf16[32,512,128]{2,1,0:T(8,128)(2,1)} %param.13) | copy-start | bytes 12582916
  35.3 13.6 %copy-start.3 = (bf16[16384,128]{1,0:T(8,128)(2,1)}, bf16[16384,128]{1,0:T(8,128)(2,1)S(1)}, u32[]{:S(2)}) copy-start(bf16[16384,128]{1,0:T(8,128)(2,1)S(1)} %multiply_convert_fusion.2) | copy-start | bytes 12582916
  35.3 7.1 %collective-permute-start.3 = (bf16[2,128]{1,0:T(2,128)(2,1)S(1)}, bf16[2,128]{1,0:T(2,128)(2,1)S(1)}, u32[]{:S(2)}, u32[]{:S(2)}) collective-permute-start(bf16[2,128]{1,0:T(2,128)(2,1)S(1)} %slice.124), channel_id=1, source_target_pairs={{0,8},{8,16},{16,24},{24,32},{32,40},{40,48},{48,56},{56,64},{64,7... | collective-permute-start | bytes 1544 | tf_op jit(solution)/shard_map/ppermute | solution.py:16
  66.3 62.4 %all-to-all-start = ((bf16[32,512,128]{2,0,1:T(8,128)(2,1)}), bf16[32,512,128]{2,0,1:T(8,128)(2,1)}, u32[]{:S(2)}, u32[]{:S(2)}) async-start(bf16[32,512,128]{2,0,1:T(8,128)(2,1)} %copy.46), calls=%async_computation | async-start | bytes 8388608 | tf_op jit(solution)/shard_map/all_to_all | solution.py:89
  128.7 60.6 %all-to-all-start.2 = ((bf16[32,512,128]{2,0,1:T(8,128)(2,1)}), bf16[32,512,128]{2,0,1:T(8,128)(2,1)}, u32[]{:S(2)}, u32[]{:S(2)}) async-start(bf16[32,512,128]{2,0,1:T(8,128)(2,1)} %copy.53), calls=%async_computation.2 | async-start | bytes 8388608 | tf_op jit(solution)/shard_map/all_to_all | solution.py:96
  189.2 61.1 %all-to-all-start.1 = ((bf16[512,32,128]{2,1,0:T(8,128)(2,1)}), bf16[512,32,128]{2,1,0:T(8,128)(2,1)}, u32[]{:S(2)}, u32[]{:S(2)}) async-start(bf16[512,32,128]{2,1,0:T(8,128)(2,1)} %copy.51), calls=%async_computation.1 | async-start | bytes 8388608 | tf_op jit(solution)/shard_map/all_to_all | solution.py:95
  194.7 14.0 %slice-start = ((s8[8388608]{0:T(1024)(128)(4,1)}), s8[4194304]{0:T(1024)(128)(4,1)S(1)}, s32[]{:S(2)}) async-start(s8[8388608]{0:T(1024)(128)(4,1)} %bitcast.99), calls=%async_computation.6 | async-start | bytes 8388608
  198.9 9.9 %slice-start.1 = ((s8[8388608]{0:T(1024)(128)(4,1)}), s8[4194304]{0:T(1024)(128)(4,1)S(1)}, s32[]{:S(2)}) async-start(s8[8388608]{0:T(1024)(128)(4,1)} %bitcast.99), calls=%async_computation.7 | async-start | bytes 8388608
  208.8 9.0 %collective-permute-start.9 = (f32[256,512]{1,0:T(8,128)}, f32[256,512]{1,0:T(8,128)}, u32[]{:S(2)}, u32[]{:S(2)}) collective-permute-start(f32[256,512]{1,0:T(8,128)} %slice_select_fusion), channel_id=1, source_target_pairs={{0,8},{8,0},{16,24},{24,16},{32,40},{40,32},{48,56},{56,48},{64,72... | collective-permute-start | bytes 1572872 | tf_op jit(solution)/shard_map/ppermute | solution.py:31
  263.7 114.3 %all-to-all-start.3 = ((bf16[512,32,128]{2,1,0:T(8,128)(2,1)}), bf16[512,32,128]{2,1,0:T(8,128)(2,1)}, u32[]{:S(2)}, u32[]{:S(2)}) async-start(bf16[512,32,128]{2,1,0:T(8,128)(2,1)} %copy.57), calls=%async_computation.3 | async-start | bytes 8388608 | tf_op jit(solution)/shard_map/all_to_all | solution.py:105
  268.6 61.2 %collective-permute-start.10 = (f32[128,512]{1,0:T(8,128)S(1)}, f32[128,512]{1,0:T(8,128)S(1)}, u32[]{:S(2)}, u32[]{:S(2)}) collective-permute-start(f32[128,512]{1,0:T(8,128)S(1)} %slice_select_fusion.1), channel_id=1, source_target_pairs={{0,16},{8,24},{16,0},{24,8},{32,48},{40,56},{48,32},{56,40},{64,80... | collective-permute-start | bytes 786440 | tf_op jit(solution)/shard_map/ppermute | solution.py:31
  329.9 4.4 collective-permute-start.11
  334.4 3.2 collective-permute-start.12
  337.6 4.3 collective-permute-start.13
  342.0 4.4 collective-permute-start.14
  346.4 4.1 collective-permute-start.15
  350.5 4.0 collective-permute-start.16
  354.5 4.2 collective-permute-start.17
  358.7 4.3 collective-permute-start.18
  362.9 3.5 collective-permute-start.19
  366.5 9.2 %collective-permute-start.20 = (f32[64,512]{1,0:T(8,128)S(1)}, f32[64,512]{1,0:T(8,128)S(1)}, u32[]{:S(2)}, u32[]{:S(2)}) collective-permute-start(f32[64,512]{1,0:T(8,128)S(1)} %maximum_select_fusion.3), channel_id=1, source_target_pairs={{0,1},{1,0},{2,3},{3,2},{4,5},{5,4},{6,7},{7,6},{8,9},{9,8},{10,11... | collective-permute-start | bytes 393224 | tf_op jit(solution)/shard_map/ppermute | solution.py:31
  367.8 13.8 %copy-start.12 = (bf16[512,512]{1,0:T(8,128)(2,1)S(1)}, bf16[512,512]{1,0:T(8,128)(2,1)}, u32[]{:S(2)}) copy-start(bf16[512,512]{1,0:T(8,128)(2,1)} %param.10) | copy-start | bytes 1572868
  375.7 71.4 %collective-permute-start.21 = (f32[128,512]{1,0:T(8,128)S(1)}, f32[128,512]{1,0:T(8,128)S(1)}, u32[]{:S(2)}, u32[]{:S(2)}) collective-permute-start(f32[128,512]{1,0:T(8,128)S(1)} %maximum_select_fusion.2), channel_id=1, source_target_pairs={{0,16},{8,24},{16,0},{24,8},{32,48},{40,56},{48,32},{56,40},{64,80... | collective-permute-start | bytes 786440 | tf_op jit(solution)/shard_map/ppermute | solution.py:31
  381.6 7.1 %copy-start.10 = (bf16[32,16,32,128]{3,2,1,0:T(8,128)(2,1)}, bf16[32,16,32,128]{3,2,1,0:T(8,128)(2,1)S(1)}, u32[]{:S(2)}) copy-start(bf16[32,16,32,128]{3,2,1,0:T(8,128)(2,1)S(1)} %copy.58) | copy-start | bytes 12582916
  398.3 31.3 %copy-start.2 = (f32[32,512,128]{2,1,0:T(8,128)S(1)}, f32[32,512,128]{2,1,0:T(8,128)}, u32[]{:S(2)}) copy-start(f32[32,512,128]{2,1,0:T(8,128)} %copy.60) | copy-start | bytes 25165828
  411.8 15.3 %collective-permute-start.5 = (f32[2,128]{1,0:T(2,128)S(1)}, f32[2,128]{1,0:T(2,128)S(1)}, u32[]{:S(2)}, u32[]{:S(2)}) collective-permute-start(f32[2,128]{1,0:T(2,128)S(1)} %slice.130), channel_id=1, source_target_pairs={{8,0},{16,8},{24,16},{32,24},{40,32},{48,40},{56,48},{64,56},{72,6... | collective-permute-start | bytes 3080 | tf_op jit(solution)/shard_map/ppermute | solution.py:16
  424.7 4.9 collective-permute-start.4
  445.9 1.2 collective-permute-start.23
  445.9 5.3 %collective-permute-start.27 = (f32[2,3,128]{2,1,0:T(4,128)S(1)}, f32[2,3,128]{2,1,0:T(4,128)S(1)}, u32[]{:S(2)}, u32[]{:S(2)}) collective-permute-start(f32[2,3,128]{2,1,0:T(4,128)S(1)} %pad_maximum_fusion.3), channel_id=1, source_target_pairs={{0,8},{8,0},{16,24},{24,16},{32,40},{40,32},{48,56},{56,48},{64,72... | collective-permute-start | bytes 9224 | tf_op jit(solution)/shard_map/ppermute | solution.py:24
  447.1 2.4 collective-permute-start.24
  447.2 25.5 %collective-permute-start.22 = (f32[256,512]{1,0:T(8,128)S(1)}, f32[256,512]{1,0:T(8,128)S(1)}, u32[]{:S(2)}, u32[]{:S(2)}) collective-permute-start(f32[256,512]{1,0:T(8,128)S(1)} %maximum_select_fusion.1), channel_id=1, source_target_pairs={{0,8},{8,0},{16,24},{24,16},{32,40},{40,32},{48,56},{56,48},{64,72... | collective-permute-start | bytes 1572872 | tf_op jit(solution)/shard_map/ppermute | solution.py:31
  449.5 18.9 %collective-permute-start.25 = (f32[128]{0:T(128)S(1)}, f32[128]{0:T(128)S(1)}, u32[]{:S(2)}, u32[]{:S(2)}) collective-permute-start(f32[128]{0:T(128)S(1)} %add.161), channel_id=1, source_target_pairs={{0,32},{8,40},{16,48},{24,56},{32,0},{40,8},{48,16},{56,24},{64,96... | collective-permute-start | bytes 1544 | tf_op jit(solution)/shard_map/ppermute | solution.py:24
  451.3 18.5 %collective-permute-start.28 = (f32[2,3,128]{2,1,0:T(4,128)S(1)}, f32[2,3,128]{2,1,0:T(4,128)S(1)}, u32[]{:S(2)}, u32[]{:S(2)}) collective-permute-start(f32[2,3,128]{2,1,0:T(4,128)S(1)} %fusion.43), channel_id=1, source_target_pairs={{0,16},{8,24},{16,0},{24,8},{32,48},{40,56},{48,32},{56,40},{64,80... | collective-permute-start | bytes 9224 | tf_op jit(solution)/shard_map/ppermute | solution.py:24
  460.3 31.4 %all-to-all-start.4 = ((f32[128,1,2048]{2,1,0:T(1,128)}), f32[128,1,2048]{2,1,0:T(1,128)S(1)}, u32[]{:S(2)}, u32[]{:S(2)}) async-start(f32[128,1,2048]{2,1,0:T(1,128)} %all_to_all.72), calls=%async_computation.4 | async-start | bytes 2097152 | tf_op jit(solution)/shard_map/all_to_all | solution.py:56
  467.0 14.0 %collective-permute-start.6 = (f32[16384]{0:T(1024)S(1)}, f32[16384]{0:T(1024)S(1)}, u32[]{:S(2)}, u32[]{:S(2)}) collective-permute-start(f32[16384]{0:T(1024)S(1)} %get-tuple-element.29), channel_id=1, source_target_pairs={{0,1},{1,0},{2,3},{3,2},{4,5},{5,4},{6,7},{7,6},{8,9},{9,8},{10,11... | collective-permute-start | bytes 196616 | tf_op jit(solution)/shard_map/ppermute | solution.py:24
  468.4 16.8 %collective-permute-start.26 = (f32[128]{0:T(128)S(1)}, f32[128]{0:T(128)S(1)}, u32[]{:S(2)}, u32[]{:S(2)}) collective-permute-start(f32[128]{0:T(128)S(1)} %add.162), channel_id=1, source_target_pairs={{0,64},{8,72},{16,80},{24,88},{32,96},{40,104},{48,112},{56,120},{... | collective-permute-start | bytes 1544 | tf_op jit(solution)/shard_map/ppermute | solution.py:24
  469.8 6.4 %collective-permute-start.29 = (f32[2,3,128]{2,1,0:T(4,128)S(1)}, f32[2,3,128]{2,1,0:T(4,128)S(1)}, u32[]{:S(2)}, u32[]{:S(2)}) collective-permute-start(f32[2,3,128]{2,1,0:T(4,128)S(1)} %fusion.53), channel_id=1, source_target_pairs={{0,32},{8,40},{16,48},{24,56},{32,0},{40,8},{48,16},{56,24},{64,96... | collective-permute-start | bytes 9224 | tf_op jit(solution)/shard_map/ppermute | solution.py:24
  476.2 13.3 %collective-permute-start.30 = (f32[2,3,128]{2,1,0:T(4,128)S(1)}, f32[2,3,128]{2,1,0:T(4,128)S(1)}, u32[]{:S(2)}, u32[]{:S(2)}) collective-permute-start(f32[2,3,128]{2,1,0:T(4,128)S(1)} %add.166), channel_id=1, source_target_pairs={{0,64},{8,72},{16,80},{24,88},{32,96},{40,104},{48,112},{56,120},{... | collective-permute-start | bytes 9224 | tf_op jit(solution)/shard_map/ppermute | solution.py:24
  481.0 5.9 %collective-permute-start.7 = (f32[16384]{0:T(1024)S(1)}, f32[16384]{0:T(1024)S(1)}, u32[]{:S(2)}, u32[]{:S(2)}) collective-permute-start(f32[16384]{0:T(1024)S(1)} %add.143), channel_id=1, source_target_pairs={{0,2},{1,3},{2,0},{3,1},{4,6},{5,7},{6,4},{7,5},{8,10},{9,11},{10,... | collective-permute-start | bytes 196616 | tf_op jit(solution)/shard_map/ppermute | solution.py:24
  486.9 4.7 collective-permute-start.8
  493.7 29.1 %all-to-all-start.5 = ((f32[128,1,2048]{2,1,0:T(1,128)}), f32[128,1,2048]{2,1,0:T(1,128)S(1)}, u32[]{:S(2)}, u32[]{:S(2)}) async-start(f32[128,1,2048]{2,1,0:T(1,128)} %broadcast_in_dim.2), calls=%async_computation.5 | async-start | bytes 2097152 | tf_op jit(solution)/shard_map/all_to_all | solution.py:59
  505.1 22.0 %copy-start.1 = (bf16[512,512]{1,0:T(8,128)(2,1)S(1)}, bf16[512,512]{1,0:T(8,128)(2,1)}, u32[]{:S(2)}) copy-start(bf16[512,512]{1,0:T(8,128)(2,1)} %param.11) | copy-start | bytes 1572868
  (6 other events, 18.8 us)

commit v6 on v4

--- a/solution.py
+++ b/solution.py
@@ -89,8 +89,7 @@
     kernel_grad = (grad_spec * columns.astype(jnp.float32)).astype(jnp.bfloat16)
     grad_section = (grad_spec * kern).astype(jnp.bfloat16)
     two_part = jnp.einsum("ijc,kjc->ik", spectrum, grad_columns, preferred_element_type=jnp.float32)
-    two_total = tree_allreduce(two_part, FACTOR_ROUNDS)
-    back_rows, grad_section = lax.optimization_barrier((back_rows, grad_section))
+    back_rows, grad_section, two_part = lax.optimization_barrier((back_rows, grad_section, two_part))
     grad_rows = lax.all_to_all(grad_section, "ctx", split_axis=0, concat_axis=1, tiled=True)
     back_flat = back_rows.reshape(rows, chans).astype(jnp.float32)
     grad_gate_pre = cotangent * back_flat * gate * (1.0 - gate)
@@ -107,7 +106,8 @@
         "ikc,jk->ijc", grad_rows, factor_one, preferred_element_type=jnp.float32
     ).reshape(rows, chans)
     one_part = jnp.einsum("ijc,ikc->jk", mixed_in, grad_rows, preferred_element_type=jnp.float32)
-    one_total = tree_allreduce(one_part, FACTOR_ROUNDS)
+    both_total = tree_allreduce(jnp.concatenate([one_part, two_part]), FACTOR_ROUNDS)
+    one_total, two_total = both_total[: one_part.shape[0]], both_total[one_part.shape[0] :]
     grad_mixed = lax.optimization_barrier(grad_mixed)
     later_value = shifted(grad_mixed[: taps_count - 1], "ctx", -1)
     ext_value = jnp.concatenate([grad_mixed, later_value], 0)

time: 547 us -> 499 us (0.912)
  waiting for transfers between devices: 219 us -> 180 us
  starting transfers between devices: 104 us -> 88.2 us
    ppermute x28 -> x14, waiting for transfers between devices: 92.3 us -> 35.3 us  [exchange(): lax.ppermute(value, axis, [(source, source ^ step) for source in range(co...]
    all_to_all x1, waiting for transfers between devices: 0.01 us -> 33.5 us  [on_device(): lax.all_to_all(section_two, 'ctx', split_axis=0, concat_axis=1, tiled=True)]
    all_to_all x1, waiting for transfers between devices: 35 us -> 12.2 us  [on_device(): lax.all_to_all(out_grad, 'ctx', split_axis=1, concat_axis=0, tiled=True)]
    ppermute x28 -> x14, starting transfers between devices: 44.5 us -> 25.1 us  [exchange(): lax.ppermute(value, axis, [(source, source ^ step) for source in range(co...]
    all_to_all x1, waiting for transfers between devices: 42.3 us -> 48.8 us  [on_device(): lax.all_to_all(section_one, 'ctx', split_axis=1, concat_axis=0, tiled=True)]
    unnamed x36 -> x62, local copies, waits for them, and re-layouts: 22.3 us -> 25.3 us
  transfers between devices with their start and end apart: 49 -> 35, of which waited for: 25 -> 19; matrix products, arithmetic and copies ran while one was open for 27% -> 32% of each run, Pallas kernels for 0% -> 0%
where the time goes in v6:
time: 499 us; the launch traced here: 490 us
  waiting for transfers between devices  180 us (36%)
  local copies, waits for them, and re-layouts  95.1 us (19%)
  starting transfers between devices  88.2 us (18%)
  other arithmetic  82.1 us (16%)
  matrix products  42.8 us (9%)
    all_to_all x1, waiting for transfers between devices, on_device(): lax.all_to_all(section_one, 'ctx', split_axis=1, concat_axis=0, tiled=True)  48.8 us
    all_to_all x1, waiting for transfers between devices, on_device(): lax.all_to_all(grad_section, 'ctx', split_axis=0, concat_axis=1, tiled=True)  39.4 us
    ppermute x14, waiting for transfers between devices, exchange(): lax.ppermute(value, axis, [(source, source ^ step) for source in range(co...  35.3 us
    all_to_all x1, waiting for transfers between devices, on_device(): lax.all_to_all(section_two, 'ctx', split_axis=0, concat_axis=1, tiled=True)  33.5 us
    unnamed x62, local copies, waits for them, and re-layouts  25.3 us
    ppermute x14, starting transfers between devices, exchange(): lax.ppermute(value, axis, [(source, source ^ step) for source in range(co...  25.1 us
    reduce_sum x1, other arithmetic, on_device(): value_taps.append(jnp.sum(grad_mixed * window, axis=0))  24.7 us
    ppermute x14, starting transfers between devices, tree_psum(): lax.ppermute(value, axis, pairs)  22.5 us
  transfers between devices with their start and end apart: 35, of which 19 were waited for; matrix products, arithmetic and copies ran while one was open for 32% of the time, Pallas kernels for 0%

profile of v6, /device:TPU:1, one launch (start us, length us, event | category | flops | bytes accessed | tf_op | source)
XLA Modules:
  0.0 490.2 jit_solution(933551036059164775)
XLA Ops:
  0.7 4.6 multiply_reduce_fusion.2
  9.1 3.1 collective-permute-start.1
  13.8 3.9 collective-permute-start.2
  19.4 4.4 multiply_convert_fusion.1
  23.9 6.9 %collective-permute-start.3 = (bf16[2,128]{1,0:T(2,128)(2,1)S(1)}, bf16[2,128]{1,0:T(2,128)(2,1)S(1)}, u32[]{:S(2)}, u32[]{:S(2)}) collective-permute-start(bf16[2,128]{1,0:T(2,128)(2,1)S(1)} %slice.126), channel_id=1, source_target_pairs={{0,8},{8,16},{16,24},{24,32},{32,40},{40,48},{48,56},{56,64},{64,7... | collective-permute-start | bytes 1544 | tf_op jit(solution)/shard_map/ppermute | solution.py:16
  31.5 6.5 %fusion.10 = (bf16[16384,128]{1,0:T(8,128)(2,1)}, bf16[16384,128]{1,0:T(8,128)(2,1)S(1)}) fusion(bf16[32,512,128]{2,1,0:T(8,128)(2,1)S(1)} %copy-done.9, bf16[16384,128]{1,0:T(8,128)(2,1)S(1)} %multiply_convert_fusion.1, bf16[2,128]{1,0:T(2,128)(2,1)S(1)} %collective-permute-done.3, f32[128]{0:T(128)S(1)} %get-tuple-element.69, ...), kind=kLoop, calls=%fused_computation.30 | loop fusion | flops 44040192 | bytes 16779264 | tf_op jit(solution)/shard_map/convert_element_type | solution.py:77
  38.1 3.0 fusion.15
  43.1 4.4 convert_bitcast_fusion.2
  47.5 7.9 %copy.58 = bf16[32,512,128]{2,0,1:T(8,128)(2,1)} copy(bf16[32,512,128]{1,2,0:T(8,128)(2,1)} %convert_bitcast_fusion.2) | data formatting | bytes 8388608 | tf_op jit(solution)/shard_map/convert_element_type | solution.py:76
  55.4 7.2 %all-to-all-start = ((bf16[32,512,128]{2,0,1:T(8,128)(2,1)}), bf16[32,512,128]{2,0,1:T(8,128)(2,1)}, u32[]{:S(2)}, u32[]{:S(2)}) async-start(bf16[32,512,128]{2,0,1:T(8,128)(2,1)} %copy.58), calls=%async_computation | async-start | bytes 8388608 | tf_op jit(solution)/shard_map/all_to_all | solution.py:78
  62.6 6.9 %copy.65 = bf16[32,512,128]{2,0,1:T(8,128)(2,1)} copy(bf16[32,512,128]{2,1,0:T(8,128)(2,1)} %bitcast.104) | data formatting | bytes 8388608 | tf_op jit(solution)/shard_map/reshape | solution.py:77
  69.5 48.8 %all-to-all-done = bf16[32,512,128]{2,0,1:T(8,128)(2,1)} async-done(((bf16[32,512,128]{2,0,1:T(8,128)(2,1)}), bf16[32,512,128]{2,0,1:T(8,128)(2,1)}, u32[]{:S(2)}, u32[]{:S(2)}) %all-to-all-start) | async-done | bytes 4194336 | tf_op jit(solution)/shard_map/all_to_all | solution.py:78
  118.3 4.9 all-to-all-start.2
  123.2 7.5 %copy.61 = bf16[512,32,128]{0,2,1:T(8,128)(2,1)} copy(bf16[512,32,128]{2,1,0:T(8,128)(2,1)} %param.12) | data formatting | bytes 8388608 | tf_op args[5]
  130.7 3.8 copy.59
  135.7 4.3 copy.60
  140.0 10.0 %copy.62 = f32[512,32,128]{0,2,1:T(8,128)} copy(f32[512,32,128]{2,1,0:T(8,128)} %bitcast.101) | data formatting | bytes 16777216 | tf_op jit(solution)/shard_map/convert_element_type | solution.py:80
  150.0 8.8 %convert_bitcast_fusion.1 = bf16[512,32,128]{0,2,1:T(8,128)(2,1)} fusion(bf16[512,512]{1,0:T(8,128)(2,1)S(1)} %copy-done, f32[512,32,128]{0,2,1:T(8,128)} %copy.62, bf16[512,32,128]{0,2,1:T(8,128)(2,1)} %copy.61), kind=kOutput, calls=%fused_computation.65 | convolution fusion | flops 2155872256 | bytes 17301504 | tf_op jit(solution)/shard_map/ijc,ik->kjc/dot_general | solution.py:81
  158.8 7.9 %copy.63 = bf16[512,32,128]{2,1,0:T(8,128)(2,1)} copy(bf16[512,32,128]{0,2,1:T(8,128)(2,1)} %convert_bitcast_fusion.1) | data formatting | bytes 8388608 | tf_op jit(solution)/shard_map/convert_element_type | solution.py:83
  166.7 12.2 %all-to-all-done.2 = bf16[32,512,128]{2,0,1:T(8,128)(2,1)} async-done(((bf16[32,512,128]{2,0,1:T(8,128)(2,1)}), bf16[32,512,128]{2,0,1:T(8,128)(2,1)}, u32[]{:S(2)}, u32[]{:S(2)}) %all-to-all-start.2) | async-done | bytes 4194336 | tf_op jit(solution)/shard_map/all_to_all | solution.py:85
  178.9 5.4 %all-to-all-start.1 = ((bf16[512,32,128]{2,1,0:T(8,128)(2,1)}), bf16[512,32,128]{2,1,0:T(8,128)(2,1)}, u32[]{:S(2)}, u32[]{:S(2)}) async-start(bf16[512,32,128]{2,1,0:T(8,128)(2,1)} %copy.63), calls=%async_computation.1 | async-start | bytes 8388608 | tf_op jit(solution)/shard_map/all_to_all | solution.py:84
  184.4 4.1 copy.67
  188.5 9.0 %fusion.36 = f32[512,512]{1,0:T(8,128)} fusion(bf16[512,32,128]{2,1,0:T(8,128)(2,1)S(1)} %bitcast.97, f32[512,32,128]{0,2,1:T(8,128)} %copy.62, bf16[512,32,128]{0,2,1:T(8,128)(2,1)S(1)} %copy-done.6), kind=kOutput, calls=%fused_computation.73 | convolution fusion | flops 2153775104 | bytes 17825792 | tf_op jit(solution)/shard_map/ijc,kjc->ik/dot_general | solution.py:91
  197.5 9.0 %fusion.30 = (bf16[512,32,128]{0,2,1:T(8,128)(2,1)}, bf16[512,32,128]{0,2,1:T(8,128)(2,1)}) fusion(f32[512,32,128]{0,2,1:T(8,128)S(1)} %bitcast.96, bf16[512,32,128]{0,2,1:T(8,128)(2,1)S(1)} %copy-done.6, bf16[512,512]{1,0:T(8,128)(2,1)S(1)} %copy-done, bf16[512,32,128]{2,1,0:T(8,128)(2,1)S(1)} %bitcast.98), kind=kOutput, calls=%fused_computation.54 | convolution fusion | flops 2157969408 | bytes 25690112 | tf_op jit(solution)/shard_map/kjc,ik->ijc/dot_general | solution.py:86
  206.5 33.5 %all-to-all-done.1 = bf16[512,32,128]{2,1,0:T(8,128)(2,1)} async-done(((bf16[512,32,128]{2,1,0:T(8,128)(2,1)}), bf16[512,32,128]{2,1,0:T(8,128)(2,1)}, u32[]{:S(2)}, u32[]{:S(2)}) %all-to-all-start.1) | async-done | bytes 4194336 | tf_op jit(solution)/shard_map/all_to_all | solution.py:84
  240.0 3.6 copy.64
  244.7 8.4 %fusion.26 = (f32[128]{0:T(128)S(1)}, f32[128]{0:T(128)S(1)}, f32[128]{0:T(128)S(1)}, f32[16384,128]{1,0:T(8,128)S(1)}) fusion(bf16[16384,128]{1,0:T(8,128)(2,1)S(1)} %copy-done.3, bf16[2,128]{1,0:T(2,128)(2,1)S(1)} %copy-done.18, bf16[16384,128]{1,0:T(8,128)(2,1)S(1)} %copy-done.5, f32[128]{0:T(128)S(1)} %get-tuple-element.69, ...), kind=kLoop, calls=%fused_computation.46 | loop fusion | flops 54525568 | bytes 25169408 | tf_op jit(solution)/shard_map/reduce_sum | solution.py:103
  253.2 3.2 copy-done.7
  258.9 7.9 %copy.71 = bf16[512,32,128]{2,1,0:T(8,128)(2,1)} copy(bf16[512,32,128]{0,2,1:T(8,128)(2,1)} %get-tuple-element.15) | data formatting | bytes 8388608 | tf_op jit(solution)/shard_map/optimization_barrier | solution.py:92
  266.8 5.9 %all-to-all-start.3 = ((bf16[512,32,128]{2,1,0:T(8,128)(2,1)}), bf16[512,32,128]{2,1,0:T(8,128)(2,1)}, u32[]{:S(2)}, u32[]{:S(2)}) async-start(bf16[512,32,128]{2,1,0:T(8,128)(2,1)} %copy.71), calls=%async_computation.3 | async-start | bytes 8388608 | tf_op jit(solution)/shard_map/all_to_all | solution.py:93
  272.7 16.3 %fusion.7 = f32[16384,128]{1,0:T(8,128)} fusion(f32[16384,128]{1,0:T(8,128)} %copy-done.7, f32[2,128]{1,0:T(2,128)S(1)} %collective-permute-done.4, f32[128]{0:T(128)S(1)} %get-tuple-element.69, f32[128]{0:T(128)S(1)} %get-tuple-element.70, f32[128]{0:T(128)S(1)} %get-tuple-element.68), kind=kLoop, calls=%fused_computation.27 | loop fusion | flops 14680064 | bytes 16779776 | tf_op jit(solution)/shard_map/add | solution.py:101
  289.0 39.4 %all-to-all-done.3 = bf16[512,32,128]{2,1,0:T(8,128)(2,1)} async-done(((bf16[512,32,128]{2,1,0:T(8,128)(2,1)}), bf16[512,32,128]{2,1,0:T(8,128)(2,1)}, u32[]{:S(2)}, u32[]{:S(2)}) %all-to-all-start.3) | async-done | bytes 4194336 | tf_op jit(solution)/shard_map/all_to_all | solution.py:93
  328.4 3.6 copy.72
  334.0 3.7 broadcast_select_fusion
  345.7 11.6 %collective-permute-done.10 = f32[256,512]{1,0:T(8,128)S(1)} collective-permute-done((f32[256,512]{1,0:T(8,128)S(1)}, f32[256,512]{1,0:T(8,128)S(1)}, u32[]{:S(2)}, u32[]{:S(2)}) %collective-permute-start.10) | collective-permute-done | bytes 524320 | tf_op jit(solution)/shard_map/ppermute | solution.py:31
  358.8 5.4 %collective-permute-done.11 = f32[128,512]{1,0:T(8,128)S(1)} collective-permute-done((f32[128,512]{1,0:T(8,128)S(1)}, f32[128,512]{1,0:T(8,128)S(1)}, u32[]{:S(2)}, u32[]{:S(2)}) %collective-permute-start.11) | collective-permute-done | bytes 262176 | tf_op jit(solution)/shard_map/ppermute | solution.py:31
  365.1 3.0 collective-permute-done.12
  369.2 3.8 collective-permute-done.13
  377.3 3.4 collective-permute-start.15
  380.7 7.9 %convolution_bitcast_fusion = f32[32,512,128]{1,2,0:T(8,128)} fusion(bf16[32,512,128]{2,1,0:T(8,128)(2,1)} %bitcast.103, bf16[512,512]{1,0:T(8,128)(2,1)S(1)} %copy-done.13), kind=kOutput, calls=%fused_computation.71 | convolution fusion | flops 2147483648 | bytes 13107200 | tf_op jit(solution)/shard_map/ikc,jk->ijc/dot_general | solution.py:105
  388.6 9.0 %copy.74 = f32[32,512,128]{2,1,0:T(8,128)} copy(f32[32,512,128]{1,2,0:T(8,128)} %convolution_bitcast_fusion) | data formatting | bytes 16777216 | tf_op jit(solution)/shard_map/ikc,jk->ijc/transpose | solution.py:105
  398.3 7.7 %collective-permute-start.5 = (f32[2,128]{1,0:T(2,128)S(1)}, f32[2,128]{1,0:T(2,128)S(1)}, u32[]{:S(2)}, u32[]{:S(2)}) collective-permute-start(f32[2,128]{1,0:T(2,128)S(1)} %slice.132), channel_id=1, source_target_pairs={{8,0},{16,8},{24,16},{32,24},{40,32},{48,40},{56,48},{64,56},{72,6... | collective-permute-start | bytes 3080 | tf_op jit(solution)/shard_map/ppermute | solution.py:16
  408.4 24.7 %fusion.23 = (f32[128]{0:T(128)S(1)}, f32[128]{0:T(128)S(1)}, f32[128]{0:T(128)S(1)}, f32[16384]{0:T(1024)S(1)}, f32[128]{0:T(128)S(1)}, /*index=5*/f32[16384,128]{1,0:T(8,128)}) fusion(f32[16384,128]{1,0:T(8,128)} %bitcast.100, bf16[16384,128]{1,0:T(8,128)(2,1)} %copy-done.2, bf16[2,128]{1,0:T(2,128)(2,1)S(1)} %copy-done.18, ...), kind=kLoop, calls=%fused_computation.43 | loop fusion | flops 56606208 | bytes 37885440 | tf_op jit(solution)/shard_map/reduce_sum | solution.py:119
  433.1 7.8 %copy.76 = bf16[512,32,128]{2,1,0:T(8,128)(2,1)} copy(bf16[512,32,128]{0,2,1:T(8,128)(2,1)} %get-tuple-element.61) | data formatting | bytes 8388608
  441.2 2.8 collective-permute-start.17
  468.0 5.3 %collective-permute-done.21 = f32[256,512]{1,0:T(8,128)S(1)} collective-permute-done((f32[256,512]{1,0:T(8,128)S(1)}, f32[256,512]{1,0:T(8,128)S(1)}, u32[]{:S(2)}, u32[]{:S(2)}) %collective-permute-start.21) | collective-permute-done | bytes 524320 | tf_op jit(solution)/shard_map/ppermute | solution.py:31
  473.4 6.3 %collective-permute-start.22 = (f32[512,512]{1,0:T(8,128)S(1)}, f32[512,512]{1,0:T(8,128)S(1)}, u32[]{:S(2)}, u32[]{:S(2)}) collective-permute-start(f32[512,512]{1,0:T(8,128)S(1)} %maximum_select_fusion.1), channel_id=1, source_target_pairs={{0,8},{8,0},{16,24},{24,16},{32,40},{40,32},{48,56},{56,48},{64,72... | collective-permute-start | bytes 3145736 | tf_op jit(solution)/shard_map/ppermute | solution.py:31
  479.7 8.2 %multiply_convert_fusion = bf16[16384,128]{1,0:T(8,128)(2,1)} fusion(f32[16384,128]{1,0:T(8,128)} %get-tuple-element.60, bf16[32,512,128]{2,1,0:T(8,128)(2,1)} %param.7, f32[16384]{0:T(1024)S(1)} %add_multiply_fusion, f32[128]{0:T(128)S(1)} %copy-done.19, f32[16384]{0:T(1024)S(1)} %copy-done.15), kind=kLoop, calls=%fused_computation.57 | loop fusion | flops 14680064 | bytes 16908800 | tf_op jit(solution)/shard_map/convert_element_type | solution.py:130
  (152 shorter events, 61.6 us)
Async XLA Ops:
  0.6 149.3 %copy-start = (bf16[512,512]{1,0:T(8,128)(2,1)S(1)}, bf16[512,512]{1,0:T(8,128)(2,1)}, u32[]{:S(2)}) copy-start(bf16[512,512]{1,0:T(8,128)(2,1)} %param.11) | copy-start | bytes 1572868
  0.6 30.1 %copy-start.26 = (f32[2,3,128]{2,0,1:T(2,128)S(1)}, f32[2,3,128]{2,0,1:T(2,128)}, u32[]{:S(2)}) copy-start(f32[2,3,128]{2,0,1:T(2,128)} %param.9) | copy-start | bytes 9220
  0.7 30.8 %copy-start.9 = (bf16[32,512,128]{2,1,0:T(8,128)(2,1)S(1)}, bf16[32,512,128]{2,1,0:T(8,128)(2,1)}, u32[]{:S(2)}) copy-start(bf16[32,512,128]{2,1,0:T(8,128)(2,1)} %param.13) | copy-start | bytes 12582916
  5.3 3.8 collective-permute-start
  9.1 4.7 collective-permute-start.1
  13.8 5.6 %collective-permute-start.2 = (f32[16384]{0:T(1024)S(1)}, f32[16384]{0:T(1024)S(1)}, u32[]{:S(2)}, u32[]{:S(2)}) collective-permute-start(f32[16384]{0:T(1024)S(1)} %add.129), channel_id=1, source_target_pairs={{0,4},{1,5},{2,6},{3,7},{4,0},{5,1},{6,2},{7,3},{8,12},{9,13},{10,... | collective-permute-start | bytes 196616 | tf_op jit(solution)/shard_map/ppermute | solution.py:24
  19.4 12.1 %copy-start.14 = (f32[16384]{0:T(1024)}, f32[16384]{0:T(1024)S(1)}, u32[]{:S(2)}) copy-start(f32[16384]{0:T(1024)S(1)} %add_rsqrt_fusion) | copy-start | bytes 196612
  23.8 14.2 %copy-start.2 = (bf16[16384,128]{1,0:T(8,128)(2,1)}, bf16[16384,128]{1,0:T(8,128)(2,1)S(1)}, u32[]{:S(2)}) copy-start(bf16[16384,128]{1,0:T(8,128)(2,1)S(1)} %multiply_convert_fusion.1) | copy-start | bytes 12582916
  23.9 7.6 %collective-permute-start.3 = (bf16[2,128]{1,0:T(2,128)(2,1)S(1)}, bf16[2,128]{1,0:T(2,128)(2,1)S(1)}, u32[]{:S(2)}, u32[]{:S(2)}) collective-permute-start(bf16[2,128]{1,0:T(2,128)(2,1)S(1)} %slice.126), channel_id=1, source_target_pairs={{0,8},{8,16},{16,24},{24,32},{32,40},{40,48},{48,56},{56,64},{64,7... | collective-permute-start | bytes 1544 | tf_op jit(solution)/shard_map/ppermute | solution.py:16
  55.4 62.9 %all-to-all-start = ((bf16[32,512,128]{2,0,1:T(8,128)(2,1)}), bf16[32,512,128]{2,0,1:T(8,128)(2,1)}, u32[]{:S(2)}, u32[]{:S(2)}) async-start(bf16[32,512,128]{2,0,1:T(8,128)(2,1)} %copy.58), calls=%async_computation | async-start | bytes 8388608 | tf_op jit(solution)/shard_map/all_to_all | solution.py:78
  118.3 60.6 %all-to-all-start.2 = ((bf16[32,512,128]{2,0,1:T(8,128)(2,1)}), bf16[32,512,128]{2,0,1:T(8,128)(2,1)}, u32[]{:S(2)}, u32[]{:S(2)}) async-start(bf16[32,512,128]{2,0,1:T(8,128)(2,1)} %copy.65), calls=%async_computation.2 | async-start | bytes 8388608 | tf_op jit(solution)/shard_map/all_to_all | solution.py:85
  178.9 61.1 %all-to-all-start.1 = ((bf16[512,32,128]{2,1,0:T(8,128)(2,1)}), bf16[512,32,128]{2,1,0:T(8,128)(2,1)}, u32[]{:S(2)}, u32[]{:S(2)}) async-start(bf16[512,32,128]{2,1,0:T(8,128)(2,1)} %copy.63), calls=%async_computation.1 | async-start | bytes 8388608 | tf_op jit(solution)/shard_map/all_to_all | solution.py:84
  184.3 13.2 %slice-start = ((s8[8388608]{0:T(1024)(128)(4,1)}), s8[4194304]{0:T(1024)(128)(4,1)S(1)}, s32[]{:S(2)}) async-start(s8[8388608]{0:T(1024)(128)(4,1)} %bitcast.95), calls=%async_computation.4 | async-start | bytes 8388608
  206.5 37.1 %copy-start.18 = (bf16[2,128]{1,0:T(2,128)(2,1)S(1)}, bf16[2,128]{1,0:T(2,128)(2,1)}, u32[]{:S(2)}) copy-start(bf16[2,128]{1,0:T(2,128)(2,1)} %copy-done.17) | copy-start | bytes 1540
  256.4 16.3 %collective-permute-start.4 = (f32[2,128]{1,0:T(2,128)S(1)}, f32[2,128]{1,0:T(2,128)S(1)}, u32[]{:S(2)}, u32[]{:S(2)}) collective-permute-start(f32[2,128]{1,0:T(2,128)S(1)} %slice.129), channel_id=1, source_target_pairs={{8,0},{16,8},{24,16},{32,24},{40,32},{48,40},{56,48},{64,56},{72,6... | collective-permute-start | bytes 3080 | tf_op jit(solution)/shard_map/ppermute | solution.py:16
  266.8 61.6 %all-to-all-start.3 = ((bf16[512,32,128]{2,1,0:T(8,128)(2,1)}), bf16[512,32,128]{2,1,0:T(8,128)(2,1)}, u32[]{:S(2)}, u32[]{:S(2)}) async-start(bf16[512,32,128]{2,1,0:T(8,128)(2,1)} %copy.71), calls=%async_computation.3 | async-start | bytes 8388608 | tf_op jit(solution)/shard_map/all_to_all | solution.py:93
  289.0 45.0 %copy-start.12 = (f32[512,512]{1,0:T(8,128)S(1)}, f32[512,512]{1,0:T(8,128)}, u32[]{:S(2)}) copy-start(f32[512,512]{1,0:T(8,128)} %fusion.36) | copy-start | bytes 3145732
  337.7 3.1 collective-permute-start.9
  343.4 13.9 %collective-permute-start.10 = (f32[256,512]{1,0:T(8,128)S(1)}, f32[256,512]{1,0:T(8,128)S(1)}, u32[]{:S(2)}, u32[]{:S(2)}) collective-permute-start(f32[256,512]{1,0:T(8,128)S(1)} %slice_select_fusion), channel_id=1, source_target_pairs={{0,16},{8,24},{16,0},{24,8},{32,48},{40,56},{48,32},{56,40},{64,80... | collective-permute-start | bytes 1572872 | tf_op jit(solution)/shard_map/ppermute | solution.py:31
  357.5 6.7 %collective-permute-start.11 = (f32[128,512]{1,0:T(8,128)S(1)}, f32[128,512]{1,0:T(8,128)S(1)}, u32[]{:S(2)}, u32[]{:S(2)}) collective-permute-start(f32[128,512]{1,0:T(8,128)S(1)} %slice_select_fusion.1), channel_id=1, source_target_pairs={{0,1},{1,0},{2,3},{3,2},{4,5},{5,4},{6,7},{7,6},{8,9},{9,8},{10,11... | collective-permute-start | bytes 786440 | tf_op jit(solution)/shard_map/ppermute | solution.py:31
  364.3 3.9 collective-permute-start.12
  368.2 4.7 collective-permute-start.13
  372.9 4.3 collective-permute-start.14
  377.3 28.7 %collective-permute-start.15 = (f32[8,512]{1,0:T(8,128)S(1)}, f32[8,512]{1,0:T(8,128)S(1)}, u32[]{:S(2)}, u32[]{:S(2)}) collective-permute-start(f32[8,512]{1,0:T(8,128)S(1)} %slice_select_fusion.5), channel_id=1, source_target_pairs={{0,4},{1,5},{2,6},{3,7},{4,0},{5,1},{6,2},{7,3},{8,12},{9,13},{10,... | collective-permute-start | bytes 49160 | tf_op jit(solution)/shard_map/ppermute | solution.py:31
  388.6 19.7 %copy-start.15 = (f32[16384]{0:T(1024)S(1)}, f32[16384]{0:T(1024)}, u32[]{:S(2)}) copy-start(f32[16384]{0:T(1024)} %copy-done.14) | copy-start | bytes 196612
  388.6 19.7 %copy-start.19 = (f32[128]{0:T(128)S(1)}, f32[128]{0:T(128)}, u32[]{:S(2)}) copy-start(f32[128]{0:T(128)} %param.8) | copy-start | bytes 1540
  388.6 19.7 %copy-start.21 = (f32[128]{0:T(128)S(1)}, f32[128]{0:T(128)}, u32[]{:S(2)}) copy-start(f32[128]{0:T(128)} %copy-done.20) | copy-start | bytes 1540
  388.6 19.7 %copy-start.23 = (f32[128]{0:T(128)S(1)}, f32[128]{0:T(128)}, u32[]{:S(2)}) copy-start(f32[128]{0:T(128)} %copy-done.22) | copy-start | bytes 1540
  388.6 19.8 %copy-start.25 = (f32[128]{0:T(128)S(1)}, f32[128]{0:T(128)}, u32[]{:S(2)}) copy-start(f32[128]{0:T(128)} %copy-done.24) | copy-start | bytes 1540
  398.3 10.1 %collective-permute-start.5 = (f32[2,128]{1,0:T(2,128)S(1)}, f32[2,128]{1,0:T(2,128)S(1)}, u32[]{:S(2)}, u32[]{:S(2)}) collective-permute-start(f32[2,128]{1,0:T(2,128)S(1)} %slice.132), channel_id=1, source_target_pairs={{8,0},{16,8},{24,16},{32,24},{40,32},{48,40},{56,48},{64,56},{72,6... | collective-permute-start | bytes 3080 | tf_op jit(solution)/shard_map/ppermute | solution.py:16
  406.1 35.1 %collective-permute-start.16 = (f32[8,512]{1,0:T(8,128)S(1)}, f32[8,512]{1,0:T(8,128)S(1)}, u32[]{:S(2)}, u32[]{:S(2)}) collective-permute-start(f32[8,512]{1,0:T(8,128)S(1)} %select_add_fusion.6), channel_id=1, source_target_pairs={{0,4},{1,5},{2,6},{3,7},{4,0},{5,1},{6,2},{7,3},{8,12},{9,13},{10,... | collective-permute-start | bytes 49160 | tf_op jit(solution)/shard_map/ppermute | solution.py:31
  433.1 7.8 %collective-permute-start.23 = (f32[128]{0:T(128)S(1)}, f32[128]{0:T(128)S(1)}, u32[]{:S(2)}, u32[]{:S(2)}) collective-permute-start(f32[128]{0:T(128)S(1)} %get-tuple-element.59), channel_id=1, source_target_pairs={{0,8},{8,0},{16,24},{24,16},{32,40},{40,32},{48,56},{56,48},{64,72... | collective-permute-start | bytes 1544 | tf_op jit(solution)/shard_map/ppermute | solution.py:24
  440.9 3.1 collective-permute-start.24
  441.2 5.4 %collective-permute-start.17 = (f32[16,512]{1,0:T(8,128)S(1)}, f32[16,512]{1,0:T(8,128)S(1)}, u32[]{:S(2)}, u32[]{:S(2)}) collective-permute-start(f32[16,512]{1,0:T(8,128)S(1)} %maximum_select_fusion.6), channel_id=1, source_target_pairs={{0,2},{1,3},{2,0},{3,1},{4,6},{5,7},{6,4},{7,5},{8,10},{9,11},{10,... | collective-permute-start | bytes 98312 | tf_op jit(solution)/shard_map/ppermute | solution.py:31
  444.0 7.5 %collective-permute-start.25 = (f32[128]{0:T(128)S(1)}, f32[128]{0:T(128)S(1)}, u32[]{:S(2)}, u32[]{:S(2)}) collective-permute-start(f32[128]{0:T(128)S(1)} %add.161), channel_id=1, source_target_pairs={{0,32},{8,40},{16,48},{24,56},{32,0},{40,8},{48,16},{56,24},{64,96... | collective-permute-start | bytes 1544 | tf_op jit(solution)/shard_map/ppermute | solution.py:24
  446.6 4.9 %collective-permute-start.18 = (f32[32,512]{1,0:T(8,128)S(1)}, f32[32,512]{1,0:T(8,128)S(1)}, u32[]{:S(2)}, u32[]{:S(2)}) collective-permute-start(f32[32,512]{1,0:T(8,128)S(1)} %maximum_select_fusion.5), channel_id=1, source_target_pairs={{0,32},{8,40},{16,48},{24,56},{32,0},{40,8},{48,16},{56,24},{64,96... | collective-permute-start | bytes 196616 | tf_op jit(solution)/shard_map/ppermute | solution.py:31
  448.1 5.0 %collective-permute-start.27 = (f32[2,3,128]{2,1,0:T(4,128)S(1)}, f32[2,3,128]{2,1,0:T(4,128)S(1)}, u32[]{:S(2)}, u32[]{:S(2)}) collective-permute-start(f32[2,3,128]{2,1,0:T(4,128)S(1)} %pad_maximum_fusion.3), channel_id=1, source_target_pairs={{0,8},{8,0},{16,24},{24,16},{32,40},{40,32},{48,56},{56,48},{64,72... | collective-permute-start | bytes 9224 | tf_op jit(solution)/shard_map/ppermute | solution.py:24
  450.3 7.7 %collective-permute-start.6 = (f32[16384]{0:T(1024)S(1)}, f32[16384]{0:T(1024)S(1)}, u32[]{:S(2)}, u32[]{:S(2)}) collective-permute-start(f32[16384]{0:T(1024)S(1)} %get-tuple-element.58), channel_id=1, source_target_pairs={{0,1},{1,0},{2,3},{3,2},{4,5},{5,4},{6,7},{7,6},{8,9},{9,8},{10,11... | collective-permute-start | bytes 196616 | tf_op jit(solution)/shard_map/ppermute | solution.py:24
  451.5 9.1 %collective-permute-start.26 = (f32[128]{0:T(128)S(1)}, f32[128]{0:T(128)S(1)}, u32[]{:S(2)}, u32[]{:S(2)}) collective-permute-start(f32[128]{0:T(128)S(1)} %add.162), channel_id=1, source_target_pairs={{0,64},{8,72},{16,80},{24,88},{32,96},{40,104},{48,112},{56,120},{... | collective-permute-start | bytes 1544 | tf_op jit(solution)/shard_map/ppermute | solution.py:24
  451.5 3.9 collective-permute-start.19
  453.1 2.7 collective-permute-start.28
  455.4 9.4 %collective-permute-start.20 = (f32[128,512]{1,0:T(8,128)S(1)}, f32[128,512]{1,0:T(8,128)S(1)}, u32[]{:S(2)}, u32[]{:S(2)}) collective-permute-start(f32[128,512]{1,0:T(8,128)S(1)} %maximum_select_fusion.3), channel_id=1, source_target_pairs={{0,1},{1,0},{2,3},{3,2},{4,5},{5,4},{6,7},{7,6},{8,9},{9,8},{10,11... | collective-permute-start | bytes 786440 | tf_op jit(solution)/shard_map/ppermute | solution.py:31
  455.8 5.3 %collective-permute-start.29 = (f32[2,3,128]{2,1,0:T(4,128)S(1)}, f32[2,3,128]{2,1,0:T(4,128)S(1)}, u32[]{:S(2)}, u32[]{:S(2)}) collective-permute-start(f32[2,3,128]{2,1,0:T(4,128)S(1)} %fusion.53), channel_id=1, source_target_pairs={{0,32},{8,40},{16,48},{24,56},{32,0},{40,8},{48,16},{56,24},{64,96... | collective-permute-start | bytes 9224 | tf_op jit(solution)/shard_map/ppermute | solution.py:24
  458.0 5.0 %collective-permute-start.7 = (f32[16384]{0:T(1024)S(1)}, f32[16384]{0:T(1024)S(1)}, u32[]{:S(2)}, u32[]{:S(2)}) collective-permute-start(f32[16384]{0:T(1024)S(1)} %add.143), channel_id=1, source_target_pairs={{0,2},{1,3},{2,0},{3,1},{4,6},{5,7},{6,4},{7,5},{8,10},{9,11},{10,... | collective-permute-start | bytes 196616 | tf_op jit(solution)/shard_map/ppermute | solution.py:24
  461.1 3.9 collective-permute-start.30
  463.0 5.0 %collective-permute-start.8 = (f32[16384]{0:T(1024)S(1)}, f32[16384]{0:T(1024)S(1)}, u32[]{:S(2)}, u32[]{:S(2)}) collective-permute-start(f32[16384]{0:T(1024)S(1)} %add.144), channel_id=1, source_target_pairs={{0,4},{1,5},{2,6},{3,7},{4,0},{5,1},{6,2},{7,3},{8,12},{9,13},{10,... | collective-permute-start | bytes 196616 | tf_op jit(solution)/shard_map/ppermute | solution.py:24
  464.9 8.4 %collective-permute-start.21 = (f32[256,512]{1,0:T(8,128)S(1)}, f32[256,512]{1,0:T(8,128)S(1)}, u32[]{:S(2)}, u32[]{:S(2)}) collective-permute-start(f32[256,512]{1,0:T(8,128)S(1)} %maximum_select_fusion.2), channel_id=1, source_target_pairs={{0,16},{8,24},{16,0},{24,8},{32,48},{40,56},{48,32},{56,40},{64,80... | collective-permute-start | bytes 1572872 | tf_op jit(solution)/shard_map/ppermute | solution.py:31
  473.4 14.5 %collective-permute-start.22 = (f32[512,512]{1,0:T(8,128)S(1)}, f32[512,512]{1,0:T(8,128)S(1)}, u32[]{:S(2)}, u32[]{:S(2)}) collective-permute-start(f32[512,512]{1,0:T(8,128)S(1)} %maximum_select_fusion.1), channel_id=1, source_target_pairs={{0,8},{8,0},{16,24},{24,16},{32,40},{40,32},{48,56},{56,48},{64,72... | collective-permute-start | bytes 3145736 | tf_op jit(solution)/shard_map/ppermute | solution.py:31
  (16 other events, 81.7 us)

commit v7 on v6

--- a/solution.py
+++ b/solution.py
@@ -34,17 +34,15 @@
 def tree_allreduce(value, rounds):
     kept = []
     for axis, step in rounds:
-        upper = (lax.axis_index(axis) // step) % 2 == 1
         half = value.shape[0] // 2
-        low, high = value[:half], value[half:]
-        keep = jnp.where(upper, high, low)
-        value = keep + exchange(jnp.where(upper, low, high), axis, step)
-        kept.append((axis, step, upper))
-    for axis, step, upper in reversed(kept):
+        offset = ((lax.axis_index(axis) // step) % 2) * half
+        keep = lax.dynamic_slice_in_dim(value, offset, half, 0)
+        send = lax.dynamic_slice_in_dim(value, half - offset, half, 0)
+        value = keep + exchange(send, axis, step)
+        kept.append((axis, step, offset))
+    for axis, step, offset in reversed(kept):
         other = exchange(value, axis, step)
-        value = jnp.where(
-            upper, jnp.concatenate([other, value]), jnp.concatenate([value, other])
-        )
+        value = lax.dynamic_update_slice_in_dim(jnp.concatenate([other, other]), value, offset, 0)
     return value
 
 

time: 499 us -> 498 us (level)
    unnamed x62 -> x64, local copies, waits for them, and re-layouts: 25.3 us -> 23.3 us
where the time goes in v7:
time: 498 us; the launch traced here: 489 us
  waiting for transfers between devices  181 us (36%)
  local copies, waits for them, and re-layouts  93.4 us (19%)
  starting transfers between devices  87.9 us (18%)
  other arithmetic  83.7 us (17%)
  matrix products  41.5 us (8%)
    all_to_all x1, waiting for transfers between devices, on_device(): lax.all_to_all(section_one, 'ctx', split_axis=1, concat_axis=0, tiled=True)  48.8 us
    all_to_all x1, waiting for transfers between devices, on_device(): lax.all_to_all(grad_section, 'ctx', split_axis=0, concat_axis=1, tiled=True)  39.4 us
    ppermute x14, waiting for transfers between devices, exchange(): lax.ppermute(value, axis, [(source, source ^ step) for source in range(co...  36.1 us
    all_to_all x1, waiting for transfers between devices, on_device(): lax.all_to_all(section_two, 'ctx', split_axis=0, concat_axis=1, tiled=True)  33.5 us
    ppermute x14, starting transfers between devices, exchange(): lax.ppermute(value, axis, [(source, source ^ step) for source in range(co...  25.2 us
    reduce_sum x1, other arithmetic, on_device(): value_taps.append(jnp.sum(grad_mixed * window, axis=0))  24.7 us
    unnamed x64, local copies, waits for them, and re-layouts  23.3 us
    ppermute x14, starting transfers between devices, tree_psum(): lax.ppermute(value, axis, pairs)  22.5 us
  transfers between devices with their start and end apart: 35, of which 19 were waited for; matrix products, arithmetic and copies ran while one was open for 32% of the time, Pallas kernels for 0%

profile of v7, /device:TPU:1, one launch (start us, length us, event | category | flops | bytes accessed | tf_op | source)
XLA Modules:
  0.0 489.3 jit_solution(1944452503183187796)
XLA Ops:
  0.7 4.6 multiply_reduce_fusion.2
  9.1 3.1 collective-permute-start.1
  13.8 3.9 collective-permute-start.2
  19.4 4.4 multiply_convert_fusion.1
  23.9 6.9 %collective-permute-start.3 = (bf16[2,128]{1,0:T(2,128)(2,1)S(1)}, bf16[2,128]{1,0:T(2,128)(2,1)S(1)}, u32[]{:S(2)}, u32[]{:S(2)}) collective-permute-start(bf16[2,128]{1,0:T(2,128)(2,1)S(1)} %slice.78), channel_id=1, source_target_pairs={{0,8},{8,16},{16,24},{24,32},{32,40},{40,48},{48,56},{56,64},{64,7... | collective-permute-start | bytes 1544 | tf_op jit(solution)/shard_map/ppermute | solution.py:16
  31.5 6.5 %fusion.10 = (bf16[16384,128]{1,0:T(8,128)(2,1)}, bf16[16384,128]{1,0:T(8,128)(2,1)S(1)}) fusion(bf16[32,512,128]{2,1,0:T(8,128)(2,1)S(1)} %copy-done.10, bf16[16384,128]{1,0:T(8,128)(2,1)S(1)} %multiply_convert_fusion.1, bf16[2,128]{1,0:T(2,128)(2,1)S(1)} %collective-permute-done.3, f32[128]{0:T(128)S(1)} %get-tuple-element.69, ...), kind=kLoop, calls=%fused_computation.30 | loop fusion | flops 44040192 | bytes 16779264 | tf_op jit(solution)/shard_map/convert_element_type | solution.py:75
  38.1 3.0 fusion.15
  43.1 4.4 convert_bitcast_fusion.2
  47.5 7.9 %copy.58 = bf16[32,512,128]{2,0,1:T(8,128)(2,1)} copy(bf16[32,512,128]{1,2,0:T(8,128)(2,1)} %convert_bitcast_fusion.2) | data formatting | bytes 8388608 | tf_op jit(solution)/shard_map/convert_element_type | solution.py:74
  55.4 7.2 %all-to-all-start = ((bf16[32,512,128]{2,0,1:T(8,128)(2,1)}), bf16[32,512,128]{2,0,1:T(8,128)(2,1)}, u32[]{:S(2)}, u32[]{:S(2)}) async-start(bf16[32,512,128]{2,0,1:T(8,128)(2,1)} %copy.58), calls=%async_computation | async-start | bytes 8388608 | tf_op jit(solution)/shard_map/all_to_all | solution.py:76
  62.6 6.9 %copy.65 = bf16[32,512,128]{2,0,1:T(8,128)(2,1)} copy(bf16[32,512,128]{2,1,0:T(8,128)(2,1)} %bitcast.104) | data formatting | bytes 8388608 | tf_op jit(solution)/shard_map/reshape | solution.py:75
  69.5 48.8 %all-to-all-done = bf16[32,512,128]{2,0,1:T(8,128)(2,1)} async-done(((bf16[32,512,128]{2,0,1:T(8,128)(2,1)}), bf16[32,512,128]{2,0,1:T(8,128)(2,1)}, u32[]{:S(2)}, u32[]{:S(2)}) %all-to-all-start) | async-done | bytes 4194336 | tf_op jit(solution)/shard_map/all_to_all | solution.py:76
  118.3 4.9 all-to-all-start.2
  123.2 7.5 %copy.61 = bf16[512,32,128]{0,2,1:T(8,128)(2,1)} copy(bf16[512,32,128]{2,1,0:T(8,128)(2,1)} %param.12) | data formatting | bytes 8388608 | tf_op args[5]
  130.7 3.8 copy.59
  135.7 4.3 copy.60
  139.9 10.0 %copy.62 = f32[512,32,128]{0,2,1:T(8,128)} copy(f32[512,32,128]{2,1,0:T(8,128)} %bitcast.101) | data formatting | bytes 16777216 | tf_op jit(solution)/shard_map/convert_element_type | solution.py:78
  150.0 8.8 %convert_bitcast_fusion.1 = bf16[512,32,128]{0,2,1:T(8,128)(2,1)} fusion(bf16[512,512]{1,0:T(8,128)(2,1)S(1)} %copy-done, f32[512,32,128]{0,2,1:T(8,128)} %copy.62, bf16[512,32,128]{0,2,1:T(8,128)(2,1)} %copy.61), kind=kOutput, calls=%fused_computation.65 | convolution fusion | flops 2155872256 | bytes 17301504 | tf_op jit(solution)/shard_map/ijc,ik->kjc/dot_general | solution.py:79
  158.8 7.9 %copy.63 = bf16[512,32,128]{2,1,0:T(8,128)(2,1)} copy(bf16[512,32,128]{0,2,1:T(8,128)(2,1)} %convert_bitcast_fusion.1) | data formatting | bytes 8388608 | tf_op jit(solution)/shard_map/convert_element_type | solution.py:81
  166.7 12.1 %all-to-all-done.2 = bf16[32,512,128]{2,0,1:T(8,128)(2,1)} async-done(((bf16[32,512,128]{2,0,1:T(8,128)(2,1)}), bf16[32,512,128]{2,0,1:T(8,128)(2,1)}, u32[]{:S(2)}, u32[]{:S(2)}) %all-to-all-start.2) | async-done | bytes 4194336 | tf_op jit(solution)/shard_map/all_to_all | solution.py:83
  178.9 5.4 %all-to-all-start.1 = ((bf16[512,32,128]{2,1,0:T(8,128)(2,1)}), bf16[512,32,128]{2,1,0:T(8,128)(2,1)}, u32[]{:S(2)}, u32[]{:S(2)}) async-start(bf16[512,32,128]{2,1,0:T(8,128)(2,1)} %copy.63), calls=%async_computation.1 | async-start | bytes 8388608 | tf_op jit(solution)/shard_map/all_to_all | solution.py:82
  184.4 4.1 copy.67
  188.5 9.0 %fusion.36 = f32[512,512]{1,0:T(8,128)} fusion(bf16[512,32,128]{2,1,0:T(8,128)(2,1)S(1)} %bitcast.97, f32[512,32,128]{0,2,1:T(8,128)} %copy.62, bf16[512,32,128]{0,2,1:T(8,128)(2,1)S(1)} %copy-done.7), kind=kOutput, calls=%fused_computation.77 | convolution fusion | flops 2153775104 | bytes 17825792 | tf_op jit(solution)/shard_map/ijc,kjc->ik/dot_general | solution.py:89
  197.5 9.0 %fusion.30 = (bf16[512,32,128]{0,2,1:T(8,128)(2,1)}, bf16[512,32,128]{0,2,1:T(8,128)(2,1)}) fusion(f32[512,32,128]{0,2,1:T(8,128)S(1)} %bitcast.96, bf16[512,32,128]{0,2,1:T(8,128)(2,1)S(1)} %copy-done.7, bf16[512,512]{1,0:T(8,128)(2,1)S(1)} %copy-done, bf16[512,32,128]{2,1,0:T(8,128)(2,1)S(1)} %bitcast.98), kind=kOutput, calls=%fused_computation.54 | convolution fusion | flops 2157969408 | bytes 25690112 | tf_op jit(solution)/shard_map/kjc,ik->ijc/dot_general | solution.py:84
  206.5 33.5 %all-to-all-done.1 = bf16[512,32,128]{2,1,0:T(8,128)(2,1)} async-done(((bf16[512,32,128]{2,1,0:T(8,128)(2,1)}), bf16[512,32,128]{2,1,0:T(8,128)(2,1)}, u32[]{:S(2)}, u32[]{:S(2)}) %all-to-all-start.1) | async-done | bytes 4194336 | tf_op jit(solution)/shard_map/all_to_all | solution.py:82
  240.0 3.6 copy.64
  244.7 8.4 %fusion.26 = (f32[128]{0:T(128)S(1)}, f32[128]{0:T(128)S(1)}, f32[128]{0:T(128)S(1)}, f32[16384,128]{1,0:T(8,128)S(1)}) fusion(bf16[16384,128]{1,0:T(8,128)(2,1)S(1)} %copy-done.3, bf16[2,128]{1,0:T(2,128)(2,1)S(1)} %copy-done.19, bf16[16384,128]{1,0:T(8,128)(2,1)S(1)} %copy-done.6, f32[128]{0:T(128)S(1)} %get-tuple-element.69, ...), kind=kLoop, calls=%fused_computation.46 | loop fusion | flops 54525568 | bytes 25169408 | tf_op jit(solution)/shard_map/reduce_sum | solution.py:101
  253.2 3.2 copy-done.8
  258.9 7.9 %copy.71 = bf16[512,32,128]{2,1,0:T(8,128)(2,1)} copy(bf16[512,32,128]{0,2,1:T(8,128)(2,1)} %get-tuple-element.15) | data formatting | bytes 8388608 | tf_op jit(solution)/shard_map/optimization_barrier | solution.py:90
  266.8 5.9 %all-to-all-start.3 = ((bf16[512,32,128]{2,1,0:T(8,128)(2,1)}), bf16[512,32,128]{2,1,0:T(8,128)(2,1)}, u32[]{:S(2)}, u32[]{:S(2)}) async-start(bf16[512,32,128]{2,1,0:T(8,128)(2,1)} %copy.71), calls=%async_computation.3 | async-start | bytes 8388608 | tf_op jit(solution)/shard_map/all_to_all | solution.py:91
  272.7 16.3 %fusion.7 = f32[16384,128]{1,0:T(8,128)} fusion(f32[16384,128]{1,0:T(8,128)} %copy-done.8, f32[2,128]{1,0:T(2,128)S(1)} %collective-permute-done.4, f32[128]{0:T(128)S(1)} %get-tuple-element.69, f32[128]{0:T(128)S(1)} %get-tuple-element.70, f32[128]{0:T(128)S(1)} %get-tuple-element.68), kind=kLoop, calls=%fused_computation.27 | loop fusion | flops 14680064 | bytes 16779776 | tf_op jit(solution)/shard_map/add | solution.py:99
  289.0 39.4 %all-to-all-done.3 = bf16[512,32,128]{2,1,0:T(8,128)(2,1)} async-done(((bf16[512,32,128]{2,1,0:T(8,128)(2,1)}), bf16[512,32,128]{2,1,0:T(8,128)(2,1)}, u32[]{:S(2)}, u32[]{:S(2)}) %all-to-all-start.3) | async-done | bytes 4194336 | tf_op jit(solution)/shard_map/all_to_all | solution.py:91
  328.4 3.6 copy.72
  344.0 11.9 %collective-permute-done.10 = f32[256,512]{1,0:T(8,128)S(1)} collective-permute-done((f32[256,512]{1,0:T(8,128)S(1)}, f32[256,512]{1,0:T(8,128)S(1)}, u32[]{:S(2)}, u32[]{:S(2)}) %collective-permute-start.10) | collective-permute-done | bytes 524320 | tf_op jit(solution)/shard_map/ppermute | solution.py:31
  358.3 5.7 %collective-permute-done.11 = f32[128,512]{1,0:T(8,128)S(1)} collective-permute-done((f32[128,512]{1,0:T(8,128)S(1)}, f32[128,512]{1,0:T(8,128)S(1)}, u32[]{:S(2)}, u32[]{:S(2)}) %collective-permute-start.11) | collective-permute-done | bytes 262176 | tf_op jit(solution)/shard_map/ppermute | solution.py:31
  365.0 3.0 collective-permute-done.12
  369.0 3.8 collective-permute-done.13
  372.8 2.8 collective-permute-start.14
  377.1 3.4 collective-permute-start.15
  380.5 7.9 %convolution_bitcast_fusion = f32[32,512,128]{1,2,0:T(8,128)} fusion(bf16[32,512,128]{2,1,0:T(8,128)(2,1)} %bitcast.103, bf16[512,512]{1,0:T(8,128)(2,1)S(1)} %copy-done.15), kind=kOutput, calls=%fused_computation.71 | convolution fusion | flops 2147483648 | bytes 13107200 | tf_op jit(solution)/shard_map/ikc,jk->ijc/dot_general | solution.py:103
  388.5 9.0 %copy.74 = f32[32,512,128]{2,1,0:T(8,128)} copy(f32[32,512,128]{1,2,0:T(8,128)} %convolution_bitcast_fusion) | data formatting | bytes 16777216 | tf_op jit(solution)/shard_map/ikc,jk->ijc/transpose | solution.py:103
  398.1 7.4 %collective-permute-start.5 = (f32[2,128]{1,0:T(2,128)S(1)}, f32[2,128]{1,0:T(2,128)S(1)}, u32[]{:S(2)}, u32[]{:S(2)}) collective-permute-start(f32[2,128]{1,0:T(2,128)S(1)} %slice.84), channel_id=1, source_target_pairs={{8,0},{16,8},{24,16},{32,24},{40,32},{48,40},{56,48},{64,56},{72,6... | collective-permute-start | bytes 3080 | tf_op jit(solution)/shard_map/ppermute | solution.py:16
  407.9 24.7 %fusion.23 = (f32[128]{0:T(128)S(1)}, f32[128]{0:T(128)S(1)}, f32[128]{0:T(128)S(1)}, f32[16384]{0:T(1024)S(1)}, f32[128]{0:T(128)S(1)}, /*index=5*/f32[16384,128]{1,0:T(8,128)}) fusion(f32[16384,128]{1,0:T(8,128)} %bitcast.100, bf16[16384,128]{1,0:T(8,128)(2,1)} %copy-done.2, bf16[2,128]{1,0:T(2,128)(2,1)S(1)} %copy-done.19, ...), kind=kLoop, calls=%fused_computation.43 | loop fusion | flops 56606208 | bytes 37885440 | tf_op jit(solution)/shard_map/reduce_sum | solution.py:117
  432.6 7.8 %copy.76 = bf16[512,32,128]{2,1,0:T(8,128)(2,1)} copy(bf16[512,32,128]{0,2,1:T(8,128)(2,1)} %get-tuple-element.61) | data formatting | bytes 8388608
  440.7 2.8 collective-permute-start.17
  467.6 5.3 %collective-permute-done.21 = f32[256,512]{1,0:T(8,128)S(1)} collective-permute-done((f32[256,512]{1,0:T(8,128)S(1)}, f32[256,512]{1,0:T(8,128)S(1)}, u32[]{:S(2)}, u32[]{:S(2)}) %collective-permute-start.21) | collective-permute-done | bytes 524320 | tf_op jit(solution)/shard_map/ppermute | solution.py:31
  473.1 6.3 %collective-permute-start.22 = (f32[512,512]{1,0:T(8,128)S(1)}, f32[512,512]{1,0:T(8,128)S(1)}, u32[]{:S(2)}, u32[]{:S(2)}) collective-permute-start(f32[512,512]{1,0:T(8,128)S(1)} %constant_dynamic-update-slice_fusion.1), channel_id=1, source_target_pairs={{0,8},{8,0},{16,24},{24,16},{32,40},{40,32},{48,56},{56,48},{64,72... | collective-permute-start | bytes 3145736 | tf_op jit(solution)/shard_map/ppermute | solution.py:31
  479.4 7.6 %multiply_convert_fusion = bf16[16384,128]{1,0:T(8,128)(2,1)} fusion(f32[16384,128]{1,0:T(8,128)} %get-tuple-element.60, bf16[32,512,128]{2,1,0:T(8,128)(2,1)S(1)} %copy-done.4, f32[16384]{0:T(1024)S(1)} %add_multiply_fusion, f32[128]{0:T(128)S(1)} %copy-done.20, f32[16384]{0:T(1024)S(1)} %copy-done.17), kind=kLoop, calls=%fused_computation.57 | loop fusion | flops 14680064 | bytes 16908800 | tf_op jit(solution)/shard_map/convert_element_type | solution.py:128
  (162 shorter events, 61.7 us)
Async XLA Ops:
  0.6 149.3 %copy-start = (bf16[512,512]{1,0:T(8,128)(2,1)S(1)}, bf16[512,512]{1,0:T(8,128)(2,1)}, u32[]{:S(2)}) copy-start(bf16[512,512]{1,0:T(8,128)(2,1)} %param.11) | copy-start | bytes 1572868
  0.6 30.2 %copy-start.27 = (f32[2,3,128]{2,0,1:T(2,128)S(1)}, f32[2,3,128]{2,0,1:T(2,128)}, u32[]{:S(2)}) copy-start(f32[2,3,128]{2,0,1:T(2,128)} %param.9) | copy-start | bytes 9220
  0.7 30.8 %copy-start.10 = (bf16[32,512,128]{2,1,0:T(8,128)(2,1)S(1)}, bf16[32,512,128]{2,1,0:T(8,128)(2,1)}, u32[]{:S(2)}) copy-start(bf16[32,512,128]{2,1,0:T(8,128)(2,1)} %param.13) | copy-start | bytes 12582916
  5.3 3.8 collective-permute-start
  9.1 4.7 collective-permute-start.1
  13.8 5.6 %collective-permute-start.2 = (f32[16384]{0:T(1024)S(1)}, f32[16384]{0:T(1024)S(1)}, u32[]{:S(2)}, u32[]{:S(2)}) collective-permute-start(f32[16384]{0:T(1024)S(1)} %add.185), channel_id=1, source_target_pairs={{0,4},{1,5},{2,6},{3,7},{4,0},{5,1},{6,2},{7,3},{8,12},{9,13},{10,... | collective-permute-start | bytes 196616 | tf_op jit(solution)/shard_map/ppermute | solution.py:24
  19.4 12.1 %copy-start.16 = (f32[16384]{0:T(1024)}, f32[16384]{0:T(1024)S(1)}, u32[]{:S(2)}) copy-start(f32[16384]{0:T(1024)S(1)} %add_rsqrt_fusion) | copy-start | bytes 196612
  23.8 14.2 %copy-start.2 = (bf16[16384,128]{1,0:T(8,128)(2,1)}, bf16[16384,128]{1,0:T(8,128)(2,1)S(1)}, u32[]{:S(2)}) copy-start(bf16[16384,128]{1,0:T(8,128)(2,1)S(1)} %multiply_convert_fusion.1) | copy-start | bytes 12582916
  23.9 7.6 %collective-permute-start.3 = (bf16[2,128]{1,0:T(2,128)(2,1)S(1)}, bf16[2,128]{1,0:T(2,128)(2,1)S(1)}, u32[]{:S(2)}, u32[]{:S(2)}) collective-permute-start(bf16[2,128]{1,0:T(2,128)(2,1)S(1)} %slice.78), channel_id=1, source_target_pairs={{0,8},{8,16},{16,24},{24,32},{32,40},{40,48},{48,56},{56,64},{64,7... | collective-permute-start | bytes 1544 | tf_op jit(solution)/shard_map/ppermute | solution.py:16
  55.4 62.9 %all-to-all-start = ((bf16[32,512,128]{2,0,1:T(8,128)(2,1)}), bf16[32,512,128]{2,0,1:T(8,128)(2,1)}, u32[]{:S(2)}, u32[]{:S(2)}) async-start(bf16[32,512,128]{2,0,1:T(8,128)(2,1)} %copy.58), calls=%async_computation | async-start | bytes 8388608 | tf_op jit(solution)/shard_map/all_to_all | solution.py:76
  118.3 60.6 %all-to-all-start.2 = ((bf16[32,512,128]{2,0,1:T(8,128)(2,1)}), bf16[32,512,128]{2,0,1:T(8,128)(2,1)}, u32[]{:S(2)}, u32[]{:S(2)}) async-start(bf16[32,512,128]{2,0,1:T(8,128)(2,1)} %copy.65), calls=%async_computation.2 | async-start | bytes 8388608 | tf_op jit(solution)/shard_map/all_to_all | solution.py:83
  178.9 61.1 %all-to-all-start.1 = ((bf16[512,32,128]{2,1,0:T(8,128)(2,1)}), bf16[512,32,128]{2,1,0:T(8,128)(2,1)}, u32[]{:S(2)}, u32[]{:S(2)}) async-start(bf16[512,32,128]{2,1,0:T(8,128)(2,1)} %copy.63), calls=%async_computation.1 | async-start | bytes 8388608 | tf_op jit(solution)/shard_map/all_to_all | solution.py:82
  184.3 13.2 %slice-start = ((s8[8388608]{0:T(1024)(128)(4,1)}), s8[4194304]{0:T(1024)(128)(4,1)S(1)}, s32[]{:S(2)}) async-start(s8[8388608]{0:T(1024)(128)(4,1)} %bitcast.95), calls=%async_computation.4 | async-start | bytes 8388608
  206.5 37.1 %copy-start.19 = (bf16[2,128]{1,0:T(2,128)(2,1)S(1)}, bf16[2,128]{1,0:T(2,128)(2,1)}, u32[]{:S(2)}) copy-start(bf16[2,128]{1,0:T(2,128)(2,1)} %copy-done.18) | copy-start | bytes 1540
  256.4 16.3 %collective-permute-start.4 = (f32[2,128]{1,0:T(2,128)S(1)}, f32[2,128]{1,0:T(2,128)S(1)}, u32[]{:S(2)}, u32[]{:S(2)}) collective-permute-start(f32[2,128]{1,0:T(2,128)S(1)} %slice.81), channel_id=1, source_target_pairs={{8,0},{16,8},{24,16},{32,24},{40,32},{48,40},{56,48},{64,56},{72,6... | collective-permute-start | bytes 3080 | tf_op jit(solution)/shard_map/ppermute | solution.py:16
  266.8 61.6 %all-to-all-start.3 = ((bf16[512,32,128]{2,1,0:T(8,128)(2,1)}), bf16[512,32,128]{2,1,0:T(8,128)(2,1)}, u32[]{:S(2)}, u32[]{:S(2)}) async-start(bf16[512,32,128]{2,1,0:T(8,128)(2,1)} %copy.71), calls=%async_computation.3 | async-start | bytes 8388608 | tf_op jit(solution)/shard_map/all_to_all | solution.py:91
  335.8 3.2 collective-permute-start.9
  341.7 14.2 %collective-permute-start.10 = (f32[256,512]{1,0:T(8,128)S(1)}, f32[256,512]{1,0:T(8,128)S(1)}, u32[]{:S(2)}, u32[]{:S(2)}) collective-permute-start(f32[256,512]{1,0:T(8,128)S(1)} %constant_dynamic-slice_fusion.5), channel_id=1, source_target_pairs={{0,16},{8,24},{16,0},{24,8},{32,48},{40,56},{48,32},{56,40},{64,80... | collective-permute-start | bytes 1572872 | tf_op jit(solution)/shard_map/ppermute | solution.py:31
  357.0 7.0 %collective-permute-start.11 = (f32[128,512]{1,0:T(8,128)S(1)}, f32[128,512]{1,0:T(8,128)S(1)}, u32[]{:S(2)}, u32[]{:S(2)}) collective-permute-start(f32[128,512]{1,0:T(8,128)S(1)} %constant_dynamic-slice_fusion.4), channel_id=1, source_target_pairs={{0,1},{1,0},{2,3},{3,2},{4,5},{5,4},{6,7},{7,6},{8,9},{9,8},{10,11... | collective-permute-start | bytes 786440 | tf_op jit(solution)/shard_map/ppermute | solution.py:31
  364.1 3.9 collective-permute-start.12
  368.0 4.7 collective-permute-start.13
  372.8 4.3 collective-permute-start.14
  377.1 28.4 %collective-permute-start.15 = (f32[8,512]{1,0:T(8,128)S(1)}, f32[8,512]{1,0:T(8,128)S(1)}, u32[]{:S(2)}, u32[]{:S(2)}) collective-permute-start(f32[8,512]{1,0:T(8,128)S(1)} %constant_dynamic-slice_fusion), channel_id=1, source_target_pairs={{0,4},{1,5},{2,6},{3,7},{4,0},{5,1},{6,2},{7,3},{8,12},{9,13},{10,... | collective-permute-start | bytes 49160 | tf_op jit(solution)/shard_map/ppermute | solution.py:31
  388.4 19.4 %copy-start.17 = (f32[16384]{0:T(1024)S(1)}, f32[16384]{0:T(1024)}, u32[]{:S(2)}) copy-start(f32[16384]{0:T(1024)} %copy-done.16) | copy-start | bytes 196612
  388.4 19.4 %copy-start.20 = (f32[128]{0:T(128)S(1)}, f32[128]{0:T(128)}, u32[]{:S(2)}) copy-start(f32[128]{0:T(128)} %param.8) | copy-start | bytes 1540
  388.4 19.4 %copy-start.22 = (f32[128]{0:T(128)S(1)}, f32[128]{0:T(128)}, u32[]{:S(2)}) copy-start(f32[128]{0:T(128)} %copy-done.21) | copy-start | bytes 1540
  388.4 19.4 %copy-start.24 = (f32[128]{0:T(128)S(1)}, f32[128]{0:T(128)}, u32[]{:S(2)}) copy-start(f32[128]{0:T(128)} %copy-done.23) | copy-start | bytes 1540
  388.4 19.4 %copy-start.26 = (f32[128]{0:T(128)S(1)}, f32[128]{0:T(128)}, u32[]{:S(2)}) copy-start(f32[128]{0:T(128)} %copy-done.25) | copy-start | bytes 1540
  398.1 9.7 %collective-permute-start.5 = (f32[2,128]{1,0:T(2,128)S(1)}, f32[2,128]{1,0:T(2,128)S(1)}, u32[]{:S(2)}, u32[]{:S(2)}) collective-permute-start(f32[2,128]{1,0:T(2,128)S(1)} %slice.84), channel_id=1, source_target_pairs={{8,0},{16,8},{24,16},{32,24},{40,32},{48,40},{56,48},{64,56},{72,6... | collective-permute-start | bytes 3080 | tf_op jit(solution)/shard_map/ppermute | solution.py:16
  405.6 35.1 %collective-permute-start.16 = (f32[8,512]{1,0:T(8,128)S(1)}, f32[8,512]{1,0:T(8,128)S(1)}, u32[]{:S(2)}, u32[]{:S(2)}) collective-permute-start(f32[8,512]{1,0:T(8,128)S(1)} %dynamic-slice_add_fusion.5), channel_id=1, source_target_pairs={{0,4},{1,5},{2,6},{3,7},{4,0},{5,1},{6,2},{7,3},{8,12},{9,13},{10,... | collective-permute-start | bytes 49160 | tf_op jit(solution)/shard_map/ppermute | solution.py:31
  432.6 7.9 %collective-permute-start.23 = (f32[128]{0:T(128)S(1)}, f32[128]{0:T(128)S(1)}, u32[]{:S(2)}, u32[]{:S(2)}) collective-permute-start(f32[128]{0:T(128)S(1)} %get-tuple-element.59), channel_id=1, source_target_pairs={{0,8},{8,0},{16,24},{24,16},{32,40},{40,32},{48,56},{56,48},{64,72... | collective-permute-start | bytes 1544 | tf_op jit(solution)/shard_map/ppermute | solution.py:24
  440.4 38.9 %copy-start.4 = (bf16[32,512,128]{2,1,0:T(8,128)(2,1)S(1)}, bf16[32,512,128]{2,1,0:T(8,128)(2,1)}, u32[]{:S(2)}) copy-start(bf16[32,512,128]{2,1,0:T(8,128)(2,1)} %param.7) | copy-start | bytes 12582916
  440.5 3.1 collective-permute-start.24
  440.7 5.4 %collective-permute-start.17 = (f32[16,512]{1,0:T(8,128)S(1)}, f32[16,512]{1,0:T(8,128)S(1)}, u32[]{:S(2)}, u32[]{:S(2)}) collective-permute-start(f32[16,512]{1,0:T(8,128)S(1)} %constant_dynamic-update-slice_fusion.6), channel_id=1, source_target_pairs={{0,2},{1,3},{2,0},{3,1},{4,6},{5,7},{6,4},{7,5},{8,10},{9,11},{10,... | collective-permute-start | bytes 98312 | tf_op jit(solution)/shard_map/ppermute | solution.py:31
  443.5 7.5 %collective-permute-start.25 = (f32[128]{0:T(128)S(1)}, f32[128]{0:T(128)S(1)}, u32[]{:S(2)}, u32[]{:S(2)}) collective-permute-start(f32[128]{0:T(128)S(1)} %add.231), channel_id=1, source_target_pairs={{0,32},{8,40},{16,48},{24,56},{32,0},{40,8},{48,16},{56,24},{64,96... | collective-permute-start | bytes 1544 | tf_op jit(solution)/shard_map/ppermute | solution.py:24
  446.1 4.9 %collective-permute-start.18 = (f32[32,512]{1,0:T(8,128)S(1)}, f32[32,512]{1,0:T(8,128)S(1)}, u32[]{:S(2)}, u32[]{:S(2)}) collective-permute-start(f32[32,512]{1,0:T(8,128)S(1)} %constant_dynamic-update-slice_fusion.5), channel_id=1, source_target_pairs={{0,32},{8,40},{16,48},{24,56},{32,0},{40,8},{48,16},{56,24},{64,96... | collective-permute-start | bytes 196616 | tf_op jit(solution)/shard_map/ppermute | solution.py:31
  447.6 5.0 %collective-permute-start.27 = (f32[2,3,128]{2,1,0:T(4,128)S(1)}, f32[2,3,128]{2,1,0:T(4,128)S(1)}, u32[]{:S(2)}, u32[]{:S(2)}) collective-permute-start(f32[2,3,128]{2,1,0:T(4,128)S(1)} %pad_maximum_fusion.10), channel_id=1, source_target_pairs={{0,8},{8,0},{16,24},{24,16},{32,40},{40,32},{48,56},{56,48},{64,72... | collective-permute-start | bytes 9224 | tf_op jit(solution)/shard_map/ppermute | solution.py:24
  449.8 7.8 %collective-permute-start.6 = (f32[16384]{0:T(1024)S(1)}, f32[16384]{0:T(1024)S(1)}, u32[]{:S(2)}, u32[]{:S(2)}) collective-permute-start(f32[16384]{0:T(1024)S(1)} %get-tuple-element.58), channel_id=1, source_target_pairs={{0,1},{1,0},{2,3},{3,2},{4,5},{5,4},{6,7},{7,6},{8,9},{9,8},{10,11... | collective-permute-start | bytes 196616 | tf_op jit(solution)/shard_map/ppermute | solution.py:24
  451.0 9.1 %collective-permute-start.26 = (f32[128]{0:T(128)S(1)}, f32[128]{0:T(128)S(1)}, u32[]{:S(2)}, u32[]{:S(2)}) collective-permute-start(f32[128]{0:T(128)S(1)} %add.232), channel_id=1, source_target_pairs={{0,64},{8,72},{16,80},{24,88},{32,96},{40,104},{48,112},{56,120},{... | collective-permute-start | bytes 1544 | tf_op jit(solution)/shard_map/ppermute | solution.py:24
  451.1 3.9 collective-permute-start.19
  452.6 2.8 collective-permute-start.28
  455.0 9.4 %collective-permute-start.20 = (f32[128,512]{1,0:T(8,128)S(1)}, f32[128,512]{1,0:T(8,128)S(1)}, u32[]{:S(2)}, u32[]{:S(2)}) collective-permute-start(f32[128,512]{1,0:T(8,128)S(1)} %constant_dynamic-update-slice_fusion.3), channel_id=1, source_target_pairs={{0,1},{1,0},{2,3},{3,2},{4,5},{5,4},{6,7},{7,6},{8,9},{9,8},{10,11... | collective-permute-start | bytes 786440 | tf_op jit(solution)/shard_map/ppermute | solution.py:31
  455.4 5.3 %collective-permute-start.29 = (f32[2,3,128]{2,1,0:T(4,128)S(1)}, f32[2,3,128]{2,1,0:T(4,128)S(1)}, u32[]{:S(2)}, u32[]{:S(2)}) collective-permute-start(f32[2,3,128]{2,1,0:T(4,128)S(1)} %fusion.56), channel_id=1, source_target_pairs={{0,32},{8,40},{16,48},{24,56},{32,0},{40,8},{48,16},{56,24},{64,96... | collective-permute-start | bytes 9224 | tf_op jit(solution)/shard_map/ppermute | solution.py:24
  457.6 5.0 %collective-permute-start.7 = (f32[16384]{0:T(1024)S(1)}, f32[16384]{0:T(1024)S(1)}, u32[]{:S(2)}, u32[]{:S(2)}) collective-permute-start(f32[16384]{0:T(1024)S(1)} %add.199), channel_id=1, source_target_pairs={{0,2},{1,3},{2,0},{3,1},{4,6},{5,7},{6,4},{7,5},{8,10},{9,11},{10,... | collective-permute-start | bytes 196616 | tf_op jit(solution)/shard_map/ppermute | solution.py:24
  460.6 4.0 collective-permute-start.30
  462.6 5.0 %collective-permute-start.8 = (f32[16384]{0:T(1024)S(1)}, f32[16384]{0:T(1024)S(1)}, u32[]{:S(2)}, u32[]{:S(2)}) collective-permute-start(f32[16384]{0:T(1024)S(1)} %add.200), channel_id=1, source_target_pairs={{0,4},{1,5},{2,6},{3,7},{4,0},{5,1},{6,2},{7,3},{8,12},{9,13},{10,... | collective-permute-start | bytes 196616 | tf_op jit(solution)/shard_map/ppermute | solution.py:24
  464.5 8.4 %collective-permute-start.21 = (f32[256,512]{1,0:T(8,128)S(1)}, f32[256,512]{1,0:T(8,128)S(1)}, u32[]{:S(2)}, u32[]{:S(2)}) collective-permute-start(f32[256,512]{1,0:T(8,128)S(1)} %constant_dynamic-update-slice_fusion.2), channel_id=1, source_target_pairs={{0,16},{8,24},{16,0},{24,8},{32,48},{40,56},{48,32},{56,40},{64,80... | collective-permute-start | bytes 1572872 | tf_op jit(solution)/shard_map/ppermute | solution.py:31
  473.1 13.9 %collective-permute-start.22 = (f32[512,512]{1,0:T(8,128)S(1)}, f32[512,512]{1,0:T(8,128)S(1)}, u32[]{:S(2)}, u32[]{:S(2)}) collective-permute-start(f32[512,512]{1,0:T(8,128)S(1)} %constant_dynamic-update-slice_fusion.1), channel_id=1, source_target_pairs={{0,8},{8,0},{16,24},{24,16},{32,40},{40,32},{48,56},{56,48},{64,72... | collective-permute-start | bytes 3145736 | tf_op jit(solution)/shard_map/ppermute | solution.py:31
  (17 other events, 83.3 us)

commit v8 on v7

--- a/solution.py
+++ b/solution.py
@@ -31,22 +31,52 @@
     return lax.ppermute(value, axis, [(source, source ^ step) for source in range(count)])
 
 
-def tree_allreduce(value, rounds):
+def coordinate_bit(spec):
+    axis, step = spec
+    return (lax.axis_index(axis) // step) % 2
+
+
+def split_exchange(value, specs, sizes):
+    ctx_size, ch_size = sizes
+    pairs = []
+    for source in range(ctx_size * ch_size):
+        row, col = divmod(source, ch_size)
+        axis, step = specs[row % 2]
+        if axis == "ctx":
+            row = row ^ step
+        else:
+            col = col ^ step
+        pairs.append((source, row * ch_size + col))
+    return lax.ppermute(value, ("ctx", "ch"), pairs)
+
+
+def tree_allreduce(value, plan):
+    sizes = (lax.axis_size("ctx"), lax.axis_size("ch"))
+    on_second = lax.axis_index("ctx") % 2 == 1
     kept = []
-    for axis, step in rounds:
+    for specs in plan:
         half = value.shape[0] // 2
-        offset = ((lax.axis_index(axis) // step) % 2) * half
+        bit = jnp.where(on_second, coordinate_bit(specs[1]), coordinate_bit(specs[0]))
+        offset = bit * half
         keep = lax.dynamic_slice_in_dim(value, offset, half, 0)
         send = lax.dynamic_slice_in_dim(value, half - offset, half, 0)
-        value = keep + exchange(send, axis, step)
-        kept.append((axis, step, offset))
-    for axis, step, offset in reversed(kept):
-        other = exchange(value, axis, step)
+        value = keep + split_exchange(send, specs, sizes)
+        kept.append((specs, offset))
+    for specs, offset in reversed(kept):
+        other = split_exchange(value, specs, sizes)
         value = lax.dynamic_update_slice_in_dim(jnp.concatenate([other, other]), value, offset, 0)
     return value
 
 
-FACTOR_ROUNDS = (("ctx", 1), ("ctx", 2), ("ch", 1), ("ctx", 8), ("ctx", 4), ("ch", 2), ("ch", 4))
+FACTOR_ROUNDS = (
+    (("ctx", 1), ("ctx", 1)),
+    (("ctx", 2), ("ch", 1)),
+    (("ch", 1), ("ctx", 2)),
+    (("ctx", 8), ("ctx", 4)),
+    (("ctx", 4), ("ctx", 8)),
+    (("ch", 2), ("ch", 4)),
+    (("ch", 4), ("ch", 2)),
+)
 
 
 def on_device(inputs, norm_gain, conv_taps, factor_one, factor_two, kernel, grad_out):

time: 498 us -> 492 us (0.988)
  waiting for transfers between devices: 181 us -> 174 us
  transfers between devices with their start and end apart: 35 -> 35, of which waited for: 19 -> 21; matrix products, arithmetic and copies ran while one was open for 32% -> 32% of each run, Pallas kernels for 0% -> 0%
where the time goes in v8:
time: 492 us; the launch traced here: 483 us
  waiting for transfers between devices  174 us (35%)
  local copies, waits for them, and re-layouts  93.4 us (19%)
  starting transfers between devices  88.6 us (18%)
  other arithmetic  83.7 us (17%)
  matrix products  41.5 us (8%)
    all_to_all x1, waiting for transfers between devices, on_device(): lax.all_to_all(section_one, 'ctx', split_axis=1, concat_axis=0, tiled=True)  48.8 us
    all_to_all x1, waiting for transfers between devices, on_device(): lax.all_to_all(grad_section, 'ctx', split_axis=0, concat_axis=1, tiled=True)  39.4 us
    all_to_all x1, waiting for transfers between devices, on_device(): lax.all_to_all(section_two, 'ctx', split_axis=0, concat_axis=1, tiled=True)  33.5 us
    ppermute x14, waiting for transfers between devices, split_exchange(): return lax.ppermute(value, ('ctx', 'ch'), pairs)  31.2 us
    ppermute x14, starting transfers between devices, split_exchange(): return lax.ppermute(value, ('ctx', 'ch'), pairs)  25.7 us
    reduce_sum x1, other arithmetic, on_device(): value_taps.append(jnp.sum(grad_mixed * window, axis=0))  24.7 us
    unnamed x64, local copies, waits for them, and re-layouts  23.3 us
    ppermute x14, starting transfers between devices, tree_psum(): lax.ppermute(value, axis, pairs)  22.4 us
  transfers between devices with their start and end apart: 35, of which 21 were waited for; matrix products, arithmetic and copies ran while one was open for 32% of the time, Pallas kernels for 0%

profile of v8, /device:TPU:1, one launch (start us, length us, event | category | flops | bytes accessed | tf_op | source)
XLA Modules:
  0.0 483.2 jit_solution(4145678370907868161)
XLA Ops:
  0.7 4.6 multiply_reduce_fusion.2
  9.1 3.1 collective-permute-start.1
  13.8 3.9 collective-permute-start.2
  19.4 4.4 multiply_convert_fusion.1
  23.9 6.9 %collective-permute-start.3 = (bf16[2,128]{1,0:T(2,128)(2,1)S(1)}, bf16[2,128]{1,0:T(2,128)(2,1)S(1)}, u32[]{:S(2)}, u32[]{:S(2)}) collective-permute-start(bf16[2,128]{1,0:T(2,128)(2,1)S(1)} %slice.78), channel_id=1, source_target_pairs={{0,8},{8,16},{16,24},{24,32},{32,40},{40,48},{48,56},{56,64},{64,7... | collective-permute-start | bytes 1544 | tf_op jit(solution)/shard_map/ppermute | solution.py:16
  31.5 6.5 %fusion.10 = (bf16[16384,128]{1,0:T(8,128)(2,1)}, bf16[16384,128]{1,0:T(8,128)(2,1)S(1)}) fusion(bf16[32,512,128]{2,1,0:T(8,128)(2,1)S(1)} %copy-done.10, bf16[16384,128]{1,0:T(8,128)(2,1)S(1)} %multiply_convert_fusion.1, bf16[2,128]{1,0:T(2,128)(2,1)S(1)} %collective-permute-done.3, f32[128]{0:T(128)S(1)} %get-tuple-element.69, ...), kind=kLoop, calls=%fused_computation.30 | loop fusion | flops 44040192 | bytes 16779264 | tf_op jit(solution)/shard_map/convert_element_type | solution.py:105
  38.1 3.0 fusion.15
  43.1 4.4 convert_bitcast_fusion.2
  47.5 7.9 %copy.58 = bf16[32,512,128]{2,0,1:T(8,128)(2,1)} copy(bf16[32,512,128]{1,2,0:T(8,128)(2,1)} %convert_bitcast_fusion.2) | data formatting | bytes 8388608 | tf_op jit(solution)/shard_map/convert_element_type | solution.py:104
  55.4 7.2 %all-to-all-start = ((bf16[32,512,128]{2,0,1:T(8,128)(2,1)}), bf16[32,512,128]{2,0,1:T(8,128)(2,1)}, u32[]{:S(2)}, u32[]{:S(2)}) async-start(bf16[32,512,128]{2,0,1:T(8,128)(2,1)} %copy.58), calls=%async_computation | async-start | bytes 8388608 | tf_op jit(solution)/shard_map/all_to_all | solution.py:106
  62.6 6.9 %copy.65 = bf16[32,512,128]{2,0,1:T(8,128)(2,1)} copy(bf16[32,512,128]{2,1,0:T(8,128)(2,1)} %bitcast.104) | data formatting | bytes 8388608 | tf_op jit(solution)/shard_map/reshape | solution.py:105
  69.5 48.8 %all-to-all-done = bf16[32,512,128]{2,0,1:T(8,128)(2,1)} async-done(((bf16[32,512,128]{2,0,1:T(8,128)(2,1)}), bf16[32,512,128]{2,0,1:T(8,128)(2,1)}, u32[]{:S(2)}, u32[]{:S(2)}) %all-to-all-start) | async-done | bytes 4194336 | tf_op jit(solution)/shard_map/all_to_all | solution.py:106
  118.3 4.9 %all-to-all-start.2 = ((bf16[32,512,128]{2,0,1:T(8,128)(2,1)}), bf16[32,512,128]{2,0,1:T(8,128)(2,1)}, u32[]{:S(2)}, u32[]{:S(2)}) async-start(bf16[32,512,128]{2,0,1:T(8,128)(2,1)} %copy.65), calls=%async_computation.2 | async-start | bytes 8388608 | tf_op jit(solution)/shard_map/all_to_all | solution.py:113
  123.2 7.5 %copy.61 = bf16[512,32,128]{0,2,1:T(8,128)(2,1)} copy(bf16[512,32,128]{2,1,0:T(8,128)(2,1)} %param.12) | data formatting | bytes 8388608 | tf_op args[5]
  130.7 3.8 copy.59
  135.7 4.3 copy.60
  139.9 10.0 %copy.62 = f32[512,32,128]{0,2,1:T(8,128)} copy(f32[512,32,128]{2,1,0:T(8,128)} %bitcast.101) | data formatting | bytes 16777216 | tf_op jit(solution)/shard_map/convert_element_type | solution.py:108
  150.0 8.8 %convert_bitcast_fusion.1 = bf16[512,32,128]{0,2,1:T(8,128)(2,1)} fusion(bf16[512,512]{1,0:T(8,128)(2,1)S(1)} %copy-done, f32[512,32,128]{0,2,1:T(8,128)} %copy.62, bf16[512,32,128]{0,2,1:T(8,128)(2,1)} %copy.61), kind=kOutput, calls=%fused_computation.65 | convolution fusion | flops 2155872256 | bytes 17301504 | tf_op jit(solution)/shard_map/ijc,ik->kjc/dot_general | solution.py:109
  158.8 7.9 %copy.63 = bf16[512,32,128]{2,1,0:T(8,128)(2,1)} copy(bf16[512,32,128]{0,2,1:T(8,128)(2,1)} %convert_bitcast_fusion.1) | data formatting | bytes 8388608 | tf_op jit(solution)/shard_map/convert_element_type | solution.py:111
  166.7 12.1 %all-to-all-done.2 = bf16[32,512,128]{2,0,1:T(8,128)(2,1)} async-done(((bf16[32,512,128]{2,0,1:T(8,128)(2,1)}), bf16[32,512,128]{2,0,1:T(8,128)(2,1)}, u32[]{:S(2)}, u32[]{:S(2)}) %all-to-all-start.2) | async-done | bytes 4194336 | tf_op jit(solution)/shard_map/all_to_all | solution.py:113
  178.9 5.4 %all-to-all-start.1 = ((bf16[512,32,128]{2,1,0:T(8,128)(2,1)}), bf16[512,32,128]{2,1,0:T(8,128)(2,1)}, u32[]{:S(2)}, u32[]{:S(2)}) async-start(bf16[512,32,128]{2,1,0:T(8,128)(2,1)} %copy.63), calls=%async_computation.1 | async-start | bytes 8388608 | tf_op jit(solution)/shard_map/all_to_all | solution.py:112
  184.4 4.1 copy.67
  188.5 9.0 %fusion.36 = f32[512,512]{1,0:T(8,128)} fusion(bf16[512,32,128]{2,1,0:T(8,128)(2,1)S(1)} %bitcast.97, f32[512,32,128]{0,2,1:T(8,128)} %copy.62, bf16[512,32,128]{0,2,1:T(8,128)(2,1)S(1)} %copy-done.7), kind=kOutput, calls=%fused_computation.77 | convolution fusion | flops 2153775104 | bytes 17825792 | tf_op jit(solution)/shard_map/ijc,kjc->ik/dot_general | solution.py:119
  197.5 9.0 %fusion.30 = (bf16[512,32,128]{0,2,1:T(8,128)(2,1)}, bf16[512,32,128]{0,2,1:T(8,128)(2,1)}) fusion(f32[512,32,128]{0,2,1:T(8,128)S(1)} %bitcast.96, bf16[512,32,128]{0,2,1:T(8,128)(2,1)S(1)} %copy-done.7, bf16[512,512]{1,0:T(8,128)(2,1)S(1)} %copy-done, bf16[512,32,128]{2,1,0:T(8,128)(2,1)S(1)} %bitcast.98), kind=kOutput, calls=%fused_computation.54 | convolution fusion | flops 2157969408 | bytes 25690112 | tf_op jit(solution)/shard_map/kjc,ik->ijc/dot_general | solution.py:114
  206.5 33.5 %all-to-all-done.1 = bf16[512,32,128]{2,1,0:T(8,128)(2,1)} async-done(((bf16[512,32,128]{2,1,0:T(8,128)(2,1)}), bf16[512,32,128]{2,1,0:T(8,128)(2,1)}, u32[]{:S(2)}, u32[]{:S(2)}) %all-to-all-start.1) | async-done | bytes 4194336 | tf_op jit(solution)/shard_map/all_to_all | solution.py:112
  240.0 3.6 copy.64
  244.7 8.4 %fusion.26 = (f32[128]{0:T(128)S(1)}, f32[128]{0:T(128)S(1)}, f32[128]{0:T(128)S(1)}, f32[16384,128]{1,0:T(8,128)S(1)}) fusion(bf16[16384,128]{1,0:T(8,128)(2,1)S(1)} %copy-done.3, bf16[2,128]{1,0:T(2,128)(2,1)S(1)} %copy-done.19, bf16[16384,128]{1,0:T(8,128)(2,1)S(1)} %copy-done.6, f32[128]{0:T(128)S(1)} %get-tuple-element.69, ...), kind=kLoop, calls=%fused_computation.46 | loop fusion | flops 54525568 | bytes 25169408 | tf_op jit(solution)/shard_map/reduce_sum | solution.py:131
  253.2 3.2 copy-done.8
  258.9 7.9 %copy.71 = bf16[512,32,128]{2,1,0:T(8,128)(2,1)} copy(bf16[512,32,128]{0,2,1:T(8,128)(2,1)} %get-tuple-element.15) | data formatting | bytes 8388608 | tf_op jit(solution)/shard_map/optimization_barrier | solution.py:120
  266.8 5.9 %all-to-all-start.3 = ((bf16[512,32,128]{2,1,0:T(8,128)(2,1)}), bf16[512,32,128]{2,1,0:T(8,128)(2,1)}, u32[]{:S(2)}, u32[]{:S(2)}) async-start(bf16[512,32,128]{2,1,0:T(8,128)(2,1)} %copy.71), calls=%async_computation.3 | async-start | bytes 8388608 | tf_op jit(solution)/shard_map/all_to_all | solution.py:121
  272.7 16.3 %fusion.7 = f32[16384,128]{1,0:T(8,128)} fusion(f32[16384,128]{1,0:T(8,128)} %copy-done.8, f32[2,128]{1,0:T(2,128)S(1)} %collective-permute-done.4, f32[128]{0:T(128)S(1)} %get-tuple-element.69, f32[128]{0:T(128)S(1)} %get-tuple-element.70, f32[128]{0:T(128)S(1)} %get-tuple-element.68), kind=kLoop, calls=%fused_computation.27 | loop fusion | flops 14680064 | bytes 16779776 | tf_op jit(solution)/shard_map/add | solution.py:129
  289.0 39.4 %all-to-all-done.3 = bf16[512,32,128]{2,1,0:T(8,128)(2,1)} async-done(((bf16[512,32,128]{2,1,0:T(8,128)(2,1)}), bf16[512,32,128]{2,1,0:T(8,128)(2,1)}, u32[]{:S(2)}, u32[]{:S(2)}) %all-to-all-start.3) | async-done | bytes 4194336 | tf_op jit(solution)/shard_map/all_to_all | solution.py:121
  328.4 3.6 copy.72
  343.0 7.1 %collective-permute-done.10 = f32[256,512]{1,0:T(8,128)S(1)} collective-permute-done((f32[256,512]{1,0:T(8,128)S(1)}, f32[256,512]{1,0:T(8,128)S(1)}, u32[]{:S(2)}, u32[]{:S(2)}) %collective-permute-start.10) | collective-permute-done | bytes 524320 | tf_op jit(solution)/shard_map/ppermute | solution.py:50
  353.5 4.1 collective-permute-done.11
  358.7 4.4 collective-permute-done.12
  366.3 3.4 collective-permute-start.14
  371.0 2.8 collective-permute-start.15
  373.9 7.9 %convolution_bitcast_fusion = f32[32,512,128]{1,2,0:T(8,128)} fusion(bf16[32,512,128]{2,1,0:T(8,128)(2,1)} %bitcast.103, bf16[512,512]{1,0:T(8,128)(2,1)S(1)} %copy-done.15), kind=kOutput, calls=%fused_computation.71 | convolution fusion | flops 2147483648 | bytes 13107200 | tf_op jit(solution)/shard_map/ikc,jk->ijc/dot_general | solution.py:133
  381.8 9.0 %copy.74 = f32[32,512,128]{2,1,0:T(8,128)} copy(f32[32,512,128]{1,2,0:T(8,128)} %convolution_bitcast_fusion) | data formatting | bytes 16777216 | tf_op jit(solution)/shard_map/ikc,jk->ijc/transpose | solution.py:133
  391.4 7.7 %collective-permute-start.5 = (f32[2,128]{1,0:T(2,128)S(1)}, f32[2,128]{1,0:T(2,128)S(1)}, u32[]{:S(2)}, u32[]{:S(2)}) collective-permute-start(f32[2,128]{1,0:T(2,128)S(1)} %slice.84), channel_id=1, source_target_pairs={{8,0},{16,8},{24,16},{32,24},{40,32},{48,40},{56,48},{64,56},{72,6... | collective-permute-start | bytes 3080 | tf_op jit(solution)/shard_map/ppermute | solution.py:16
  399.1 3.1 collective-permute-start.16
  402.2 24.7 %fusion.23 = (f32[128]{0:T(128)S(1)}, f32[128]{0:T(128)S(1)}, f32[128]{0:T(128)S(1)}, f32[16384]{0:T(1024)S(1)}, f32[128]{0:T(128)S(1)}, /*index=5*/f32[16384,128]{1,0:T(8,128)}) fusion(f32[16384,128]{1,0:T(8,128)} %bitcast.100, bf16[16384,128]{1,0:T(8,128)(2,1)} %copy-done.2, bf16[2,128]{1,0:T(2,128)(2,1)S(1)} %copy-done.19, ...), kind=kLoop, calls=%fused_computation.43 | loop fusion | flops 56606208 | bytes 37885440 | tf_op jit(solution)/shard_map/reduce_sum | solution.py:147
  426.9 7.8 %copy.76 = bf16[512,32,128]{2,1,0:T(8,128)(2,1)} copy(bf16[512,32,128]{0,2,1:T(8,128)(2,1)} %get-tuple-element.61) | data formatting | bytes 8388608
  450.4 3.0 collective-permute-start.29
  463.6 4.0 collective-permute-done.21
  467.8 5.5 %collective-permute-start.22 = (f32[512,512]{1,0:T(8,128)S(1)}, f32[512,512]{1,0:T(8,128)S(1)}, u32[]{:S(2)}, u32[]{:S(2)}) collective-permute-start(f32[512,512]{1,0:T(8,128)S(1)} %constant_dynamic-update-slice_fusion.1), channel_id=1, source_target_pairs={{0,8},{1,9},{2,10},{3,11},{4,12},{5,13},{6,14},{7,15},{8,0},{9,1},... | collective-permute-start | bytes 3145736 | tf_op jit(solution)/shard_map/ppermute | solution.py:50
  473.3 7.6 %multiply_convert_fusion = bf16[16384,128]{1,0:T(8,128)(2,1)} fusion(f32[16384,128]{1,0:T(8,128)} %get-tuple-element.60, bf16[32,512,128]{2,1,0:T(8,128)(2,1)S(1)} %copy-done.4, f32[16384]{0:T(1024)S(1)} %add_multiply_fusion, f32[128]{0:T(128)S(1)} %copy-done.20, f32[16384]{0:T(1024)S(1)} %copy-done.17), kind=kLoop, calls=%fused_computation.57 | loop fusion | flops 14680064 | bytes 16908800 | tf_op jit(solution)/shard_map/convert_element_type | solution.py:158
  (162 shorter events, 63.1 us)
Async XLA Ops:
  0.6 149.3 %copy-start = (bf16[512,512]{1,0:T(8,128)(2,1)S(1)}, bf16[512,512]{1,0:T(8,128)(2,1)}, u32[]{:S(2)}) copy-start(bf16[512,512]{1,0:T(8,128)(2,1)} %param.11) | copy-start | bytes 1572868
  0.6 30.2 %copy-start.27 = (f32[2,3,128]{2,0,1:T(2,128)S(1)}, f32[2,3,128]{2,0,1:T(2,128)}, u32[]{:S(2)}) copy-start(f32[2,3,128]{2,0,1:T(2,128)} %param.9) | copy-start | bytes 9220
  0.7 30.8 %copy-start.10 = (bf16[32,512,128]{2,1,0:T(8,128)(2,1)S(1)}, bf16[32,512,128]{2,1,0:T(8,128)(2,1)}, u32[]{:S(2)}) copy-start(bf16[32,512,128]{2,1,0:T(8,128)(2,1)} %param.13) | copy-start | bytes 12582916
  5.3 3.8 collective-permute-start
  9.1 4.7 collective-permute-start.1
  13.8 5.6 %collective-permute-start.2 = (f32[16384]{0:T(1024)S(1)}, f32[16384]{0:T(1024)S(1)}, u32[]{:S(2)}, u32[]{:S(2)}) collective-permute-start(f32[16384]{0:T(1024)S(1)} %add.193), channel_id=1, source_target_pairs={{0,4},{1,5},{2,6},{3,7},{4,0},{5,1},{6,2},{7,3},{8,12},{9,13},{10,... | collective-permute-start | bytes 196616 | tf_op jit(solution)/shard_map/ppermute | solution.py:24
  19.4 12.1 %copy-start.16 = (f32[16384]{0:T(1024)}, f32[16384]{0:T(1024)S(1)}, u32[]{:S(2)}) copy-start(f32[16384]{0:T(1024)S(1)} %add_rsqrt_fusion) | copy-start | bytes 196612
  23.8 14.2 %copy-start.2 = (bf16[16384,128]{1,0:T(8,128)(2,1)}, bf16[16384,128]{1,0:T(8,128)(2,1)S(1)}, u32[]{:S(2)}) copy-start(bf16[16384,128]{1,0:T(8,128)(2,1)S(1)} %multiply_convert_fusion.1) | copy-start | bytes 12582916
  23.9 7.6 %collective-permute-start.3 = (bf16[2,128]{1,0:T(2,128)(2,1)S(1)}, bf16[2,128]{1,0:T(2,128)(2,1)S(1)}, u32[]{:S(2)}, u32[]{:S(2)}) collective-permute-start(bf16[2,128]{1,0:T(2,128)(2,1)S(1)} %slice.78), channel_id=1, source_target_pairs={{0,8},{8,16},{16,24},{24,32},{32,40},{40,48},{48,56},{56,64},{64,7... | collective-permute-start | bytes 1544 | tf_op jit(solution)/shard_map/ppermute | solution.py:16
  55.4 62.9 %all-to-all-start = ((bf16[32,512,128]{2,0,1:T(8,128)(2,1)}), bf16[32,512,128]{2,0,1:T(8,128)(2,1)}, u32[]{:S(2)}, u32[]{:S(2)}) async-start(bf16[32,512,128]{2,0,1:T(8,128)(2,1)} %copy.58), calls=%async_computation | async-start | bytes 8388608 | tf_op jit(solution)/shard_map/all_to_all | solution.py:106
  118.3 60.6 %all-to-all-start.2 = ((bf16[32,512,128]{2,0,1:T(8,128)(2,1)}), bf16[32,512,128]{2,0,1:T(8,128)(2,1)}, u32[]{:S(2)}, u32[]{:S(2)}) async-start(bf16[32,512,128]{2,0,1:T(8,128)(2,1)} %copy.65), calls=%async_computation.2 | async-start | bytes 8388608 | tf_op jit(solution)/shard_map/all_to_all | solution.py:113
  178.9 61.1 %all-to-all-start.1 = ((bf16[512,32,128]{2,1,0:T(8,128)(2,1)}), bf16[512,32,128]{2,1,0:T(8,128)(2,1)}, u32[]{:S(2)}, u32[]{:S(2)}) async-start(bf16[512,32,128]{2,1,0:T(8,128)(2,1)} %copy.63), calls=%async_computation.1 | async-start | bytes 8388608 | tf_op jit(solution)/shard_map/all_to_all | solution.py:112
  184.3 13.2 %slice-start = ((s8[8388608]{0:T(1024)(128)(4,1)}), s8[4194304]{0:T(1024)(128)(4,1)S(1)}, s32[]{:S(2)}) async-start(s8[8388608]{0:T(1024)(128)(4,1)} %bitcast.95), calls=%async_computation.4 | async-start | bytes 8388608
  206.5 37.1 %copy-start.19 = (bf16[2,128]{1,0:T(2,128)(2,1)S(1)}, bf16[2,128]{1,0:T(2,128)(2,1)}, u32[]{:S(2)}) copy-start(bf16[2,128]{1,0:T(2,128)(2,1)} %copy-done.18) | copy-start | bytes 1540
  256.4 16.3 %collective-permute-start.4 = (f32[2,128]{1,0:T(2,128)S(1)}, f32[2,128]{1,0:T(2,128)S(1)}, u32[]{:S(2)}, u32[]{:S(2)}) collective-permute-start(f32[2,128]{1,0:T(2,128)S(1)} %slice.81), channel_id=1, source_target_pairs={{8,0},{16,8},{24,16},{32,24},{40,32},{48,40},{56,48},{64,56},{72,6... | collective-permute-start | bytes 3080 | tf_op jit(solution)/shard_map/ppermute | solution.py:16
  266.8 61.6 %all-to-all-start.3 = ((bf16[512,32,128]{2,1,0:T(8,128)(2,1)}), bf16[512,32,128]{2,1,0:T(8,128)(2,1)}, u32[]{:S(2)}, u32[]{:S(2)}) async-start(bf16[512,32,128]{2,1,0:T(8,128)(2,1)} %copy.71), calls=%async_computation.3 | async-start | bytes 8388608 | tf_op jit(solution)/shard_map/all_to_all | solution.py:121
  335.8 3.2 collective-permute-start.9
  341.7 8.4 %collective-permute-start.10 = (f32[256,512]{1,0:T(8,128)S(1)}, f32[256,512]{1,0:T(8,128)S(1)}, u32[]{:S(2)}, u32[]{:S(2)}) collective-permute-start(f32[256,512]{1,0:T(8,128)S(1)} %constant_dynamic-slice_fusion.5), channel_id=1, source_target_pairs={{0,16},{1,17},{2,18},{3,19},{4,20},{5,21},{6,22},{7,23},{8,9},{9,8... | collective-permute-start | bytes 1572872 | tf_op jit(solution)/shard_map/ppermute | solution.py:50
  351.2 6.3 %collective-permute-start.11 = (f32[128,512]{1,0:T(8,128)S(1)}, f32[128,512]{1,0:T(8,128)S(1)}, u32[]{:S(2)}, u32[]{:S(2)}) collective-permute-start(f32[128,512]{1,0:T(8,128)S(1)} %constant_dynamic-slice_fusion.4), channel_id=1, source_target_pairs={{0,1},{1,0},{2,3},{3,2},{4,5},{5,4},{6,7},{7,6},{8,24},{9,25},{10,... | collective-permute-start | bytes 786440 | tf_op jit(solution)/shard_map/ppermute | solution.py:50
  357.6 5.4 %collective-permute-start.12 = (f32[64,512]{1,0:T(8,128)S(1)}, f32[64,512]{1,0:T(8,128)S(1)}, u32[]{:S(2)}, u32[]{:S(2)}) collective-permute-start(f32[64,512]{1,0:T(8,128)S(1)} %constant_dynamic-slice_fusion.3), channel_id=1, source_target_pairs={{0,64},{1,65},{2,66},{3,67},{4,68},{5,69},{6,70},{7,71},{8,40},{9,... | collective-permute-start | bytes 393224 | tf_op jit(solution)/shard_map/ppermute | solution.py:50
  363.1 3.2 collective-permute-start.13
  366.3 4.7 collective-permute-start.14
  371.0 28.1 %collective-permute-start.15 = (f32[8,512]{1,0:T(8,128)S(1)}, f32[8,512]{1,0:T(8,128)S(1)}, u32[]{:S(2)}, u32[]{:S(2)}) collective-permute-start(f32[8,512]{1,0:T(8,128)S(1)} %constant_dynamic-slice_fusion), channel_id=1, source_target_pairs={{0,4},{1,5},{2,6},{3,7},{4,0},{5,1},{6,2},{7,3},{8,10},{9,11},{10,... | collective-permute-start | bytes 49160 | tf_op jit(solution)/shard_map/ppermute | solution.py:50
  381.7 20.4 %copy-start.17 = (f32[16384]{0:T(1024)S(1)}, f32[16384]{0:T(1024)}, u32[]{:S(2)}) copy-start(f32[16384]{0:T(1024)} %copy-done.16) | copy-start | bytes 196612
  381.7 20.4 %copy-start.20 = (f32[128]{0:T(128)S(1)}, f32[128]{0:T(128)}, u32[]{:S(2)}) copy-start(f32[128]{0:T(128)} %param.8) | copy-start | bytes 1540
  381.7 20.5 %copy-start.22 = (f32[128]{0:T(128)S(1)}, f32[128]{0:T(128)}, u32[]{:S(2)}) copy-start(f32[128]{0:T(128)} %copy-done.21) | copy-start | bytes 1540
  381.7 20.5 %copy-start.24 = (f32[128]{0:T(128)S(1)}, f32[128]{0:T(128)}, u32[]{:S(2)}) copy-start(f32[128]{0:T(128)} %copy-done.23) | copy-start | bytes 1540
  381.8 20.5 %copy-start.26 = (f32[128]{0:T(128)S(1)}, f32[128]{0:T(128)}, u32[]{:S(2)}) copy-start(f32[128]{0:T(128)} %copy-done.25) | copy-start | bytes 1540
  391.4 10.8 %collective-permute-start.5 = (f32[2,128]{1,0:T(2,128)S(1)}, f32[2,128]{1,0:T(2,128)S(1)}, u32[]{:S(2)}, u32[]{:S(2)}) collective-permute-start(f32[2,128]{1,0:T(2,128)S(1)} %slice.84), channel_id=1, source_target_pairs={{8,0},{16,8},{24,16},{32,24},{40,32},{48,40},{56,48},{64,56},{72,6... | collective-permute-start | bytes 3080 | tf_op jit(solution)/shard_map/ppermute | solution.py:16
  399.1 37.5 %collective-permute-start.16 = (f32[8,512]{1,0:T(8,128)S(1)}, f32[8,512]{1,0:T(8,128)S(1)}, u32[]{:S(2)}, u32[]{:S(2)}) collective-permute-start(f32[8,512]{1,0:T(8,128)S(1)} %dynamic-slice_add_fusion.5), channel_id=1, source_target_pairs={{0,4},{1,5},{2,6},{3,7},{4,0},{5,1},{6,2},{7,3},{8,10},{9,11},{10,... | collective-permute-start | bytes 49160 | tf_op jit(solution)/shard_map/ppermute | solution.py:50
  426.9 7.9 %collective-permute-start.23 = (f32[128]{0:T(128)S(1)}, f32[128]{0:T(128)S(1)}, u32[]{:S(2)}, u32[]{:S(2)}) collective-permute-start(f32[128]{0:T(128)S(1)} %get-tuple-element.59), channel_id=1, source_target_pairs={{0,8},{8,0},{16,24},{24,16},{32,40},{40,32},{48,56},{56,48},{64,72... | collective-permute-start | bytes 1544 | tf_op jit(solution)/shard_map/ppermute | solution.py:24
  434.8 38.5 %copy-start.4 = (bf16[32,512,128]{2,1,0:T(8,128)(2,1)S(1)}, bf16[32,512,128]{2,1,0:T(8,128)(2,1)}, u32[]{:S(2)}) copy-start(bf16[32,512,128]{2,1,0:T(8,128)(2,1)} %param.7) | copy-start | bytes 12582916
  434.8 2.8 collective-permute-start.24
  436.6 4.3 collective-permute-start.17
  437.6 7.0 %collective-permute-start.25 = (f32[128]{0:T(128)S(1)}, f32[128]{0:T(128)S(1)}, u32[]{:S(2)}, u32[]{:S(2)}) collective-permute-start(f32[128]{0:T(128)S(1)} %add.239), channel_id=1, source_target_pairs={{0,32},{8,40},{16,48},{24,56},{32,0},{40,8},{48,16},{56,24},{64,96... | collective-permute-start | bytes 1544 | tf_op jit(solution)/shard_map/ppermute | solution.py:24
  441.0 3.6 collective-permute-start.18
  441.3 5.6 %collective-permute-start.27 = (f32[2,3,128]{2,1,0:T(4,128)S(1)}, f32[2,3,128]{2,1,0:T(4,128)S(1)}, u32[]{:S(2)}, u32[]{:S(2)}) collective-permute-start(f32[2,3,128]{2,1,0:T(4,128)S(1)} %pad_maximum_fusion.10), channel_id=1, source_target_pairs={{0,8},{8,0},{16,24},{24,16},{32,40},{40,32},{48,56},{56,48},{64,72... | collective-permute-start | bytes 9224 | tf_op jit(solution)/shard_map/ppermute | solution.py:24
  443.6 9.8 %collective-permute-start.6 = (f32[16384]{0:T(1024)S(1)}, f32[16384]{0:T(1024)S(1)}, u32[]{:S(2)}, u32[]{:S(2)}) collective-permute-start(f32[16384]{0:T(1024)S(1)} %get-tuple-element.58), channel_id=1, source_target_pairs={{0,1},{1,0},{2,3},{3,2},{4,5},{5,4},{6,7},{7,6},{8,9},{9,8},{10,11... | collective-permute-start | bytes 196616 | tf_op jit(solution)/shard_map/ppermute | solution.py:24
  444.5 11.4 %collective-permute-start.26 = (f32[128]{0:T(128)S(1)}, f32[128]{0:T(128)S(1)}, u32[]{:S(2)}, u32[]{:S(2)}) collective-permute-start(f32[128]{0:T(128)S(1)} %add.240), channel_id=1, source_target_pairs={{0,64},{8,72},{16,80},{24,88},{32,96},{40,104},{48,112},{56,120},{... | collective-permute-start | bytes 1544 | tf_op jit(solution)/shard_map/ppermute | solution.py:24
  444.6 5.4 %collective-permute-start.19 = (f32[64,512]{1,0:T(8,128)S(1)}, f32[64,512]{1,0:T(8,128)S(1)}, u32[]{:S(2)}, u32[]{:S(2)}) collective-permute-start(f32[64,512]{1,0:T(8,128)S(1)} %constant_dynamic-update-slice_fusion.4), channel_id=1, source_target_pairs={{0,64},{1,65},{2,66},{3,67},{4,68},{5,69},{6,70},{7,71},{8,40},{9,... | collective-permute-start | bytes 393224 | tf_op jit(solution)/shard_map/ppermute | solution.py:50
  446.9 3.5 collective-permute-start.28
  450.1 9.1 %collective-permute-start.20 = (f32[128,512]{1,0:T(8,128)S(1)}, f32[128,512]{1,0:T(8,128)S(1)}, u32[]{:S(2)}, u32[]{:S(2)}) collective-permute-start(f32[128,512]{1,0:T(8,128)S(1)} %constant_dynamic-update-slice_fusion.3), channel_id=1, source_target_pairs={{0,1},{1,0},{2,3},{3,2},{4,5},{5,4},{6,7},{7,6},{8,24},{9,25},{10,... | collective-permute-start | bytes 786440 | tf_op jit(solution)/shard_map/ppermute | solution.py:50
  450.4 6.7 %collective-permute-start.29 = (f32[2,3,128]{2,1,0:T(4,128)S(1)}, f32[2,3,128]{2,1,0:T(4,128)S(1)}, u32[]{:S(2)}, u32[]{:S(2)}) collective-permute-start(f32[2,3,128]{2,1,0:T(4,128)S(1)} %fusion.56), channel_id=1, source_target_pairs={{0,32},{8,40},{16,48},{24,56},{32,0},{40,8},{48,16},{56,24},{64,96... | collective-permute-start | bytes 9224 | tf_op jit(solution)/shard_map/ppermute | solution.py:24
  453.4 5.4 %collective-permute-start.7 = (f32[16384]{0:T(1024)S(1)}, f32[16384]{0:T(1024)S(1)}, u32[]{:S(2)}, u32[]{:S(2)}) collective-permute-start(f32[16384]{0:T(1024)S(1)} %add.207), channel_id=1, source_target_pairs={{0,2},{1,3},{2,0},{3,1},{4,6},{5,7},{6,4},{7,5},{8,10},{9,11},{10,... | collective-permute-start | bytes 196616 | tf_op jit(solution)/shard_map/ppermute | solution.py:24
  457.1 3.5 collective-permute-start.30
  458.8 4.7 collective-permute-start.8
  459.2 8.4 %collective-permute-start.21 = (f32[256,512]{1,0:T(8,128)S(1)}, f32[256,512]{1,0:T(8,128)S(1)}, u32[]{:S(2)}, u32[]{:S(2)}) collective-permute-start(f32[256,512]{1,0:T(8,128)S(1)} %constant_dynamic-update-slice_fusion.2), channel_id=1, source_target_pairs={{0,16},{1,17},{2,18},{3,19},{4,20},{5,21},{6,22},{7,23},{8,9},{9,8... | collective-permute-start | bytes 1572872 | tf_op jit(solution)/shard_map/ppermute | solution.py:50
  467.8 13.0 %collective-permute-start.22 = (f32[512,512]{1,0:T(8,128)S(1)}, f32[512,512]{1,0:T(8,128)S(1)}, u32[]{:S(2)}, u32[]{:S(2)}) collective-permute-start(f32[512,512]{1,0:T(8,128)S(1)} %constant_dynamic-update-slice_fusion.1), channel_id=1, source_target_pairs={{0,8},{1,9},{2,10},{3,11},{4,12},{5,13},{6,14},{7,15},{8,0},{9,1},... | collective-permute-start | bytes 3145736 | tf_op jit(solution)/shard_map/ppermute | solution.py:50
  (17 other events, 83.3 us)

commit v9 on v8

--- a/solution.py
+++ b/solution.py
@@ -50,7 +50,8 @@
     return lax.ppermute(value, ("ctx", "ch"), pairs)
 
 
-def tree_allreduce(value, plan):
+def tree_allreduce(value, plan, fillers=None, state=None):
+    fillers = fillers or {}
     sizes = (lax.axis_size("ctx"), lax.axis_size("ch"))
     on_second = lax.axis_index("ctx") % 2 == 1
     kept = []
@@ -60,12 +61,16 @@
         offset = bit * half
         keep = lax.dynamic_slice_in_dim(value, offset, half, 0)
         send = lax.dynamic_slice_in_dim(value, half - offset, half, 0)
-        value = keep + split_exchange(send, specs, sizes)
+        received = split_exchange(send, specs, sizes)
+        if len(kept) in fillers:
+            state = fillers[len(kept)](state)
+            received, state = lax.optimization_barrier((received, state))
+        value = keep + received
         kept.append((specs, offset))
     for specs, offset in reversed(kept):
         other = split_exchange(value, specs, sizes)
         value = lax.dynamic_update_slice_in_dim(jnp.concatenate([other, other]), value, offset, 0)
-    return value
+    return value, state
 
 
 FACTOR_ROUNDS = (
@@ -130,29 +135,39 @@
         window = extended[taps_count - 1 - offset : taps_count - 1 - offset + rows]
         gate_taps.append(jnp.sum(grad_gate_pre * window, axis=0))
     gate_normed, gate_taps, grad_rows = lax.optimization_barrier((gate_normed, gate_taps, grad_rows))
-    grad_mixed = jnp.einsum(
-        "ikc,jk->ijc", grad_rows, factor_one, preferred_element_type=jnp.float32
-    ).reshape(rows, chans)
     one_part = jnp.einsum("ijc,ikc->jk", mixed_in, grad_rows, preferred_element_type=jnp.float32)
-    both_total = tree_allreduce(jnp.concatenate([one_part, two_part]), FACTOR_ROUNDS)
+
+    def fill_mixed(_):
+        return jnp.einsum(
+            "ikc,jk->ijc", grad_rows, factor_one, preferred_element_type=jnp.float32
+        ).reshape(rows, chans)
+
+    def fill_normed(grad_mixed):
+        later_value = shifted(grad_mixed[: taps_count - 1], "ctx", -1)
+        ext_value = jnp.concatenate([grad_mixed, later_value], 0)
+        grad_normed = gate_normed
+        value_taps = []
+        for offset in range(taps_count):
+            grad_normed = grad_normed + conv_taps[0, offset] * ext_value[offset : offset + rows]
+            window = extended[taps_count - 1 - offset : taps_count - 1 - offset + rows]
+            value_taps.append(jnp.sum(grad_mixed * window, axis=0))
+        scaled = grad_normed * norm_gain
+        gain_part = jnp.sum(grad_normed * hat, axis=0)
+        return scaled, jnp.sum(scaled * hat, axis=1), value_taps, gain_part
+
+    def fill_rows(state):
+        scaled, row_part, value_taps, gain_part = state
+        return scaled, tree_psum(row_part, "ch"), value_taps, gain_part
+
+    both_total, (scaled, row_total, value_taps, gain_part) = tree_allreduce(
+        jnp.concatenate([one_part, two_part]),
+        FACTOR_ROUNDS,
+        {1: fill_mixed, 2: fill_normed, 4: fill_rows},
+    )
     one_total, two_total = both_total[: one_part.shape[0]], both_total[one_part.shape[0] :]
-    grad_mixed = lax.optimization_barrier(grad_mixed)
-    later_value = shifted(grad_mixed[: taps_count - 1], "ctx", -1)
-    ext_value = jnp.concatenate([grad_mixed, later_value], 0)
-    grad_normed = gate_normed
-    value_taps = []
-    for offset in range(taps_count):
-        grad_normed = grad_normed + conv_taps[0, offset] * ext_value[offset : offset + rows]
-        window = extended[taps_count - 1 - offset : taps_count - 1 - offset + rows]
-        value_taps.append(jnp.sum(grad_mixed * window, axis=0))
     tap_part = jnp.stack([jnp.stack(value_taps), jnp.stack(gate_taps)])
-    gain_part = jnp.sum(grad_normed * hat, axis=0)
     gain_total, taps_total = tree_psum((gain_part, tap_part), "ctx")
-    scaled = grad_normed * norm_gain
-    row_mean = (
-        tree_psum(jnp.sum(scaled * hat, axis=1), "ch")
-        / WIDTH
-    )
+    row_mean = row_total / WIDTH
     input_grad = (
         (inverse[:, None] * (scaled - hat * row_mean[:, None]))
         .astype(jnp.bfloat16)

time: 492 us -> 486 us (0.988)
  other arithmetic: 83.7 us -> 78.5 us
    ppermute x14, starting transfers between devices: 22.4 us -> 34.3 us  [tree_psum(): lax.ppermute(value, axis, pairs)]
    ppermute x14, starting transfers between devices: 25.7 us -> 16.5 us  [split_exchange(): return lax.ppermute(value, ('ctx', 'ch'), pairs)]
    ppermute x14, waiting for transfers between devices: 31.2 us -> 25.7 us  [split_exchange(): return lax.ppermute(value, ('ctx', 'ch'), pairs)]
    ppermute x14, waiting for transfers between devices: 8.77 us -> 14.1 us  [tree_psum(): lax.ppermute(value, axis, pairs)]
    reduce_sum x1 -> x2, other arithmetic: 24.7 us -> 20.1 us  [the longest x1 11 us: fill_normed(): gain_part = jnp.sum(grad_normed * hat, axis=0)]
    unnamed x64 -> x70, local copies, waits for them, and re-layouts: 23.3 us -> 24 us
  transfers between devices with their start and end apart: 35 -> 35, of which waited for: 21 -> 24; matrix products, arithmetic and copies ran while one was open for 32% -> 32% of each run, Pallas kernels for 0% -> 0%
where the time goes in v9:
time: 486 us; the launch traced here: 477 us
  waiting for transfers between devices  174 us (36%)
  local copies, waits for them, and re-layouts  94.3 us (19%)
  starting transfers between devices  87.1 us (18%)
  other arithmetic  78.5 us (16%)
  matrix products  41.5 us (9%)
    all_to_all x1, waiting for transfers between devices, on_device(): lax.all_to_all(section_one, 'ctx', split_axis=1, concat_axis=0, tiled=True)  48.8 us
    all_to_all x1, waiting for transfers between devices, on_device(): lax.all_to_all(grad_section, 'ctx', split_axis=0, concat_axis=1, tiled=True)  39.4 us
    ppermute x14, starting transfers between devices, tree_psum(): lax.ppermute(value, axis, pairs)  34.3 us
    all_to_all x1, waiting for transfers between devices, on_device(): lax.all_to_all(section_two, 'ctx', split_axis=0, concat_axis=1, tiled=True)  33.5 us
    ppermute x14, waiting for transfers between devices, split_exchange(): return lax.ppermute(value, ('ctx', 'ch'), pairs)  25.7 us
    unnamed x70, local copies, waits for them, and re-layouts  24 us
    ppermute x14, starting transfers between devices, split_exchange(): return lax.ppermute(value, ('ctx', 'ch'), pairs)  16.5 us
    add x1, other arithmetic, on_device(): gate_normed + conv_taps[1, offset] * ext_gate[offset:offset + rows]  16.3 us
  transfers between devices with their start and end apart: 35, of which 24 were waited for; matrix products, arithmetic and copies ran while one was open for 32% of the time, Pallas kernels for 0%

profile of v9, /device:TPU:1, one launch (start us, length us, event | category | flops | bytes accessed | tf_op | source)
XLA Modules:
  0.0 477.4 jit_solution(7839456343286201366)
XLA Ops:
  0.7 4.6 multiply_reduce_fusion.2
  9.1 3.1 collective-permute-start.1
  13.8 3.9 collective-permute-start.2
  19.4 4.4 multiply_convert_fusion.1
  23.9 6.9 %collective-permute-start.3 = (bf16[2,128]{1,0:T(2,128)(2,1)S(1)}, bf16[2,128]{1,0:T(2,128)(2,1)S(1)}, u32[]{:S(2)}, u32[]{:S(2)}) collective-permute-start(bf16[2,128]{1,0:T(2,128)(2,1)S(1)} %slice.78), channel_id=1, source_target_pairs={{0,8},{8,16},{16,24},{24,32},{32,40},{40,48},{48,56},{56,64},{64,7... | collective-permute-start | bytes 1544 | tf_op jit(solution)/shard_map/ppermute | solution.py:16
  31.5 6.5 %fusion.6 = (bf16[16384,128]{1,0:T(8,128)(2,1)}, bf16[16384,128]{1,0:T(8,128)(2,1)S(1)}) fusion(bf16[32,512,128]{2,1,0:T(8,128)(2,1)S(1)} %copy-done.10, bf16[16384,128]{1,0:T(8,128)(2,1)S(1)} %multiply_convert_fusion.1, bf16[2,128]{1,0:T(2,128)(2,1)S(1)} %collective-permute-done.3, f32[128]{0:T(128)S(1)} %get-tuple-element.93, ...), kind=kLoop, calls=%fused_computation.24 | loop fusion | flops 44040192 | bytes 16779264 | tf_op jit(solution)/shard_map/convert_element_type | solution.py:110
  38.0 3.0 fusion.11
  43.1 4.4 convert_bitcast_fusion.2
  47.5 8.0 %copy.41 = bf16[32,512,128]{2,0,1:T(8,128)(2,1)} copy(bf16[32,512,128]{1,2,0:T(8,128)(2,1)} %convert_bitcast_fusion.2) | data formatting | bytes 8388608 | tf_op jit(solution)/shard_map/convert_element_type | solution.py:109
  55.5 7.2 %all-to-all-start = ((bf16[32,512,128]{2,0,1:T(8,128)(2,1)}), bf16[32,512,128]{2,0,1:T(8,128)(2,1)}, u32[]{:S(2)}, u32[]{:S(2)}) async-start(bf16[32,512,128]{2,0,1:T(8,128)(2,1)} %copy.41), calls=%async_computation | async-start | bytes 8388608 | tf_op jit(solution)/shard_map/all_to_all | solution.py:111
  62.7 6.9 %copy.48 = bf16[32,512,128]{2,0,1:T(8,128)(2,1)} copy(bf16[32,512,128]{2,1,0:T(8,128)(2,1)} %bitcast.107) | data formatting | bytes 8388608 | tf_op jit(solution)/shard_map/reshape | solution.py:110
  69.6 48.8 %all-to-all-done = bf16[32,512,128]{2,0,1:T(8,128)(2,1)} async-done(((bf16[32,512,128]{2,0,1:T(8,128)(2,1)}), bf16[32,512,128]{2,0,1:T(8,128)(2,1)}, u32[]{:S(2)}, u32[]{:S(2)}) %all-to-all-start) | async-done | bytes 4194336 | tf_op jit(solution)/shard_map/all_to_all | solution.py:111
  118.4 4.8 %all-to-all-start.2 = ((bf16[32,512,128]{2,0,1:T(8,128)(2,1)}), bf16[32,512,128]{2,0,1:T(8,128)(2,1)}, u32[]{:S(2)}, u32[]{:S(2)}) async-start(bf16[32,512,128]{2,0,1:T(8,128)(2,1)} %copy.48), calls=%async_computation.2 | async-start | bytes 8388608 | tf_op jit(solution)/shard_map/all_to_all | solution.py:118
  123.2 7.5 %copy.44 = bf16[512,32,128]{0,2,1:T(8,128)(2,1)} copy(bf16[512,32,128]{2,1,0:T(8,128)(2,1)} %param.12) | data formatting | bytes 8388608 | tf_op args[5]
  130.7 3.8 copy.42
  135.7 4.3 copy.43
  140.0 10.0 %copy.45 = f32[512,32,128]{0,2,1:T(8,128)} copy(f32[512,32,128]{2,1,0:T(8,128)} %bitcast.104) | data formatting | bytes 16777216 | tf_op jit(solution)/shard_map/convert_element_type | solution.py:113
  150.0 8.9 %convert_bitcast_fusion.1 = bf16[512,32,128]{0,2,1:T(8,128)(2,1)} fusion(bf16[512,512]{1,0:T(8,128)(2,1)S(1)} %copy-done, f32[512,32,128]{0,2,1:T(8,128)} %copy.45, bf16[512,32,128]{0,2,1:T(8,128)(2,1)} %copy.44), kind=kOutput, calls=%fused_computation.61 | convolution fusion | flops 2155872256 | bytes 17301504 | tf_op jit(solution)/shard_map/ijc,ik->kjc/dot_general | solution.py:114
  158.9 8.0 %copy.46 = bf16[512,32,128]{2,1,0:T(8,128)(2,1)} copy(bf16[512,32,128]{0,2,1:T(8,128)(2,1)} %convert_bitcast_fusion.1) | data formatting | bytes 8388608 | tf_op jit(solution)/shard_map/convert_element_type | solution.py:116
  166.9 12.1 %all-to-all-done.2 = bf16[32,512,128]{2,0,1:T(8,128)(2,1)} async-done(((bf16[32,512,128]{2,0,1:T(8,128)(2,1)}), bf16[32,512,128]{2,0,1:T(8,128)(2,1)}, u32[]{:S(2)}, u32[]{:S(2)}) %all-to-all-start.2) | async-done | bytes 4194336 | tf_op jit(solution)/shard_map/all_to_all | solution.py:118
  178.9 5.4 %all-to-all-start.1 = ((bf16[512,32,128]{2,1,0:T(8,128)(2,1)}), bf16[512,32,128]{2,1,0:T(8,128)(2,1)}, u32[]{:S(2)}, u32[]{:S(2)}) async-start(bf16[512,32,128]{2,1,0:T(8,128)(2,1)} %copy.46), calls=%async_computation.1 | async-start | bytes 8388608 | tf_op jit(solution)/shard_map/all_to_all | solution.py:117
  184.4 4.1 copy.50
  188.5 9.0 %fusion.33 = f32[512,512]{1,0:T(8,128)} fusion(bf16[512,32,128]{2,1,0:T(8,128)(2,1)S(1)} %bitcast.102, f32[512,32,128]{0,2,1:T(8,128)} %copy.45, bf16[512,32,128]{0,2,1:T(8,128)(2,1)S(1)} %copy-done.6), kind=kOutput, calls=%fused_computation.74 | convolution fusion | flops 2153775104 | bytes 17825792 | tf_op jit(solution)/shard_map/ijc,kjc->ik/dot_general | solution.py:124
  197.5 9.0 %fusion.27 = (bf16[512,32,128]{0,2,1:T(8,128)(2,1)}, bf16[512,32,128]{0,2,1:T(8,128)(2,1)}) fusion(f32[512,32,128]{0,2,1:T(8,128)S(1)} %bitcast.96, bf16[512,32,128]{0,2,1:T(8,128)(2,1)S(1)} %copy-done.6, bf16[512,512]{1,0:T(8,128)(2,1)S(1)} %copy-done, bf16[512,32,128]{2,1,0:T(8,128)(2,1)S(1)} %bitcast.103), kind=kOutput, calls=%fused_computation.50 | convolution fusion | flops 2157969408 | bytes 25690112 | tf_op jit(solution)/shard_map/kjc,ik->ijc/dot_general | solution.py:119
  206.5 33.5 %all-to-all-done.1 = bf16[512,32,128]{2,1,0:T(8,128)(2,1)} async-done(((bf16[512,32,128]{2,1,0:T(8,128)(2,1)}), bf16[512,32,128]{2,1,0:T(8,128)(2,1)}, u32[]{:S(2)}, u32[]{:S(2)}) %all-to-all-start.1) | async-done | bytes 4194336 | tf_op jit(solution)/shard_map/all_to_all | solution.py:117
  240.1 3.6 copy.47
  244.8 8.4 %fusion.22 = (f32[128]{0:T(128)S(1)}, f32[128]{0:T(128)S(1)}, f32[128]{0:T(128)S(1)}, f32[16384,128]{1,0:T(8,128)S(1)}) fusion(bf16[16384,128]{1,0:T(8,128)(2,1)S(1)} %copy-done.3, bf16[2,128]{1,0:T(2,128)(2,1)S(1)} %collective-permute-done.3, bf16[16384,128]{1,0:T(8,128)(2,1)S(1)} %copy-done.5, f32[128]{0:T(128)S(1)} %get-tuple-element.93, ...), kind=kLoop, calls=%fused_computation.40 | loop fusion | flops 54525568 | bytes 25169408 | tf_op jit(solution)/shard_map/reduce_sum | solution.py:136
  253.2 3.3 copy-done.8
  259.0 7.9 %copy.54 = bf16[512,32,128]{2,1,0:T(8,128)(2,1)} copy(bf16[512,32,128]{0,2,1:T(8,128)(2,1)} %get-tuple-element.31) | data formatting | bytes 8388608 | tf_op jit(solution)/shard_map/optimization_barrier | solution.py:125
  266.9 5.9 %all-to-all-start.3 = ((bf16[512,32,128]{2,1,0:T(8,128)(2,1)}), bf16[512,32,128]{2,1,0:T(8,128)(2,1)}, u32[]{:S(2)}, u32[]{:S(2)}) async-start(bf16[512,32,128]{2,1,0:T(8,128)(2,1)} %copy.54), calls=%async_computation.3 | async-start | bytes 8388608 | tf_op jit(solution)/shard_map/all_to_all | solution.py:126
  272.8 16.3 %fusion.3 = f32[16384,128]{1,0:T(8,128)} fusion(f32[16384,128]{1,0:T(8,128)} %copy-done.8, f32[2,128]{1,0:T(2,128)S(1)} %collective-permute-done.4, f32[128]{0:T(128)S(1)} %get-tuple-element.93, f32[128]{0:T(128)S(1)} %copy-done.20, f32[128]{0:T(128)S(1)} %get-tuple-element.90), kind=kLoop, calls=%fused_computation.21 | loop fusion | flops 14680064 | bytes 16779776 | tf_op jit(solution)/shard_map/add | solution.py:134
  289.1 39.4 %all-to-all-done.3 = bf16[512,32,128]{2,1,0:T(8,128)(2,1)} async-done(((bf16[512,32,128]{2,1,0:T(8,128)(2,1)}), bf16[512,32,128]{2,1,0:T(8,128)(2,1)}, u32[]{:S(2)}, u32[]{:S(2)}) %all-to-all-start.3) | async-done | bytes 4194336 | tf_op jit(solution)/shard_map/all_to_all | solution.py:126
  328.5 3.6 copy.55
  343.0 7.9 %convolution_bitcast_fusion = f32[32,512,128]{1,2,0:T(8,128)} fusion(bf16[32,512,128]{2,1,0:T(8,128)(2,1)} %bitcast.106, bf16[512,512]{1,0:T(8,128)(2,1)S(1)} %copy-done.16), kind=kOutput, calls=%fused_computation.68 | convolution fusion | flops 2147483648 | bytes 13107200 | tf_op jit(solution)/shard_map/ikc,jk->ijc/dot_general | solution.py:141
  350.9 9.0 %copy.57 = f32[32,512,128]{2,1,0:T(8,128)} copy(f32[32,512,128]{1,2,0:T(8,128)} %convolution_bitcast_fusion) | data formatting | bytes 16777216 | tf_op jit(solution)/shard_map/ikc,jk->ijc/transpose | solution.py:141
  360.7 3.5 collective-permute-start.8
  365.4 9.0 %fusion.23 = (f32[128]{0:T(128)S(1)}, f32[128]{0:T(128)S(1)}, f32[128]{0:T(128)S(1)}, f32[16386,128]{1,0:T(8,128)S(1)}) fusion(f32[16384,128]{1,0:T(8,128)} %bitcast.98, bf16[16384,128]{1,0:T(8,128)(2,1)} %copy-done.2, bf16[2,128]{1,0:T(2,128)(2,1)S(1)} %collective-permute-done.3, bf16[16384,128]{1,0:T(8,128)(2,1)} %copy-done.4), kind=kLoop, calls=%fused_computation.41 | loop fusion | flops 25165440 | bytes 25167872 | tf_op jit(solution)/shard_map/reduce_sum | solution.py:153
  375.1 11.0 %multiply_reduce_fusion = (f32[128]{0:T(128)S(1)}, f32[16384]{0:T(1024)S(1)}, f32[16384,128]{1,0:T(8,128)}) fusion(bf16[32,512,128]{2,1,0:T(8,128)(2,1)S(1)} %copy-done.7, f32[16384]{0:T(1024)S(1)} %copy-done.18, f32[128]{0:T(128)S(1)} %copy-done.28, f32[16386,128]{1,0:T(8,128)S(1)} %constant_dynamic-update-slice_fusion, f32[128]{0:T(128)S(1)} %copy-done.24, ...), kind=kLoop, calls=%fused_computation.53 | loop fusion | flops 27246464 | bytes 46270976 | tf_op jit(solution)/shard_map/reduce_sum | solution.py:155
  389.8 3.1 collective-permute-start.12
  394.6 3.4 collective-permute-start.13
  402.7 3.2 collective-permute-done.14
  405.9 3.0 collective-permute-start.15
  415.3 3.2 collective-permute-done.17
  422.5 4.8 %collective-permute-done.19 = f32[64,512]{1,0:T(8,128)S(1)} collective-permute-done((f32[64,512]{1,0:T(8,128)S(1)}, f32[64,512]{1,0:T(8,128)S(1)}, u32[]{:S(2)}, u32[]{:S(2)}) %collective-permute-start.19) | collective-permute-done | bytes 131104 | tf_op jit(solution)/shard_map/ppermute | solution.py:50
  428.5 12.2 %collective-permute-start.27 = (f32[2,3,128]{2,1,0:T(4,128)S(1)}, f32[2,3,128]{2,1,0:T(4,128)S(1)}, u32[]{:S(2)}, u32[]{:S(2)}) collective-permute-start(f32[2,3,128]{2,1,0:T(4,128)S(1)} %pad_maximum_fusion.9), channel_id=1, source_target_pairs={{0,8},{8,0},{16,24},{24,16},{32,40},{40,32},{48,56},{56,48},{64,72... | collective-permute-start | bytes 9224 | tf_op jit(solution)/shard_map/ppermute | solution.py:24
  442.0 7.8 %copy.59 = bf16[512,32,128]{2,1,0:T(8,128)(2,1)} copy(bf16[512,32,128]{0,2,1:T(8,128)(2,1)} %get-tuple-element.84) | data formatting | bytes 8388608
  456.4 5.2 %collective-permute-done.21 = f32[256,512]{1,0:T(8,128)S(1)} collective-permute-done((f32[256,512]{1,0:T(8,128)S(1)}, f32[256,512]{1,0:T(8,128)S(1)}, u32[]{:S(2)}, u32[]{:S(2)}) %collective-permute-start.21) | collective-permute-done | bytes 524320 | tf_op jit(solution)/shard_map/ppermute | solution.py:50
  463.8 8.1 %multiply_convert_fusion = bf16[16384,128]{1,0:T(8,128)(2,1)} fusion(f32[16384,128]{1,0:T(8,128)} %get-tuple-element.44, bf16[32,512,128]{2,1,0:T(8,128)(2,1)} %param.7, f32[16384]{0:T(1024)S(1)} %broadcast_multiply_fusion.1, f32[16384]{0:T(1024)S(1)} %copy-done.18), kind=kLoop, calls=%fused_computation.52 | loop fusion | flops 12582912 | bytes 16908288 | tf_op jit(solution)/shard_map/convert_element_type | solution.py:173
  (172 shorter events, 64.4 us)
Async XLA Ops:
  0.6 149.4 %copy-start = (bf16[512,512]{1,0:T(8,128)(2,1)S(1)}, bf16[512,512]{1,0:T(8,128)(2,1)}, u32[]{:S(2)}) copy-start(bf16[512,512]{1,0:T(8,128)(2,1)} %param.11) | copy-start | bytes 1572868
  0.6 30.2 %copy-start.27 = (f32[2,3,128]{2,0,1:T(2,128)S(1)}, f32[2,3,128]{2,0,1:T(2,128)}, u32[]{:S(2)}) copy-start(f32[2,3,128]{2,0,1:T(2,128)} %param.9) | copy-start | bytes 9220
  0.7 30.8 %copy-start.10 = (bf16[32,512,128]{2,1,0:T(8,128)(2,1)S(1)}, bf16[32,512,128]{2,1,0:T(8,128)(2,1)}, u32[]{:S(2)}) copy-start(bf16[32,512,128]{2,1,0:T(8,128)(2,1)} %param.13) | copy-start | bytes 12582916
  5.3 3.8 collective-permute-start
  9.1 4.7 collective-permute-start.1
  13.8 5.6 %collective-permute-start.2 = (f32[16384]{0:T(1024)S(1)}, f32[16384]{0:T(1024)S(1)}, u32[]{:S(2)}, u32[]{:S(2)}) collective-permute-start(f32[16384]{0:T(1024)S(1)} %add.193), channel_id=1, source_target_pairs={{0,4},{1,5},{2,6},{3,7},{4,0},{5,1},{6,2},{7,3},{8,12},{9,13},{10,... | collective-permute-start | bytes 196616 | tf_op jit(solution)/shard_map/ppermute | solution.py:24
  19.4 12.1 %copy-start.17 = (f32[16384]{0:T(1024)}, f32[16384]{0:T(1024)S(1)}, u32[]{:S(2)}) copy-start(f32[16384]{0:T(1024)S(1)} %add_rsqrt_fusion) | copy-start | bytes 196612
  23.8 14.2 %copy-start.2 = (bf16[16384,128]{1,0:T(8,128)(2,1)}, bf16[16384,128]{1,0:T(8,128)(2,1)S(1)}, u32[]{:S(2)}) copy-start(bf16[16384,128]{1,0:T(8,128)(2,1)S(1)} %multiply_convert_fusion.1) | copy-start | bytes 12582916
  23.9 7.6 %collective-permute-start.3 = (bf16[2,128]{1,0:T(2,128)(2,1)S(1)}, bf16[2,128]{1,0:T(2,128)(2,1)S(1)}, u32[]{:S(2)}, u32[]{:S(2)}) collective-permute-start(bf16[2,128]{1,0:T(2,128)(2,1)S(1)} %slice.78), channel_id=1, source_target_pairs={{0,8},{8,16},{16,24},{24,32},{32,40},{40,48},{48,56},{56,64},{64,7... | collective-permute-start | bytes 1544 | tf_op jit(solution)/shard_map/ppermute | solution.py:16
  55.5 62.9 %all-to-all-start = ((bf16[32,512,128]{2,0,1:T(8,128)(2,1)}), bf16[32,512,128]{2,0,1:T(8,128)(2,1)}, u32[]{:S(2)}, u32[]{:S(2)}) async-start(bf16[32,512,128]{2,0,1:T(8,128)(2,1)} %copy.41), calls=%async_computation | async-start | bytes 8388608 | tf_op jit(solution)/shard_map/all_to_all | solution.py:111
  118.4 60.5 %all-to-all-start.2 = ((bf16[32,512,128]{2,0,1:T(8,128)(2,1)}), bf16[32,512,128]{2,0,1:T(8,128)(2,1)}, u32[]{:S(2)}, u32[]{:S(2)}) async-start(bf16[32,512,128]{2,0,1:T(8,128)(2,1)} %copy.48), calls=%async_computation.2 | async-start | bytes 8388608 | tf_op jit(solution)/shard_map/all_to_all | solution.py:118
  178.9 61.1 %all-to-all-start.1 = ((bf16[512,32,128]{2,1,0:T(8,128)(2,1)}), bf16[512,32,128]{2,1,0:T(8,128)(2,1)}, u32[]{:S(2)}, u32[]{:S(2)}) async-start(bf16[512,32,128]{2,1,0:T(8,128)(2,1)} %copy.46), calls=%async_computation.1 | async-start | bytes 8388608 | tf_op jit(solution)/shard_map/all_to_all | solution.py:117
  184.4 13.2 %slice-start = ((s8[8388608]{0:T(1024)(128)(4,1)}), s8[4194304]{0:T(1024)(128)(4,1)S(1)}, s32[]{:S(2)}) async-start(s8[8388608]{0:T(1024)(128)(4,1)} %bitcast.95), calls=%async_computation.4 | async-start | bytes 8388608
  206.5 37.1 %copy-start.20 = (f32[128]{0:T(128)S(1)}, f32[128]{0:T(128)}, u32[]{:S(2)}) copy-start(f32[128]{0:T(128)} %copy-done.19) | copy-start | bytes 1540
  256.5 16.3 %collective-permute-start.4 = (f32[2,128]{1,0:T(2,128)S(1)}, f32[2,128]{1,0:T(2,128)S(1)}, u32[]{:S(2)}, u32[]{:S(2)}) collective-permute-start(f32[2,128]{1,0:T(2,128)S(1)} %slice.81), channel_id=1, source_target_pairs={{8,0},{16,8},{24,16},{32,24},{40,32},{48,40},{56,48},{64,56},{72,6... | collective-permute-start | bytes 3080 | tf_op jit(solution)/shard_map/ppermute | solution.py:16
  266.9 61.5 %all-to-all-start.3 = ((bf16[512,32,128]{2,1,0:T(8,128)(2,1)}), bf16[512,32,128]{2,1,0:T(8,128)(2,1)}, u32[]{:S(2)}, u32[]{:S(2)}) async-start(bf16[512,32,128]{2,1,0:T(8,128)(2,1)} %copy.54), calls=%async_computation.3 | async-start | bytes 8388608 | tf_op jit(solution)/shard_map/all_to_all | solution.py:126
  335.9 3.2 collective-permute-start.5
  341.8 18.2 %collective-permute-start.6 = (f32[256,512]{1,0:T(8,128)S(1)}, f32[256,512]{1,0:T(8,128)S(1)}, u32[]{:S(2)}, u32[]{:S(2)}) collective-permute-start(f32[256,512]{1,0:T(8,128)S(1)} %constant_dynamic-slice_fusion.5), channel_id=1, source_target_pairs={{0,16},{1,17},{2,18},{3,19},{4,20},{5,21},{6,22},{7,23},{8,9},{9,8... | collective-permute-start | bytes 1572872 | tf_op jit(solution)/shard_map/ppermute | solution.py:50
  350.9 13.3 %copy-start.15 = (f32[512,512]{1,0:T(8,128)S(1)}, f32[512,512]{1,0:T(8,128)}, u32[]{:S(2)}) copy-start(f32[512,512]{1,0:T(8,128)} %copy-done.14) | copy-start | bytes 3145732
  360.7 13.7 %collective-permute-start.8 = (f32[2,128]{1,0:T(2,128)S(1)}, f32[2,128]{1,0:T(2,128)S(1)}, u32[]{:S(2)}, u32[]{:S(2)}) collective-permute-start(f32[2,128]{1,0:T(2,128)S(1)} %slice.73), channel_id=1, source_target_pairs={{8,0},{16,8},{24,16},{32,24},{40,32},{48,40},{56,48},{64,56},{72,6... | collective-permute-start | bytes 3080 | tf_op jit(solution)/shard_map/ppermute | solution.py:16
  364.4 10.7 %copy-start.7 = (bf16[32,512,128]{2,1,0:T(8,128)(2,1)S(1)}, bf16[32,512,128]{2,1,0:T(8,128)(2,1)}, u32[]{:S(2)}) copy-start(bf16[32,512,128]{2,1,0:T(8,128)(2,1)} %param.7) | copy-start | bytes 12582916
  364.4 10.7 %copy-start.18 = (f32[16384]{0:T(1024)S(1)}, f32[16384]{0:T(1024)}, u32[]{:S(2)}) copy-start(f32[16384]{0:T(1024)} %copy-done.17) | copy-start | bytes 196612
  364.4 10.6 %copy-start.22 = (f32[128]{0:T(128)S(1)}, f32[128]{0:T(128)}, u32[]{:S(2)}) copy-start(f32[128]{0:T(128)} %copy-done.21) | copy-start | bytes 1540
  364.4 10.6 %copy-start.24 = (f32[128]{0:T(128)S(1)}, f32[128]{0:T(128)}, u32[]{:S(2)}) copy-start(f32[128]{0:T(128)} %copy-done.23) | copy-start | bytes 1540
  364.5 21.7 %collective-permute-start.7 = (f32[128,512]{1,0:T(8,128)S(1)}, f32[128,512]{1,0:T(8,128)S(1)}, u32[]{:S(2)}, u32[]{:S(2)}) collective-permute-start(f32[128,512]{1,0:T(8,128)S(1)} %constant_dynamic-slice_fusion.4), channel_id=1, source_target_pairs={{0,1},{1,0},{2,3},{3,2},{4,5},{5,4},{6,7},{7,6},{8,24},{9,25},{10,... | collective-permute-start | bytes 786440 | tf_op jit(solution)/shard_map/ppermute | solution.py:50
  386.1 3.6 collective-permute-start.11
  387.4 10.6 %collective-permute-start.9 = (f32[64,512]{1,0:T(8,128)S(1)}, f32[64,512]{1,0:T(8,128)S(1)}, u32[]{:S(2)}, u32[]{:S(2)}) collective-permute-start(f32[64,512]{1,0:T(8,128)S(1)} %constant_dynamic-slice_fusion.3), channel_id=1, source_target_pairs={{0,64},{1,65},{2,66},{3,67},{4,68},{5,69},{6,70},{7,71},{8,40},{9,... | collective-permute-start | bytes 393224 | tf_op jit(solution)/shard_map/ppermute | solution.py:50
  389.8 4.8 %collective-permute-start.12 = (f32[16384]{0:T(1024)S(1)}, f32[16384]{0:T(1024)S(1)}, u32[]{:S(2)}, u32[]{:S(2)}) collective-permute-start(f32[16384]{0:T(1024)S(1)} %add.225), channel_id=1, source_target_pairs={{0,2},{1,3},{2,0},{3,1},{4,6},{5,7},{6,4},{7,5},{8,10},{9,11},{10,... | collective-permute-start | bytes 196616 | tf_op jit(solution)/shard_map/ppermute | solution.py:24
  394.6 5.0 %collective-permute-start.13 = (f32[16384]{0:T(1024)S(1)}, f32[16384]{0:T(1024)S(1)}, u32[]{:S(2)}, u32[]{:S(2)}) collective-permute-start(f32[16384]{0:T(1024)S(1)} %add.226), channel_id=1, source_target_pairs={{0,4},{1,5},{2,6},{3,7},{4,0},{5,1},{6,2},{7,3},{8,12},{9,13},{10,... | collective-permute-start | bytes 196616 | tf_op jit(solution)/shard_map/ppermute | solution.py:24
  398.0 3.5 collective-permute-start.10
  401.5 4.3 collective-permute-start.14
  405.9 4.2 collective-permute-start.15
  410.1 4.1 collective-permute-start.16
  414.2 4.3 collective-permute-start.17
  418.5 3.5 collective-permute-start.18
  422.0 5.4 %collective-permute-start.19 = (f32[64,512]{1,0:T(8,128)S(1)}, f32[64,512]{1,0:T(8,128)S(1)}, u32[]{:S(2)}, u32[]{:S(2)}) collective-permute-start(f32[64,512]{1,0:T(8,128)S(1)} %constant_dynamic-update-slice_fusion.6), channel_id=1, source_target_pairs={{0,64},{1,65},{2,66},{3,67},{4,68},{5,69},{6,70},{7,71},{8,40},{9,... | collective-permute-start | bytes 393224 | tf_op jit(solution)/shard_map/ppermute | solution.py:50
  427.4 25.7 %collective-permute-start.20 = (f32[128,512]{1,0:T(8,128)S(1)}, f32[128,512]{1,0:T(8,128)S(1)}, u32[]{:S(2)}, u32[]{:S(2)}) collective-permute-start(f32[128,512]{1,0:T(8,128)S(1)} %constant_dynamic-update-slice_fusion.5), channel_id=1, source_target_pairs={{0,1},{1,0},{2,3},{3,2},{4,5},{5,4},{6,7},{7,6},{8,24},{9,25},{10,... | collective-permute-start | bytes 786440 | tf_op jit(solution)/shard_map/ppermute | solution.py:50
  428.5 23.6 %collective-permute-start.27 = (f32[2,3,128]{2,1,0:T(4,128)S(1)}, f32[2,3,128]{2,1,0:T(4,128)S(1)}, u32[]{:S(2)}, u32[]{:S(2)}) collective-permute-start(f32[2,3,128]{2,1,0:T(4,128)S(1)} %pad_maximum_fusion.9), channel_id=1, source_target_pairs={{0,8},{8,0},{16,24},{24,16},{32,40},{40,32},{48,56},{56,48},{64,72... | collective-permute-start | bytes 9224 | tf_op jit(solution)/shard_map/ppermute | solution.py:24
  440.7 1.2 collective-permute-start.23
  441.9 8.0 %collective-permute-start.24 = (f32[128]{0:T(128)S(1)}, f32[128]{0:T(128)S(1)}, u32[]{:S(2)}, u32[]{:S(2)}) collective-permute-start(f32[128]{0:T(128)S(1)} %add.238), channel_id=1, source_target_pairs={{0,16},{8,24},{16,0},{24,8},{32,48},{40,56},{48,32},{56,40},{64,80... | collective-permute-start | bytes 1544 | tf_op jit(solution)/shard_map/ppermute | solution.py:24
  449.9 4.0 collective-permute-start.25
  452.2 2.8 collective-permute-start.28
  453.2 8.4 %collective-permute-start.21 = (f32[256,512]{1,0:T(8,128)S(1)}, f32[256,512]{1,0:T(8,128)S(1)}, u32[]{:S(2)}, u32[]{:S(2)}) collective-permute-start(f32[256,512]{1,0:T(8,128)S(1)} %constant_dynamic-update-slice_fusion.4), channel_id=1, source_target_pairs={{0,16},{1,17},{2,18},{3,19},{4,20},{5,21},{6,22},{7,23},{8,9},{9,8... | collective-permute-start | bytes 1572872 | tf_op jit(solution)/shard_map/ppermute | solution.py:50
  453.9 18.3 %collective-permute-start.26 = (f32[128]{0:T(128)S(1)}, f32[128]{0:T(128)S(1)}, u32[]{:S(2)}, u32[]{:S(2)}) collective-permute-start(f32[128]{0:T(128)S(1)} %add.240), channel_id=1, source_target_pairs={{0,64},{8,72},{16,80},{24,88},{32,96},{40,104},{48,112},{56,120},{... | collective-permute-start | bytes 1544 | tf_op jit(solution)/shard_map/ppermute | solution.py:24
  455.0 16.9 %collective-permute-start.29 = (f32[2,3,128]{2,1,0:T(4,128)S(1)}, f32[2,3,128]{2,1,0:T(4,128)S(1)}, u32[]{:S(2)}, u32[]{:S(2)}) collective-permute-start(f32[2,3,128]{2,1,0:T(4,128)S(1)} %fusion.52), channel_id=1, source_target_pairs={{0,32},{8,40},{16,48},{24,56},{32,0},{40,8},{48,16},{56,24},{64,96... | collective-permute-start | bytes 9224 | tf_op jit(solution)/shard_map/ppermute | solution.py:24
  461.8 13.2 %collective-permute-start.22 = (f32[512,512]{1,0:T(8,128)S(1)}, f32[512,512]{1,0:T(8,128)S(1)}, u32[]{:S(2)}, u32[]{:S(2)}) collective-permute-start(f32[512,512]{1,0:T(8,128)S(1)} %constant_dynamic-update-slice_fusion.3), channel_id=1, source_target_pairs={{0,8},{1,9},{2,10},{3,11},{4,12},{5,13},{6,14},{7,15},{8,0},{9,1},... | collective-permute-start | bytes 3145736 | tf_op jit(solution)/shard_map/ppermute | solution.py:50
  463.8 13.2 %copy-start.1 = (bf16[512,512]{1,0:T(8,128)(2,1)S(1)}, bf16[512,512]{1,0:T(8,128)(2,1)}, u32[]{:S(2)}) copy-start(bf16[512,512]{1,0:T(8,128)(2,1)} %param.11) | copy-start | bytes 1572868
  471.9 2.5 collective-permute-start.30
  (20 other events, 115.8 us)

commit v10 on v9

--- a/solution.py
+++ b/solution.py
@@ -114,7 +114,6 @@
     section_two = jnp.einsum(
         "ijc,ik->kjc", spectrum, factor_two, preferred_element_type=jnp.float32
     ).astype(jnp.bfloat16)
-    back_rows = lax.all_to_all(section_two, "ctx", split_axis=0, concat_axis=1, tiled=True)
     grad_columns = lax.all_to_all(out_grad, "ctx", split_axis=1, concat_axis=0, tiled=True)
     grad_spec = jnp.einsum(
         "kjc,ik->ijc", grad_columns, factor_two, preferred_element_type=jnp.float32
@@ -122,47 +121,48 @@
     kernel_grad = (grad_spec * columns.astype(jnp.float32)).astype(jnp.bfloat16)
     grad_section = (grad_spec * kern).astype(jnp.bfloat16)
     two_part = jnp.einsum("ijc,kjc->ik", spectrum, grad_columns, preferred_element_type=jnp.float32)
-    back_rows, grad_section, two_part = lax.optimization_barrier((back_rows, grad_section, two_part))
     grad_rows = lax.all_to_all(grad_section, "ctx", split_axis=0, concat_axis=1, tiled=True)
-    back_flat = back_rows.reshape(rows, chans).astype(jnp.float32)
-    grad_gate_pre = cotangent * back_flat * gate * (1.0 - gate)
-    later_gate = shifted(grad_gate_pre[: taps_count - 1], "ctx", -1)
-    ext_gate = jnp.concatenate([grad_gate_pre, later_gate], 0)
-    gate_normed = jnp.zeros((rows, chans), jnp.float32)
-    gate_taps = []
+    grad_rows, section_two, two_part = lax.optimization_barrier((grad_rows, section_two, two_part))
+    back_rows = lax.all_to_all(section_two, "ctx", split_axis=0, concat_axis=1, tiled=True)
+    one_part = jnp.einsum("ijc,ikc->jk", mixed_in, grad_rows, preferred_element_type=jnp.float32)
+    grad_mixed = jnp.einsum(
+        "ikc,jk->ijc", grad_rows, factor_one, preferred_element_type=jnp.float32
+    ).reshape(rows, chans)
+    later_value = shifted(grad_mixed[: taps_count - 1], "ctx", -1)
+    ext_value = jnp.concatenate([grad_mixed, later_value], 0)
+    value_normed = jnp.zeros((rows, chans), jnp.float32)
+    value_taps = []
     for offset in range(taps_count):
-        gate_normed = gate_normed + conv_taps[1, offset] * ext_gate[offset : offset + rows]
+        value_normed = value_normed + conv_taps[0, offset] * ext_value[offset : offset + rows]
         window = extended[taps_count - 1 - offset : taps_count - 1 - offset + rows]
-        gate_taps.append(jnp.sum(grad_gate_pre * window, axis=0))
-    gate_normed, gate_taps, grad_rows = lax.optimization_barrier((gate_normed, gate_taps, grad_rows))
-    one_part = jnp.einsum("ijc,ikc->jk", mixed_in, grad_rows, preferred_element_type=jnp.float32)
-
-    def fill_mixed(_):
-        return jnp.einsum(
-            "ikc,jk->ijc", grad_rows, factor_one, preferred_element_type=jnp.float32
-        ).reshape(rows, chans)
-
-    def fill_normed(grad_mixed):
-        later_value = shifted(grad_mixed[: taps_count - 1], "ctx", -1)
-        ext_value = jnp.concatenate([grad_mixed, later_value], 0)
-        grad_normed = gate_normed
-        value_taps = []
+        value_taps.append(jnp.sum(grad_mixed * window, axis=0))
+    value_normed, value_taps, one_part, back_rows = lax.optimization_barrier(
+        (value_normed, value_taps, one_part, back_rows)
+    )
+
+    def fill_normed(_):
+        back_flat = back_rows.reshape(rows, chans).astype(jnp.float32)
+        grad_gate_pre = cotangent * back_flat * gate * (1.0 - gate)
+        later_gate = shifted(grad_gate_pre[: taps_count - 1], "ctx", -1)
+        ext_gate = jnp.concatenate([grad_gate_pre, later_gate], 0)
+        grad_normed = value_normed
+        gate_taps = []
         for offset in range(taps_count):
-            grad_normed = grad_normed + conv_taps[0, offset] * ext_value[offset : offset + rows]
+            grad_normed = grad_normed + conv_taps[1, offset] * ext_gate[offset : offset + rows]
             window = extended[taps_count - 1 - offset : taps_count - 1 - offset + rows]
-            value_taps.append(jnp.sum(grad_mixed * window, axis=0))
+            gate_taps.append(jnp.sum(grad_gate_pre * window, axis=0))
         scaled = grad_normed * norm_gain
         gain_part = jnp.sum(grad_normed * hat, axis=0)
-        return scaled, jnp.sum(scaled * hat, axis=1), value_taps, gain_part
+        return scaled, jnp.sum(scaled * hat, axis=1), gate_taps, gain_part
 
     def fill_rows(state):
-        scaled, row_part, value_taps, gain_part = state
-        return scaled, tree_psum(row_part, "ch"), value_taps, gain_part
-
-    both_total, (scaled, row_total, value_taps, gain_part) = tree_allreduce(
+        scaled, row_part, gate_taps, gain_part = state
+        return scaled, tree_psum(row_part, "ch"), gate_taps, gain_part
+
+    both_total, (scaled, row_total, gate_taps, gain_part) = tree_allreduce(
         jnp.concatenate([one_part, two_part]),
         FACTOR_ROUNDS,
-        {1: fill_mixed, 2: fill_normed, 4: fill_rows},
+        {1: fill_normed, 3: fill_rows},
     )
     one_total, two_total = both_total[: one_part.shape[0]], both_total[one_part.shape[0] :]
     tap_part = jnp.stack([jnp.stack(value_taps), jnp.stack(gate_taps)])

time: 486 us -> 497 us (1.023)
  local copies, waits for them, and re-layouts: 94.3 us -> 106 us
    all_to_all x1, waiting for transfers between devices: 33.5 us -> 0.01 us  [on_device(): lax.all_to_all(section_two, 'ctx', split_axis=0, concat_axis=1, tiled=True)]
    ppermute x3, waiting for transfers between devices: 0.64 us -> 26.6 us  [shifted(): lax.ppermute(value, axis, [(source, source + steps) for source in range(i...]
    all_to_all x1, waiting for transfers between devices: 12.1 us -> 28.7 us  [on_device(): lax.all_to_all(out_grad, 'ctx', split_axis=1, concat_axis=0, tiled=True)]
    add x1, other arithmetic: 16.3 us -> 7.9 us  [on_device(): value_normed + conv_taps[0, offset] * ext_value[offset:offset + rows]]
    convert_element_type x1 -> x2, local copies, waits for them, and re-layouts: 7.97 us -> 15.1 us  [the longest x1 7.94 us: on_device(): grad_section = (grad_spec * kern).astype(jnp.bfloat16)]
    all_to_all x1, waiting for transfers between devices: 48.8 us -> 42.1 us  [on_device(): lax.all_to_all(section_one, 'ctx', split_axis=1, concat_axis=0, tiled=True)]
    unnamed x70 -> x46, local copies, waits for them, and re-layouts: 24 us -> 29 us
  transfers between devices with their start and end apart: 35 -> 35, of which waited for: 24 -> 21; matrix products, arithmetic and copies ran while one was open for 32% -> 29% of each run, Pallas kernels for 0% -> 0%
where the time goes in v10:
time: 497 us; the launch traced here: 490 us
  waiting for transfers between devices  175 us (35%)
  local copies, waits for them, and re-layouts  106 us (21%)
  starting transfers between devices  86.4 us (17%)
  other arithmetic  74 us (15%)
  matrix products  46.2 us (9%)
    all_to_all x1, waiting for transfers between devices, on_device(): lax.all_to_all(section_one, 'ctx', split_axis=1, concat_axis=0, tiled=True)  42.1 us
    all_to_all x1, waiting for transfers between devices, on_device(): lax.all_to_all(grad_section, 'ctx', split_axis=0, concat_axis=1, tiled=True)  39 us
    ppermute x14, starting transfers between devices, tree_psum(): lax.ppermute(value, axis, pairs)  35.8 us
    unnamed x46, local copies, waits for them, and re-layouts  29 us
    all_to_all x1, waiting for transfers between devices, on_device(): lax.all_to_all(out_grad, 'ctx', split_axis=1, concat_axis=0, tiled=True)  28.7 us
    ppermute x3, waiting for transfers between devices, shifted(): lax.ppermute(value, axis, [(source, source + steps) for source in range(i...  26.6 us
    ppermute x14, waiting for transfers between devices, split_exchange(): return lax.ppermute(value, ('ctx', 'ch'), pairs)  25.4 us
    ppermute x14, starting transfers between devices, split_exchange(): return lax.ppermute(value, ('ctx', 'ch'), pairs)  16.3 us
  transfers between devices with their start and end apart: 35, of which 21 were waited for; matrix products, arithmetic and copies ran while one was open for 29% of the time, Pallas kernels for 0%

profile of v10, /device:TPU:1, one launch (start us, length us, event | category | flops | bytes accessed | tf_op | source)
XLA Modules:
  0.0 489.7 jit_solution(4072191008075064331)
XLA Ops:
  0.6 6.5 %copy.62 = bf16[32,512,128]{1,2,0:T(8,128)(2,1)} copy(bf16[32,512,128]{2,1,0:T(8,128)(2,1)} %param.7) | data formatting | bytes 8388608 | tf_op args[0]
  7.1 3.1 multiply_reduce_fusion.3
  14.1 3.1 collective-permute-start.1
  18.8 3.9 collective-permute-start.2
  22.7 7.1 %copy.63 = f32[32,512,128]{2,1,0:T(8,128)} copy(bf16[32,512,128]{1,2,0:T(8,128)(2,1)} %copy.62) | data formatting | bytes 12582912 | tf_op jit(solution)/shard_map/convert_element_type | solution.py:91
  29.9 5.2 %multiply_convert_fusion.2 = bf16[16384,128]{1,0:T(8,128)(2,1)S(1)} fusion(f32[32,512,128]{2,1,0:T(8,128)} %copy.63, f32[128]{0:T(128)S(1)} %copy-done.15, f32[16384]{0:T(1024)S(1)} %add_rsqrt_fusion), kind=kLoop, calls=%fused_computation.59 | loop fusion | flops 6291456 | bytes 12648960 | tf_op jit(solution)/shard_map/convert_element_type | solution.py:95
  35.1 6.5 %collective-permute-start.3 = (bf16[2,128]{1,0:T(2,128)(2,1)S(1)}, bf16[2,128]{1,0:T(2,128)(2,1)S(1)}, u32[]{:S(2)}, u32[]{:S(2)}) collective-permute-start(bf16[2,128]{1,0:T(2,128)(2,1)S(1)} %slice.78), channel_id=1, source_target_pairs={{0,8},{8,16},{16,24},{24,32},{32,40},{40,48},{48,56},{56,64},{64,7... | collective-permute-start | bytes 1544 | tf_op jit(solution)/shard_map/ppermute | solution.py:16
  42.3 4.7 fusion.21
  49.0 4.4 convert_bitcast_fusion.2
  53.4 7.9 %copy.72 = bf16[32,512,128]{2,0,1:T(8,128)(2,1)} copy(bf16[32,512,128]{1,2,0:T(8,128)(2,1)} %convert_bitcast_fusion.2) | data formatting | bytes 8388608 | tf_op jit(solution)/shard_map/convert_element_type | solution.py:109
  61.3 6.5 %all-to-all-start.2 = ((bf16[32,512,128]{2,0,1:T(8,128)(2,1)}), bf16[32,512,128]{2,0,1:T(8,128)(2,1)}, u32[]{:S(2)}, u32[]{:S(2)}) async-start(bf16[32,512,128]{2,0,1:T(8,128)(2,1)} %copy.72), calls=%async_computation.2 | async-start | bytes 8388608 | tf_op jit(solution)/shard_map/all_to_all | solution.py:111
  67.8 8.8 %fusion.10 = bf16[16384,128]{1,0:T(8,128)(2,1)S(1)} fusion(bf16[32,512,128]{2,1,0:T(8,128)(2,1)} %param.13, bf16[16384,128]{1,0:T(8,128)(2,1)} %copy-done.3, bf16[2,128]{1,0:T(2,128)(2,1)S(1)} %collective-permute-done.3, f32[128]{0:T(128)S(1)} %get-tuple-element.92, bf16[16384,128]{1,0:T(8,128)(2,1)} %get-tuple-element.86, f32[128]{0:T(128)S(1)} %get-tuple-element.93, ...), kind=kLoop, calls=%fused_computation.29 | loop fusion | flops 35651584 | bytes 16779264 | tf_op jit(solution)/shard_map/convert_element_type | solution.py:110
  76.6 4.8 copy.64
  81.4 42.1 %all-to-all-done.2 = bf16[32,512,128]{2,0,1:T(8,128)(2,1)} async-done(((bf16[32,512,128]{2,0,1:T(8,128)(2,1)}), bf16[32,512,128]{2,0,1:T(8,128)(2,1)}, u32[]{:S(2)}, u32[]{:S(2)}) %all-to-all-start.2) | async-done | bytes 4194336 | tf_op jit(solution)/shard_map/all_to_all | solution.py:111
  123.5 5.5 %all-to-all-start = ((bf16[32,512,128]{2,0,1:T(8,128)(2,1)}), bf16[32,512,128]{2,0,1:T(8,128)(2,1)}, u32[]{:S(2)}, u32[]{:S(2)}) async-start(bf16[32,512,128]{2,0,1:T(8,128)(2,1)} %copy.64), calls=%async_computation | async-start | bytes 8388608 | tf_op jit(solution)/shard_map/all_to_all | solution.py:117
  129.0 7.6 %copy.68 = bf16[512,32,128]{0,2,1:T(8,128)(2,1)} copy(bf16[512,32,128]{2,1,0:T(8,128)(2,1)} %param.12) | data formatting | bytes 8388608 | tf_op args[5]
  136.6 3.8 copy.73
  141.6 4.3 copy.74
  145.9 9.9 %copy.75 = f32[512,32,128]{0,2,1:T(8,128)} copy(f32[512,32,128]{2,1,0:T(8,128)} %bitcast.107) | data formatting | bytes 16777216 | tf_op jit(solution)/shard_map/convert_element_type | solution.py:113
  155.8 28.7 %all-to-all-done = bf16[32,512,128]{2,0,1:T(8,128)(2,1)} async-done(((bf16[32,512,128]{2,0,1:T(8,128)(2,1)}), bf16[32,512,128]{2,0,1:T(8,128)(2,1)}, u32[]{:S(2)}, u32[]{:S(2)}) %all-to-all-start) | async-done | bytes 4194336 | tf_op jit(solution)/shard_map/all_to_all | solution.py:117
  184.5 4.1 copy.66
  189.2 11.6 %fusion.29 = (bf16[512,32,128]{0,2,1:T(8,128)(2,1)}, bf16[512,32,128]{0,2,1:T(8,128)(2,1)}) fusion(f32[512,32,128]{0,2,1:T(8,128)S(1)} %copy-done.2, bf16[512,32,128]{0,2,1:T(8,128)(2,1)} %copy.68, bf16[512,512]{1,0:T(8,128)(2,1)S(1)} %copy-done, bf16[512,32,128]{2,1,0:T(8,128)(2,1)S(1)} %bitcast.105), kind=kOutput, calls=%fused_computation.52 | convolution fusion | flops 2157969408 | bytes 25690112 | tf_op jit(solution)/shard_map/kjc,ik->ijc/dot_general | solution.py:118
  200.7 7.9 %copy.69 = bf16[512,32,128]{2,1,0:T(8,128)(2,1)} copy(bf16[512,32,128]{0,2,1:T(8,128)(2,1)} %get-tuple-element.88) | data formatting | bytes 8388608 | tf_op jit(solution)/shard_map/convert_element_type | solution.py:122
  208.7 5.5 %all-to-all-start.1 = ((bf16[512,32,128]{2,1,0:T(8,128)(2,1)}), bf16[512,32,128]{2,1,0:T(8,128)(2,1)}, u32[]{:S(2)}, u32[]{:S(2)}) async-start(bf16[512,32,128]{2,1,0:T(8,128)(2,1)} %copy.69), calls=%async_computation.1 | async-start | bytes 8388608 | tf_op jit(solution)/shard_map/all_to_all | solution.py:124
  214.3 9.0 %convert_bitcast_fusion.1 = bf16[512,32,128]{0,2,1:T(8,128)(2,1)} fusion(bf16[512,512]{1,0:T(8,128)(2,1)S(1)} %copy-done, f32[512,32,128]{0,2,1:T(8,128)} %copy.75, bf16[512,32,128]{0,2,1:T(8,128)(2,1)} %copy.68), kind=kOutput, calls=%fused_computation.65 | convolution fusion | flops 2155872256 | bytes 17301504 | tf_op jit(solution)/shard_map/ijc,ik->kjc/dot_general | solution.py:114
  223.3 7.5 %fusion.35 = f32[512,512]{1,0:T(8,128)S(1)} fusion(bf16[512,32,128]{2,1,0:T(8,128)(2,1)S(1)} %bitcast.106, f32[512,32,128]{0,2,1:T(8,128)} %copy.75, bf16[512,32,128]{0,2,1:T(8,128)(2,1)S(1)} %copy-done.6), kind=kOutput, calls=%fused_computation.74 | convolution fusion | flops 2153775104 | bytes 17825792 | tf_op jit(solution)/shard_map/ijc,kjc->ik/dot_general | solution.py:123
  230.8 39.0 %all-to-all-done.1 = bf16[512,32,128]{2,1,0:T(8,128)(2,1)} async-done(((bf16[512,32,128]{2,1,0:T(8,128)(2,1)}), bf16[512,32,128]{2,1,0:T(8,128)(2,1)}, u32[]{:S(2)}, u32[]{:S(2)}) %all-to-all-start.1) | async-done | bytes 4194336 | tf_op jit(solution)/shard_map/all_to_all | solution.py:124
  269.8 3.6 copy.70
  275.5 3.3 convolution_bitcast_fusion.1
  278.8 7.9 %copy.80 = bf16[512,32,128]{2,1,0:T(8,128)(2,1)} copy(bf16[512,32,128]{0,2,1:T(8,128)(2,1)} %convert_bitcast_fusion.1) | data formatting | bytes 8388608 | tf_op jit(solution)/shard_map/optimization_barrier | solution.py:125
  286.7 5.2 %all-to-all-start.3 = ((bf16[512,32,128]{2,1,0:T(8,128)(2,1)}), bf16[512,32,128]{2,1,0:T(8,128)(2,1)}, u32[]{:S(2)}, u32[]{:S(2)}) async-start(bf16[512,32,128]{2,1,0:T(8,128)(2,1)} %copy.80), calls=%async_computation.3 | async-start | bytes 8388608 | tf_op jit(solution)/shard_map/all_to_all | solution.py:126
  291.9 10.3 %multiply_reduce_fusion.2 = (f32[128]{0:T(128)S(1)}, f32[32,512,128]{1,2,0:T(8,128)}) fusion(f32[128]{0:T(128)S(1)} %copy-done.15, f32[32,512]{1,0:T(8,128)S(1)} %mul.256, bf16[32,512,128]{1,2,0:T(8,128)(2,1)} %copy.62, bf16[32,512,128]{2,1,0:T(8,128)(2,1)} %bitcast.115, bf16[512,512]{1,0:T(8,128)(2,1)S(1)} %copy-done.13), kind=kOutput, calls=%fused_computation.57 | convolution fusion | flops 2162163712 | bytes 17368064 | tf_op jit(solution)/shard_map/ikc,jk->ijc/dot_general | solution.py:128
  302.3 9.0 %copy.79 = f32[32,512,128]{2,1,0:T(8,128)} copy(f32[32,512,128]{1,2,0:T(8,128)} %get-tuple-element.98) | data formatting | bytes 16777216 | tf_op jit(solution)/shard_map/ikc,jk->ijc/transpose | solution.py:128
  314.4 7.0 %fusion.25 = (f32[128]{0:T(128)S(1)}, f32[128]{0:T(128)S(1)}) fusion(bf16[16384,128]{1,0:T(8,128)(2,1)} %copy-done.3, bf16[2,128]{1,0:T(2,128)(2,1)S(1)} %collective-permute-done.3, f32[32,512,128]{2,1,0:T(8,128)} %copy.79, bf16[16384,128]{1,0:T(8,128)(2,1)} %get-tuple-element.86), kind=kLoop, calls=%fused_computation.44 | loop fusion | flops 18874112 | bytes 16778752 | tf_op jit(solution)/shard_map/reduce_sum | solution.py:138
  321.4 20.0 %collective-permute-done.4 = f32[2,128]{1,0:T(2,128)S(1)} collective-permute-done((f32[2,128]{1,0:T(2,128)S(1)}, f32[2,128]{1,0:T(2,128)S(1)}, u32[]{:S(2)}, u32[]{:S(2)}) %collective-permute-start.4) | collective-permute-done | bytes 1056 | tf_op jit(solution)/shard_map/ppermute | solution.py:16
  341.4 7.9 %fusion.7 = f32[16384,128]{1,0:T(8,128)} fusion(f32[16384,128]{1,0:T(8,128)S(1)} %bitcast.104, f32[2,128]{1,0:T(2,128)S(1)} %collective-permute-done.4, f32[128]{0:T(128)S(1)} %get-tuple-element.95, f32[128]{0:T(128)S(1)} %get-tuple-element.96, f32[128]{0:T(128)S(1)} %get-tuple-element.94), kind=kLoop, calls=%fused_computation.26 | loop fusion | flops 14680064 | bytes 16779776 | tf_op jit(solution)/shard_map/add | solution.py:136
  349.3 5.7 %copy.81 = bf16[32,16,32,128]{3,2,1,0:T(8,128)(2,1)} copy(bf16[32,16,32,128]{3,2,0,1:T(8,128)(2,1)} %bitcast.30) | data formatting | bytes 8388608 | tf_op jit(solution)/shard_map/all_to_all | solution.py:126
  357.3 8.7 %fusion.26 = (f32[128]{0:T(128)S(1)}, f32[128]{0:T(128)S(1)}, f32[128]{0:T(128)S(1)}, f32[16384,128]{1,0:T(8,128)S(1)}) fusion(bf16[16384,128]{1,0:T(8,128)(2,1)S(1)} %copy-done.4, bf16[2,128]{1,0:T(2,128)(2,1)S(1)} %collective-permute-done.3, bf16[16384,128]{1,0:T(8,128)(2,1)S(1)} %copy-done.5, f32[128]{0:T(128)S(1)} %get-tuple-element.92, ...), kind=kLoop, calls=%fused_computation.45 | loop fusion | flops 54525568 | bytes 25169408 | tf_op jit(solution)/shard_map/reduce_sum | solution.py:153
  370.7 6.0 %collective-permute-done.7 = f32[2,128]{1,0:T(2,128)S(1)} collective-permute-done((f32[2,128]{1,0:T(2,128)S(1)}, f32[2,128]{1,0:T(2,128)S(1)}, u32[]{:S(2)}, u32[]{:S(2)}) %collective-permute-start.7) | collective-permute-done | bytes 1056 | tf_op jit(solution)/shard_map/ppermute | solution.py:16
  376.7 12.9 %multiply_reduce_fusion = (f32[128]{0:T(128)S(1)}, f32[16384]{0:T(1024)S(1)}, f32[16384,128]{1,0:T(8,128)}) fusion(f32[32,512,128]{2,1,0:T(8,128)S(1)} %bitcast.100, f32[16384]{0:T(1024)S(1)} %add_rsqrt_fusion, f32[128]{0:T(128)S(1)} %copy-done.15, f32[2,128]{1,0:T(2,128)S(1)} %collective-permute-done.7, f32[16384,128]{1,0:T(8,128)S(1)} %get-tuple-element.83, ...), kind=kLoop, calls=%fused_computation.55 | loop fusion | flops 29343616 | bytes 33689088 | tf_op jit(solution)/shard_map/reduce_sum | solution.py:155
  402.1 4.1 collective-permute-done.12
  411.0 3.1 collective-permute-done.14
  427.2 3.0 collective-permute-done.18
  432.0 4.0 collective-permute-done.19
  436.1 13.5 %collective-permute-start.27 = (f32[2,3,128]{2,1,0:T(4,128)S(1)}, f32[2,3,128]{2,1,0:T(4,128)S(1)}, u32[]{:S(2)}, u32[]{:S(2)}) collective-permute-start(f32[2,3,128]{2,1,0:T(4,128)S(1)} %pad_maximum_fusion.10), channel_id=1, source_target_pairs={{0,8},{8,0},{16,24},{24,16},{32,40},{40,32},{48,56},{56,48},{64,72... | collective-permute-start | bytes 9224 | tf_op jit(solution)/shard_map/ppermute | solution.py:24
  451.2 7.8 %copy.83 = bf16[512,32,128]{2,1,0:T(8,128)(2,1)} copy(bf16[512,32,128]{0,2,1:T(8,128)(2,1)} %get-tuple-element.87) | data formatting | bytes 8388608
  466.9 3.7 collective-permute-done.21
  472.7 11.5 %multiply_convert_fusion = bf16[16384,128]{1,0:T(8,128)(2,1)} fusion(f32[16384,128]{1,0:T(8,128)} %get-tuple-element.42, f32[32,512,128]{2,1,0:T(8,128)} %copy.63, f32[16384]{0:T(1024)S(1)} %broadcast_multiply_fusion.1, f32[16384]{0:T(1024)S(1)} %add_rsqrt_fusion), kind=kLoop, calls=%fused_computation.54 | loop fusion | flops 10485760 | bytes 21102592 | tf_op jit(solution)/shard_map/convert_element_type | solution.py:173
  (150 shorter events, 70.6 us)
Async XLA Ops:
  0.6 188.0 %copy-start = (bf16[512,512]{1,0:T(8,128)(2,1)S(1)}, bf16[512,512]{1,0:T(8,128)(2,1)}, u32[]{:S(2)}) copy-start(bf16[512,512]{1,0:T(8,128)(2,1)} %param.11) | copy-start | bytes 1572868
  7.1 22.7 %copy-start.15 = (f32[128]{0:T(128)S(1)}, f32[128]{0:T(128)}, u32[]{:S(2)}) copy-start(f32[128]{0:T(128)} %param.8) | copy-start | bytes 1540
  10.3 3.8 collective-permute-start
  14.1 4.7 collective-permute-start.1
  18.8 11.0 %collective-permute-start.2 = (f32[16384]{0:T(1024)S(1)}, f32[16384]{0:T(1024)S(1)}, u32[]{:S(2)}, u32[]{:S(2)}) collective-permute-start(f32[16384]{0:T(1024)S(1)} %add.193), channel_id=1, source_target_pairs={{0,4},{1,5},{2,6},{3,7},{4,0},{5,1},{6,2},{7,3},{8,12},{9,13},{10,... | collective-permute-start | bytes 196616 | tf_op jit(solution)/shard_map/ppermute | solution.py:24
  29.8 11.8 %copy-start.14 = (f32[2,3,128]{2,0,1:T(2,128)S(1)}, f32[2,3,128]{2,0,1:T(2,128)}, u32[]{:S(2)}) copy-start(f32[2,3,128]{2,0,1:T(2,128)} %param.9) | copy-start | bytes 9220
  35.1 13.9 %copy-start.13 = (bf16[512,512]{1,0:T(8,128)(2,1)S(1)}, bf16[512,512]{1,0:T(8,128)(2,1)}, u32[]{:S(2)}) copy-start(bf16[512,512]{1,0:T(8,128)(2,1)} %param.10) | copy-start | bytes 1572868
  35.1 7.2 %collective-permute-start.3 = (bf16[2,128]{1,0:T(2,128)(2,1)S(1)}, bf16[2,128]{1,0:T(2,128)(2,1)S(1)}, u32[]{:S(2)}, u32[]{:S(2)}) collective-permute-start(bf16[2,128]{1,0:T(2,128)(2,1)S(1)} %slice.78), channel_id=1, source_target_pairs={{0,8},{8,16},{16,24},{24,32},{32,40},{40,48},{48,56},{56,64},{64,7... | collective-permute-start | bytes 1544 | tf_op jit(solution)/shard_map/ppermute | solution.py:16
  61.3 62.2 %all-to-all-start.2 = ((bf16[32,512,128]{2,0,1:T(8,128)(2,1)}), bf16[32,512,128]{2,0,1:T(8,128)(2,1)}, u32[]{:S(2)}, u32[]{:S(2)}) async-start(bf16[32,512,128]{2,0,1:T(8,128)(2,1)} %copy.72), calls=%async_computation.2 | async-start | bytes 8388608 | tf_op jit(solution)/shard_map/all_to_all | solution.py:111
  123.5 61.1 %all-to-all-start = ((bf16[32,512,128]{2,0,1:T(8,128)(2,1)}), bf16[32,512,128]{2,0,1:T(8,128)(2,1)}, u32[]{:S(2)}, u32[]{:S(2)}) async-start(bf16[32,512,128]{2,0,1:T(8,128)(2,1)} %copy.64), calls=%async_computation | async-start | bytes 8388608 | tf_op jit(solution)/shard_map/all_to_all | solution.py:117
  188.6 12.1 %copy-start.7 = (bf16[16,32,32,128]{3,2,1,0:T(8,128)(2,1)}, bf16[16,32,32,128]{3,2,1,0:T(8,128)(2,1)S(1)}, u32[]{:S(2)}) copy-start(bf16[16,32,32,128]{3,2,1,0:T(8,128)(2,1)S(1)} %copy.66) | copy-start | bytes 12582916
  208.7 61.1 %all-to-all-start.1 = ((bf16[512,32,128]{2,1,0:T(8,128)(2,1)}), bf16[512,32,128]{2,1,0:T(8,128)(2,1)}, u32[]{:S(2)}, u32[]{:S(2)}) async-start(bf16[512,32,128]{2,1,0:T(8,128)(2,1)} %copy.69), calls=%async_computation.1 | async-start | bytes 8388608 | tf_op jit(solution)/shard_map/all_to_all | solution.py:124
  214.2 9.1 %copy-start.6 = (bf16[512,32,128]{0,2,1:T(8,128)(2,1)S(1)}, bf16[512,32,128]{0,2,1:T(8,128)(2,1)}, u32[]{:S(2)}) copy-start(bf16[512,32,128]{0,2,1:T(8,128)(2,1)} %copy.68) | copy-start | bytes 12582916
  214.3 9.1 %copy-start.8 = (bf16[16,32,32,128]{3,2,1,0:T(8,128)(2,1)S(1)}, bf16[16,32,32,128]{3,2,1,0:T(8,128)(2,1)}, u32[]{:S(2)}) copy-start(bf16[16,32,32,128]{3,2,1,0:T(8,128)(2,1)} %copy-done.7) | copy-start | bytes 12582916
  286.7 62.6 %all-to-all-start.3 = ((bf16[512,32,128]{2,1,0:T(8,128)(2,1)}), bf16[512,32,128]{2,1,0:T(8,128)(2,1)}, u32[]{:S(2)}, u32[]{:S(2)}) async-start(bf16[512,32,128]{2,1,0:T(8,128)(2,1)} %copy.80), calls=%async_computation.3 | async-start | bytes 8388608 | tf_op jit(solution)/shard_map/all_to_all | solution.py:126
  311.3 30.1 %slice-start.2 = ((s8[8388608]{0:T(1024)(128)(4,1)}), s8[4194304]{0:T(1024)(128)(4,1)S(1)}, s32[]{:S(2)}) async-start(s8[8388608]{0:T(1024)(128)(4,1)} %bitcast.102), calls=%async_computation.6 | async-start | bytes 8388608
  312.1 29.2 %slice-start.3 = ((s8[8388608]{0:T(1024)(128)(4,1)}), s8[4194304]{0:T(1024)(128)(4,1)S(1)}, s32[]{:S(2)}) async-start(s8[8388608]{0:T(1024)(128)(4,1)} %bitcast.102), calls=%async_computation.7 | async-start | bytes 8388608
  312.1 29.2 %collective-permute-start.4 = (f32[2,128]{1,0:T(2,128)S(1)}, f32[2,128]{1,0:T(2,128)S(1)}, u32[]{:S(2)}, u32[]{:S(2)}) collective-permute-start(f32[2,128]{1,0:T(2,128)S(1)} %slice.81), channel_id=1, source_target_pairs={{8,0},{16,8},{24,16},{32,24},{40,32},{48,40},{56,48},{64,56},{72,6... | collective-permute-start | bytes 3080 | tf_op jit(solution)/shard_map/ppermute | solution.py:16
  349.3 8.0 %copy-start.9 = (bf16[32,512,128]{2,1,0:T(8,128)(2,1)S(1)}, bf16[32,512,128]{2,1,0:T(8,128)(2,1)}, u32[]{:S(2)}) copy-start(bf16[32,512,128]{2,1,0:T(8,128)(2,1)} %param.13) | copy-start | bytes 12582916
  357.1 19.6 %slice-start = ((s8[8388608]{0:T(1024)(128)(4,1)}), s8[4194304]{0:T(1024)(128)(4,1)S(1)}, s32[]{:S(2)}) async-start(s8[8388608]{0:T(1024)(128)(4,1)} %bitcast.99), calls=%async_computation.4 | async-start | bytes 8388608
  357.2 19.5 %slice-start.1 = ((s8[8388608]{0:T(1024)(128)(4,1)}), s8[4194304]{0:T(1024)(128)(4,1)S(1)}, s32[]{:S(2)}) async-start(s8[8388608]{0:T(1024)(128)(4,1)} %bitcast.99), calls=%async_computation.5 | async-start | bytes 8388608
  357.2 11.7 %collective-permute-start.5 = (f32[512,512]{1,0:T(8,128)S(1)}, f32[512,512]{1,0:T(8,128)S(1)}, u32[]{:S(2)}, u32[]{:S(2)}) collective-permute-start(f32[512,512]{1,0:T(8,128)S(1)} %constant_dynamic-slice_fusion.6), channel_id=1, source_target_pairs={{0,8},{1,9},{2,10},{3,11},{4,12},{5,13},{6,14},{7,15},{8,0},{9,1},... | collective-permute-start | bytes 3145736 | tf_op jit(solution)/shard_map/ppermute | solution.py:50
  366.0 10.7 %collective-permute-start.7 = (f32[2,128]{1,0:T(2,128)S(1)}, f32[2,128]{1,0:T(2,128)S(1)}, u32[]{:S(2)}, u32[]{:S(2)}) collective-permute-start(f32[2,128]{1,0:T(2,128)S(1)} %slice.84), channel_id=1, source_target_pairs={{8,0},{16,8},{24,16},{32,24},{40,32},{48,40},{56,48},{64,56},{72,6... | collective-permute-start | bytes 3080 | tf_op jit(solution)/shard_map/ppermute | solution.py:16
  369.1 20.4 %collective-permute-start.6 = (f32[256,512]{1,0:T(8,128)S(1)}, f32[256,512]{1,0:T(8,128)S(1)}, u32[]{:S(2)}, u32[]{:S(2)}) collective-permute-start(f32[256,512]{1,0:T(8,128)S(1)} %constant_dynamic-slice_fusion.5), channel_id=1, source_target_pairs={{0,16},{1,17},{2,18},{3,19},{4,20},{5,21},{6,22},{7,23},{8,9},{9,8... | collective-permute-start | bytes 1572872 | tf_op jit(solution)/shard_map/ppermute | solution.py:50
  389.7 8.6 %collective-permute-start.8 = (f32[128,512]{1,0:T(8,128)S(1)}, f32[128,512]{1,0:T(8,128)S(1)}, u32[]{:S(2)}, u32[]{:S(2)}) collective-permute-start(f32[128,512]{1,0:T(8,128)S(1)} %constant_dynamic-slice_fusion.4), channel_id=1, source_target_pairs={{0,1},{1,0},{2,3},{3,2},{4,5},{5,4},{6,7},{7,6},{8,24},{9,25},{10,... | collective-permute-start | bytes 786440 | tf_op jit(solution)/shard_map/ppermute | solution.py:50
  391.3 4.1 collective-permute-start.10
  395.4 5.7 %collective-permute-start.11 = (f32[16384]{0:T(1024)S(1)}, f32[16384]{0:T(1024)S(1)}, u32[]{:S(2)}, u32[]{:S(2)}) collective-permute-start(f32[16384]{0:T(1024)S(1)} %add.222), channel_id=1, source_target_pairs={{0,2},{1,3},{2,0},{3,1},{4,6},{5,7},{6,4},{7,5},{8,10},{9,11},{10,... | collective-permute-start | bytes 196616 | tf_op jit(solution)/shard_map/ppermute | solution.py:24
  398.3 7.9 %collective-permute-start.9 = (f32[64,512]{1,0:T(8,128)S(1)}, f32[64,512]{1,0:T(8,128)S(1)}, u32[]{:S(2)}, u32[]{:S(2)}) collective-permute-start(f32[64,512]{1,0:T(8,128)S(1)} %constant_dynamic-slice_fusion.3), channel_id=1, source_target_pairs={{0,64},{1,65},{2,66},{3,67},{4,68},{5,69},{6,70},{7,71},{8,40},{9,... | collective-permute-start | bytes 393224 | tf_op jit(solution)/shard_map/ppermute | solution.py:50
  401.1 5.1 %collective-permute-start.12 = (f32[16384]{0:T(1024)S(1)}, f32[16384]{0:T(1024)S(1)}, u32[]{:S(2)}, u32[]{:S(2)}) collective-permute-start(f32[16384]{0:T(1024)S(1)} %add.223), channel_id=1, source_target_pairs={{0,4},{1,5},{2,6},{3,7},{4,0},{5,1},{6,2},{7,3},{8,12},{9,13},{10,... | collective-permute-start | bytes 196616 | tf_op jit(solution)/shard_map/ppermute | solution.py:24
  406.3 3.2 collective-permute-start.13
  409.5 4.6 collective-permute-start.14
  414.2 4.2 collective-permute-start.15
  418.4 4.1 collective-permute-start.16
  422.5 4.3 collective-permute-start.17
  426.7 3.5 collective-permute-start.18
  430.3 5.7 %collective-permute-start.19 = (f32[64,512]{1,0:T(8,128)S(1)}, f32[64,512]{1,0:T(8,128)S(1)}, u32[]{:S(2)}, u32[]{:S(2)}) collective-permute-start(f32[64,512]{1,0:T(8,128)S(1)} %constant_dynamic-update-slice_fusion.6), channel_id=1, source_target_pairs={{0,64},{1,65},{2,66},{3,67},{4,68},{5,69},{6,70},{7,71},{8,40},{9,... | collective-permute-start | bytes 393224 | tf_op jit(solution)/shard_map/ppermute | solution.py:50
  436.0 26.1 %collective-permute-start.20 = (f32[128,512]{1,0:T(8,128)S(1)}, f32[128,512]{1,0:T(8,128)S(1)}, u32[]{:S(2)}, u32[]{:S(2)}) collective-permute-start(f32[128,512]{1,0:T(8,128)S(1)} %constant_dynamic-update-slice_fusion.5), channel_id=1, source_target_pairs={{0,1},{1,0},{2,3},{3,2},{4,5},{5,4},{6,7},{7,6},{8,24},{9,25},{10,... | collective-permute-start | bytes 786440 | tf_op jit(solution)/shard_map/ppermute | solution.py:50
  436.1 25.5 %collective-permute-start.27 = (f32[2,3,128]{2,1,0:T(4,128)S(1)}, f32[2,3,128]{2,1,0:T(4,128)S(1)}, u32[]{:S(2)}, u32[]{:S(2)}) collective-permute-start(f32[2,3,128]{2,1,0:T(4,128)S(1)} %pad_maximum_fusion.10), channel_id=1, source_target_pairs={{0,8},{8,0},{16,24},{24,16},{32,40},{40,32},{48,56},{56,48},{64,72... | collective-permute-start | bytes 9224 | tf_op jit(solution)/shard_map/ppermute | solution.py:24
  449.6 1.2 collective-permute-start.23
  450.7 8.3 %collective-permute-start.24 = (f32[128]{0:T(128)S(1)}, f32[128]{0:T(128)S(1)}, u32[]{:S(2)}, u32[]{:S(2)}) collective-permute-start(f32[128]{0:T(128)S(1)} %add.238), channel_id=1, source_target_pairs={{0,16},{8,24},{16,0},{24,8},{32,48},{40,56},{48,32},{56,40},{64,80... | collective-permute-start | bytes 1544 | tf_op jit(solution)/shard_map/ppermute | solution.py:24
  459.1 4.0 collective-permute-start.25
  461.7 2.6 collective-permute-start.28
  462.2 8.4 %collective-permute-start.21 = (f32[256,512]{1,0:T(8,128)S(1)}, f32[256,512]{1,0:T(8,128)S(1)}, u32[]{:S(2)}, u32[]{:S(2)}) collective-permute-start(f32[256,512]{1,0:T(8,128)S(1)} %constant_dynamic-update-slice_fusion.4), channel_id=1, source_target_pairs={{0,16},{1,17},{2,18},{3,19},{4,20},{5,21},{6,22},{7,23},{8,9},{9,8... | collective-permute-start | bytes 1572872 | tf_op jit(solution)/shard_map/ppermute | solution.py:50
  463.1 22.1 %collective-permute-start.26 = (f32[128]{0:T(128)S(1)}, f32[128]{0:T(128)S(1)}, u32[]{:S(2)}, u32[]{:S(2)}) collective-permute-start(f32[128]{0:T(128)S(1)} %add.240), channel_id=1, source_target_pairs={{0,64},{8,72},{16,80},{24,88},{32,96},{40,104},{48,112},{56,120},{... | collective-permute-start | bytes 1544 | tf_op jit(solution)/shard_map/ppermute | solution.py:24
  464.3 19.9 %collective-permute-start.29 = (f32[2,3,128]{2,1,0:T(4,128)S(1)}, f32[2,3,128]{2,1,0:T(4,128)S(1)}, u32[]{:S(2)}, u32[]{:S(2)}) collective-permute-start(f32[2,3,128]{2,1,0:T(4,128)S(1)} %fusion.51), channel_id=1, source_target_pairs={{0,32},{8,40},{16,48},{24,56},{32,0},{40,8},{48,16},{56,24},{64,96... | collective-permute-start | bytes 9224 | tf_op jit(solution)/shard_map/ppermute | solution.py:24
  470.8 16.6 %collective-permute-start.22 = (f32[512,512]{1,0:T(8,128)S(1)}, f32[512,512]{1,0:T(8,128)S(1)}, u32[]{:S(2)}, u32[]{:S(2)}) collective-permute-start(f32[512,512]{1,0:T(8,128)S(1)} %constant_dynamic-update-slice_fusion.3), channel_id=1, source_target_pairs={{0,8},{1,9},{2,10},{3,11},{4,12},{5,13},{6,14},{7,15},{8,0},{9,1},... | collective-permute-start | bytes 3145736 | tf_op jit(solution)/shard_map/ppermute | solution.py:50
  472.7 16.6 %copy-start.1 = (bf16[512,512]{1,0:T(8,128)(2,1)S(1)}, bf16[512,512]{1,0:T(8,128)(2,1)}, u32[]{:S(2)}) copy-start(bf16[512,512]{1,0:T(8,128)(2,1)} %param.11) | copy-start | bytes 1572868
  484.2 2.5 collective-permute-start.30
  (7 other events, 37.5 us)

commit v11 on v9

--- a/solution.py
+++ b/solution.py
@@ -36,16 +36,24 @@
     return (lax.axis_index(axis) // step) % 2
 
 
-def split_exchange(value, specs, sizes):
+def group_digit(group):
+    digit = 0
+    for place, (axis, step) in enumerate(group):
+        digit = digit + ((lax.axis_index(axis) // step) % 2) * (1 << place)
+    return digit
+
+
+def group_exchange(value, groups, shift, sizes):
     ctx_size, ch_size = sizes
     pairs = []
     for source in range(ctx_size * ch_size):
         row, col = divmod(source, ch_size)
-        axis, step = specs[row % 2]
-        if axis == "ctx":
-            row = row ^ step
-        else:
-            col = col ^ step
+        for place, (axis, step) in enumerate(groups[row % 2]):
+            if shift >> place & 1:
+                if axis == "ctx":
+                    row = row ^ step
+                else:
+                    col = col ^ step
         pairs.append((source, row * ch_size + col))
     return lax.ppermute(value, ("ctx", "ch"), pairs)
 
@@ -55,32 +63,36 @@
     sizes = (lax.axis_size("ctx"), lax.axis_size("ch"))
     on_second = lax.axis_index("ctx") % 2 == 1
     kept = []
-    for specs in plan:
-        half = value.shape[0] // 2
-        bit = jnp.where(on_second, coordinate_bit(specs[1]), coordinate_bit(specs[0]))
-        offset = bit * half
-        keep = lax.dynamic_slice_in_dim(value, offset, half, 0)
-        send = lax.dynamic_slice_in_dim(value, half - offset, half, 0)
-        received = split_exchange(send, specs, sizes)
+    for groups in plan:
+        count = 1 << len(groups[0])
+        digit = jnp.where(on_second, group_digit(groups[1]), group_digit(groups[0]))
+        pieces = value.reshape((count, value.shape[0] // count) + value.shape[1:])
+        total = pieces[digit]
+        received = [
+            group_exchange(pieces[digit ^ shift], groups, shift, sizes) for shift in range(1, count)
+        ]
         if len(kept) in fillers:
             state = fillers[len(kept)](state)
             received, state = lax.optimization_barrier((received, state))
-        value = keep + received
-        kept.append((specs, offset))
-    for specs, offset in reversed(kept):
-        other = split_exchange(value, specs, sizes)
-        value = lax.dynamic_update_slice_in_dim(jnp.concatenate([other, other]), value, offset, 0)
+        for part in received:
+            total = total + part
+        value = total
+        kept.append((groups, count, digit))
+    for groups, count, digit in reversed(kept):
+        parts = [value] + [group_exchange(value, groups, shift, sizes) for shift in range(1, count)]
+        order = jnp.arange(count) ^ digit
+        value = jnp.take(jnp.stack(parts), order, axis=0).reshape((-1,) + value.shape[1:])
     return value, state
 
 
+Y_GROUP = (("ctx", 2), ("ctx", 4))
+X_GROUP = (("ch", 1), ("ch", 2))
+Z_GROUP = (("ctx", 8), ("ch", 4))
 FACTOR_ROUNDS = (
-    (("ctx", 1), ("ctx", 1)),
-    (("ctx", 2), ("ch", 1)),
-    (("ch", 1), ("ctx", 2)),
-    (("ctx", 8), ("ctx", 4)),
-    (("ctx", 4), ("ctx", 8)),
-    (("ch", 2), ("ch", 4)),
-    (("ch", 4), ("ch", 2)),
+    ((("ctx", 1),), (("ctx", 1),)),
+    (Y_GROUP, X_GROUP),
+    (X_GROUP, Y_GROUP),
+    (Z_GROUP, Z_GROUP),
 )
 
 
@@ -162,7 +174,7 @@
     both_total, (scaled, row_total, value_taps, gain_part) = tree_allreduce(
         jnp.concatenate([one_part, two_part]),
         FACTOR_ROUNDS,
-        {1: fill_mixed, 2: fill_normed, 4: fill_rows},
+        {1: fill_mixed, 2: fill_normed, 3: fill_rows},
     )
     one_total, two_total = both_total[: one_part.shape[0]], both_total[one_part.shape[0] :]
     tap_part = jnp.stack([jnp.stack(value_taps), jnp.stack(gate_taps)])

time: 486 us -> 479 us (0.986)
  waiting for transfers between devices: 174 us -> 154 us
  local copies, waits for them, and re-layouts: 94.3 us -> 100 us
    ppermute x14 -> x20, waiting for transfers between devices: 25.7 us -> 10.3 us  [group_exchange(): return lax.ppermute(value, ('ctx', 'ch'), pairs)]
    ppermute x14 -> x20, starting transfers between devices: 16.5 us -> 27.5 us  [group_exchange(): return lax.ppermute(value, ('ctx', 'ch'), pairs)]
    ppermute x14, starting transfers between devices: 34.3 us -> 27.5 us  [tree_psum(): lax.ppermute(value, axis, pairs)]
    unnamed x70 -> x72, local copies, waits for them, and re-layouts: 24 us -> 24.7 us
  transfers between devices with their start and end apart: 35 -> 41, of which waited for: 24 -> 18; matrix products, arithmetic and copies ran while one was open for 32% -> 33% of each run, Pallas kernels for 0% -> 0%
where the time goes in v11:
time: 479 us; the launch traced here: 470 us
  waiting for transfers between devices  154 us (32%)
  local copies, waits for them, and re-layouts  100 us (21%)
  starting transfers between devices  91.4 us (19%)
  other arithmetic  81.5 us (17%)
  matrix products  41.6 us (9%)
    all_to_all x1, waiting for transfers between devices, on_device(): lax.all_to_all(section_one, 'ctx', split_axis=1, concat_axis=0, tiled=True)  48.8 us
    all_to_all x1, waiting for transfers between devices, on_device(): lax.all_to_all(grad_section, 'ctx', split_axis=0, concat_axis=1, tiled=True)  39.2 us
    all_to_all x1, waiting for transfers between devices, on_device(): lax.all_to_all(section_two, 'ctx', split_axis=0, concat_axis=1, tiled=True)  32.3 us
    ppermute x14, starting transfers between devices, tree_psum(): lax.ppermute(value, axis, pairs)  27.5 us
    ppermute x20, starting transfers between devices, group_exchange(): return lax.ppermute(value, ('ctx', 'ch'), pairs)  27.5 us
    unnamed x72, local copies, waits for them, and re-layouts  24.7 us
    add x1, other arithmetic, on_device(): gate_normed + conv_taps[1, offset] * ext_gate[offset:offset + rows]  16.5 us
    convert_element_type x2, local copies, waits for them, and re-layouts, on_device(): spectrum = (columns.astype(jnp.float32) * kern).astype(jnp.bfloat16)  14.4 us
  transfers between devices with their start and end apart: 41, of which 18 were waited for; matrix products, arithmetic and copies ran while one was open for 33% of the time, Pallas kernels for 0%

profile of v11, /device:TPU:1, one launch (start us, length us, event | category | flops | bytes accessed | tf_op | source)
XLA Modules:
  0.0 470.4 jit_solution(15321222794223454207)
XLA Ops:
  0.7 4.6 multiply_reduce_fusion.2
  9.1 3.1 collective-permute-start.1
  13.8 3.9 collective-permute-start.2
  19.4 4.4 multiply_convert_fusion.1
  23.9 6.9 %collective-permute-start.3 = (bf16[2,128]{1,0:T(2,128)(2,1)S(1)}, bf16[2,128]{1,0:T(2,128)(2,1)S(1)}, u32[]{:S(2)}, u32[]{:S(2)}) collective-permute-start(bf16[2,128]{1,0:T(2,128)(2,1)S(1)} %slice.88), channel_id=1, source_target_pairs={{0,8},{8,16},{16,24},{24,32},{32,40},{40,48},{48,56},{56,64},{64,7... | collective-permute-start | bytes 1544 | tf_op jit(solution)/shard_map/ppermute | solution.py:16
  31.5 6.5 %fusion.6 = (bf16[16384,128]{1,0:T(8,128)(2,1)}, bf16[16384,128]{1,0:T(8,128)(2,1)S(1)}) fusion(bf16[32,512,128]{2,1,0:T(8,128)(2,1)S(1)} %copy-done.10, bf16[16384,128]{1,0:T(8,128)(2,1)S(1)} %multiply_convert_fusion.1, bf16[2,128]{1,0:T(2,128)(2,1)S(1)} %collective-permute-done.3, f32[128]{0:T(128)S(1)} %get-tuple-element.114, ...), kind=kLoop, calls=%fused_computation.28 | loop fusion | flops 44040192 | bytes 16779264 | tf_op jit(solution)/shard_map/convert_element_type | solution.py:122
  38.0 3.0 fusion.11
  43.1 4.4 convert_bitcast_fusion.2
  47.5 8.0 %copy.41 = bf16[32,512,128]{2,0,1:T(8,128)(2,1)} copy(bf16[32,512,128]{1,2,0:T(8,128)(2,1)} %convert_bitcast_fusion.2) | data formatting | bytes 8388608 | tf_op jit(solution)/shard_map/convert_element_type | solution.py:121
  55.5 7.2 %all-to-all-start = ((bf16[32,512,128]{2,0,1:T(8,128)(2,1)}), bf16[32,512,128]{2,0,1:T(8,128)(2,1)}, u32[]{:S(2)}, u32[]{:S(2)}) async-start(bf16[32,512,128]{2,0,1:T(8,128)(2,1)} %copy.41), calls=%async_computation | async-start | bytes 8388608 | tf_op jit(solution)/shard_map/all_to_all | solution.py:123
  62.7 6.9 %copy.48 = bf16[32,512,128]{2,0,1:T(8,128)(2,1)} copy(bf16[32,512,128]{2,1,0:T(8,128)(2,1)} %bitcast.193) | data formatting | bytes 8388608 | tf_op jit(solution)/shard_map/reshape | solution.py:122
  69.6 48.8 %all-to-all-done = bf16[32,512,128]{2,0,1:T(8,128)(2,1)} async-done(((bf16[32,512,128]{2,0,1:T(8,128)(2,1)}), bf16[32,512,128]{2,0,1:T(8,128)(2,1)}, u32[]{:S(2)}, u32[]{:S(2)}) %all-to-all-start) | async-done | bytes 4194336 | tf_op jit(solution)/shard_map/all_to_all | solution.py:123
  118.4 4.8 %all-to-all-start.2 = ((bf16[32,512,128]{2,0,1:T(8,128)(2,1)}), bf16[32,512,128]{2,0,1:T(8,128)(2,1)}, u32[]{:S(2)}, u32[]{:S(2)}) async-start(bf16[32,512,128]{2,0,1:T(8,128)(2,1)} %copy.48), calls=%async_computation.2 | async-start | bytes 8388608 | tf_op jit(solution)/shard_map/all_to_all | solution.py:130
  123.2 7.5 %copy.44 = bf16[512,32,128]{0,2,1:T(8,128)(2,1)} copy(bf16[512,32,128]{2,1,0:T(8,128)(2,1)} %param.12) | data formatting | bytes 8388608 | tf_op args[5]
  130.7 3.8 copy.42
  135.7 4.3 copy.43
  140.0 10.0 %copy.45 = f32[512,32,128]{0,2,1:T(8,128)} copy(f32[512,32,128]{2,1,0:T(8,128)} %bitcast.190) | data formatting | bytes 16777216 | tf_op jit(solution)/shard_map/convert_element_type | solution.py:125
  150.1 8.9 %convert_bitcast_fusion.1 = bf16[512,32,128]{0,2,1:T(8,128)(2,1)} fusion(bf16[512,512]{1,0:T(8,128)(2,1)S(1)} %copy-done, f32[512,32,128]{0,2,1:T(8,128)} %copy.45, bf16[512,32,128]{0,2,1:T(8,128)(2,1)} %copy.44), kind=kOutput, calls=%fused_computation.65 | convolution fusion | flops 2155872256 | bytes 17301504 | tf_op jit(solution)/shard_map/ijc,ik->kjc/dot_general | solution.py:126
  159.0 8.0 %copy.46 = bf16[512,32,128]{2,1,0:T(8,128)(2,1)} copy(bf16[512,32,128]{0,2,1:T(8,128)(2,1)} %convert_bitcast_fusion.1) | data formatting | bytes 8388608 | tf_op jit(solution)/shard_map/convert_element_type | solution.py:128
  167.0 12.0 %all-to-all-done.2 = bf16[32,512,128]{2,0,1:T(8,128)(2,1)} async-done(((bf16[32,512,128]{2,0,1:T(8,128)(2,1)}), bf16[32,512,128]{2,0,1:T(8,128)(2,1)}, u32[]{:S(2)}, u32[]{:S(2)}) %all-to-all-start.2) | async-done | bytes 4194336 | tf_op jit(solution)/shard_map/all_to_all | solution.py:130
  179.0 5.4 %all-to-all-start.1 = ((bf16[512,32,128]{2,1,0:T(8,128)(2,1)}), bf16[512,32,128]{2,1,0:T(8,128)(2,1)}, u32[]{:S(2)}, u32[]{:S(2)}) async-start(bf16[512,32,128]{2,1,0:T(8,128)(2,1)} %copy.46), calls=%async_computation.1 | async-start | bytes 8388608 | tf_op jit(solution)/shard_map/all_to_all | solution.py:129
  185.7 4.1 copy.50
  189.8 9.0 %fusion.33 = f32[512,512]{1,0:T(8,128)} fusion(bf16[512,32,128]{2,1,0:T(8,128)(2,1)S(1)} %bitcast.188, f32[512,32,128]{0,2,1:T(8,128)} %copy.45, bf16[512,32,128]{0,2,1:T(8,128)(2,1)S(1)} %copy-done.6), kind=kOutput, calls=%fused_computation.75 | convolution fusion | flops 2153775104 | bytes 17825792 | tf_op jit(solution)/shard_map/ijc,kjc->ik/dot_general | solution.py:136
  198.8 9.0 %fusion.27 = (bf16[512,32,128]{0,2,1:T(8,128)(2,1)}, bf16[512,32,128]{0,2,1:T(8,128)(2,1)}) fusion(f32[512,32,128]{0,2,1:T(8,128)S(1)} %bitcast.182, bf16[512,32,128]{0,2,1:T(8,128)(2,1)S(1)} %copy-done.6, bf16[512,512]{1,0:T(8,128)(2,1)S(1)} %copy-done, bf16[512,32,128]{2,1,0:T(8,128)(2,1)S(1)} %bitcast.189), kind=kOutput, calls=%fused_computation.54 | convolution fusion | flops 2157969408 | bytes 25690112 | tf_op jit(solution)/shard_map/kjc,ik->ijc/dot_general | solution.py:131
  207.8 32.3 %all-to-all-done.1 = bf16[512,32,128]{2,1,0:T(8,128)(2,1)} async-done(((bf16[512,32,128]{2,1,0:T(8,128)(2,1)}), bf16[512,32,128]{2,1,0:T(8,128)(2,1)}, u32[]{:S(2)}, u32[]{:S(2)}) %all-to-all-start.1) | async-done | bytes 4194336 | tf_op jit(solution)/shard_map/all_to_all | solution.py:129
  240.1 3.6 copy.47
  244.8 8.4 %fusion.22 = (f32[128]{0:T(128)S(1)}, f32[128]{0:T(128)S(1)}, f32[128]{0:T(128)S(1)}, f32[16384,128]{1,0:T(8,128)S(1)}) fusion(bf16[16384,128]{1,0:T(8,128)(2,1)S(1)} %copy-done.3, bf16[2,128]{1,0:T(2,128)(2,1)S(1)} %collective-permute-done.3, bf16[16384,128]{1,0:T(8,128)(2,1)S(1)} %copy-done.5, f32[128]{0:T(128)S(1)} %get-tuple-element.114, ...), kind=kLoop, calls=%fused_computation.44 | loop fusion | flops 54525568 | bytes 25169408 | tf_op jit(solution)/shard_map/reduce_sum | solution.py:148
  253.2 3.3 copy-done.8
  259.0 8.0 %copy.54 = bf16[512,32,128]{2,1,0:T(8,128)(2,1)} copy(bf16[512,32,128]{0,2,1:T(8,128)(2,1)} %get-tuple-element.37) | data formatting | bytes 8388608 | tf_op jit(solution)/shard_map/optimization_barrier | solution.py:137
  267.0 5.9 %all-to-all-start.3 = ((bf16[512,32,128]{2,1,0:T(8,128)(2,1)}), bf16[512,32,128]{2,1,0:T(8,128)(2,1)}, u32[]{:S(2)}, u32[]{:S(2)}) async-start(bf16[512,32,128]{2,1,0:T(8,128)(2,1)} %copy.54), calls=%async_computation.3 | async-start | bytes 8388608 | tf_op jit(solution)/shard_map/all_to_all | solution.py:138
  272.9 16.5 %fusion.3 = f32[16384,128]{1,0:T(8,128)} fusion(f32[16384,128]{1,0:T(8,128)} %copy-done.8, f32[2,128]{1,0:T(2,128)S(1)} %collective-permute-done.4, f32[128]{0:T(128)S(1)} %get-tuple-element.114, f32[128]{0:T(128)S(1)} %copy-done.19, f32[128]{0:T(128)S(1)} %get-tuple-element.111), kind=kLoop, calls=%fused_computation.25 | loop fusion | flops 14680064 | bytes 16779776 | tf_op jit(solution)/shard_map/add | solution.py:146
  289.4 39.2 %all-to-all-done.3 = bf16[512,32,128]{2,1,0:T(8,128)(2,1)} async-done(((bf16[512,32,128]{2,1,0:T(8,128)(2,1)}), bf16[512,32,128]{2,1,0:T(8,128)(2,1)}, u32[]{:S(2)}, u32[]{:S(2)}) %all-to-all-start.3) | async-done | bytes 4194336 | tf_op jit(solution)/shard_map/all_to_all | solution.py:138
  328.6 3.6 copy.55
  341.5 2.6 collective-permute-start.8
  344.9 7.9 %convolution_bitcast_fusion = f32[32,512,128]{1,2,0:T(8,128)} fusion(bf16[32,512,128]{2,1,0:T(8,128)(2,1)} %bitcast.192, bf16[512,512]{1,0:T(8,128)(2,1)S(1)} %copy-done.15), kind=kOutput, calls=%fused_computation.72 | convolution fusion | flops 2147483648 | bytes 13107200 | tf_op jit(solution)/shard_map/ikc,jk->ijc/dot_general | solution.py:153
  352.8 8.9 %copy.57 = f32[32,512,128]{2,1,0:T(8,128)} copy(f32[32,512,128]{1,2,0:T(8,128)} %convolution_bitcast_fusion) | data formatting | bytes 16777216 | tf_op jit(solution)/shard_map/ikc,jk->ijc/transpose | solution.py:153
  362.4 3.6 collective-permute-start.12
  367.5 3.1 collective-permute-start.10
  371.0 8.9 %fusion.23 = (f32[128]{0:T(128)S(1)}, f32[128]{0:T(128)S(1)}, f32[128]{0:T(128)S(1)}, f32[16386,128]{1,0:T(8,128)S(1)}) fusion(f32[16384,128]{1,0:T(8,128)} %bitcast.184, bf16[16384,128]{1,0:T(8,128)(2,1)} %copy-done.2, bf16[2,128]{1,0:T(2,128)(2,1)S(1)} %collective-permute-done.3, bf16[16384,128]{1,0:T(8,128)(2,1)} %copy-done.4), kind=kLoop, calls=%fused_computation.45 | loop fusion | flops 25165440 | bytes 25167872 | tf_op jit(solution)/shard_map/reduce_sum | solution.py:165
  381.4 11.0 %multiply_reduce_fusion = (f32[128]{0:T(128)S(1)}, f32[16384]{0:T(1024)S(1)}, f32[16384,128]{1,0:T(8,128)}) fusion(bf16[32,512,128]{2,1,0:T(8,128)(2,1)S(1)} %copy-done.7, f32[16384]{0:T(1024)S(1)} %copy-done.17, f32[128]{0:T(128)S(1)} %copy-done.27, f32[16386,128]{1,0:T(8,128)S(1)} %constant_dynamic-update-slice_fusion, f32[128]{0:T(128)S(1)} %copy-done.23, ...), kind=kLoop, calls=%fused_computation.57 | loop fusion | flops 27246464 | bytes 46270976 | tf_op jit(solution)/shard_map/reduce_sum | solution.py:167
  393.7 2.6 collective-permute-done.16
  398.8 3.4 collective-permute-start.15
  402.9 2.5 collective-permute-start.18
  405.7 7.8 %copy.59 = bf16[512,32,128]{2,1,0:T(8,128)(2,1)} copy(bf16[512,32,128]{0,2,1:T(8,128)(2,1)} %get-tuple-element.96) | data formatting | bytes 8388608
  417.0 2.5 collective-permute-start.29
  441.3 4.6 collective-permute-done.27
  447.4 5.6 %collective-permute-start.28 = (f32[512,512]{1,0:T(8,128)S(1)}, f32[512,512]{1,0:T(8,128)S(1)}, u32[]{:S(2)}, u32[]{:S(2)}) collective-permute-start(f32[512,512]{1,0:T(8,128)S(1)} %bitcast_select_fusion), channel_id=1, source_target_pairs={{0,8},{1,9},{2,10},{3,11},{4,12},{5,13},{6,14},{7,15},{8,0},{9,1},... | collective-permute-start | bytes 3145736 | tf_op jit(solution)/shard_map/ppermute | solution.py:58
  453.0 8.1 %multiply_convert_fusion = bf16[16384,128]{1,0:T(8,128)(2,1)} fusion(f32[16384,128]{1,0:T(8,128)} %get-tuple-element.54, bf16[32,512,128]{2,1,0:T(8,128)(2,1)} %param.7, f32[16384]{0:T(1024)S(1)} %broadcast_multiply_fusion.1, f32[16384]{0:T(1024)S(1)} %copy-done.17), kind=kLoop, calls=%fused_computation.56 | loop fusion | flops 12582912 | bytes 16908288 | tf_op jit(solution)/shard_map/convert_element_type | solution.py:185
  (199 shorter events, 69.9 us)
Async XLA Ops:
  0.6 149.5 %copy-start = (bf16[512,512]{1,0:T(8,128)(2,1)S(1)}, bf16[512,512]{1,0:T(8,128)(2,1)}, u32[]{:S(2)}) copy-start(bf16[512,512]{1,0:T(8,128)(2,1)} %param.11) | copy-start | bytes 1572868
  0.6 30.2 %copy-start.26 = (f32[2,3,128]{2,0,1:T(2,128)S(1)}, f32[2,3,128]{2,0,1:T(2,128)}, u32[]{:S(2)}) copy-start(f32[2,3,128]{2,0,1:T(2,128)} %param.9) | copy-start | bytes 9220
  0.7 30.8 %copy-start.10 = (bf16[32,512,128]{2,1,0:T(8,128)(2,1)S(1)}, bf16[32,512,128]{2,1,0:T(8,128)(2,1)}, u32[]{:S(2)}) copy-start(bf16[32,512,128]{2,1,0:T(8,128)(2,1)} %param.13) | copy-start | bytes 12582916
  5.3 3.8 collective-permute-start
  9.1 4.7 %collective-permute-start.1 = (f32[16384]{0:T(1024)S(1)}, f32[16384]{0:T(1024)S(1)}, u32[]{:S(2)}, u32[]{:S(2)}) collective-permute-start(f32[16384]{0:T(1024)S(1)} %add.259), channel_id=1, source_target_pairs={{0,2},{1,3},{2,0},{3,1},{4,6},{5,7},{6,4},{7,5},{8,10},{9,11},{10,... | collective-permute-start | bytes 196616 | tf_op jit(solution)/shard_map/ppermute | solution.py:24
  13.8 5.6 %collective-permute-start.2 = (f32[16384]{0:T(1024)S(1)}, f32[16384]{0:T(1024)S(1)}, u32[]{:S(2)}, u32[]{:S(2)}) collective-permute-start(f32[16384]{0:T(1024)S(1)} %add.260), channel_id=1, source_target_pairs={{0,4},{1,5},{2,6},{3,7},{4,0},{5,1},{6,2},{7,3},{8,12},{9,13},{10,... | collective-permute-start | bytes 196616 | tf_op jit(solution)/shard_map/ppermute | solution.py:24
  19.4 12.1 %copy-start.16 = (f32[16384]{0:T(1024)}, f32[16384]{0:T(1024)S(1)}, u32[]{:S(2)}) copy-start(f32[16384]{0:T(1024)S(1)} %add_rsqrt_fusion) | copy-start | bytes 196612
  23.8 14.2 %copy-start.2 = (bf16[16384,128]{1,0:T(8,128)(2,1)}, bf16[16384,128]{1,0:T(8,128)(2,1)S(1)}, u32[]{:S(2)}) copy-start(bf16[16384,128]{1,0:T(8,128)(2,1)S(1)} %multiply_convert_fusion.1) | copy-start | bytes 12582916
  23.9 7.6 %collective-permute-start.3 = (bf16[2,128]{1,0:T(2,128)(2,1)S(1)}, bf16[2,128]{1,0:T(2,128)(2,1)S(1)}, u32[]{:S(2)}, u32[]{:S(2)}) collective-permute-start(bf16[2,128]{1,0:T(2,128)(2,1)S(1)} %slice.88), channel_id=1, source_target_pairs={{0,8},{8,16},{16,24},{24,32},{32,40},{40,48},{48,56},{56,64},{64,7... | collective-permute-start | bytes 1544 | tf_op jit(solution)/shard_map/ppermute | solution.py:16
  55.5 62.9 %all-to-all-start = ((bf16[32,512,128]{2,0,1:T(8,128)(2,1)}), bf16[32,512,128]{2,0,1:T(8,128)(2,1)}, u32[]{:S(2)}, u32[]{:S(2)}) async-start(bf16[32,512,128]{2,0,1:T(8,128)(2,1)} %copy.41), calls=%async_computation | async-start | bytes 8388608 | tf_op jit(solution)/shard_map/all_to_all | solution.py:123
  118.4 60.6 %all-to-all-start.2 = ((bf16[32,512,128]{2,0,1:T(8,128)(2,1)}), bf16[32,512,128]{2,0,1:T(8,128)(2,1)}, u32[]{:S(2)}, u32[]{:S(2)}) async-start(bf16[32,512,128]{2,0,1:T(8,128)(2,1)} %copy.48), calls=%async_computation.2 | async-start | bytes 8388608 | tf_op jit(solution)/shard_map/all_to_all | solution.py:130
  179.0 61.1 %all-to-all-start.1 = ((bf16[512,32,128]{2,1,0:T(8,128)(2,1)}), bf16[512,32,128]{2,1,0:T(8,128)(2,1)}, u32[]{:S(2)}, u32[]{:S(2)}) async-start(bf16[512,32,128]{2,1,0:T(8,128)(2,1)} %copy.46), calls=%async_computation.1 | async-start | bytes 8388608 | tf_op jit(solution)/shard_map/all_to_all | solution.py:129
  185.7 13.2 %slice-start = ((s8[8388608]{0:T(1024)(128)(4,1)}), s8[4194304]{0:T(1024)(128)(4,1)S(1)}, s32[]{:S(2)}) async-start(s8[8388608]{0:T(1024)(128)(4,1)} %bitcast.181), calls=%async_computation.4 | async-start | bytes 8388608
  207.8 35.9 %copy-start.19 = (f32[128]{0:T(128)S(1)}, f32[128]{0:T(128)}, u32[]{:S(2)}) copy-start(f32[128]{0:T(128)} %copy-done.18) | copy-start | bytes 1540
  256.5 16.4 %collective-permute-start.4 = (f32[2,128]{1,0:T(2,128)S(1)}, f32[2,128]{1,0:T(2,128)S(1)}, u32[]{:S(2)}, u32[]{:S(2)}) collective-permute-start(f32[2,128]{1,0:T(2,128)S(1)} %slice.91), channel_id=1, source_target_pairs={{8,0},{16,8},{24,16},{32,24},{40,32},{48,40},{56,48},{64,56},{72,6... | collective-permute-start | bytes 3080 | tf_op jit(solution)/shard_map/ppermute | solution.py:16
  267.0 61.6 %all-to-all-start.3 = ((bf16[512,32,128]{2,1,0:T(8,128)(2,1)}), bf16[512,32,128]{2,1,0:T(8,128)(2,1)}, u32[]{:S(2)}, u32[]{:S(2)}) async-start(bf16[512,32,128]{2,1,0:T(8,128)(2,1)} %copy.54), calls=%async_computation.3 | async-start | bytes 8388608 | tf_op jit(solution)/shard_map/all_to_all | solution.py:138
  335.8 3.2 collective-permute-start.5
  341.5 20.2 %collective-permute-start.8 = (f32[128,512]{1,0:T(8,128)S(1)}, f32[128,512]{1,0:T(8,128)S(1)}, u32[]{:S(2)}, u32[]{:S(2)}) collective-permute-start(f32[128,512]{1,0:T(8,128)S(1)} %get-tuple-element.101), channel_id=1, source_target_pairs={{0,48},{1,49},{2,50},{3,51},{4,52},{5,53},{6,54},{7,55},{8,11},{9,... | collective-permute-start | bytes 786440 | tf_op jit(solution)/shard_map/ppermute | solution.py:58
  344.1 17.6 %collective-permute-start.7 = (f32[128,512]{1,0:T(8,128)S(1)}, f32[128,512]{1,0:T(8,128)S(1)}, u32[]{:S(2)}, u32[]{:S(2)}) collective-permute-start(f32[128,512]{1,0:T(8,128)S(1)} %get-tuple-element.102), channel_id=1, source_target_pairs={{0,32},{1,33},{2,34},{3,35},{4,36},{5,37},{6,38},{7,39},{8,10},{9,... | collective-permute-start | bytes 786440 | tf_op jit(solution)/shard_map/ppermute | solution.py:58
  344.6 17.1 %collective-permute-start.6 = (f32[128,512]{1,0:T(8,128)S(1)}, f32[128,512]{1,0:T(8,128)S(1)}, u32[]{:S(2)}, u32[]{:S(2)}) collective-permute-start(f32[128,512]{1,0:T(8,128)S(1)} %get-tuple-element.103), channel_id=1, source_target_pairs={{0,16},{1,17},{2,18},{3,19},{4,20},{5,21},{6,22},{7,23},{8,9},{9,8... | collective-permute-start | bytes 786440 | tf_op jit(solution)/shard_map/ppermute | solution.py:58
  362.4 17.6 %collective-permute-start.12 = (f32[2,128]{1,0:T(2,128)S(1)}, f32[2,128]{1,0:T(2,128)S(1)}, u32[]{:S(2)}, u32[]{:S(2)}) collective-permute-start(f32[2,128]{1,0:T(2,128)S(1)} %slice.75), channel_id=1, source_target_pairs={{8,0},{16,8},{24,16},{32,24},{40,32},{48,40},{56,48},{64,56},{72,6... | collective-permute-start | bytes 3080 | tf_op jit(solution)/shard_map/ppermute | solution.py:16
  367.0 25.4 %collective-permute-start.11 = (f32[32,512]{1,0:T(8,128)S(1)}, f32[32,512]{1,0:T(8,128)S(1)}, u32[]{:S(2)}, u32[]{:S(2)}) collective-permute-start(f32[32,512]{1,0:T(8,128)S(1)} %get-tuple-element.104), channel_id=1, source_target_pairs={{0,3},{1,2},{2,1},{3,0},{4,7},{5,6},{6,5},{7,4},{8,56},{9,57},{10,... | collective-permute-start | bytes 196616 | tf_op jit(solution)/shard_map/ppermute | solution.py:58
  367.5 24.9 %collective-permute-start.10 = (f32[32,512]{1,0:T(8,128)S(1)}, f32[32,512]{1,0:T(8,128)S(1)}, u32[]{:S(2)}, u32[]{:S(2)}) collective-permute-start(f32[32,512]{1,0:T(8,128)S(1)} %get-tuple-element.105), channel_id=1, source_target_pairs={{0,2},{1,3},{2,0},{3,1},{4,6},{5,7},{6,4},{7,5},{8,40},{9,41},{10,... | collective-permute-start | bytes 196616 | tf_op jit(solution)/shard_map/ppermute | solution.py:58
  370.7 21.7 %collective-permute-start.9 = (f32[32,512]{1,0:T(8,128)S(1)}, f32[32,512]{1,0:T(8,128)S(1)}, u32[]{:S(2)}, u32[]{:S(2)}) collective-permute-start(f32[32,512]{1,0:T(8,128)S(1)} %get-tuple-element.106), channel_id=1, source_target_pairs={{0,1},{1,0},{2,3},{3,2},{4,5},{5,4},{6,7},{7,6},{8,24},{9,25},{10,... | collective-permute-start | bytes 196616 | tf_op jit(solution)/shard_map/ppermute | solution.py:58
  392.4 3.9 collective-permute-start.16
  396.4 6.5 %collective-permute-start.17 = (f32[16384]{0:T(1024)S(1)}, f32[16384]{0:T(1024)S(1)}, u32[]{:S(2)}, u32[]{:S(2)}) collective-permute-start(f32[16384]{0:T(1024)S(1)} %add.304), channel_id=1, source_target_pairs={{0,2},{1,3},{2,0},{3,1},{4,6},{5,7},{6,4},{7,5},{8,10},{9,11},{10,... | collective-permute-start | bytes 196616 | tf_op jit(solution)/shard_map/ppermute | solution.py:24
  398.8 14.8 %collective-permute-start.15 = (f32[8,512]{1,0:T(8,128)S(1)}, f32[8,512]{1,0:T(8,128)S(1)}, u32[]{:S(2)}, u32[]{:S(2)}) collective-permute-start(f32[8,512]{1,0:T(8,128)S(1)} %get-tuple-element.107), channel_id=1, source_target_pairs={{0,68},{1,69},{2,70},{3,71},{4,64},{5,65},{6,66},{7,67},{8,76},{9,... | collective-permute-start | bytes 49160 | tf_op jit(solution)/shard_map/ppermute | solution.py:58
  402.2 11.4 %collective-permute-start.14 = (f32[8,512]{1,0:T(8,128)S(1)}, f32[8,512]{1,0:T(8,128)S(1)}, u32[]{:S(2)}, u32[]{:S(2)}) collective-permute-start(f32[8,512]{1,0:T(8,128)S(1)} %get-tuple-element.108), channel_id=1, source_target_pairs={{0,4},{1,5},{2,6},{3,7},{4,0},{5,1},{6,2},{7,3},{8,12},{9,13},{10,... | collective-permute-start | bytes 49160 | tf_op jit(solution)/shard_map/ppermute | solution.py:58
  402.2 11.4 %collective-permute-start.13 = (f32[8,512]{1,0:T(8,128)S(1)}, f32[8,512]{1,0:T(8,128)S(1)}, u32[]{:S(2)}, u32[]{:S(2)}) collective-permute-start(f32[8,512]{1,0:T(8,128)S(1)} %get-tuple-element.109), channel_id=1, source_target_pairs={{0,64},{1,65},{2,66},{3,67},{4,68},{5,69},{6,70},{7,71},{8,72},{9,... | collective-permute-start | bytes 49160 | tf_op jit(solution)/shard_map/ppermute | solution.py:58
  402.9 10.7 %collective-permute-start.18 = (f32[16384]{0:T(1024)S(1)}, f32[16384]{0:T(1024)S(1)}, u32[]{:S(2)}, u32[]{:S(2)}) collective-permute-start(f32[16384]{0:T(1024)S(1)} %add.305), channel_id=1, source_target_pairs={{0,4},{1,5},{2,6},{3,7},{4,0},{5,1},{6,2},{7,3},{8,12},{9,13},{10,... | collective-permute-start | bytes 196616 | tf_op jit(solution)/shard_map/ppermute | solution.py:24
  413.6 15.4 %collective-permute-start.21 = (f32[8,512]{1,0:T(8,128)S(1)}, f32[8,512]{1,0:T(8,128)S(1)}, u32[]{:S(2)}, u32[]{:S(2)}) collective-permute-start(f32[8,512]{1,0:T(8,128)S(1)} %fusion.48), channel_id=1, source_target_pairs={{0,68},{1,69},{2,70},{3,71},{4,64},{5,65},{6,66},{7,67},{8,76},{9,... | collective-permute-start | bytes 49160 | tf_op jit(solution)/shard_map/ppermute | solution.py:58
  414.5 14.6 %collective-permute-start.20 = (f32[8,512]{1,0:T(8,128)S(1)}, f32[8,512]{1,0:T(8,128)S(1)}, u32[]{:S(2)}, u32[]{:S(2)}) collective-permute-start(f32[8,512]{1,0:T(8,128)S(1)} %fusion.48), channel_id=1, source_target_pairs={{0,4},{1,5},{2,6},{3,7},{4,0},{5,1},{6,2},{7,3},{8,12},{9,13},{10,... | collective-permute-start | bytes 49160 | tf_op jit(solution)/shard_map/ppermute | solution.py:58
  416.2 12.8 %collective-permute-start.19 = (f32[8,512]{1,0:T(8,128)S(1)}, f32[8,512]{1,0:T(8,128)S(1)}, u32[]{:S(2)}, u32[]{:S(2)}) collective-permute-start(f32[8,512]{1,0:T(8,128)S(1)} %fusion.48), channel_id=1, source_target_pairs={{0,64},{1,65},{2,66},{3,67},{4,68},{5,69},{6,70},{7,71},{8,72},{9,... | collective-permute-start | bytes 49160 | tf_op jit(solution)/shard_map/ppermute | solution.py:58
  417.0 3.3 collective-permute-start.29
  420.3 3.0 collective-permute-start.30
  422.4 5.3 %collective-permute-start.33 = (f32[2,3,128]{2,1,0:T(4,128)S(1)}, f32[2,3,128]{2,1,0:T(4,128)S(1)}, u32[]{:S(2)}, u32[]{:S(2)}) collective-permute-start(f32[2,3,128]{2,1,0:T(4,128)S(1)} %pad_maximum_fusion.7), channel_id=1, source_target_pairs={{0,8},{8,0},{16,24},{24,16},{32,40},{40,32},{48,56},{56,48},{64,72... | collective-permute-start | bytes 9224 | tf_op jit(solution)/shard_map/ppermute | solution.py:24
  423.4 3.9 collective-permute-start.31
  427.3 35.1 %collective-permute-start.32 = (f32[128]{0:T(128)S(1)}, f32[128]{0:T(128)S(1)}, u32[]{:S(2)}, u32[]{:S(2)}) collective-permute-start(f32[128]{0:T(128)S(1)} %add.321), channel_id=1, source_target_pairs={{0,64},{8,72},{16,80},{24,88},{32,96},{40,104},{48,112},{56,120},{... | collective-permute-start | bytes 1544 | tf_op jit(solution)/shard_map/ppermute | solution.py:24
  427.7 11.9 %collective-permute-start.34 = (f32[2,3,128]{2,1,0:T(4,128)S(1)}, f32[2,3,128]{2,1,0:T(4,128)S(1)}, u32[]{:S(2)}, u32[]{:S(2)}) collective-permute-start(f32[2,3,128]{2,1,0:T(4,128)S(1)} %fusion.53), channel_id=1, source_target_pairs={{0,16},{8,24},{16,0},{24,8},{32,48},{40,56},{48,32},{56,40},{64,80... | collective-permute-start | bytes 9224 | tf_op jit(solution)/shard_map/ppermute | solution.py:24
  429.7 4.3 collective-permute-start.24
  431.0 4.6 collective-permute-start.23
  431.7 3.9 collective-permute-start.22
  436.3 9.6 %collective-permute-start.27 = (f32[128,512]{1,0:T(8,128)S(1)}, f32[128,512]{1,0:T(8,128)S(1)}, u32[]{:S(2)}, u32[]{:S(2)}) collective-permute-start(f32[128,512]{1,0:T(8,128)S(1)} %bitcast_select_fusion.2), channel_id=1, source_target_pairs={{0,48},{1,49},{2,50},{3,51},{4,52},{5,53},{6,54},{7,55},{8,11},{9,... | collective-permute-start | bytes 786440 | tf_op jit(solution)/shard_map/ppermute | solution.py:58
  437.4 8.5 %collective-permute-start.26 = (f32[128,512]{1,0:T(8,128)S(1)}, f32[128,512]{1,0:T(8,128)S(1)}, u32[]{:S(2)}, u32[]{:S(2)}) collective-permute-start(f32[128,512]{1,0:T(8,128)S(1)} %bitcast_select_fusion.2), channel_id=1, source_target_pairs={{0,32},{1,33},{2,34},{3,35},{4,36},{5,37},{6,38},{7,39},{8,10},{9,... | collective-permute-start | bytes 786440 | tf_op jit(solution)/shard_map/ppermute | solution.py:58
  438.3 8.2 %collective-permute-start.25 = (f32[128,512]{1,0:T(8,128)S(1)}, f32[128,512]{1,0:T(8,128)S(1)}, u32[]{:S(2)}, u32[]{:S(2)}) collective-permute-start(f32[128,512]{1,0:T(8,128)S(1)} %bitcast_select_fusion.2), channel_id=1, source_target_pairs={{0,16},{1,17},{2,18},{3,19},{4,20},{5,21},{6,22},{7,23},{8,9},{9,8... | collective-permute-start | bytes 786440 | tf_op jit(solution)/shard_map/ppermute | solution.py:58
  439.6 21.4 %collective-permute-start.35 = (f32[2,3,128]{2,1,0:T(4,128)S(1)}, f32[2,3,128]{2,1,0:T(4,128)S(1)}, u32[]{:S(2)}, u32[]{:S(2)}) collective-permute-start(f32[2,3,128]{2,1,0:T(4,128)S(1)} %fusion.62), channel_id=1, source_target_pairs={{0,32},{8,40},{16,48},{24,56},{32,0},{40,8},{48,16},{56,24},{64,96... | collective-permute-start | bytes 9224 | tf_op jit(solution)/shard_map/ppermute | solution.py:24
  447.4 16.9 %collective-permute-start.28 = (f32[512,512]{1,0:T(8,128)S(1)}, f32[512,512]{1,0:T(8,128)S(1)}, u32[]{:S(2)}, u32[]{:S(2)}) collective-permute-start(f32[512,512]{1,0:T(8,128)S(1)} %bitcast_select_fusion), channel_id=1, source_target_pairs={{0,8},{1,9},{2,10},{3,11},{4,12},{5,13},{6,14},{7,15},{8,0},{9,1},... | collective-permute-start | bytes 3145736 | tf_op jit(solution)/shard_map/ppermute | solution.py:58
  461.0 2.5 collective-permute-start.36
  (27 other events, 171.7 us)

commit v12 on v11

--- a/solution.py
+++ b/solution.py
@@ -18,12 +18,16 @@
 
 def tree_psum(value, axis):
     count = lax.axis_size(axis)
-    step = 1
-    while step < count:
-        pairs = [(source, source ^ step) for source in range(count)]
-        value = jax.tree.map(lambda v, r: v + r, value, lax.ppermute(value, axis, pairs))
-        step *= 2
-    return value
+    order = jnp.arange(count) ^ lax.axis_index(axis)
+
+    def total(leaf):
+        parts = [leaf] + [
+            lax.ppermute(leaf, axis, [(source, source ^ shift) for source in range(count)])
+            for shift in range(1, count)
+        ]
+        return jnp.sum(jnp.take(jnp.stack(parts), order, axis=0), axis=0)
+
+    return jax.tree.map(total, value)
 
 
 def exchange(value, axis, step):

time: 479 us -> 545 us (1.14)
  starting transfers between devices: 91.4 us -> 135 us
  waiting for transfers between devices: 154 us -> 165 us
    ppermute x14 -> x44, starting transfers between devices: 27.5 us -> 79.3 us  [total(): lax.ppermute(leaf, axis, [(source, source ^ shift) for source in range(co...]
    ppermute x14 -> x44, waiting for transfers between devices: 10.9 us -> 22.7 us  [total(): lax.ppermute(leaf, axis, [(source, source ^ shift) for source in range(co...]
    ppermute x20, starting transfers between devices: 27.5 us -> 21.7 us  [group_exchange(): return lax.ppermute(value, ('ctx', 'ch'), pairs)]
    unnamed x72 -> x103, local copies, waits for them, and re-layouts: 24.7 us -> 25 us
  transfers between devices with their start and end apart: 41 -> 71, of which waited for: 18 -> 28; matrix products, arithmetic and copies ran while one was open for 33% -> 30% of each run, Pallas kernels for 0% -> 0%
where the time goes in v12:
time: 545 us; the launch traced here: 534 us
  waiting for transfers between devices  165 us (30%)
  starting transfers between devices  135 us (25%)
  local copies, waits for them, and re-layouts  104 us (19%)
  other arithmetic  85.8 us (16%)
  matrix products  41.6 us (8%)
    ppermute x44, starting transfers between devices, total(): lax.ppermute(leaf, axis, [(source, source ^ shift) for source in range(co...  79.3 us
    all_to_all x1, waiting for transfers between devices, on_device(): lax.all_to_all(section_one, 'ctx', split_axis=1, concat_axis=0, tiled=True)  48.8 us
    all_to_all x1, waiting for transfers between devices, on_device(): lax.all_to_all(grad_section, 'ctx', split_axis=0, concat_axis=1, tiled=True)  39.1 us
    all_to_all x1, waiting for transfers between devices, on_device(): lax.all_to_all(section_two, 'ctx', split_axis=0, concat_axis=1, tiled=True)  30 us
    unnamed x103, local copies, waits for them, and re-layouts  25 us
    ppermute x44, waiting for transfers between devices, total(): lax.ppermute(leaf, axis, [(source, source ^ shift) for source in range(co...  22.7 us
    ppermute x20, starting transfers between devices, group_exchange(): return lax.ppermute(value, ('ctx', 'ch'), pairs)  21.7 us
    add x1, other arithmetic, on_device(): gate_normed + conv_taps[1, offset] * ext_gate[offset:offset + rows]  16.6 us
  transfers between devices with their start and end apart: 71, of which 28 were waited for; matrix products, arithmetic and copies ran while one was open for 30% of the time, Pallas kernels for 0%

profile of v12, /device:TPU:1, one launch (start us, length us, event | category | flops | bytes accessed | tf_op | source)
XLA Modules:
  0.0 534.2 jit_solution(2945609645814444575)
XLA Ops:
  0.7 4.5 multiply_reduce_fusion.2
  5.2 6.7 %collective-permute-start.6 = (f32[16384]{0:T(1024)S(1)}, f32[16384]{0:T(1024)S(1)}, u32[]{:S(2)}, u32[]{:S(2)}) collective-permute-start(f32[16384]{0:T(1024)S(1)} %bitcast.296), channel_id=1, source_target_pairs={{0,7},{1,6},{2,5},{3,4},{4,3},{5,2},{6,1},{7,0},{8,15},{9,14},{10,... | collective-permute-start | bytes 196616 | tf_op jit(solution)/shard_map/ppermute | solution.py:25
  24.9 4.6 multiply_convert_fusion.1
  29.5 5.4 %collective-permute-start.7 = (bf16[2,128]{1,0:T(2,128)(2,1)S(1)}, bf16[2,128]{1,0:T(2,128)(2,1)S(1)}, u32[]{:S(2)}, u32[]{:S(2)}) collective-permute-start(bf16[2,128]{1,0:T(2,128)(2,1)S(1)} %slice.96), channel_id=1, source_target_pairs={{0,8},{8,16},{16,24},{24,32},{32,40},{40,48},{48,56},{56,64},{64,7... | collective-permute-start | bytes 1544 | tf_op jit(solution)/shard_map/ppermute | solution.py:16
  35.6 6.5 %fusion.6 = (bf16[16384,128]{1,0:T(8,128)(2,1)}, bf16[16384,128]{1,0:T(8,128)(2,1)S(1)}) fusion(bf16[32,512,128]{2,1,0:T(8,128)(2,1)S(1)} %copy-done.10, bf16[16384,128]{1,0:T(8,128)(2,1)S(1)} %multiply_convert_fusion.1, bf16[2,128]{1,0:T(2,128)(2,1)S(1)} %collective-permute-done.7, f32[128]{0:T(128)S(1)} %get-tuple-element.115, ...), kind=kLoop, calls=%fused_computation.32 | loop fusion | flops 44040192 | bytes 16779264 | tf_op jit(solution)/shard_map/convert_element_type | solution.py:126
  47.2 4.4 convert_bitcast_fusion.2
  51.7 7.9 %copy.39 = bf16[32,512,128]{2,0,1:T(8,128)(2,1)} copy(bf16[32,512,128]{1,2,0:T(8,128)(2,1)} %convert_bitcast_fusion.2) | data formatting | bytes 8388608 | tf_op jit(solution)/shard_map/convert_element_type | solution.py:125
  59.6 6.9 %all-to-all-start = ((bf16[32,512,128]{2,0,1:T(8,128)(2,1)}), bf16[32,512,128]{2,0,1:T(8,128)(2,1)}, u32[]{:S(2)}, u32[]{:S(2)}) async-start(bf16[32,512,128]{2,0,1:T(8,128)(2,1)} %copy.39), calls=%async_computation | async-start | bytes 8388608 | tf_op jit(solution)/shard_map/all_to_all | solution.py:127
  66.5 6.9 %copy.46 = bf16[32,512,128]{2,0,1:T(8,128)(2,1)} copy(bf16[32,512,128]{2,1,0:T(8,128)(2,1)} %bitcast.261) | data formatting | bytes 8388608 | tf_op jit(solution)/shard_map/reshape | solution.py:126
  73.4 48.8 %all-to-all-done = bf16[32,512,128]{2,0,1:T(8,128)(2,1)} async-done(((bf16[32,512,128]{2,0,1:T(8,128)(2,1)}), bf16[32,512,128]{2,0,1:T(8,128)(2,1)}, u32[]{:S(2)}, u32[]{:S(2)}) %all-to-all-start) | async-done | bytes 4194336 | tf_op jit(solution)/shard_map/all_to_all | solution.py:127
  122.2 4.9 all-to-all-start.2
  127.1 7.5 %copy.42 = bf16[512,32,128]{0,2,1:T(8,128)(2,1)} copy(bf16[512,32,128]{2,1,0:T(8,128)(2,1)} %param.14) | data formatting | bytes 8388608 | tf_op args[5]
  134.5 3.8 copy.40
  139.5 4.4 copy.41
  143.9 10.0 %copy.43 = f32[512,32,128]{0,2,1:T(8,128)} copy(f32[512,32,128]{2,1,0:T(8,128)} %bitcast.258) | data formatting | bytes 16777216 | tf_op jit(solution)/shard_map/convert_element_type | solution.py:129
  153.9 8.9 %convert_bitcast_fusion.1 = bf16[512,32,128]{0,2,1:T(8,128)(2,1)} fusion(bf16[512,512]{1,0:T(8,128)(2,1)S(1)} %copy-done, f32[512,32,128]{0,2,1:T(8,128)} %copy.43, bf16[512,32,128]{0,2,1:T(8,128)(2,1)} %copy.42), kind=kOutput, calls=%fused_computation.69 | convolution fusion | flops 2155872256 | bytes 17301504 | tf_op jit(solution)/shard_map/ijc,ik->kjc/dot_general | solution.py:130
  162.8 7.9 %copy.44 = bf16[512,32,128]{2,1,0:T(8,128)(2,1)} copy(bf16[512,32,128]{0,2,1:T(8,128)(2,1)} %convert_bitcast_fusion.1) | data formatting | bytes 8388608 | tf_op jit(solution)/shard_map/convert_element_type | solution.py:132
  170.7 12.0 %all-to-all-done.2 = bf16[32,512,128]{2,0,1:T(8,128)(2,1)} async-done(((bf16[32,512,128]{2,0,1:T(8,128)(2,1)}), bf16[32,512,128]{2,0,1:T(8,128)(2,1)}, u32[]{:S(2)}, u32[]{:S(2)}) %all-to-all-start.2) | async-done | bytes 4194336 | tf_op jit(solution)/shard_map/all_to_all | solution.py:134
  182.8 5.7 %all-to-all-start.1 = ((bf16[512,32,128]{2,1,0:T(8,128)(2,1)}), bf16[512,32,128]{2,1,0:T(8,128)(2,1)}, u32[]{:S(2)}, u32[]{:S(2)}) async-start(bf16[512,32,128]{2,1,0:T(8,128)(2,1)} %copy.44), calls=%async_computation.1 | async-start | bytes 8388608 | tf_op jit(solution)/shard_map/all_to_all | solution.py:133
  192.0 4.1 copy.48
  196.1 9.0 %fusion.33 = f32[512,512]{1,0:T(8,128)} fusion(bf16[512,32,128]{2,1,0:T(8,128)(2,1)S(1)} %bitcast.256, f32[512,32,128]{0,2,1:T(8,128)} %copy.43, bf16[512,32,128]{0,2,1:T(8,128)(2,1)S(1)} %copy-done.6), kind=kOutput, calls=%fused_computation.79 | convolution fusion | flops 2153775104 | bytes 17825792 | tf_op jit(solution)/shard_map/ijc,kjc->ik/dot_general | solution.py:140
  205.1 9.0 %fusion.27 = (bf16[512,32,128]{0,2,1:T(8,128)(2,1)}, bf16[512,32,128]{0,2,1:T(8,128)(2,1)}) fusion(f32[512,32,128]{0,2,1:T(8,128)S(1)} %bitcast.250, bf16[512,32,128]{0,2,1:T(8,128)(2,1)S(1)} %copy-done.6, bf16[512,512]{1,0:T(8,128)(2,1)S(1)} %copy-done, bf16[512,32,128]{2,1,0:T(8,128)(2,1)S(1)} %bitcast.257), kind=kOutput, calls=%fused_computation.58 | convolution fusion | flops 2157969408 | bytes 25690112 | tf_op jit(solution)/shard_map/kjc,ik->ijc/dot_general | solution.py:135
  214.1 30.0 %all-to-all-done.1 = bf16[512,32,128]{2,1,0:T(8,128)(2,1)} async-done(((bf16[512,32,128]{2,1,0:T(8,128)(2,1)}), bf16[512,32,128]{2,1,0:T(8,128)(2,1)}, u32[]{:S(2)}, u32[]{:S(2)}) %all-to-all-start.1) | async-done | bytes 4194336 | tf_op jit(solution)/shard_map/all_to_all | solution.py:133
  244.1 3.6 copy.45
  248.8 8.4 %fusion.22 = (f32[128]{0:T(128)S(1)}, f32[128]{0:T(128)S(1)}, f32[128]{0:T(128)S(1)}, f32[16384,128]{1,0:T(8,128)S(1)}) fusion(bf16[16384,128]{1,0:T(8,128)(2,1)S(1)} %copy-done.3, bf16[2,128]{1,0:T(2,128)(2,1)S(1)} %collective-permute-done.7, bf16[16384,128]{1,0:T(8,128)(2,1)S(1)} %copy-done.5, f32[128]{0:T(128)S(1)} %get-tuple-element.115, ...), kind=kLoop, calls=%fused_computation.48 | loop fusion | flops 54525568 | bytes 25169408 | tf_op jit(solution)/shard_map/reduce_sum | solution.py:152
  257.3 3.3 copy-done.8
  263.1 7.9 %copy.52 = bf16[512,32,128]{2,1,0:T(8,128)(2,1)} copy(bf16[512,32,128]{0,2,1:T(8,128)(2,1)} %get-tuple-element.38) | data formatting | bytes 8388608 | tf_op jit(solution)/shard_map/optimization_barrier | solution.py:141
  271.0 5.8 %all-to-all-start.3 = ((bf16[512,32,128]{2,1,0:T(8,128)(2,1)}), bf16[512,32,128]{2,1,0:T(8,128)(2,1)}, u32[]{:S(2)}, u32[]{:S(2)}) async-start(bf16[512,32,128]{2,1,0:T(8,128)(2,1)} %copy.52), calls=%async_computation.3 | async-start | bytes 8388608 | tf_op jit(solution)/shard_map/all_to_all | solution.py:142
  276.9 16.6 %fusion.3 = f32[16384,128]{1,0:T(8,128)} fusion(f32[16384,128]{1,0:T(8,128)} %copy-done.8, f32[2,128]{1,0:T(2,128)S(1)} %collective-permute-done.8, f32[128]{0:T(128)S(1)} %get-tuple-element.115, f32[128]{0:T(128)S(1)} %copy-done.19, f32[128]{0:T(128)S(1)} %get-tuple-element.112), kind=kLoop, calls=%fused_computation.29 | loop fusion | flops 14680064 | bytes 16779776 | tf_op jit(solution)/shard_map/add | solution.py:150
  293.4 39.1 %all-to-all-done.3 = bf16[512,32,128]{2,1,0:T(8,128)(2,1)} async-done(((bf16[512,32,128]{2,1,0:T(8,128)(2,1)}), bf16[512,32,128]{2,1,0:T(8,128)(2,1)}, u32[]{:S(2)}, u32[]{:S(2)}) %all-to-all-start.3) | async-done | bytes 4194336 | tf_op jit(solution)/shard_map/all_to_all | solution.py:142
  332.5 3.6 copy.53
  340.9 7.8 %copy.57 = bf16[512,32,128]{2,1,0:T(8,128)(2,1)} copy(bf16[512,32,128]{0,2,1:T(8,128)(2,1)} %get-tuple-element.97) | data formatting | bytes 8388608
  354.6 7.9 %convolution_bitcast_fusion = f32[32,512,128]{1,2,0:T(8,128)} fusion(bf16[32,512,128]{2,1,0:T(8,128)(2,1)} %bitcast.260, bf16[512,512]{1,0:T(8,128)(2,1)S(1)} %copy-done.15), kind=kOutput, calls=%fused_computation.76 | convolution fusion | flops 2147483648 | bytes 13107200 | tf_op jit(solution)/shard_map/ikc,jk->ijc/dot_general | solution.py:157
  362.5 9.0 %copy.55 = f32[32,512,128]{2,1,0:T(8,128)} copy(f32[32,512,128]{1,2,0:T(8,128)} %convolution_bitcast_fusion) | data formatting | bytes 16777216 | tf_op jit(solution)/shard_map/ikc,jk->ijc/transpose | solution.py:157
  372.2 3.3 collective-permute-start.16
  377.0 3.1 collective-permute-start.14
  380.5 9.0 %fusion.23 = (f32[128]{0:T(128)S(1)}, f32[128]{0:T(128)S(1)}, f32[128]{0:T(128)S(1)}, f32[16386,128]{1,0:T(8,128)S(1)}) fusion(f32[16384,128]{1,0:T(8,128)} %bitcast.252, bf16[16384,128]{1,0:T(8,128)(2,1)} %copy-done.2, bf16[2,128]{1,0:T(2,128)(2,1)S(1)} %collective-permute-done.7, bf16[16384,128]{1,0:T(8,128)(2,1)} %copy-done.4), kind=kLoop, calls=%fused_computation.49 | loop fusion | flops 25165440 | bytes 25167872 | tf_op jit(solution)/shard_map/reduce_sum | solution.py:169
  390.9 11.0 %multiply_reduce_fusion = (f32[128]{0:T(128)S(1)}, f32[16384]{0:T(1024)S(1)}, f32[16384,128]{1,0:T(8,128)}) fusion(bf16[32,512,128]{2,1,0:T(8,128)(2,1)S(1)} %copy-done.7, f32[16384]{0:T(1024)S(1)} %copy-done.17, f32[128]{0:T(128)S(1)} %copy-done.29, f32[16386,128]{1,0:T(8,128)S(1)} %constant_dynamic-update-slice_fusion, f32[128]{0:T(128)S(1)} %copy-done.24, ...), kind=kLoop, calls=%fused_computation.61 | loop fusion | flops 27246464 | bytes 46270976 | tf_op jit(solution)/shard_map/reduce_sum | solution.py:171
  401.9 4.2 collective-permute-start.26
  406.9 3.8 collective-permute-start.24
  420.9 3.3 collective-permute-start.51
  424.2 3.1 collective-permute-start.50
  428.9 3.2 collective-permute-start.47
  432.1 8.1 %multiply_convert_fusion = bf16[16384,128]{1,0:T(8,128)(2,1)} fusion(f32[16384,128]{1,0:T(8,128)} %get-tuple-element.55, bf16[32,512,128]{2,1,0:T(8,128)(2,1)} %param.9, f32[16384]{0:T(1024)S(1)} %broadcast_multiply_fusion.1, f32[16384]{0:T(1024)S(1)} %copy-done.17), kind=kLoop, calls=%fused_computation.60 | loop fusion | flops 12582912 | bytes 16908288 | tf_op jit(solution)/shard_map/convert_element_type | solution.py:189
  470.5 4.5 collective-permute-start.56
  490.9 3.3 collective-permute-done.61
  504.8 7.0 %collective-permute-start.66 = (f32[2,3,128]{2,1,0:T(4,128)S(1)}, f32[2,3,128]{2,1,0:T(4,128)S(1)}, u32[]{:S(2)}, u32[]{:S(2)}) collective-permute-start(f32[2,3,128]{2,1,0:T(4,128)S(1)} %pad_maximum_fusion.7), channel_id=1, source_target_pairs={{0,120},{8,112},{16,104},{24,96},{32,88},{40,80},{48,72},{56,64},{... | collective-permute-start | bytes 9224 | tf_op jit(solution)/shard_map/ppermute | solution.py:25
  515.9 6.2 %collective-permute-done.35 = f32[128,512]{1,0:T(8,128)S(1)} collective-permute-done((f32[128,512]{1,0:T(8,128)S(1)}, f32[128,512]{1,0:T(8,128)S(1)}, u32[]{:S(2)}, u32[]{:S(2)}) %collective-permute-start.35) | collective-permute-done | bytes 262176 | tf_op jit(solution)/shard_map/ppermute | solution.py:62
  (298 shorter events, 126.2 us)
Async XLA Ops:
  5.2 12.5 %collective-permute-start.6 = (f32[16384]{0:T(1024)S(1)}, f32[16384]{0:T(1024)S(1)}, u32[]{:S(2)}, u32[]{:S(2)}) collective-permute-start(f32[16384]{0:T(1024)S(1)} %bitcast.296), channel_id=1, source_target_pairs={{0,7},{1,6},{2,5},{3,4},{4,3},{5,2},{6,1},{7,0},{8,15},{9,14},{10,... | collective-permute-start | bytes 196616 | tf_op jit(solution)/shard_map/ppermute | solution.py:25
  11.9 7.5 %collective-permute-start.5 = (f32[16384]{0:T(1024)S(1)}, f32[16384]{0:T(1024)S(1)}, u32[]{:S(2)}, u32[]{:S(2)}) collective-permute-start(f32[16384]{0:T(1024)S(1)} %bitcast.297), channel_id=1, source_target_pairs={{0,6},{1,7},{2,4},{3,5},{4,2},{5,3},{6,0},{7,1},{8,14},{9,15},{10,... | collective-permute-start | bytes 196616 | tf_op jit(solution)/shard_map/ppermute | solution.py:25
  12.2 7.2 %collective-permute-start.4 = (f32[16384]{0:T(1024)S(1)}, f32[16384]{0:T(1024)S(1)}, u32[]{:S(2)}, u32[]{:S(2)}) collective-permute-start(f32[16384]{0:T(1024)S(1)} %bitcast.298), channel_id=1, source_target_pairs={{0,5},{1,4},{2,7},{3,6},{4,1},{5,0},{6,3},{7,2},{8,13},{9,12},{10,... | collective-permute-start | bytes 196616 | tf_op jit(solution)/shard_map/ppermute | solution.py:25
  15.1 6.3 %collective-permute-start.3 = (f32[16384]{0:T(1024)S(1)}, f32[16384]{0:T(1024)S(1)}, u32[]{:S(2)}, u32[]{:S(2)}) collective-permute-start(f32[16384]{0:T(1024)S(1)} %bitcast.299), channel_id=1, source_target_pairs={{0,4},{1,5},{2,6},{3,7},{4,0},{5,1},{6,2},{7,3},{8,12},{9,13},{10,... | collective-permute-start | bytes 196616 | tf_op jit(solution)/shard_map/ppermute | solution.py:25
  15.2 6.1 %collective-permute-start.2 = (f32[16384]{0:T(1024)S(1)}, f32[16384]{0:T(1024)S(1)}, u32[]{:S(2)}, u32[]{:S(2)}) collective-permute-start(f32[16384]{0:T(1024)S(1)} %bitcast.300), channel_id=1, source_target_pairs={{0,3},{1,2},{2,1},{3,0},{4,7},{5,6},{6,5},{7,4},{8,11},{9,10},{10,... | collective-permute-start | bytes 196616 | tf_op jit(solution)/shard_map/ppermute | solution.py:25
  29.5 6.1 %collective-permute-start.7 = (bf16[2,128]{1,0:T(2,128)(2,1)S(1)}, bf16[2,128]{1,0:T(2,128)(2,1)S(1)}, u32[]{:S(2)}, u32[]{:S(2)}) collective-permute-start(bf16[2,128]{1,0:T(2,128)(2,1)S(1)} %slice.96), channel_id=1, source_target_pairs={{0,8},{8,16},{16,24},{24,32},{32,40},{40,48},{48,56},{56,64},{64,7... | collective-permute-start | bytes 1544 | tf_op jit(solution)/shard_map/ppermute | solution.py:16
  59.6 62.6 %all-to-all-start = ((bf16[32,512,128]{2,0,1:T(8,128)(2,1)}), bf16[32,512,128]{2,0,1:T(8,128)(2,1)}, u32[]{:S(2)}, u32[]{:S(2)}) async-start(bf16[32,512,128]{2,0,1:T(8,128)(2,1)} %copy.39), calls=%async_computation | async-start | bytes 8388608 | tf_op jit(solution)/shard_map/all_to_all | solution.py:127
  122.2 60.6 %all-to-all-start.2 = ((bf16[32,512,128]{2,0,1:T(8,128)(2,1)}), bf16[32,512,128]{2,0,1:T(8,128)(2,1)}, u32[]{:S(2)}, u32[]{:S(2)}) async-start(bf16[32,512,128]{2,0,1:T(8,128)(2,1)} %copy.46), calls=%async_computation.2 | async-start | bytes 8388608 | tf_op jit(solution)/shard_map/all_to_all | solution.py:134
  182.8 61.4 %all-to-all-start.1 = ((bf16[512,32,128]{2,1,0:T(8,128)(2,1)}), bf16[512,32,128]{2,1,0:T(8,128)(2,1)}, u32[]{:S(2)}, u32[]{:S(2)}) async-start(bf16[512,32,128]{2,1,0:T(8,128)(2,1)} %copy.44), calls=%async_computation.1 | async-start | bytes 8388608 | tf_op jit(solution)/shard_map/all_to_all | solution.py:133
  260.6 16.2 %collective-permute-start.8 = (f32[2,128]{1,0:T(2,128)S(1)}, f32[2,128]{1,0:T(2,128)S(1)}, u32[]{:S(2)}, u32[]{:S(2)}) collective-permute-start(f32[2,128]{1,0:T(2,128)S(1)} %slice.99), channel_id=1, source_target_pairs={{8,0},{16,8},{24,16},{32,24},{40,32},{48,40},{56,48},{64,56},{72,6... | collective-permute-start | bytes 3080 | tf_op jit(solution)/shard_map/ppermute | solution.py:16
  271.0 61.5 %all-to-all-start.3 = ((bf16[512,32,128]{2,1,0:T(8,128)(2,1)}), bf16[512,32,128]{2,1,0:T(8,128)(2,1)}, u32[]{:S(2)}, u32[]{:S(2)}) async-start(bf16[512,32,128]{2,1,0:T(8,128)(2,1)} %copy.52), calls=%async_computation.3 | async-start | bytes 8388608 | tf_op jit(solution)/shard_map/all_to_all | solution.py:142
  339.8 9.0 %collective-permute-start.9 = (f32[512,512]{1,0:T(8,128)}, f32[512,512]{1,0:T(8,128)}, u32[]{:S(2)}, u32[]{:S(2)}) collective-permute-start(f32[512,512]{1,0:T(8,128)} %dynamic-slice_bitcast_fusion), channel_id=1, source_target_pairs={{0,8},{1,9},{2,10},{3,11},{4,12},{5,13},{6,14},{7,15},{8,0},{9,1},... | collective-permute-start | bytes 3145736 | tf_op jit(solution)/shard_map/ppermute | solution.py:62
  351.2 20.2 %collective-permute-start.12 = (f32[128,512]{1,0:T(8,128)S(1)}, f32[128,512]{1,0:T(8,128)S(1)}, u32[]{:S(2)}, u32[]{:S(2)}) collective-permute-start(f32[128,512]{1,0:T(8,128)S(1)} %get-tuple-element.102), channel_id=1, source_target_pairs={{0,48},{1,49},{2,50},{3,51},{4,52},{5,53},{6,54},{7,55},{8,11},{9,... | collective-permute-start | bytes 786440 | tf_op jit(solution)/shard_map/ppermute | solution.py:62
  352.4 19.0 %collective-permute-start.11 = (f32[128,512]{1,0:T(8,128)S(1)}, f32[128,512]{1,0:T(8,128)S(1)}, u32[]{:S(2)}, u32[]{:S(2)}) collective-permute-start(f32[128,512]{1,0:T(8,128)S(1)} %get-tuple-element.103), channel_id=1, source_target_pairs={{0,32},{1,33},{2,34},{3,35},{4,36},{5,37},{6,38},{7,39},{8,10},{9,... | collective-permute-start | bytes 786440 | tf_op jit(solution)/shard_map/ppermute | solution.py:62
  353.2 18.3 %collective-permute-start.10 = (f32[128,512]{1,0:T(8,128)S(1)}, f32[128,512]{1,0:T(8,128)S(1)}, u32[]{:S(2)}, u32[]{:S(2)}) collective-permute-start(f32[128,512]{1,0:T(8,128)S(1)} %get-tuple-element.104), channel_id=1, source_target_pairs={{0,16},{1,17},{2,18},{3,19},{4,20},{5,21},{6,22},{7,23},{8,9},{9,8... | collective-permute-start | bytes 786440 | tf_op jit(solution)/shard_map/ppermute | solution.py:62
  372.2 17.3 %collective-permute-start.16 = (f32[2,128]{1,0:T(2,128)S(1)}, f32[2,128]{1,0:T(2,128)S(1)}, u32[]{:S(2)}, u32[]{:S(2)}) collective-permute-start(f32[2,128]{1,0:T(2,128)S(1)} %slice.75), channel_id=1, source_target_pairs={{8,0},{16,8},{24,16},{32,24},{40,32},{48,40},{56,48},{64,56},{72,6... | collective-permute-start | bytes 3080 | tf_op jit(solution)/shard_map/ppermute | solution.py:16
  376.5 25.4 %collective-permute-start.15 = (f32[32,512]{1,0:T(8,128)S(1)}, f32[32,512]{1,0:T(8,128)S(1)}, u32[]{:S(2)}, u32[]{:S(2)}) collective-permute-start(f32[32,512]{1,0:T(8,128)S(1)} %get-tuple-element.105), channel_id=1, source_target_pairs={{0,3},{1,2},{2,1},{3,0},{4,7},{5,6},{6,5},{7,4},{8,56},{9,57},{10,... | collective-permute-start | bytes 196616 | tf_op jit(solution)/shard_map/ppermute | solution.py:62
  377.0 24.9 %collective-permute-start.14 = (f32[32,512]{1,0:T(8,128)S(1)}, f32[32,512]{1,0:T(8,128)S(1)}, u32[]{:S(2)}, u32[]{:S(2)}) collective-permute-start(f32[32,512]{1,0:T(8,128)S(1)} %get-tuple-element.106), channel_id=1, source_target_pairs={{0,2},{1,3},{2,0},{3,1},{4,6},{5,7},{6,4},{7,5},{8,40},{9,41},{10,... | collective-permute-start | bytes 196616 | tf_op jit(solution)/shard_map/ppermute | solution.py:62
  380.2 21.7 %collective-permute-start.13 = (f32[32,512]{1,0:T(8,128)S(1)}, f32[32,512]{1,0:T(8,128)S(1)}, u32[]{:S(2)}, u32[]{:S(2)}) collective-permute-start(f32[32,512]{1,0:T(8,128)S(1)} %get-tuple-element.107), channel_id=1, source_target_pairs={{0,1},{1,0},{2,3},{3,2},{4,5},{5,4},{6,7},{7,6},{8,24},{9,25},{10,... | collective-permute-start | bytes 196616 | tf_op jit(solution)/shard_map/ppermute | solution.py:62
  401.9 9.9 %collective-permute-start.26 = (f32[16384]{0:T(1024)S(1)}, f32[16384]{0:T(1024)S(1)}, u32[]{:S(2)}, u32[]{:S(2)}) collective-permute-start(f32[16384]{0:T(1024)S(1)} %get-tuple-element.50), channel_id=1, source_target_pairs={{0,7},{1,6},{2,5},{3,4},{4,3},{5,2},{6,1},{7,0},{8,15},{9,14},{10,... | collective-permute-start | bytes 196616 | tf_op jit(solution)/shard_map/ppermute | solution.py:25
  406.1 8.7 %collective-permute-start.25 = (f32[16384]{0:T(1024)S(1)}, f32[16384]{0:T(1024)S(1)}, u32[]{:S(2)}, u32[]{:S(2)}) collective-permute-start(f32[16384]{0:T(1024)S(1)} %get-tuple-element.50), channel_id=1, source_target_pairs={{0,6},{1,7},{2,4},{3,5},{4,2},{5,3},{6,0},{7,1},{8,14},{9,15},{10,... | collective-permute-start | bytes 196616 | tf_op jit(solution)/shard_map/ppermute | solution.py:25
  406.9 8.3 %collective-permute-start.24 = (f32[16384]{0:T(1024)S(1)}, f32[16384]{0:T(1024)S(1)}, u32[]{:S(2)}, u32[]{:S(2)}) collective-permute-start(f32[16384]{0:T(1024)S(1)} %get-tuple-element.50), channel_id=1, source_target_pairs={{0,5},{1,4},{2,7},{3,6},{4,1},{5,0},{6,3},{7,2},{8,13},{9,12},{10,... | collective-permute-start | bytes 196616 | tf_op jit(solution)/shard_map/ppermute | solution.py:25
  410.7 6.1 %collective-permute-start.23 = (f32[16384]{0:T(1024)S(1)}, f32[16384]{0:T(1024)S(1)}, u32[]{:S(2)}, u32[]{:S(2)}) collective-permute-start(f32[16384]{0:T(1024)S(1)} %get-tuple-element.50), channel_id=1, source_target_pairs={{0,4},{1,5},{2,6},{3,7},{4,0},{5,1},{6,2},{7,3},{8,12},{9,13},{10,... | collective-permute-start | bytes 196616 | tf_op jit(solution)/shard_map/ppermute | solution.py:25
  410.7 6.7 %collective-permute-start.22 = (f32[16384]{0:T(1024)S(1)}, f32[16384]{0:T(1024)S(1)}, u32[]{:S(2)}, u32[]{:S(2)}) collective-permute-start(f32[16384]{0:T(1024)S(1)} %get-tuple-element.50), channel_id=1, source_target_pairs={{0,3},{1,2},{2,1},{3,0},{4,7},{5,6},{6,5},{7,4},{8,11},{9,10},{10,... | collective-permute-start | bytes 196616 | tf_op jit(solution)/shard_map/ppermute | solution.py:25
  411.8 6.6 %collective-permute-start.21 = (f32[16384]{0:T(1024)S(1)}, f32[16384]{0:T(1024)S(1)}, u32[]{:S(2)}, u32[]{:S(2)}) collective-permute-start(f32[16384]{0:T(1024)S(1)} %get-tuple-element.50), channel_id=1, source_target_pairs={{0,2},{1,3},{2,0},{3,1},{4,6},{5,7},{6,4},{7,5},{8,10},{9,11},{10,... | collective-permute-start | bytes 196616 | tf_op jit(solution)/shard_map/ppermute | solution.py:25
  420.9 19.3 %collective-permute-start.51 = (f32[128]{0:T(128)S(1)}, f32[128]{0:T(128)S(1)}, u32[]{:S(2)}, u32[]{:S(2)}) collective-permute-start(f32[128]{0:T(128)S(1)} %get-tuple-element.60), channel_id=1, source_target_pairs={{0,120},{8,112},{16,104},{24,96},{32,88},{40,80},{48,72},{56,64},{... | collective-permute-start | bytes 1544 | tf_op jit(solution)/shard_map/ppermute | solution.py:25
  424.2 18.1 %collective-permute-start.50 = (f32[128]{0:T(128)S(1)}, f32[128]{0:T(128)S(1)}, u32[]{:S(2)}, u32[]{:S(2)}) collective-permute-start(f32[128]{0:T(128)S(1)} %get-tuple-element.60), channel_id=1, source_target_pairs={{0,112},{8,120},{16,96},{24,104},{32,80},{40,88},{48,64},{56,72},{... | collective-permute-start | bytes 1544 | tf_op jit(solution)/shard_map/ppermute | solution.py:25
  427.3 15.0 %collective-permute-start.49 = (f32[128]{0:T(128)S(1)}, f32[128]{0:T(128)S(1)}, u32[]{:S(2)}, u32[]{:S(2)}) collective-permute-start(f32[128]{0:T(128)S(1)} %get-tuple-element.60), channel_id=1, source_target_pairs={{0,104},{8,96},{16,120},{24,112},{32,72},{40,64},{48,88},{56,80},{... | collective-permute-start | bytes 1544 | tf_op jit(solution)/shard_map/ppermute | solution.py:25
  428.5 14.0 %collective-permute-start.48 = (f32[128]{0:T(128)S(1)}, f32[128]{0:T(128)S(1)}, u32[]{:S(2)}, u32[]{:S(2)}) collective-permute-start(f32[128]{0:T(128)S(1)} %get-tuple-element.60), channel_id=1, source_target_pairs={{0,96},{8,104},{16,112},{24,120},{32,64},{40,72},{48,80},{56,88},{... | collective-permute-start | bytes 1544 | tf_op jit(solution)/shard_map/ppermute | solution.py:25
  428.9 16.3 %collective-permute-start.47 = (f32[128]{0:T(128)S(1)}, f32[128]{0:T(128)S(1)}, u32[]{:S(2)}, u32[]{:S(2)}) collective-permute-start(f32[128]{0:T(128)S(1)} %get-tuple-element.60), channel_id=1, source_target_pairs={{0,88},{8,80},{16,72},{24,64},{32,120},{40,112},{48,104},{56,96},{... | collective-permute-start | bytes 1544 | tf_op jit(solution)/shard_map/ppermute | solution.py:25
  440.2 6.9 %collective-permute-start.46 = (f32[128]{0:T(128)S(1)}, f32[128]{0:T(128)S(1)}, u32[]{:S(2)}, u32[]{:S(2)}) collective-permute-start(f32[128]{0:T(128)S(1)} %get-tuple-element.60), channel_id=1, source_target_pairs={{0,80},{8,88},{16,64},{24,72},{32,112},{40,120},{48,96},{56,104},{... | collective-permute-start | bytes 1544 | tf_op jit(solution)/shard_map/ppermute | solution.py:25
  442.3 6.4 %collective-permute-start.44 = (f32[128]{0:T(128)S(1)}, f32[128]{0:T(128)S(1)}, u32[]{:S(2)}, u32[]{:S(2)}) collective-permute-start(f32[128]{0:T(128)S(1)} %get-tuple-element.60), channel_id=1, source_target_pairs={{0,64},{8,72},{16,80},{24,88},{32,96},{40,104},{48,112},{56,120},{... | collective-permute-start | bytes 1544 | tf_op jit(solution)/shard_map/ppermute | solution.py:25
  442.4 7.5 %collective-permute-start.43 = (f32[128]{0:T(128)S(1)}, f32[128]{0:T(128)S(1)}, u32[]{:S(2)}, u32[]{:S(2)}) collective-permute-start(f32[128]{0:T(128)S(1)} %get-tuple-element.60), channel_id=1, source_target_pairs={{0,56},{8,48},{16,40},{24,32},{32,24},{40,16},{48,8},{56,0},{64,12... | collective-permute-start | bytes 1544 | tf_op jit(solution)/shard_map/ppermute | solution.py:25
  445.2 6.9 %collective-permute-start.42 = (f32[128]{0:T(128)S(1)}, f32[128]{0:T(128)S(1)}, u32[]{:S(2)}, u32[]{:S(2)}) collective-permute-start(f32[128]{0:T(128)S(1)} %get-tuple-element.60), channel_id=1, source_target_pairs={{0,48},{8,56},{16,32},{24,40},{32,16},{40,24},{48,0},{56,8},{64,11... | collective-permute-start | bytes 1544 | tf_op jit(solution)/shard_map/ppermute | solution.py:25
  447.0 6.0 %collective-permute-start.40 = (f32[128]{0:T(128)S(1)}, f32[128]{0:T(128)S(1)}, u32[]{:S(2)}, u32[]{:S(2)}) collective-permute-start(f32[128]{0:T(128)S(1)} %get-tuple-element.60), channel_id=1, source_target_pairs={{0,32},{8,40},{16,48},{24,56},{32,0},{40,8},{48,16},{56,24},{64,96... | collective-permute-start | bytes 1544 | tf_op jit(solution)/shard_map/ppermute | solution.py:25
  448.7 6.8 %collective-permute-start.39 = (f32[128]{0:T(128)S(1)}, f32[128]{0:T(128)S(1)}, u32[]{:S(2)}, u32[]{:S(2)}) collective-permute-start(f32[128]{0:T(128)S(1)} %get-tuple-element.60), channel_id=1, source_target_pairs={{0,24},{8,16},{16,8},{24,0},{32,56},{40,48},{48,40},{56,32},{64,88... | collective-permute-start | bytes 1544 | tf_op jit(solution)/shard_map/ppermute | solution.py:25
  449.9 7.4 %collective-permute-start.38 = (f32[128]{0:T(128)S(1)}, f32[128]{0:T(128)S(1)}, u32[]{:S(2)}, u32[]{:S(2)}) collective-permute-start(f32[128]{0:T(128)S(1)} %get-tuple-element.60), channel_id=1, source_target_pairs={{0,16},{8,24},{16,0},{24,8},{32,48},{40,56},{48,32},{56,40},{64,80... | collective-permute-start | bytes 1544 | tf_op jit(solution)/shard_map/ppermute | solution.py:25
  452.0 6.1 %collective-permute-start.37 = (f32[128]{0:T(128)S(1)}, f32[128]{0:T(128)S(1)}, u32[]{:S(2)}, u32[]{:S(2)}) collective-permute-start(f32[128]{0:T(128)S(1)} %get-tuple-element.60), channel_id=1, source_target_pairs={{0,8},{8,0},{16,24},{24,16},{32,40},{40,32},{48,56},{56,48},{64,72... | collective-permute-start | bytes 1544 | tf_op jit(solution)/shard_map/ppermute | solution.py:25
  452.1 72.3 %collective-permute-start.65 = (f32[2,3,128]{2,1,0:T(4,128)S(1)}, f32[2,3,128]{2,1,0:T(4,128)S(1)}, u32[]{:S(2)}, u32[]{:S(2)}) collective-permute-start(f32[2,3,128]{2,1,0:T(4,128)S(1)} %pad_maximum_fusion.7), channel_id=1, source_target_pairs={{0,112},{8,120},{16,96},{24,104},{32,80},{40,88},{48,64},{56,72},{... | collective-permute-start | bytes 9224 | tf_op jit(solution)/shard_map/ppermute | solution.py:25
  453.1 60.7 %collective-permute-start.64 = (f32[2,3,128]{2,1,0:T(4,128)S(1)}, f32[2,3,128]{2,1,0:T(4,128)S(1)}, u32[]{:S(2)}, u32[]{:S(2)}) collective-permute-start(f32[2,3,128]{2,1,0:T(4,128)S(1)} %pad_maximum_fusion.7), channel_id=1, source_target_pairs={{0,104},{8,96},{16,120},{24,112},{32,72},{40,64},{48,88},{56,80},{... | collective-permute-start | bytes 9224 | tf_op jit(solution)/shard_map/ppermute | solution.py:25
  455.6 41.3 %collective-permute-start.63 = (f32[2,3,128]{2,1,0:T(4,128)S(1)}, f32[2,3,128]{2,1,0:T(4,128)S(1)}, u32[]{:S(2)}, u32[]{:S(2)}) collective-permute-start(f32[2,3,128]{2,1,0:T(4,128)S(1)} %pad_maximum_fusion.7), channel_id=1, source_target_pairs={{0,96},{8,104},{16,112},{24,120},{32,64},{40,72},{48,80},{56,88},{... | collective-permute-start | bytes 9224 | tf_op jit(solution)/shard_map/ppermute | solution.py:25
  457.3 38.3 %collective-permute-start.62 = (f32[2,3,128]{2,1,0:T(4,128)S(1)}, f32[2,3,128]{2,1,0:T(4,128)S(1)}, u32[]{:S(2)}, u32[]{:S(2)}) collective-permute-start(f32[2,3,128]{2,1,0:T(4,128)S(1)} %pad_maximum_fusion.7), channel_id=1, source_target_pairs={{0,88},{8,80},{16,72},{24,64},{32,120},{40,112},{48,104},{56,96},{... | collective-permute-start | bytes 9224 | tf_op jit(solution)/shard_map/ppermute | solution.py:25
  502.3 9.5 %collective-permute-start.31 = (f32[32,512]{1,0:T(8,128)S(1)}, f32[32,512]{1,0:T(8,128)S(1)}, u32[]{:S(2)}, u32[]{:S(2)}) collective-permute-start(f32[32,512]{1,0:T(8,128)S(1)} %bitcast_select_fusion.4), channel_id=1, source_target_pairs={{0,2},{1,3},{2,0},{3,1},{4,6},{5,7},{6,4},{7,5},{8,40},{9,41},{10,... | collective-permute-start | bytes 196616 | tf_op jit(solution)/shard_map/ppermute | solution.py:62
  502.3 9.5 %collective-permute-start.30 = (f32[32,512]{1,0:T(8,128)S(1)}, f32[32,512]{1,0:T(8,128)S(1)}, u32[]{:S(2)}, u32[]{:S(2)}) collective-permute-start(f32[32,512]{1,0:T(8,128)S(1)} %bitcast_select_fusion.4), channel_id=1, source_target_pairs={{0,1},{1,0},{2,3},{3,2},{4,5},{5,4},{6,7},{7,6},{8,24},{9,25},{10,... | collective-permute-start | bytes 196616 | tf_op jit(solution)/shard_map/ppermute | solution.py:62
  504.8 19.6 %collective-permute-start.66 = (f32[2,3,128]{2,1,0:T(4,128)S(1)}, f32[2,3,128]{2,1,0:T(4,128)S(1)}, u32[]{:S(2)}, u32[]{:S(2)}) collective-permute-start(f32[2,3,128]{2,1,0:T(4,128)S(1)} %pad_maximum_fusion.7), channel_id=1, source_target_pairs={{0,120},{8,112},{16,104},{24,96},{32,88},{40,80},{48,72},{56,64},{... | collective-permute-start | bytes 9224 | tf_op jit(solution)/shard_map/ppermute | solution.py:25
  512.4 9.6 %collective-permute-start.35 = (f32[128,512]{1,0:T(8,128)S(1)}, f32[128,512]{1,0:T(8,128)S(1)}, u32[]{:S(2)}, u32[]{:S(2)}) collective-permute-start(f32[128,512]{1,0:T(8,128)S(1)} %bitcast_select_fusion.2), channel_id=1, source_target_pairs={{0,48},{1,49},{2,50},{3,51},{4,52},{5,53},{6,54},{7,55},{8,11},{9,... | collective-permute-start | bytes 786440 | tf_op jit(solution)/shard_map/ppermute | solution.py:62
  513.7 8.3 %collective-permute-start.34 = (f32[128,512]{1,0:T(8,128)S(1)}, f32[128,512]{1,0:T(8,128)S(1)}, u32[]{:S(2)}, u32[]{:S(2)}) collective-permute-start(f32[128,512]{1,0:T(8,128)S(1)} %bitcast_select_fusion.2), channel_id=1, source_target_pairs={{0,32},{1,33},{2,34},{3,35},{4,36},{5,37},{6,38},{7,39},{8,10},{9,... | collective-permute-start | bytes 786440 | tf_op jit(solution)/shard_map/ppermute | solution.py:62
  513.8 8.9 %collective-permute-start.33 = (f32[128,512]{1,0:T(8,128)S(1)}, f32[128,512]{1,0:T(8,128)S(1)}, u32[]{:S(2)}, u32[]{:S(2)}) collective-permute-start(f32[128,512]{1,0:T(8,128)S(1)} %bitcast_select_fusion.2), channel_id=1, source_target_pairs={{0,16},{1,17},{2,18},{3,19},{4,20},{5,21},{6,22},{7,23},{8,9},{9,8... | collective-permute-start | bytes 786440 | tf_op jit(solution)/shard_map/ppermute | solution.py:62
  (65 other events, 658.2 us)

commit v13 on v11

--- a/solution.py
+++ b/solution.py
@@ -178,7 +178,8 @@
     )
     one_total, two_total = both_total[: one_part.shape[0]], both_total[one_part.shape[0] :]
     tap_part = jnp.stack([jnp.stack(value_taps), jnp.stack(gate_taps)])
-    gain_total, taps_total = tree_psum((gain_part, tap_part), "ctx")
+    packed = tree_psum(jnp.concatenate([gain_part[None], tap_part.reshape(-1, chans)]), "ctx")
+    gain_total, taps_total = packed[0], packed[1:].reshape(tap_part.shape)
     row_mean = row_total / WIDTH
     input_grad = (
         (inverse[:, None] * (scaled - hat * row_mean[:, None]))

time: 479 us -> 472 us (0.985)
  starting transfers between devices: 91.4 us -> 83 us
    ppermute x14 -> x10, starting transfers between devices: 27.5 us -> 21.5 us  [tree_psum(): lax.ppermute(value, axis, pairs)]
    ppermute x14 -> x10, waiting for transfers between devices: 10.9 us -> 9.73 us  [tree_psum(): lax.ppermute(value, axis, pairs)]
    unnamed x72 -> x70, local copies, waits for them, and re-layouts: 24.7 us -> 24.8 us
  transfers between devices with their start and end apart: 41 -> 37, of which waited for: 18 -> 15; matrix products, arithmetic and copies ran while one was open for 33% -> 34% of each run, Pallas kernels for 0% -> 0%
where the time goes in v13:
time: 472 us; the launch traced here: 463 us
  waiting for transfers between devices  154 us (33%)
  local copies, waits for them, and re-layouts  100 us (21%)
  starting transfers between devices  83 us (18%)
  other arithmetic  82.3 us (17%)
  matrix products  41.6 us (9%)
    all_to_all x1, waiting for transfers between devices, on_device(): lax.all_to_all(section_one, 'ctx', split_axis=1, concat_axis=0, tiled=True)  48.8 us
    all_to_all x1, waiting for transfers between devices, on_device(): lax.all_to_all(grad_section, 'ctx', split_axis=0, concat_axis=1, tiled=True)  39.2 us
    all_to_all x1, waiting for transfers between devices, on_device(): lax.all_to_all(section_two, 'ctx', split_axis=0, concat_axis=1, tiled=True)  32.7 us
    ppermute x20, starting transfers between devices, group_exchange(): return lax.ppermute(value, ('ctx', 'ch'), pairs)  25.1 us
    unnamed x70, local copies, waits for them, and re-layouts  24.8 us
    ppermute x10, starting transfers between devices, tree_psum(): lax.ppermute(value, axis, pairs)  21.5 us
    add x1, other arithmetic, on_device(): gate_normed + conv_taps[1, offset] * ext_gate[offset:offset + rows]  16.5 us
    convert_element_type x2, local copies, waits for them, and re-layouts, on_device(): spectrum = (columns.astype(jnp.float32) * kern).astype(jnp.bfloat16)  14.4 us
  transfers between devices with their start and end apart: 37, of which 15 were waited for; matrix products, arithmetic and copies ran while one was open for 34% of the time, Pallas kernels for 0%

profile of v13, /device:TPU:1, one launch (start us, length us, event | category | flops | bytes accessed | tf_op | source)
XLA Modules:
  0.0 463.1 jit_solution(5459238615232378678)
XLA Ops:
  0.7 4.6 multiply_reduce_fusion.2
  9.1 3.1 collective-permute-start.1
  13.8 3.9 collective-permute-start.2
  19.4 4.4 multiply_convert_fusion.1
  23.9 6.9 %collective-permute-start.3 = (bf16[2,128]{1,0:T(2,128)(2,1)S(1)}, bf16[2,128]{1,0:T(2,128)(2,1)S(1)}, u32[]{:S(2)}, u32[]{:S(2)}) collective-permute-start(bf16[2,128]{1,0:T(2,128)(2,1)S(1)} %slice.96), channel_id=1, source_target_pairs={{0,8},{8,16},{16,24},{24,32},{32,40},{40,48},{48,56},{56,64},{64,7... | collective-permute-start | bytes 1544 | tf_op jit(solution)/shard_map/ppermute | solution.py:16
  31.5 6.5 %fusion.6 = (bf16[16384,128]{1,0:T(8,128)(2,1)}, bf16[16384,128]{1,0:T(8,128)(2,1)S(1)}) fusion(bf16[32,512,128]{2,1,0:T(8,128)(2,1)S(1)} %copy-done.10, bf16[16384,128]{1,0:T(8,128)(2,1)S(1)} %multiply_convert_fusion.1, bf16[2,128]{1,0:T(2,128)(2,1)S(1)} %collective-permute-done.3, f32[128]{0:T(128)S(1)} %get-tuple-element.114, ...), kind=kLoop, calls=%fused_computation.28 | loop fusion | flops 44040192 | bytes 16779264 | tf_op jit(solution)/shard_map/convert_element_type | solution.py:122
  38.0 3.0 fusion.11
  43.1 4.4 convert_bitcast_fusion.2
  47.5 8.0 %copy.40 = bf16[32,512,128]{2,0,1:T(8,128)(2,1)} copy(bf16[32,512,128]{1,2,0:T(8,128)(2,1)} %convert_bitcast_fusion.2) | data formatting | bytes 8388608 | tf_op jit(solution)/shard_map/convert_element_type | solution.py:121
  55.6 7.2 %all-to-all-start = ((bf16[32,512,128]{2,0,1:T(8,128)(2,1)}), bf16[32,512,128]{2,0,1:T(8,128)(2,1)}, u32[]{:S(2)}, u32[]{:S(2)}) async-start(bf16[32,512,128]{2,0,1:T(8,128)(2,1)} %copy.40), calls=%async_computation | async-start | bytes 8388608 | tf_op jit(solution)/shard_map/all_to_all | solution.py:123
  62.7 6.9 %copy.47 = bf16[32,512,128]{2,0,1:T(8,128)(2,1)} copy(bf16[32,512,128]{2,1,0:T(8,128)(2,1)} %bitcast.196) | data formatting | bytes 8388608 | tf_op jit(solution)/shard_map/reshape | solution.py:122
  69.6 48.8 %all-to-all-done = bf16[32,512,128]{2,0,1:T(8,128)(2,1)} async-done(((bf16[32,512,128]{2,0,1:T(8,128)(2,1)}), bf16[32,512,128]{2,0,1:T(8,128)(2,1)}, u32[]{:S(2)}, u32[]{:S(2)}) %all-to-all-start) | async-done | bytes 4194336 | tf_op jit(solution)/shard_map/all_to_all | solution.py:123
  118.4 4.9 %all-to-all-start.2 = ((bf16[32,512,128]{2,0,1:T(8,128)(2,1)}), bf16[32,512,128]{2,0,1:T(8,128)(2,1)}, u32[]{:S(2)}, u32[]{:S(2)}) async-start(bf16[32,512,128]{2,0,1:T(8,128)(2,1)} %copy.47), calls=%async_computation.2 | async-start | bytes 8388608 | tf_op jit(solution)/shard_map/all_to_all | solution.py:130
  123.3 7.5 %copy.43 = bf16[512,32,128]{0,2,1:T(8,128)(2,1)} copy(bf16[512,32,128]{2,1,0:T(8,128)(2,1)} %param.12) | data formatting | bytes 8388608 | tf_op args[5]
  130.8 3.8 copy.41
  135.8 4.3 copy.42
  140.1 10.0 %copy.44 = f32[512,32,128]{0,2,1:T(8,128)} copy(f32[512,32,128]{2,1,0:T(8,128)} %bitcast.193) | data formatting | bytes 16777216 | tf_op jit(solution)/shard_map/convert_element_type | solution.py:125
  150.1 8.9 %convert_bitcast_fusion.1 = bf16[512,32,128]{0,2,1:T(8,128)(2,1)} fusion(bf16[512,512]{1,0:T(8,128)(2,1)S(1)} %copy-done, f32[512,32,128]{0,2,1:T(8,128)} %copy.44, bf16[512,32,128]{0,2,1:T(8,128)(2,1)} %copy.43), kind=kOutput, calls=%fused_computation.65 | convolution fusion | flops 2155872256 | bytes 17301504 | tf_op jit(solution)/shard_map/ijc,ik->kjc/dot_general | solution.py:126
  159.0 8.0 %copy.45 = bf16[512,32,128]{2,1,0:T(8,128)(2,1)} copy(bf16[512,32,128]{0,2,1:T(8,128)(2,1)} %convert_bitcast_fusion.1) | data formatting | bytes 8388608 | tf_op jit(solution)/shard_map/convert_element_type | solution.py:128
  167.0 11.9 %all-to-all-done.2 = bf16[32,512,128]{2,0,1:T(8,128)(2,1)} async-done(((bf16[32,512,128]{2,0,1:T(8,128)(2,1)}), bf16[32,512,128]{2,0,1:T(8,128)(2,1)}, u32[]{:S(2)}, u32[]{:S(2)}) %all-to-all-start.2) | async-done | bytes 4194336 | tf_op jit(solution)/shard_map/all_to_all | solution.py:130
  179.0 5.4 %all-to-all-start.1 = ((bf16[512,32,128]{2,1,0:T(8,128)(2,1)}), bf16[512,32,128]{2,1,0:T(8,128)(2,1)}, u32[]{:S(2)}, u32[]{:S(2)}) async-start(bf16[512,32,128]{2,1,0:T(8,128)(2,1)} %copy.45), calls=%async_computation.1 | async-start | bytes 8388608 | tf_op jit(solution)/shard_map/all_to_all | solution.py:129
  185.1 4.2 copy.49
  189.4 9.0 %fusion.33 = f32[512,512]{1,0:T(8,128)} fusion(bf16[512,32,128]{2,1,0:T(8,128)(2,1)S(1)} %bitcast.191, f32[512,32,128]{0,2,1:T(8,128)} %copy.44, bf16[512,32,128]{0,2,1:T(8,128)(2,1)S(1)} %copy-done.6), kind=kOutput, calls=%fused_computation.75 | convolution fusion | flops 2153775104 | bytes 17825792 | tf_op jit(solution)/shard_map/ijc,kjc->ik/dot_general | solution.py:136
  198.4 9.0 %fusion.27 = (bf16[512,32,128]{0,2,1:T(8,128)(2,1)}, bf16[512,32,128]{0,2,1:T(8,128)(2,1)}) fusion(f32[512,32,128]{0,2,1:T(8,128)S(1)} %bitcast.185, bf16[512,32,128]{0,2,1:T(8,128)(2,1)S(1)} %copy-done.6, bf16[512,512]{1,0:T(8,128)(2,1)S(1)} %copy-done, bf16[512,32,128]{2,1,0:T(8,128)(2,1)S(1)} %bitcast.192), kind=kOutput, calls=%fused_computation.54 | convolution fusion | flops 2157969408 | bytes 25690112 | tf_op jit(solution)/shard_map/kjc,ik->ijc/dot_general | solution.py:131
  207.4 32.7 %all-to-all-done.1 = bf16[512,32,128]{2,1,0:T(8,128)(2,1)} async-done(((bf16[512,32,128]{2,1,0:T(8,128)(2,1)}), bf16[512,32,128]{2,1,0:T(8,128)(2,1)}, u32[]{:S(2)}, u32[]{:S(2)}) %all-to-all-start.1) | async-done | bytes 4194336 | tf_op jit(solution)/shard_map/all_to_all | solution.py:129
  240.1 3.6 copy.46
  244.9 8.4 %fusion.22 = (f32[128]{0:T(128)S(1)}, f32[128]{0:T(128)S(1)}, f32[128]{0:T(128)S(1)}, f32[16384,128]{1,0:T(8,128)S(1)}) fusion(bf16[16384,128]{1,0:T(8,128)(2,1)S(1)} %copy-done.3, bf16[2,128]{1,0:T(2,128)(2,1)S(1)} %collective-permute-done.3, bf16[16384,128]{1,0:T(8,128)(2,1)S(1)} %copy-done.5, f32[128]{0:T(128)S(1)} %get-tuple-element.114, ...), kind=kLoop, calls=%fused_computation.44 | loop fusion | flops 54525568 | bytes 25169408 | tf_op jit(solution)/shard_map/reduce_sum | solution.py:148
  253.3 3.3 copy-done.8
  259.1 8.0 %copy.53 = bf16[512,32,128]{2,1,0:T(8,128)(2,1)} copy(bf16[512,32,128]{0,2,1:T(8,128)(2,1)} %get-tuple-element.37) | data formatting | bytes 8388608 | tf_op jit(solution)/shard_map/optimization_barrier | solution.py:137
  267.1 5.9 %all-to-all-start.3 = ((bf16[512,32,128]{2,1,0:T(8,128)(2,1)}), bf16[512,32,128]{2,1,0:T(8,128)(2,1)}, u32[]{:S(2)}, u32[]{:S(2)}) async-start(bf16[512,32,128]{2,1,0:T(8,128)(2,1)} %copy.53), calls=%async_computation.3 | async-start | bytes 8388608 | tf_op jit(solution)/shard_map/all_to_all | solution.py:138
  273.0 16.5 %fusion.3 = f32[16384,128]{1,0:T(8,128)} fusion(f32[16384,128]{1,0:T(8,128)} %copy-done.8, f32[2,128]{1,0:T(2,128)S(1)} %collective-permute-done.4, f32[128]{0:T(128)S(1)} %get-tuple-element.114, f32[128]{0:T(128)S(1)} %copy-done.19, f32[128]{0:T(128)S(1)} %get-tuple-element.111), kind=kLoop, calls=%fused_computation.25 | loop fusion | flops 14680064 | bytes 16779776 | tf_op jit(solution)/shard_map/add | solution.py:146
  289.4 39.2 %all-to-all-done.3 = bf16[512,32,128]{2,1,0:T(8,128)(2,1)} async-done(((bf16[512,32,128]{2,1,0:T(8,128)(2,1)}), bf16[512,32,128]{2,1,0:T(8,128)(2,1)}, u32[]{:S(2)}, u32[]{:S(2)}) %all-to-all-start.3) | async-done | bytes 4194336 | tf_op jit(solution)/shard_map/all_to_all | solution.py:138
  328.6 3.6 copy.54
  344.9 7.9 %convolution_bitcast_fusion = f32[32,512,128]{1,2,0:T(8,128)} fusion(bf16[32,512,128]{2,1,0:T(8,128)(2,1)} %bitcast.195, bf16[512,512]{1,0:T(8,128)(2,1)S(1)} %copy-done.15), kind=kOutput, calls=%fused_computation.72 | convolution fusion | flops 2147483648 | bytes 13107200 | tf_op jit(solution)/shard_map/ikc,jk->ijc/dot_general | solution.py:153
  352.8 9.0 %copy.56 = f32[32,512,128]{2,1,0:T(8,128)} copy(f32[32,512,128]{1,2,0:T(8,128)} %convolution_bitcast_fusion) | data formatting | bytes 16777216 | tf_op jit(solution)/shard_map/ikc,jk->ijc/transpose | solution.py:153
  362.5 3.6 collective-permute-start.12
  367.6 3.1 collective-permute-start.10
  371.2 8.9 %fusion.23 = (f32[128]{0:T(128)S(1)}, f32[128]{0:T(128)S(1)}, f32[128]{0:T(128)S(1)}, f32[16386,128]{1,0:T(8,128)S(1)}) fusion(f32[16384,128]{1,0:T(8,128)} %bitcast.187, bf16[16384,128]{1,0:T(8,128)(2,1)} %copy-done.2, bf16[2,128]{1,0:T(2,128)(2,1)S(1)} %collective-permute-done.3, bf16[16384,128]{1,0:T(8,128)(2,1)} %copy-done.4), kind=kLoop, calls=%fused_computation.45 | loop fusion | flops 25165440 | bytes 25167872 | tf_op jit(solution)/shard_map/reduce_sum | solution.py:165
  381.5 11.1 %multiply_reduce_fusion = (f32[128]{0:T(128)S(1)}, f32[16384]{0:T(1024)S(1)}, f32[16384,128]{1,0:T(8,128)}) fusion(bf16[32,512,128]{2,1,0:T(8,128)(2,1)S(1)} %copy-done.7, f32[16384]{0:T(1024)S(1)} %copy-done.17, f32[128]{0:T(128)S(1)} %copy-done.27, f32[16386,128]{1,0:T(8,128)S(1)} %constant_dynamic-update-slice_fusion, f32[128]{0:T(128)S(1)} %copy-done.23, ...), kind=kLoop, calls=%fused_computation.57 | loop fusion | flops 27246464 | bytes 46270976 | tf_op jit(solution)/shard_map/reduce_sum | solution.py:167
  393.9 2.6 collective-permute-done.16
  398.9 3.4 collective-permute-start.15
  403.0 2.6 collective-permute-start.18
  407.8 2.7 collective-permute-start.29
  410.5 3.0 collective-permute-start.21
  415.8 7.8 %copy.58 = bf16[512,32,128]{2,1,0:T(8,128)(2,1)} copy(bf16[512,32,128]{0,2,1:T(8,128)(2,1)} %get-tuple-element.96) | data formatting | bytes 8388608
  436.9 5.0 %collective-permute-done.27 = f32[128,512]{1,0:T(8,128)S(1)} collective-permute-done((f32[128,512]{1,0:T(8,128)S(1)}, f32[128,512]{1,0:T(8,128)S(1)}, u32[]{:S(2)}, u32[]{:S(2)}) %collective-permute-start.27) | collective-permute-done | bytes 262176 | tf_op jit(solution)/shard_map/ppermute | solution.py:58
  443.4 2.9 collective-permute-start.28
  446.3 8.1 %multiply_convert_fusion = bf16[16384,128]{1,0:T(8,128)(2,1)} fusion(f32[16384,128]{1,0:T(8,128)} %get-tuple-element.54, bf16[32,512,128]{2,1,0:T(8,128)(2,1)} %param.7, f32[16384]{0:T(1024)S(1)} %broadcast_multiply_fusion.1, f32[16384]{0:T(1024)S(1)} %copy-done.17), kind=kLoop, calls=%fused_computation.56 | loop fusion | flops 12582912 | bytes 16908288 | tf_op jit(solution)/shard_map/convert_element_type | solution.py:186
  (190 shorter events, 63.6 us)
Async XLA Ops:
  0.6 149.5 %copy-start = (bf16[512,512]{1,0:T(8,128)(2,1)S(1)}, bf16[512,512]{1,0:T(8,128)(2,1)}, u32[]{:S(2)}) copy-start(bf16[512,512]{1,0:T(8,128)(2,1)} %param.11) | copy-start | bytes 1572868
  0.6 30.2 %copy-start.26 = (f32[2,3,128]{2,0,1:T(2,128)S(1)}, f32[2,3,128]{2,0,1:T(2,128)}, u32[]{:S(2)}) copy-start(f32[2,3,128]{2,0,1:T(2,128)} %param.9) | copy-start | bytes 9220
  0.7 30.8 %copy-start.10 = (bf16[32,512,128]{2,1,0:T(8,128)(2,1)S(1)}, bf16[32,512,128]{2,1,0:T(8,128)(2,1)}, u32[]{:S(2)}) copy-start(bf16[32,512,128]{2,1,0:T(8,128)(2,1)} %param.13) | copy-start | bytes 12582916
  5.3 3.8 collective-permute-start
  9.1 4.7 %collective-permute-start.1 = (f32[16384]{0:T(1024)S(1)}, f32[16384]{0:T(1024)S(1)}, u32[]{:S(2)}, u32[]{:S(2)}) collective-permute-start(f32[16384]{0:T(1024)S(1)} %add.247), channel_id=1, source_target_pairs={{0,2},{1,3},{2,0},{3,1},{4,6},{5,7},{6,4},{7,5},{8,10},{9,11},{10,... | collective-permute-start | bytes 196616 | tf_op jit(solution)/shard_map/ppermute | solution.py:24
  13.8 5.6 %collective-permute-start.2 = (f32[16384]{0:T(1024)S(1)}, f32[16384]{0:T(1024)S(1)}, u32[]{:S(2)}, u32[]{:S(2)}) collective-permute-start(f32[16384]{0:T(1024)S(1)} %add.248), channel_id=1, source_target_pairs={{0,4},{1,5},{2,6},{3,7},{4,0},{5,1},{6,2},{7,3},{8,12},{9,13},{10,... | collective-permute-start | bytes 196616 | tf_op jit(solution)/shard_map/ppermute | solution.py:24
  19.4 12.1 %copy-start.16 = (f32[16384]{0:T(1024)}, f32[16384]{0:T(1024)S(1)}, u32[]{:S(2)}) copy-start(f32[16384]{0:T(1024)S(1)} %add_rsqrt_fusion) | copy-start | bytes 196612
  23.8 14.2 %copy-start.2 = (bf16[16384,128]{1,0:T(8,128)(2,1)}, bf16[16384,128]{1,0:T(8,128)(2,1)S(1)}, u32[]{:S(2)}) copy-start(bf16[16384,128]{1,0:T(8,128)(2,1)S(1)} %multiply_convert_fusion.1) | copy-start | bytes 12582916
  23.9 7.6 %collective-permute-start.3 = (bf16[2,128]{1,0:T(2,128)(2,1)S(1)}, bf16[2,128]{1,0:T(2,128)(2,1)S(1)}, u32[]{:S(2)}, u32[]{:S(2)}) collective-permute-start(bf16[2,128]{1,0:T(2,128)(2,1)S(1)} %slice.96), channel_id=1, source_target_pairs={{0,8},{8,16},{16,24},{24,32},{32,40},{40,48},{48,56},{56,64},{64,7... | collective-permute-start | bytes 1544 | tf_op jit(solution)/shard_map/ppermute | solution.py:16
  55.6 62.9 %all-to-all-start = ((bf16[32,512,128]{2,0,1:T(8,128)(2,1)}), bf16[32,512,128]{2,0,1:T(8,128)(2,1)}, u32[]{:S(2)}, u32[]{:S(2)}) async-start(bf16[32,512,128]{2,0,1:T(8,128)(2,1)} %copy.40), calls=%async_computation | async-start | bytes 8388608 | tf_op jit(solution)/shard_map/all_to_all | solution.py:123
  118.4 60.6 %all-to-all-start.2 = ((bf16[32,512,128]{2,0,1:T(8,128)(2,1)}), bf16[32,512,128]{2,0,1:T(8,128)(2,1)}, u32[]{:S(2)}, u32[]{:S(2)}) async-start(bf16[32,512,128]{2,0,1:T(8,128)(2,1)} %copy.47), calls=%async_computation.2 | async-start | bytes 8388608 | tf_op jit(solution)/shard_map/all_to_all | solution.py:130
  179.0 61.1 %all-to-all-start.1 = ((bf16[512,32,128]{2,1,0:T(8,128)(2,1)}), bf16[512,32,128]{2,1,0:T(8,128)(2,1)}, u32[]{:S(2)}, u32[]{:S(2)}) async-start(bf16[512,32,128]{2,1,0:T(8,128)(2,1)} %copy.45), calls=%async_computation.1 | async-start | bytes 8388608 | tf_op jit(solution)/shard_map/all_to_all | solution.py:129
  185.1 13.3 %slice-start = ((s8[8388608]{0:T(1024)(128)(4,1)}), s8[4194304]{0:T(1024)(128)(4,1)S(1)}, s32[]{:S(2)}) async-start(s8[8388608]{0:T(1024)(128)(4,1)} %bitcast.184), calls=%async_computation.4 | async-start | bytes 8388608
  207.4 36.3 %copy-start.19 = (f32[128]{0:T(128)S(1)}, f32[128]{0:T(128)}, u32[]{:S(2)}) copy-start(f32[128]{0:T(128)} %copy-done.18) | copy-start | bytes 1540
  256.6 16.3 %collective-permute-start.4 = (f32[2,128]{1,0:T(2,128)S(1)}, f32[2,128]{1,0:T(2,128)S(1)}, u32[]{:S(2)}, u32[]{:S(2)}) collective-permute-start(f32[2,128]{1,0:T(2,128)S(1)} %slice.99), channel_id=1, source_target_pairs={{8,0},{16,8},{24,16},{32,24},{40,32},{48,40},{56,48},{64,56},{72,6... | collective-permute-start | bytes 3080 | tf_op jit(solution)/shard_map/ppermute | solution.py:16
  267.1 61.5 %all-to-all-start.3 = ((bf16[512,32,128]{2,1,0:T(8,128)(2,1)}), bf16[512,32,128]{2,1,0:T(8,128)(2,1)}, u32[]{:S(2)}, u32[]{:S(2)}) async-start(bf16[512,32,128]{2,1,0:T(8,128)(2,1)} %copy.53), calls=%async_computation.3 | async-start | bytes 8388608 | tf_op jit(solution)/shard_map/all_to_all | solution.py:138
  335.9 3.2 collective-permute-start.5
  341.6 20.3 %collective-permute-start.8 = (f32[128,512]{1,0:T(8,128)S(1)}, f32[128,512]{1,0:T(8,128)S(1)}, u32[]{:S(2)}, u32[]{:S(2)}) collective-permute-start(f32[128,512]{1,0:T(8,128)S(1)} %get-tuple-element.101), channel_id=1, source_target_pairs={{0,48},{1,49},{2,50},{3,51},{4,52},{5,53},{6,54},{7,55},{8,11},{9,... | collective-permute-start | bytes 786440 | tf_op jit(solution)/shard_map/ppermute | solution.py:58
  344.1 17.7 %collective-permute-start.7 = (f32[128,512]{1,0:T(8,128)S(1)}, f32[128,512]{1,0:T(8,128)S(1)}, u32[]{:S(2)}, u32[]{:S(2)}) collective-permute-start(f32[128,512]{1,0:T(8,128)S(1)} %get-tuple-element.102), channel_id=1, source_target_pairs={{0,32},{1,33},{2,34},{3,35},{4,36},{5,37},{6,38},{7,39},{8,10},{9,... | collective-permute-start | bytes 786440 | tf_op jit(solution)/shard_map/ppermute | solution.py:58
  344.6 17.2 %collective-permute-start.6 = (f32[128,512]{1,0:T(8,128)S(1)}, f32[128,512]{1,0:T(8,128)S(1)}, u32[]{:S(2)}, u32[]{:S(2)}) collective-permute-start(f32[128,512]{1,0:T(8,128)S(1)} %get-tuple-element.103), channel_id=1, source_target_pairs={{0,16},{1,17},{2,18},{3,19},{4,20},{5,21},{6,22},{7,23},{8,9},{9,8... | collective-permute-start | bytes 786440 | tf_op jit(solution)/shard_map/ppermute | solution.py:58
  362.5 17.6 %collective-permute-start.12 = (f32[2,128]{1,0:T(2,128)S(1)}, f32[2,128]{1,0:T(2,128)S(1)}, u32[]{:S(2)}, u32[]{:S(2)}) collective-permute-start(f32[2,128]{1,0:T(2,128)S(1)} %slice.81), channel_id=1, source_target_pairs={{8,0},{16,8},{24,16},{32,24},{40,32},{48,40},{56,48},{64,56},{72,6... | collective-permute-start | bytes 3080 | tf_op jit(solution)/shard_map/ppermute | solution.py:16
  367.1 25.4 %collective-permute-start.11 = (f32[32,512]{1,0:T(8,128)S(1)}, f32[32,512]{1,0:T(8,128)S(1)}, u32[]{:S(2)}, u32[]{:S(2)}) collective-permute-start(f32[32,512]{1,0:T(8,128)S(1)} %get-tuple-element.104), channel_id=1, source_target_pairs={{0,3},{1,2},{2,1},{3,0},{4,7},{5,6},{6,5},{7,4},{8,56},{9,57},{10,... | collective-permute-start | bytes 196616 | tf_op jit(solution)/shard_map/ppermute | solution.py:58
  367.6 24.9 %collective-permute-start.10 = (f32[32,512]{1,0:T(8,128)S(1)}, f32[32,512]{1,0:T(8,128)S(1)}, u32[]{:S(2)}, u32[]{:S(2)}) collective-permute-start(f32[32,512]{1,0:T(8,128)S(1)} %get-tuple-element.105), channel_id=1, source_target_pairs={{0,2},{1,3},{2,0},{3,1},{4,6},{5,7},{6,4},{7,5},{8,40},{9,41},{10,... | collective-permute-start | bytes 196616 | tf_op jit(solution)/shard_map/ppermute | solution.py:58
  370.8 10.7 %copy-start.7 = (bf16[32,512,128]{2,1,0:T(8,128)(2,1)S(1)}, bf16[32,512,128]{2,1,0:T(8,128)(2,1)}, u32[]{:S(2)}) copy-start(bf16[32,512,128]{2,1,0:T(8,128)(2,1)} %param.7) | copy-start | bytes 12582916
  370.8 10.7 %copy-start.17 = (f32[16384]{0:T(1024)S(1)}, f32[16384]{0:T(1024)}, u32[]{:S(2)}) copy-start(f32[16384]{0:T(1024)} %copy-done.16) | copy-start | bytes 196612
  370.8 10.7 %copy-start.21 = (f32[128]{0:T(128)S(1)}, f32[128]{0:T(128)}, u32[]{:S(2)}) copy-start(f32[128]{0:T(128)} %copy-done.20) | copy-start | bytes 1540
  370.8 10.7 %copy-start.23 = (f32[128]{0:T(128)S(1)}, f32[128]{0:T(128)}, u32[]{:S(2)}) copy-start(f32[128]{0:T(128)} %copy-done.22) | copy-start | bytes 1540
  370.8 21.7 %collective-permute-start.9 = (f32[32,512]{1,0:T(8,128)S(1)}, f32[32,512]{1,0:T(8,128)S(1)}, u32[]{:S(2)}, u32[]{:S(2)}) collective-permute-start(f32[32,512]{1,0:T(8,128)S(1)} %get-tuple-element.106), channel_id=1, source_target_pairs={{0,1},{1,0},{2,3},{3,2},{4,5},{5,4},{6,7},{7,6},{8,24},{9,25},{10,... | collective-permute-start | bytes 196616 | tf_op jit(solution)/shard_map/ppermute | solution.py:58
  392.6 3.9 collective-permute-start.16
  396.5 6.5 %collective-permute-start.17 = (f32[16384]{0:T(1024)S(1)}, f32[16384]{0:T(1024)S(1)}, u32[]{:S(2)}, u32[]{:S(2)}) collective-permute-start(f32[16384]{0:T(1024)S(1)} %add.292), channel_id=1, source_target_pairs={{0,2},{1,3},{2,0},{3,1},{4,6},{5,7},{6,4},{7,5},{8,10},{9,11},{10,... | collective-permute-start | bytes 196616 | tf_op jit(solution)/shard_map/ppermute | solution.py:24
  398.9 8.8 %collective-permute-start.15 = (f32[8,512]{1,0:T(8,128)S(1)}, f32[8,512]{1,0:T(8,128)S(1)}, u32[]{:S(2)}, u32[]{:S(2)}) collective-permute-start(f32[8,512]{1,0:T(8,128)S(1)} %get-tuple-element.107), channel_id=1, source_target_pairs={{0,68},{1,69},{2,70},{3,71},{4,64},{5,65},{6,66},{7,67},{8,76},{9,... | collective-permute-start | bytes 49160 | tf_op jit(solution)/shard_map/ppermute | solution.py:58
  402.3 5.4 %collective-permute-start.14 = (f32[8,512]{1,0:T(8,128)S(1)}, f32[8,512]{1,0:T(8,128)S(1)}, u32[]{:S(2)}, u32[]{:S(2)}) collective-permute-start(f32[8,512]{1,0:T(8,128)S(1)} %get-tuple-element.108), channel_id=1, source_target_pairs={{0,4},{1,5},{2,6},{3,7},{4,0},{5,1},{6,2},{7,3},{8,12},{9,13},{10,... | collective-permute-start | bytes 49160 | tf_op jit(solution)/shard_map/ppermute | solution.py:58
  402.3 5.4 %collective-permute-start.13 = (f32[8,512]{1,0:T(8,128)S(1)}, f32[8,512]{1,0:T(8,128)S(1)}, u32[]{:S(2)}, u32[]{:S(2)}) collective-permute-start(f32[8,512]{1,0:T(8,128)S(1)} %get-tuple-element.109), channel_id=1, source_target_pairs={{0,64},{1,65},{2,66},{3,67},{4,68},{5,69},{6,70},{7,71},{8,72},{9,... | collective-permute-start | bytes 49160 | tf_op jit(solution)/shard_map/ppermute | solution.py:58
  403.0 4.7 %collective-permute-start.18 = (f32[16384]{0:T(1024)S(1)}, f32[16384]{0:T(1024)S(1)}, u32[]{:S(2)}, u32[]{:S(2)}) collective-permute-start(f32[16384]{0:T(1024)S(1)} %add.293), channel_id=1, source_target_pairs={{0,4},{1,5},{2,6},{3,7},{4,0},{5,1},{6,2},{7,3},{8,12},{9,13},{10,... | collective-permute-start | bytes 196616 | tf_op jit(solution)/shard_map/ppermute | solution.py:24
  407.8 6.3 %collective-permute-start.29 = (f32[7,128]{1,0:T(8,128)S(1)}, f32[7,128]{1,0:T(8,128)S(1)}, u32[]{:S(2)}, u32[]{:S(2)}) collective-permute-start(f32[7,128]{1,0:T(8,128)S(1)} %pad_maximum_fusion.8), channel_id=1, source_target_pairs={{0,8},{8,0},{16,24},{24,16},{32,40},{40,32},{48,56},{56,48},{64,72... | collective-permute-start | bytes 10760 | tf_op jit(solution)/shard_map/ppermute | solution.py:24
  410.5 14.2 %collective-permute-start.21 = (f32[8,512]{1,0:T(8,128)S(1)}, f32[8,512]{1,0:T(8,128)S(1)}, u32[]{:S(2)}, u32[]{:S(2)}) collective-permute-start(f32[8,512]{1,0:T(8,128)S(1)} %fusion.48), channel_id=1, source_target_pairs={{0,68},{1,69},{2,70},{3,71},{4,64},{5,65},{6,66},{7,67},{8,76},{9,... | collective-permute-start | bytes 49160 | tf_op jit(solution)/shard_map/ppermute | solution.py:58
  413.4 11.2 %collective-permute-start.20 = (f32[8,512]{1,0:T(8,128)S(1)}, f32[8,512]{1,0:T(8,128)S(1)}, u32[]{:S(2)}, u32[]{:S(2)}) collective-permute-start(f32[8,512]{1,0:T(8,128)S(1)} %fusion.48), channel_id=1, source_target_pairs={{0,4},{1,5},{2,6},{3,7},{4,0},{5,1},{6,2},{7,3},{8,12},{9,13},{10,... | collective-permute-start | bytes 49160 | tf_op jit(solution)/shard_map/ppermute | solution.py:58
  413.4 11.2 %collective-permute-start.19 = (f32[8,512]{1,0:T(8,128)S(1)}, f32[8,512]{1,0:T(8,128)S(1)}, u32[]{:S(2)}, u32[]{:S(2)}) collective-permute-start(f32[8,512]{1,0:T(8,128)S(1)} %fusion.48), channel_id=1, source_target_pairs={{0,64},{1,65},{2,66},{3,67},{4,68},{5,69},{6,70},{7,71},{8,72},{9,... | collective-permute-start | bytes 49160 | tf_op jit(solution)/shard_map/ppermute | solution.py:58
  414.1 9.5 %collective-permute-start.30 = (f32[7,128]{1,0:T(8,128)S(1)}, f32[7,128]{1,0:T(8,128)S(1)}, u32[]{:S(2)}, u32[]{:S(2)}) collective-permute-start(f32[7,128]{1,0:T(8,128)S(1)} %fusion.61), channel_id=1, source_target_pairs={{0,16},{8,24},{16,0},{24,8},{32,48},{40,56},{48,32},{56,40},{64,80... | collective-permute-start | bytes 10760 | tf_op jit(solution)/shard_map/ppermute | solution.py:24
  423.6 12.0 %collective-permute-start.31 = (f32[7,128]{1,0:T(8,128)S(1)}, f32[7,128]{1,0:T(8,128)S(1)}, u32[]{:S(2)}, u32[]{:S(2)}) collective-permute-start(f32[7,128]{1,0:T(8,128)S(1)} %add.308), channel_id=1, source_target_pairs={{0,32},{8,40},{16,48},{24,56},{32,0},{40,8},{48,16},{56,24},{64,96... | collective-permute-start | bytes 10760 | tf_op jit(solution)/shard_map/ppermute | solution.py:24
  425.3 4.4 collective-permute-start.24
  427.0 4.6 collective-permute-start.23
  428.0 3.6 collective-permute-start.22
  432.3 9.6 %collective-permute-start.27 = (f32[128,512]{1,0:T(8,128)S(1)}, f32[128,512]{1,0:T(8,128)S(1)}, u32[]{:S(2)}, u32[]{:S(2)}) collective-permute-start(f32[128,512]{1,0:T(8,128)S(1)} %bitcast_select_fusion.2), channel_id=1, source_target_pairs={{0,48},{1,49},{2,50},{3,51},{4,52},{5,53},{6,54},{7,55},{8,11},{9,... | collective-permute-start | bytes 786440 | tf_op jit(solution)/shard_map/ppermute | solution.py:58
  433.5 8.4 %collective-permute-start.26 = (f32[128,512]{1,0:T(8,128)S(1)}, f32[128,512]{1,0:T(8,128)S(1)}, u32[]{:S(2)}, u32[]{:S(2)}) collective-permute-start(f32[128,512]{1,0:T(8,128)S(1)} %bitcast_select_fusion.2), channel_id=1, source_target_pairs={{0,32},{1,33},{2,34},{3,35},{4,36},{5,37},{6,38},{7,39},{8,10},{9,... | collective-permute-start | bytes 786440 | tf_op jit(solution)/shard_map/ppermute | solution.py:58
  434.5 8.1 %collective-permute-start.25 = (f32[128,512]{1,0:T(8,128)S(1)}, f32[128,512]{1,0:T(8,128)S(1)}, u32[]{:S(2)}, u32[]{:S(2)}) collective-permute-start(f32[128,512]{1,0:T(8,128)S(1)} %bitcast_select_fusion.2), channel_id=1, source_target_pairs={{0,16},{1,17},{2,18},{3,19},{4,20},{5,21},{6,22},{7,23},{8,9},{9,8... | collective-permute-start | bytes 786440 | tf_op jit(solution)/shard_map/ppermute | solution.py:58
  435.7 18.7 %collective-permute-start.32 = (f32[7,128]{1,0:T(8,128)S(1)}, f32[7,128]{1,0:T(8,128)S(1)}, u32[]{:S(2)}, u32[]{:S(2)}) collective-permute-start(f32[7,128]{1,0:T(8,128)S(1)} %add.309), channel_id=1, source_target_pairs={{0,64},{8,72},{16,80},{24,88},{32,96},{40,104},{48,112},{56,120},{... | collective-permute-start | bytes 10760 | tf_op jit(solution)/shard_map/ppermute | solution.py:24
  443.4 12.3 %collective-permute-start.28 = (f32[512,512]{1,0:T(8,128)S(1)}, f32[512,512]{1,0:T(8,128)}, u32[]{:S(2)}, u32[]{:S(2)}) collective-permute-start(f32[512,512]{1,0:T(8,128)S(1)} %bitcast_select_fusion), channel_id=1, source_target_pairs={{0,8},{1,9},{2,10},{3,11},{4,12},{5,13},{6,14},{7,15},{8,0},{9,1},... | collective-permute-start | bytes 3145736 | tf_op jit(solution)/shard_map/ppermute | solution.py:58
  (22 other events, 125.6 us)
